TPU v7x, 32 devices: a whole 2x2x4 slice. The times are simulated.
32 devices in a mesh: leaf: 8 (over z, y), coef: 4 (over x, core).
Axes of the slice: x: 2, y: 2, z: 4, core: 2. Of those that a mesh axis runs over, the one named last changes fastest.
Arguments:
- vectors: float32 [16, 16384], P(None, ('leaf', 'coef')), may hold values from -6 to 6
- sigma_point: float32 [1], replicated, may hold values from 0.5 to 1.5
- leaf_basis: bfloat16 [128, 64, 128], P(('leaf', 'coef')), may hold values from -0.5 to 0.5
- near_blocks: bfloat16 [3, 128, 8, 128, 128], P(None, ('leaf', 'coef')), may hold values from -0.109375 to 0.109375
- near_list: int32 [128, 8], P(('leaf', 'coef')), may hold values from 0 to 127, as said below
- coupling: bfloat16 [3, 128, 16, 4096], P(None, 'leaf', 'coef'), may hold values from -0.1875 to 0.1875
- far_list: int32 [128, 16], P('leaf', 'coef'), may hold values from 0 to 127, as said below
- far_rank: int32 [128, 16], P('leaf', 'coef'), may hold values from 0 to 64, as said below
- krylov: float32 [64, 16384], P(None, ('leaf', 'coef')), as said below
Outputs:
- new_block: float32 [16, 16384], P(None, ('leaf', 'coef'))
- coeffs: float32 [64, 16], replicated
- chol_factor: float32 [16, 16], replicated
Inputs may be any that keep to these rules, and one draw needn't show every extreme that they name: near_list[c, 0] = c, and every entry names a cluster held by the same device as c or by the device just before or after it in the order of leaf+coef, 4 consecutive clusters a device. `far_list`: every entry of cluster c names a cluster whose group (clusters taken 16 at a time) is at most 2 groups from the group of c. `far_rank`: 0 marks a padded slot. The rows of krylov are orthonormal.
All inputs are finite; a program needn't handle non-finite values.
Results may differ from a plain program's by a relative error of at most 0.008.
Values may be sent and summed in bfloat16 or wider, within the bound.
No kernel may reach another device: no remote copies, remote signals or barrier semaphores. Data moves between devices by JAX's collectives and lax.ppermute only.
A program may use at most 64 MiB of HBM per device.

v0:
```python
import jax
import jax.numpy as jnp
from jax import lax
from jax.sharding import PartitionSpec as P


def shifted(block, axis, distance):
    devices = range(lax.axis_size(axis))
    route = [(i - distance, i) for i in devices if i - distance in devices]
    return lax.ppermute(block, axis, route)


def extended_2(block, sides, width):
    for axis, dim in sides:
        count = lax.axis_size(axis)
        forward = [(i, i + 1) for i in range(count - 1)]
        backward = [(target, source) for source, target in forward]
        low = lax.ppermute(
            lax.slice_in_dim(block, block.shape[dim] - width, None, axis=dim), axis, forward
        )
        high = lax.ppermute(lax.slice_in_dim(block, 0, width, axis=dim), axis, backward)
        block = jnp.concatenate([low, block, high], axis=dim)
    return block


def group_reach(grouped, offsets):
    pieces = []
    for offset in offsets:
        if offset == 0:
            pieces.append(grouped)
        else:
            pieces.append(shifted(grouped, "leaf", -offset))
    return jnp.concatenate(pieces, axis=0)


def on_device(
    vectors, sigma_point, leaf_basis, near_blocks, near_list, coupling, far_list, far_rank, krylov
):
    highest = lax.Precision.HIGHEST
    local_count, rank_width, leaf_size = leaf_basis.shape
    vec_count = vectors.shape[0]
    near_count = near_list.shape[1]
    slot_count = far_list.shape[1]
    coef_count = lax.axis_size("coef")
    leaf_count = lax.axis_size("leaf")
    group_size = local_count * coef_count
    reach_groups = min(8, leaf_count // 4)
    total_points = local_count * leaf_size * coef_count * leaf_count
    sigma_val = sigma_point[0]
    powers = jnp.stack([jnp.ones((), jnp.float32), sigma_val, sigma_val * sigma_val])
    rounded = vectors.astype(jnp.bfloat16)
    by_cluster = rounded.reshape(vec_count, local_count, leaf_size)
    coarse = jnp.einsum(
        "cki,vci->cvk", leaf_basis, by_cluster, preferred_element_type=jnp.float32
    ).astype(jnp.bfloat16)
    own_rows = coarse.reshape(1, local_count, vec_count * rank_width)
    offsets = list(range(-reach_groups, reach_groups + 1))
    grouped = lax.all_gather(own_rows, "coef", axis=1, tiled=True)
    window = group_reach(grouped, offsets)
    flat_rows = window.reshape(-1, vec_count * rank_width)
    group_pos = lax.axis_index("leaf")
    local_ids = (far_list - (group_pos - reach_groups) * group_size).reshape(-1)
    sources = jnp.take(flat_rows, local_ids, axis=0).reshape(
        group_size, slot_count, vec_count, rank_width
    )
    lane_ids = jnp.arange(rank_width, dtype=jnp.int32)
    keep_mask = lane_ids[None, None, :] < far_rank[:, :, None]
    sources = jnp.where(keep_mask[:, :, None, :], sources, jnp.zeros((), jnp.bfloat16))
    couple = coupling.reshape(3, group_size, slot_count, rank_width, rank_width)
    far_terms = jnp.einsum("jcfkl,cfvl->jcfvk", couple, sources, preferred_element_type=jnp.float32)
    combined = jnp.tensordot(powers, far_terms, 1) * keep_mask[:, :, None, :].astype(jnp.float32)
    partial_far = jnp.sum(combined, axis=1).reshape(group_size, vec_count * rank_width)
    far_hat = lax.psum_scatter(partial_far, "coef", scatter_dimension=0, tiled=True)
    far_round = far_hat.astype(jnp.bfloat16).reshape(local_count, vec_count, rank_width)
    far_part = jnp.einsum("cki,cvk->vci", leaf_basis, far_round, preferred_element_type=jnp.float32)
    extended = extended_2(rounded, ((("leaf", "coef"), 1),), local_count * leaf_size)
    extended = extended.reshape(vec_count, 3 * local_count, leaf_size)
    device_pos = lax.axis_index("leaf") * coef_count + lax.axis_index("coef")
    near_ids = (near_list - (device_pos - 1) * local_count).reshape(-1)
    near_src = jnp.take(extended, near_ids, axis=1).reshape(
        vec_count, local_count, near_count, leaf_size
    )
    near_terms = jnp.einsum(
        "jcnil,vcnl->jvci", near_blocks, near_src, preferred_element_type=jnp.float32
    )
    near_part = jnp.tensordot(powers, near_terms, 1)
    applied = (far_part + near_part).reshape(vec_count, local_count * leaf_size)
    proj_part = jnp.dot(krylov, applied.T, precision=highest)
    coeffs = lax.psum(proj_part, ("leaf", "coef"))
    residue = applied - jnp.dot(coeffs.T, krylov, precision=highest)
    gram_matrix = (
        lax.psum(jnp.dot(residue, residue.T, precision=highest), ("leaf", "coef")) / total_points
    )
    chol_factor = jnp.linalg.cholesky(gram_matrix)
    new_block = jax.scipy.linalg.solve_triangular(chol_factor, residue, lower=True)
    return (new_block, coeffs, chol_factor)


def solution(mesh):
    in_specs = (
        P(None, ("leaf", "coef")),
        P(),
        P(("leaf", "coef"), None, None),
        P(None, ("leaf", "coef"), None, None, None),
        P(("leaf", "coef"), None),
        P(None, "leaf", "coef", None),
        P("leaf", "coef"),
        P("leaf", "coef"),
        P(None, ("leaf", "coef")),
    )
    out_specs = (P(None, ("leaf", "coef")), P(), P())
    return jax.shard_map(
        on_device, mesh=mesh, in_specs=in_specs, out_specs=out_specs, check_vma=False
    )
```

profile of v0, /device:TPU:0, one launch (start us, length us, event | category | flops | bytes accessed | tf_op | source)
XLA Modules:
  0.0 149.5 jit_solution(12520437069913932664)
XLA Ops:
  0.7 1.1 convolution_convert_fusion
  1.9 6.2 %all_gather.3 = bf16[1,16,1024]{2,0,1:T(2,128)(2,1)S(1)} all-gather(bf16[1,4,1024]{2,0,1:T(2,128)(2,1)S(1)} %reshape.165), channel_id=1, replica_groups=mesh['leaf'=8,'coef'=4] {'coef'}, dimensions={1}, use_global_device_ids=true | all-gather | bytes 40960 | tf_op jit(solution)/shard_map/all_gather | solution.py:58
  8.1 4.0 %collective-permute-start = (bf16[1,16,1024]{2,0,1:T(2,128)(2,1)S(1)}, bf16[1,16,1024]{2,0,1:T(2,128)(2,1)S(1)}, u32[]{:S(2)}, u32[]{:S(2)}) collective-permute-start(bf16[1,16,1024]{2,0,1:T(2,128)(2,1)S(1)} %all_gather.3), channel_id=1, source_target_pairs={{0,8},{4,12},{8,16},{12,20},{16,24},{20,28},{1,9},{5,13},{9,17},{1... | collective-permute-start | bytes 98312 | tf_op jit(solution)/shard_map/ppermute | solution.py:10
  12.1 3.4 %collective-permute-start.1 = (bf16[1,16,1024]{2,0,1:T(2,128)(2,1)S(1)}, bf16[1,16,1024]{2,0,1:T(2,128)(2,1)S(1)}, u32[]{:S(2)}, u32[]{:S(2)}) collective-permute-start(bf16[1,16,1024]{2,0,1:T(2,128)(2,1)S(1)} %all_gather.3), channel_id=1, source_target_pairs={{0,4},{4,8},{8,12},{12,16},{16,20},{20,24},{24,28},{1,5},{5,9},{9,... | collective-permute-start | bytes 98312 | tf_op jit(solution)/shard_map/ppermute | solution.py:10
  15.5 1.3 collective-permute-start.2
  17.6 1.7 %collective-permute-start.4 = (bf16[16,512]{1,0:T(8,128)(2,1)S(1)}, bf16[16,512]{1,0:T(8,128)(2,1)S(1)}, u32[]{:S(2)}, u32[]{:S(2)}) collective-permute-start(bf16[16,512]{1,0:T(8,128)(2,1)S(1)} %convert_element_type.17), channel_id=1, source_target_pairs={{0,1},{1,2},{2,3},{3,4},{4,5},{5,6},{6,7},{7,8},{8,9},{9,10},{10,1... | collective-permute-start | bytes 49160 | tf_op jit(solution)/shard_map/ppermute | solution.py:18
  19.3 1.3 collective-permute-start.5
  23.8 5.6 %reshape.136 = bf16[3,16,4,64,64]{4,3,2,1,0:T(8,128)(2,1)} reshape(bf16[3,16,4,4096]{3,2,1,0:T(4,128)(2,1)} %param.14) | data formatting | bytes 3145728 | tf_op jit(solution)/shard_map/reshape | solution.py:69
  31.4 1.3 collective-permute-start.3
  33.3 0.9 fusion.9
  34.3 0.9 fusion.20
  35.1 8.5 %collective-permute-done.3 = bf16[1,16,1024]{2,0,1:T(2,128)(2,1)} collective-permute-done((bf16[1,16,1024]{2,0,1:T(2,128)(2,1)S(1)}, bf16[1,16,1024]{2,0,1:T(2,128)(2,1)}, u32[]{:S(2)}, u32[]{:S(2)}) %collective-permute-start.3) | collective-permute-done | bytes 32800 | tf_op jit(solution)/shard_map/ppermute | solution.py:10
  43.6 1.9 %concatenate.6 = bf16[5,16,1024]{2,0,1:T(8,128)(2,1)} concatenate(bf16[1,16,1024]{2,0,1:T(2,128)(2,1)S(1)} %collective-permute-done, bf16[1,16,1024]{2,0,1:T(2,128)(2,1)S(1)} %collective-permute-done.1, bf16[1,16,1024]{2,0,1:T(2,128)(2,1)S(1)} %all_gather.3, bf16[1,16,1024]{2,0,1:T(2,128)(2,1)} %collective-permute-done.2, bf16[1,16,1024]{2,0,1:T(2,128)(2,1)} %collective-permute-done.3), dimensions={0} | concatenate | bytes 327680 | tf_op jit(solution)/shard_map/concatenate | solution.py:33
  45.5 1.1 copy.42
  47.5 4.2 %fusion.6 = bf16[3,16,4,16,64]{4,3,0,2,1:T(8,128)(2,1)S(1)} fusion(bf16[3,16,4,64,64]{4,3,2,1,0:T(8,128)(2,1)} %reshape.136, bf16[16,4,16,64]{3,2,1,0:T(8,128)(2,1)S(1)} %gather.13, pred[16,4]{1,0:T(8,128)(4,1)S(1)} %copy.39, pred[16,4,64]{2,1,0:T(4,128)(4,1)S(1)} %get-tuple-element.10), kind=kOutput, calls=%fused_computation.8 | convolution fusion | flops 25296896 | bytes 2101312 | tf_op jit(solution)/shard_map/jcfkl,cfvl->jcfvk/dot_general | solution.py:70
  51.8 0.8 fusion.4
  52.7 10.7 %all-reduce = bf16[16,1024]{1,0:T(8,128)(2,1)S(1)} all-reduce(f32[16,1024]{1,0:T(8,128)S(1)} %reshape.137), channel_id=2, replica_groups=mesh['leaf'=8,'coef'=4] {'coef'}, use_global_device_ids=true, to_apply=%region_1.2.clone | all-reduce | flops 16384 | bytes 98304
  63.5 1.0 fusion.13
  64.7 39.9 %psum.14 = f32[64,16]{0,1:T(8,128)S(1)} all-reduce(f32[64,16]{0,1:T(8,128)S(1)} %convolution_bitcast_fusion.1), channel_id=1, replica_groups=mesh['leaf'=8,'coef'=4] {'leaf','coef'}, use_global_device_ids=true, to_apply=%region_2.3 | all-reduce | flops 1024 | bytes 8192 | tf_op jit(solution)/shard_map/psum | solution.py:89
  105.0 38.9 %psum.15 = f32[16,16]{0,1:T(8,128)S(1)} all-reduce(f32[16,16]{0,1:T(8,128)S(1)} %fusion.42), channel_id=1, replica_groups=mesh['leaf'=8,'coef'=4] {'leaf','coef'}, use_global_device_ids=true, to_apply=%region_3.4 | all-reduce | flops 256 | bytes 2048 | tf_op jit(solution)/shard_map/psum | solution.py:92
  144.0 1.5 cholesky.16
  146.1 1.2 select_bitcast_fusion
  147.4 1.2 custom-call.7
  148.6 0.9 fusion.31
  (46 shorter events, 7.8 us)
Async XLA Ops:
  0.6 32.7 %copy-start = (bf16[3,4,8,128,128]{4,3,2,1,0:T(8,128)(2,1)S(1)}, bf16[3,4,8,128,128]{4,3,2,1,0:T(8,128)(2,1)}, u32[]{:S(2)}) copy-start(bf16[3,4,8,128,128]{4,3,2,1,0:T(8,128)(2,1)} %param.12) | copy-start | bytes 9437188
  0.6 29.5 %copy-start.4 = (u32[32]{0:T(128)S(1)}, u32[32]{0:T(128)}, u32[]{:S(2)}) copy-start(u32[32]{0:T(128)} %constant.105) | copy-start | bytes 388
  8.1 27.1 %collective-permute-start = (bf16[1,16,1024]{2,0,1:T(2,128)(2,1)S(1)}, bf16[1,16,1024]{2,0,1:T(2,128)(2,1)S(1)}, u32[]{:S(2)}, u32[]{:S(2)}) collective-permute-start(bf16[1,16,1024]{2,0,1:T(2,128)(2,1)S(1)} %all_gather.3), channel_id=1, source_target_pairs={{0,8},{4,12},{8,16},{12,20},{16,24},{20,28},{1,9},{5,13},{9,17},{1... | collective-permute-start | bytes 98312 | tf_op jit(solution)/shard_map/ppermute | solution.py:10
  12.1 23.0 %collective-permute-start.1 = (bf16[1,16,1024]{2,0,1:T(2,128)(2,1)S(1)}, bf16[1,16,1024]{2,0,1:T(2,128)(2,1)S(1)}, u32[]{:S(2)}, u32[]{:S(2)}) collective-permute-start(bf16[1,16,1024]{2,0,1:T(2,128)(2,1)S(1)} %all_gather.3), channel_id=1, source_target_pairs={{0,4},{4,8},{8,12},{12,16},{16,20},{20,24},{24,28},{1,5},{5,9},{9,... | collective-permute-start | bytes 98312 | tf_op jit(solution)/shard_map/ppermute | solution.py:10
  15.5 19.6 %collective-permute-start.2 = (bf16[1,16,1024]{2,0,1:T(2,128)(2,1)S(1)}, bf16[1,16,1024]{2,0,1:T(2,128)(2,1)}, u32[]{:S(2)}, u32[]{:S(2)}) collective-permute-start(bf16[1,16,1024]{2,0,1:T(2,128)(2,1)S(1)} %all_gather.3), channel_id=1, source_target_pairs={{4,0},{8,4},{12,8},{16,12},{20,16},{24,20},{28,24},{5,1},{9,5},{13... | collective-permute-start | bytes 98312 | tf_op jit(solution)/shard_map/ppermute | solution.py:10
  17.6 13.8 %collective-permute-start.4 = (bf16[16,512]{1,0:T(8,128)(2,1)S(1)}, bf16[16,512]{1,0:T(8,128)(2,1)S(1)}, u32[]{:S(2)}, u32[]{:S(2)}) collective-permute-start(bf16[16,512]{1,0:T(8,128)(2,1)S(1)} %convert_element_type.17), channel_id=1, source_target_pairs={{0,1},{1,2},{2,3},{3,4},{4,5},{5,6},{6,7},{7,8},{8,9},{9,10},{10,1... | collective-permute-start | bytes 49160 | tf_op jit(solution)/shard_map/ppermute | solution.py:18
  19.3 13.4 %collective-permute-start.5 = (bf16[16,512]{1,0:T(8,128)(2,1)S(1)}, bf16[16,512]{1,0:T(8,128)(2,1)S(1)}, u32[]{:S(2)}, u32[]{:S(2)}) collective-permute-start(bf16[16,512]{1,0:T(8,128)(2,1)S(1)} %convert_element_type.17), channel_id=1, source_target_pairs={{1,0},{2,1},{3,2},{4,3},{5,4},{6,5},{7,6},{8,7},{9,8},{10,9},{11,1... | collective-permute-start | bytes 49160 | tf_op jit(solution)/shard_map/ppermute | solution.py:21
  31.4 12.2 %collective-permute-start.3 = (bf16[1,16,1024]{2,0,1:T(2,128)(2,1)S(1)}, bf16[1,16,1024]{2,0,1:T(2,128)(2,1)}, u32[]{:S(2)}, u32[]{:S(2)}) collective-permute-start(bf16[1,16,1024]{2,0,1:T(2,128)(2,1)S(1)} %all_gather.3), channel_id=1, source_target_pairs={{8,0},{12,4},{16,8},{20,12},{24,16},{28,20},{9,1},{13,5},{17,9},{2... | collective-permute-start | bytes 98312 | tf_op jit(solution)/shard_map/ppermute | solution.py:10
  47.5 5.1 %copy-start.2 = (f32[16,4,64]{2,1,0:T(4,128)S(1)}, f32[16,4,64]{2,1,0:T(4,128)}, u32[]{:S(2)}) copy-start(f32[16,4,64]{2,1,0:T(4,128)} %get-tuple-element.9) | copy-start | bytes 49156
  47.5 17.0 %copy-start.1 = (f32[64,512]{1,0:T(8,128)S(1)}, f32[64,512]{1,0:T(8,128)}, u32[]{:S(2)}) copy-start(f32[64,512]{1,0:T(8,128)} %param.17) | copy-start | bytes 393220
  104.6 44.8 %copy-start.3 = (f32[64,16]{0,1:T(8,128)}, f32[64,16]{0,1:T(8,128)S(1)}, u32[]{:S(2)}) copy-start(f32[64,16]{0,1:T(8,128)S(1)} %psum.14) | copy-start | bytes 12292
where the time goes:
time: 150 us; the launch traced here: 149 us
  blocking collectives  95.8 us (64%)
  starting transfers between devices  13 us (9%)
  local copies, waits for them, and re-layouts  12.2 us (8%)
  matrix products  10.3 us (7%)
  waiting for transfers between devices  8.5 us (6%)
  other arithmetic  7.57 us (5%)
  between operations  2.17 us (1%)
    psum x1, blocking collectives, on_device(): coeffs = lax.psum(proj_part, ('leaf', 'coef'))  39.9 us
    psum x1, blocking collectives, on_device(): lax.psum(jnp.dot(residue, residue.T, precision=highest), ('leaf', 'coef'))  38.9 us
    unnamed x1, blocking collectives  10.7 us
    ppermute x4, starting transfers between devices, shifted(): return lax.ppermute(block, axis, route)  10 us
    ppermute x4, waiting for transfers between devices, shifted(): return lax.ppermute(block, axis, route)  8.49 us
    all_gather x1, blocking collectives, on_device(): grouped = lax.all_gather(own_rows, 'coef', axis=1, tiled=True)  6.18 us
    reshape x1, local copies, waits for them, and re-layouts, on_device(): couple = coupling.reshape(3, group_size, slot_count, rank_width, rank_width)  5.65 us
    dot_general x1, matrix products, on_device(): jnp.einsum('jcfkl,cfvl->jcfvk', couple, sources, preferred_element_type=j...  4.24 us
  transfers between devices with their start and end apart: 6, of which 1 were waited for; matrix products, arithmetic and copies ran while one was open for 8% of the time, Pallas kernels for 0%

commit v1 on v0

--- a/solution.py
+++ b/solution.py
@@ -21,6 +21,42 @@
         high = lax.ppermute(lax.slice_in_dim(block, 0, width, axis=dim), axis, backward)
         block = jnp.concatenate([low, block, high], axis=dim)
     return block
+
+
+def is_power_of_two(count):
+    return count > 0 and count & (count - 1) == 0
+
+
+def butterfly_sum(block, axes):
+    total = 1
+    for axis in axes:
+        total *= lax.axis_size(axis)
+    if not is_power_of_two(total):
+        return lax.psum(block, axes)
+    distance = 1
+    while distance < total:
+        route = [(i, i ^ distance) for i in range(total)]
+        block = block + lax.ppermute(block, axes, route)
+        distance *= 2
+    return block
+
+
+def butterfly_scatter(block, axis):
+    count = lax.axis_size(axis)
+    if not is_power_of_two(count):
+        return lax.psum_scatter(block, axis, scatter_dimension=0, tiled=True)
+    me = lax.axis_index(axis)
+    parts = block.reshape(count, -1, *block.shape[1:])
+    distance = 1
+    while distance < count:
+        bit = (me // distance) % 2
+        pairs = parts.reshape(parts.shape[0] // 2, 2, *parts.shape[1:])
+        keep = lax.dynamic_index_in_dim(pairs, bit, axis=1, keepdims=False)
+        give = lax.dynamic_index_in_dim(pairs, 1 - bit, axis=1, keepdims=False)
+        route = [(i, i ^ distance) for i in range(count)]
+        parts = keep + lax.ppermute(give, axis, route)
+        distance *= 2
+    return parts.reshape(-1, *block.shape[1:])
 
 
 def group_reach(grouped, offsets):
@@ -70,7 +106,7 @@
     far_terms = jnp.einsum("jcfkl,cfvl->jcfvk", couple, sources, preferred_element_type=jnp.float32)
     combined = jnp.tensordot(powers, far_terms, 1) * keep_mask[:, :, None, :].astype(jnp.float32)
     partial_far = jnp.sum(combined, axis=1).reshape(group_size, vec_count * rank_width)
-    far_hat = lax.psum_scatter(partial_far, "coef", scatter_dimension=0, tiled=True)
+    far_hat = butterfly_scatter(partial_far, "coef")
     far_round = far_hat.astype(jnp.bfloat16).reshape(local_count, vec_count, rank_width)
     far_part = jnp.einsum("cki,cvk->vci", leaf_basis, far_round, preferred_element_type=jnp.float32)
     extended = extended_2(rounded, ((("leaf", "coef"), 1),), local_count * leaf_size)
@@ -85,12 +121,20 @@
     )
     near_part = jnp.tensordot(powers, near_terms, 1)
     applied = (far_part + near_part).reshape(vec_count, local_count * leaf_size)
+    basis_count = krylov.shape[0]
+    both_axes = ("leaf", "coef")
     proj_part = jnp.dot(krylov, applied.T, precision=highest)
-    coeffs = lax.psum(proj_part, ("leaf", "coef"))
+    self_part = jnp.dot(applied, applied.T, precision=highest)
+    summed = butterfly_sum(jnp.concatenate([proj_part, self_part], axis=0), both_axes)
+    coeffs = summed[:basis_count]
+    outer = summed[basis_count:]
     residue = applied - jnp.dot(coeffs.T, krylov, precision=highest)
-    gram_matrix = (
-        lax.psum(jnp.dot(residue, residue.T, precision=highest), ("leaf", "coef")) / total_points
-    )
+    short_gram = (outer - jnp.dot(coeffs.T, coeffs, precision=highest)) / total_points
+    kept = jnp.diagonal(short_gram) * (64 * total_points) >= jnp.diagonal(outer)
+    def exact_gram():
+        part = jnp.dot(residue, residue.T, precision=highest)
+        return butterfly_sum(part, both_axes) / total_points
+    gram_matrix = lax.cond(jnp.all(kept), lambda: short_gram, exact_gram)
     chol_factor = jnp.linalg.cholesky(gram_matrix)
     new_block = jax.scipy.linalg.solve_triangular(chol_factor, residue, lower=True)
     return (new_block, coeffs, chol_factor)

time: 150 us -> 82.2 us (0.55)
  blocking collectives: 95.8 us -> 6.18 us
  starting transfers between devices: 13 us -> 25.3 us
  waiting for transfers between devices: 8.5 us -> 14.6 us
  other arithmetic: 7.57 us -> 10.3 us
    psum x2 -> x0, blocking collectives: 78.9 us -> none  [the longest x1 39.9 us: on_device(): coeffs = lax.psum(proj_part, ('leaf', 'coef'))]
    unnamed x1 -> x0, blocking collectives: 10.7 us -> none
    ppermute x0 -> x7, waiting for transfers between devices: none -> 10.5 us  [the longest x5 8.65 us: butterfly_sum(): block = block + lax.ppermute(block, axes, route)]
    ppermute x0 -> x7, starting transfers between devices: none -> 10.3 us  [the longest x5 8.32 us: butterfly_sum(): block = block + lax.ppermute(block, axes, route)]
    ppermute x4, waiting for transfers between devices: 8.49 us -> 4.09 us  [shifted(): return lax.ppermute(block, axis, route)]
    ppermute x1, starting transfers between devices: 1.68 us -> 3.63 us  [extended_2(): lax.ppermute(lax.slice_in_dim(block, block.shape[dim] - width, None, axis...]
  transfers between devices with their start and end apart: 6 -> 13, of which waited for: 1 -> 7; matrix products, arithmetic and copies ran while one was open for 8% -> 18% of each run, Pallas kernels for 0% -> 0%
where the time goes in v1:
time: 82.2 us; the launch traced here: 81.5 us
  starting transfers between devices  25.3 us (31%)
  waiting for transfers between devices  14.6 us (18%)
  local copies, waits for them, and re-layouts  13.2 us (16%)
  other arithmetic  10.3 us (13%)
  matrix products  9.79 us (12%)
  blocking collectives  6.18 us (8%)
  between operations  2.22 us (3%)
    ppermute x4, starting transfers between devices, shifted(): return lax.ppermute(block, axis, route)  10 us
    ppermute x5, waiting for transfers between devices, butterfly_sum(): block = block + lax.ppermute(block, axes, route)  8.65 us
    ppermute x5, starting transfers between devices, butterfly_sum(): block = block + lax.ppermute(block, axes, route)  8.32 us
    all_gather x1, blocking collectives, on_device(): grouped = lax.all_gather(own_rows, 'coef', axis=1, tiled=True)  6.18 us
    reshape x1, local copies, waits for them, and re-layouts, on_device(): couple = coupling.reshape(3, group_size, slot_count, rank_width, rank_width)  5.62 us
    dot_general x1, matrix products, on_device(): jnp.einsum('jcfkl,cfvl->jcfvk', couple, sources, preferred_element_type=j...  4.22 us
    ppermute x4, waiting for transfers between devices, shifted(): return lax.ppermute(block, axis, route)  4.09 us
    ppermute x1, starting transfers between devices, extended_2(): lax.ppermute(lax.slice_in_dim(block, block.shape[dim] - width, None, axis...  3.63 us
  transfers between devices with their start and end apart: 13, of which 7 were waited for; matrix products, arithmetic and copies ran while one was open for 18% of the time, Pallas kernels for 0%

profile of v1, /device:TPU:0, one launch (start us, length us, event | category | flops | bytes accessed | tf_op | source)
XLA Modules:
  0.0 81.5 jit_solution(5222524911088985280)
XLA Ops:
  1.9 6.2 %all_gather.3 = bf16[1,16,1024]{2,0,1:T(2,128)(2,1)S(1)} all-gather(bf16[1,4,1024]{2,0,1:T(2,128)(2,1)S(1)} %reshape.179), channel_id=1, replica_groups=mesh['leaf'=8,'coef'=4] {'coef'}, dimensions={1}, use_global_device_ids=true | all-gather | bytes 40960 | tf_op jit(solution)/shard_map/all_gather | solution.py:94
  8.1 4.0 %collective-permute-start.5 = (bf16[1,16,1024]{2,0,1:T(2,128)(2,1)S(1)}, bf16[1,16,1024]{2,0,1:T(2,128)(2,1)S(1)}, u32[]{:S(2)}, u32[]{:S(2)}) collective-permute-start(bf16[1,16,1024]{2,0,1:T(2,128)(2,1)S(1)} %all_gather.3), channel_id=1, source_target_pairs={{0,8},{4,12},{8,16},{12,20},{16,24},{20,28},{1,9},{5,13},{9,17},{1... | collective-permute-start | bytes 98312 | tf_op jit(solution)/shard_map/ppermute | solution.py:10
  12.1 3.4 %collective-permute-start.6 = (bf16[1,16,1024]{2,0,1:T(2,128)(2,1)S(1)}, bf16[1,16,1024]{2,0,1:T(2,128)(2,1)S(1)}, u32[]{:S(2)}, u32[]{:S(2)}) collective-permute-start(bf16[1,16,1024]{2,0,1:T(2,128)(2,1)S(1)} %all_gather.3), channel_id=1, source_target_pairs={{0,4},{4,8},{8,12},{12,16},{16,20},{20,24},{24,28},{1,5},{5,9},{9,... | collective-permute-start | bytes 98312 | tf_op jit(solution)/shard_map/ppermute | solution.py:10
  15.5 1.3 %collective-permute-start.7 = (bf16[1,16,1024]{2,0,1:T(2,128)(2,1)S(1)}, bf16[1,16,1024]{2,0,1:T(2,128)(2,1)S(1)}, u32[]{:S(2)}, u32[]{:S(2)}) collective-permute-start(bf16[1,16,1024]{2,0,1:T(2,128)(2,1)S(1)} %all_gather.3), channel_id=1, source_target_pairs={{4,0},{8,4},{12,8},{16,12},{20,16},{24,20},{28,24},{5,1},{9,5},{13... | collective-permute-start | bytes 98312 | tf_op jit(solution)/shard_map/ppermute | solution.py:10
  17.6 1.3 %collective-permute-start.12 = (bf16[16,512]{1,0:T(8,128)(2,1)S(1)}, bf16[16,512]{1,0:T(8,128)(2,1)S(1)}, u32[]{:S(2)}, u32[]{:S(2)}) collective-permute-start(bf16[16,512]{1,0:T(8,128)(2,1)S(1)} %convert_element_type.24), channel_id=1, source_target_pairs={{1,0},{2,1},{3,2},{4,3},{5,4},{6,5},{7,6},{8,7},{9,8},{10,9},{11,1... | collective-permute-start | bytes 49160 | tf_op jit(solution)/shard_map/ppermute | solution.py:21
  18.9 3.6 %collective-permute-start.11 = (bf16[16,512]{1,0:T(8,128)(2,1)S(1)}, bf16[16,512]{1,0:T(8,128)(2,1)}, u32[]{:S(2)}, u32[]{:S(2)}) collective-permute-start(bf16[16,512]{1,0:T(8,128)(2,1)S(1)} %convert_element_type.24), channel_id=1, source_target_pairs={{0,1},{1,2},{2,3},{3,4},{4,5},{5,6},{6,7},{7,8},{8,9},{9,10},{10,1... | collective-permute-start | bytes 49160 | tf_op jit(solution)/shard_map/ppermute | solution.py:18
  26.7 5.6 %reshape.139 = bf16[3,16,4,64,64]{4,3,2,1,0:T(8,128)(2,1)} reshape(bf16[3,16,4,4096]{3,2,1,0:T(4,128)(2,1)} %param.16) | data formatting | bytes 3145728 | tf_op jit(solution)/shard_map/reshape | solution.py:105
  33.2 1.3 %collective-permute-start.8 = (bf16[1,16,1024]{2,0,1:T(2,128)(2,1)S(1)}, bf16[1,16,1024]{2,0,1:T(2,128)(2,1)S(1)}, u32[]{:S(2)}, u32[]{:S(2)}) collective-permute-start(bf16[1,16,1024]{2,0,1:T(2,128)(2,1)S(1)} %all_gather.3), channel_id=1, source_target_pairs={{8,0},{12,4},{16,8},{20,12},{24,16},{28,20},{9,1},{13,5},{17,9},{2... | collective-permute-start | bytes 98312 | tf_op jit(solution)/shard_map/ppermute | solution.py:10
  35.2 1.4 %gather_fusion.1 = bf16[32,16,128]{2,1,0:T(8,128)(2,1)} fusion(bf16[16,12,128]{2,0,1:T(8,128)(2,1)S(1)} %copy_bitcast_fusion, s32[1024]{0:T(1024)} %pad_clamp_fusion), kind=kCustom, calls=%fused_computation.1 | custom fusion | bytes 262272 | tf_op jit(solution)/shard_map/jit(_take)/gather | solution.py:116
  36.6 4.1 %collective-permute-done.8 = bf16[1,16,1024]{2,0,1:T(2,128)(2,1)S(1)} collective-permute-done((bf16[1,16,1024]{2,0,1:T(2,128)(2,1)S(1)}, bf16[1,16,1024]{2,0,1:T(2,128)(2,1)S(1)}, u32[]{:S(2)}, u32[]{:S(2)}) %collective-permute-start.8) | collective-permute-done | bytes 32800 | tf_op jit(solution)/shard_map/ppermute | solution.py:10
  43.8 4.2 %fusion.6 = bf16[3,16,4,16,64]{4,3,0,2,1:T(8,128)(2,1)S(1)} fusion(bf16[3,16,4,64,64]{4,3,2,1,0:T(8,128)(2,1)} %reshape.139, bf16[16,4,16,64]{3,2,1,0:T(8,128)(2,1)S(1)} %gather.20, pred[16,4]{1,0:T(8,128)(4,1)S(1)} %copy.42, pred[16,4,64]{2,1,0:T(4,128)(4,1)S(1)} %get-tuple-element.17), kind=kOutput, calls=%fused_computation.11 | convolution fusion | flops 25296896 | bytes 2101312 | tf_op jit(solution)/shard_map/jcfkl,cfvl->jcfvk/dot_general | solution.py:106
  49.3 1.8 %fusion.9 = bf16[3,16,4,128]{3,1,0,2:T(8,128)(2,1)S(1)} fusion(bf16[3,4,8,128,128]{4,3,2,1,0:T(8,128)(2,1)S(1)} %copy-done, bf16[16,4,8,128]{3,0,2,1:T(8,128)(2,1)} %bitcast.103, pred[4,8]{1,0:T(4,128)(4,1)S(1)} %copy-done.6), kind=kOutput, calls=%fused_computation.12 | convolution fusion | flops 50397184 | bytes 3325984 | tf_op jit(solution)/shard_map/jcnil,vcnl->jvci/dot_general | solution.py:119
  51.2 1.8 %collective-permute-start.10 = (f32[1,4,1024]{2,1,0:T(4,128)S(1)}, f32[1,4,1024]{2,1,0:T(4,128)S(1)}, u32[]{:S(2)}, u32[]{:S(2)}) collective-permute-start(f32[1,4,1024]{2,1,0:T(4,128)S(1)} %constant_dynamic-slice_fusion), channel_id=1, source_target_pairs={{0,2},{1,3},{2,0},{3,1},{4,6},{5,7},{6,4},{7,5},{8,10},{9,11},{10,... | collective-permute-start | bytes 49160 | tf_op jit(solution)/shard_map/ppermute | solution.py:57
  53.2 1.8 %collective-permute-done.10 = f32[1,4,1024]{2,1,0:T(4,128)S(1)} collective-permute-done((f32[1,4,1024]{2,1,0:T(4,128)S(1)}, f32[1,4,1024]{2,1,0:T(4,128)S(1)}, u32[]{:S(2)}, u32[]{:S(2)}) %collective-permute-start.10) | collective-permute-done | bytes 16416 | tf_op jit(solution)/shard_map/ppermute | solution.py:57
  57.0 1.7 %collective-permute-start.14 = (f32[80,16]{0,1:T(8,128)S(1)}, f32[80,16]{0,1:T(8,128)S(1)}, u32[]{:S(2)}, u32[]{:S(2)}) collective-permute-start(f32[80,16]{0,1:T(8,128)S(1)} %fusion.56), channel_id=1, source_target_pairs={{0,2},{1,3},{2,0},{3,1},{4,6},{5,7},{6,4},{7,5},{8,10},{9,11},{10,... | collective-permute-start | bytes 15368 | tf_op jit(solution)/shard_map/ppermute | solution.py:39
  58.7 2.0 %collective-permute-done.14 = f32[80,16]{0,1:T(8,128)S(1)} collective-permute-done((f32[80,16]{0,1:T(8,128)S(1)}, f32[80,16]{0,1:T(8,128)S(1)}, u32[]{:S(2)}, u32[]{:S(2)}) %collective-permute-start.14) | collective-permute-done | bytes 5152 | tf_op jit(solution)/shard_map/ppermute | solution.py:39
  60.7 1.4 %collective-permute-start.15 = (f32[80,16]{0,1:T(8,128)S(1)}, f32[80,16]{0,1:T(8,128)S(1)}, u32[]{:S(2)}, u32[]{:S(2)}) collective-permute-start(f32[80,16]{0,1:T(8,128)S(1)} %add.150), channel_id=1, source_target_pairs={{0,4},{1,5},{2,6},{3,7},{4,0},{5,1},{6,2},{7,3},{8,12},{9,13},{10,... | collective-permute-start | bytes 15368 | tf_op jit(solution)/shard_map/ppermute | solution.py:39
  62.0 2.3 %collective-permute-done.15 = f32[80,16]{0,1:T(8,128)S(1)} collective-permute-done((f32[80,16]{0,1:T(8,128)S(1)}, f32[80,16]{0,1:T(8,128)S(1)}, u32[]{:S(2)}, u32[]{:S(2)}) %collective-permute-start.15) | collective-permute-done | bytes 5152 | tf_op jit(solution)/shard_map/ppermute | solution.py:39
  64.3 2.2 %collective-permute-start.16 = (f32[80,16]{0,1:T(8,128)S(1)}, f32[80,16]{0,1:T(8,128)S(1)}, u32[]{:S(2)}, u32[]{:S(2)}) collective-permute-start(f32[80,16]{0,1:T(8,128)S(1)} %add.151), channel_id=1, source_target_pairs={{0,8},{1,9},{2,10},{3,11},{4,12},{5,13},{6,14},{7,15},{8,0},{9,1},... | collective-permute-start | bytes 15368 | tf_op jit(solution)/shard_map/ppermute | solution.py:39
  66.5 1.6 %collective-permute-done.16 = f32[80,16]{0,1:T(8,128)S(1)} collective-permute-done((f32[80,16]{0,1:T(8,128)S(1)}, f32[80,16]{0,1:T(8,128)S(1)}, u32[]{:S(2)}, u32[]{:S(2)}) %collective-permute-start.16) | collective-permute-done | bytes 5152 | tf_op jit(solution)/shard_map/ppermute | solution.py:39
  68.2 3.0 %collective-permute-start.17 = (f32[80,16]{0,1:T(8,128)S(1)}, f32[80,16]{0,1:T(8,128)S(1)}, u32[]{:S(2)}, u32[]{:S(2)}) collective-permute-start(f32[80,16]{0,1:T(8,128)S(1)} %add.152), channel_id=1, source_target_pairs={{0,16},{1,17},{2,18},{3,19},{4,20},{5,21},{6,22},{7,23},{8,24},{9,... | collective-permute-start | bytes 15368 | tf_op jit(solution)/shard_map/ppermute | solution.py:39
  71.2 1.6 %collective-permute-done.17 = f32[80,16]{0,1:T(8,128)S(1)} collective-permute-done((f32[80,16]{0,1:T(8,128)S(1)}, f32[80,16]{0,1:T(8,128)S(1)}, u32[]{:S(2)}, u32[]{:S(2)}) %collective-permute-start.17) | collective-permute-done | bytes 5152 | tf_op jit(solution)/shard_map/ppermute | solution.py:39
  76.0 1.5 %cholesky.16 = f32[16,16]{1,0:T(8,128)S(1)} custom-call(f32[16,16]{1,0:T(8,128)S(1)} %fusion.33), custom_call_target="Cholesky" | custom-call | tf_op jit(solution)/shard_map/jit(cholesky)/cholesky | solution.py:138
  78.2 1.2 %select_bitcast_fusion = (f32[1,16,16]{2,1,0:T(8,128)S(1)}, f32[16,16]{1,0:T(8,128)}) fusion(f32[16,16]{1,0:T(8,128)S(1)} %cholesky.16, pred[]{:T(512)} %compare_reduce_fusion), kind=kLoop, calls=%fused_computation.50 | loop fusion | flops 1024 | bytes 3073 | tf_op jit(solution)/shard_map/jit(_solve_triangular)/triangular_solve | solution.py:139
  (76 shorter events, 19.1 us)
Async XLA Ops:
  0.6 48.7 %copy-start = (bf16[3,4,8,128,128]{4,3,2,1,0:T(8,128)(2,1)S(1)}, bf16[3,4,8,128,128]{4,3,2,1,0:T(8,128)(2,1)}, u32[]{:S(2)}) copy-start(bf16[3,4,8,128,128]{4,3,2,1,0:T(8,128)(2,1)} %param.14) | copy-start | bytes 9437188
  8.1 28.5 %collective-permute-start.5 = (bf16[1,16,1024]{2,0,1:T(2,128)(2,1)S(1)}, bf16[1,16,1024]{2,0,1:T(2,128)(2,1)S(1)}, u32[]{:S(2)}, u32[]{:S(2)}) collective-permute-start(bf16[1,16,1024]{2,0,1:T(2,128)(2,1)S(1)} %all_gather.3), channel_id=1, source_target_pairs={{0,8},{4,12},{8,16},{12,20},{16,24},{20,28},{1,9},{5,13},{9,17},{1... | collective-permute-start | bytes 98312 | tf_op jit(solution)/shard_map/ppermute | solution.py:10
  12.1 24.5 %collective-permute-start.6 = (bf16[1,16,1024]{2,0,1:T(2,128)(2,1)S(1)}, bf16[1,16,1024]{2,0,1:T(2,128)(2,1)S(1)}, u32[]{:S(2)}, u32[]{:S(2)}) collective-permute-start(bf16[1,16,1024]{2,0,1:T(2,128)(2,1)S(1)} %all_gather.3), channel_id=1, source_target_pairs={{0,4},{4,8},{8,12},{12,16},{16,20},{20,24},{24,28},{1,5},{5,9},{9,... | collective-permute-start | bytes 98312 | tf_op jit(solution)/shard_map/ppermute | solution.py:10
  15.5 21.1 %collective-permute-start.7 = (bf16[1,16,1024]{2,0,1:T(2,128)(2,1)S(1)}, bf16[1,16,1024]{2,0,1:T(2,128)(2,1)S(1)}, u32[]{:S(2)}, u32[]{:S(2)}) collective-permute-start(bf16[1,16,1024]{2,0,1:T(2,128)(2,1)S(1)} %all_gather.3), channel_id=1, source_target_pairs={{4,0},{8,4},{12,8},{16,12},{20,16},{24,20},{28,24},{5,1},{9,5},{13... | collective-permute-start | bytes 98312 | tf_op jit(solution)/shard_map/ppermute | solution.py:10
  17.6 15.6 %collective-permute-start.12 = (bf16[16,512]{1,0:T(8,128)(2,1)S(1)}, bf16[16,512]{1,0:T(8,128)(2,1)S(1)}, u32[]{:S(2)}, u32[]{:S(2)}) collective-permute-start(bf16[16,512]{1,0:T(8,128)(2,1)S(1)} %convert_element_type.24), channel_id=1, source_target_pairs={{1,0},{2,1},{3,2},{4,3},{5,4},{6,5},{7,6},{8,7},{9,8},{10,9},{11,1... | collective-permute-start | bytes 49160 | tf_op jit(solution)/shard_map/ppermute | solution.py:21
  18.9 15.6 %collective-permute-start.11 = (bf16[16,512]{1,0:T(8,128)(2,1)S(1)}, bf16[16,512]{1,0:T(8,128)(2,1)}, u32[]{:S(2)}, u32[]{:S(2)}) collective-permute-start(bf16[16,512]{1,0:T(8,128)(2,1)S(1)} %convert_element_type.24), channel_id=1, source_target_pairs={{0,1},{1,2},{2,3},{3,4},{4,5},{5,6},{6,7},{7,8},{8,9},{9,10},{10,1... | collective-permute-start | bytes 49160 | tf_op jit(solution)/shard_map/ppermute | solution.py:18
  33.1 1.3 %copy-start.5 = (bf16[16,512]{1,0:T(8,128)(2,1)}, bf16[16,512]{1,0:T(8,128)(2,1)S(1)}, u32[]{:S(2)}) copy-start(bf16[16,512]{1,0:T(8,128)(2,1)S(1)} %collective-permute-done.12) | copy-start | bytes 49156
  33.2 7.5 %collective-permute-start.8 = (bf16[1,16,1024]{2,0,1:T(2,128)(2,1)S(1)}, bf16[1,16,1024]{2,0,1:T(2,128)(2,1)S(1)}, u32[]{:S(2)}, u32[]{:S(2)}) collective-permute-start(bf16[1,16,1024]{2,0,1:T(2,128)(2,1)S(1)} %all_gather.3), channel_id=1, source_target_pairs={{8,0},{12,4},{16,8},{20,12},{24,16},{28,20},{9,1},{13,5},{17,9},{2... | collective-permute-start | bytes 98312 | tf_op jit(solution)/shard_map/ppermute | solution.py:10
  43.8 5.0 %copy-start.4 = (f32[16,4,64]{2,1,0:T(4,128)S(1)}, f32[16,4,64]{2,1,0:T(4,128)}, u32[]{:S(2)}) copy-start(f32[16,4,64]{2,1,0:T(4,128)} %get-tuple-element.16) | copy-start | bytes 49156
  43.8 5.5 %copy-start.6 = (pred[4,8]{1,0:T(4,128)(4,1)S(1)}, pred[4,8]{1,0:T(4,128)(4,1)}, u32[]{:S(2)}) copy-start(pred[4,8]{1,0:T(4,128)(4,1)} %get-tuple-element.12) | copy-start | bytes 100
  48.1 7.1 %copy-start.3 = (bf16[4,64,128]{2,1,0:T(8,128)(2,1)S(1)}, bf16[4,64,128]{2,1,0:T(8,128)(2,1)}, u32[]{:S(2)}) copy-start(bf16[4,64,128]{2,1,0:T(8,128)(2,1)} %param.13) | copy-start | bytes 196612
  48.1 7.4 %copy-start.1 = (f32[64,512]{1,0:T(8,128)S(1)}, f32[64,512]{1,0:T(8,128)}, u32[]{:S(2)}) copy-start(f32[64,512]{1,0:T(8,128)} %param.19) | copy-start | bytes 393220
  49.1 2.1 %collective-permute-start.9 = (f32[2,4,1024]{2,1,0:T(4,128)S(1)}, f32[2,4,1024]{2,1,0:T(4,128)S(1)}, u32[]{:S(2)}, u32[]{:S(2)}) collective-permute-start(f32[2,4,1024]{2,1,0:T(4,128)S(1)} %dynamic-slice_bitcast_fusion), channel_id=1, source_target_pairs={{0,1},{1,0},{2,3},{3,2},{4,5},{5,4},{6,7},{7,6},{8,9},{9,8},{10,11... | collective-permute-start | bytes 98312 | tf_op jit(solution)/shard_map/ppermute | solution.py:57
  51.2 3.8 %collective-permute-start.10 = (f32[1,4,1024]{2,1,0:T(4,128)S(1)}, f32[1,4,1024]{2,1,0:T(4,128)S(1)}, u32[]{:S(2)}, u32[]{:S(2)}) collective-permute-start(f32[1,4,1024]{2,1,0:T(4,128)S(1)} %constant_dynamic-slice_fusion), channel_id=1, source_target_pairs={{0,2},{1,3},{2,0},{3,1},{4,6},{5,7},{6,4},{7,5},{8,10},{9,11},{10,... | collective-permute-start | bytes 49160 | tf_op jit(solution)/shard_map/ppermute | solution.py:57
  55.8 1.2 %collective-permute-start.13 = (f32[80,16]{0,1:T(8,128)S(1)}, f32[80,16]{0,1:T(8,128)S(1)}, u32[]{:S(2)}, u32[]{:S(2)}) collective-permute-start(f32[80,16]{0,1:T(8,128)S(1)} %pad_maximum_fusion), channel_id=1, source_target_pairs={{0,1},{1,0},{2,3},{3,2},{4,5},{5,4},{6,7},{7,6},{8,9},{9,8},{10,11... | collective-permute-start | bytes 15368 | tf_op jit(solution)/shard_map/ppermute | solution.py:39
  57.0 3.7 %collective-permute-start.14 = (f32[80,16]{0,1:T(8,128)S(1)}, f32[80,16]{0,1:T(8,128)S(1)}, u32[]{:S(2)}, u32[]{:S(2)}) collective-permute-start(f32[80,16]{0,1:T(8,128)S(1)} %fusion.56), channel_id=1, source_target_pairs={{0,2},{1,3},{2,0},{3,1},{4,6},{5,7},{6,4},{7,5},{8,10},{9,11},{10,... | collective-permute-start | bytes 15368 | tf_op jit(solution)/shard_map/ppermute | solution.py:39
  60.7 3.7 %collective-permute-start.15 = (f32[80,16]{0,1:T(8,128)S(1)}, f32[80,16]{0,1:T(8,128)S(1)}, u32[]{:S(2)}, u32[]{:S(2)}) collective-permute-start(f32[80,16]{0,1:T(8,128)S(1)} %add.150), channel_id=1, source_target_pairs={{0,4},{1,5},{2,6},{3,7},{4,0},{5,1},{6,2},{7,3},{8,12},{9,13},{10,... | collective-permute-start | bytes 15368 | tf_op jit(solution)/shard_map/ppermute | solution.py:39
  64.3 3.8 %collective-permute-start.16 = (f32[80,16]{0,1:T(8,128)S(1)}, f32[80,16]{0,1:T(8,128)S(1)}, u32[]{:S(2)}, u32[]{:S(2)}) collective-permute-start(f32[80,16]{0,1:T(8,128)S(1)} %add.151), channel_id=1, source_target_pairs={{0,8},{1,9},{2,10},{3,11},{4,12},{5,13},{6,14},{7,15},{8,0},{9,1},... | collective-permute-start | bytes 15368 | tf_op jit(solution)/shard_map/ppermute | solution.py:39
  68.2 4.7 %collective-permute-start.17 = (f32[80,16]{0,1:T(8,128)S(1)}, f32[80,16]{0,1:T(8,128)S(1)}, u32[]{:S(2)}, u32[]{:S(2)}) collective-permute-start(f32[80,16]{0,1:T(8,128)S(1)} %add.152), channel_id=1, source_target_pairs={{0,16},{1,17},{2,18},{3,19},{4,20},{5,21},{6,22},{7,23},{8,24},{9,... | collective-permute-start | bytes 15368 | tf_op jit(solution)/shard_map/ppermute | solution.py:39
  72.8 8.7 %copy-start.2 = (f32[80,16]{0,1:T(8,128)}, f32[80,16]{0,1:T(8,128)S(1)}, u32[]{:S(2)}) copy-start(f32[80,16]{0,1:T(8,128)S(1)} %add.153) | copy-start | bytes 15364

commit v2 on v1

--- a/solution.py
+++ b/solution.py
@@ -37,6 +37,27 @@
     while distance < total:
         route = [(i, i ^ distance) for i in range(total)]
         block = block + lax.ppermute(block, axes, route)
+        distance *= 2
+    return block
+
+
+def butterfly_gather(block, axes):
+    total = 1
+    for axis in axes:
+        total *= lax.axis_size(axis)
+    if not is_power_of_two(total):
+        return lax.all_gather(block, axes, axis=0, tiled=True)
+    me = lax.axis_index(axes[0])
+    for axis in axes[1:]:
+        me = me * lax.axis_size(axis) + lax.axis_index(axis)
+    distance = 1
+    while distance < total:
+        route = [(i, i ^ distance) for i in range(total)]
+        other = lax.ppermute(block, axes, route)
+        upper = (me // distance) % 2 == 1
+        block = jnp.where(
+            upper, jnp.concatenate([other, block], axis=0), jnp.concatenate([block, other], axis=0)
+        )
         distance *= 2
     return block
 
@@ -89,23 +110,35 @@
     coarse = jnp.einsum(
         "cki,vci->cvk", leaf_basis, by_cluster, preferred_element_type=jnp.float32
     ).astype(jnp.bfloat16)
-    own_rows = coarse.reshape(1, local_count, vec_count * rank_width)
-    offsets = list(range(-reach_groups, reach_groups + 1))
-    grouped = lax.all_gather(own_rows, "coef", axis=1, tiled=True)
-    window = group_reach(grouped, offsets)
-    flat_rows = window.reshape(-1, vec_count * rank_width)
-    group_pos = lax.axis_index("leaf")
-    local_ids = (far_list - (group_pos - reach_groups) * group_size).reshape(-1)
-    sources = jnp.take(flat_rows, local_ids, axis=0).reshape(
+    all_rows = butterfly_gather(coarse.reshape(local_count, vec_count * rank_width), ("leaf", "coef"))
+    sources = jnp.take(all_rows, far_list.reshape(-1), axis=0).reshape(
         group_size, slot_count, vec_count, rank_width
     )
     lane_ids = jnp.arange(rank_width, dtype=jnp.int32)
     keep_mask = lane_ids[None, None, :] < far_rank[:, :, None]
     sources = jnp.where(keep_mask[:, :, None, :], sources, jnp.zeros((), jnp.bfloat16))
-    couple = coupling.reshape(3, group_size, slot_count, rank_width, rank_width)
-    far_terms = jnp.einsum("jcfkl,cfvl->jcfvk", couple, sources, preferred_element_type=jnp.float32)
-    combined = jnp.tensordot(powers, far_terms, 1) * keep_mask[:, :, None, :].astype(jnp.float32)
-    partial_far = jnp.sum(combined, axis=1).reshape(group_size, vec_count * rank_width)
+    lane_width = 128
+    halves = lane_width // rank_width
+    tiles = rank_width * rank_width // lane_width
+    wide_lanes = jnp.arange(lane_width, dtype=jnp.int32)
+    spread = jnp.tile(jnp.swapaxes(sources, 2, 3), (1, 1, halves, 1))
+    half_of_lane = (wide_lanes // rank_width)[:, None] == jnp.arange(halves, dtype=jnp.int32)[None, :]
+    slot_eye = jnp.eye(slot_count, dtype=jnp.bool_)
+    spread = jnp.where(
+        slot_eye[None, :, None, :, None, None] & half_of_lane[None, None, :, None, :, None],
+        spread[:, :, :, None, None, :],
+        jnp.zeros((), jnp.bfloat16),
+    ).reshape(group_size, slot_count, lane_width, slot_count * halves * vec_count)
+    couple = jnp.swapaxes(coupling.reshape(3, group_size, slot_count, tiles, lane_width), 2, 3)
+    far_terms = jnp.einsum("jchfL,cfLw->jchw", couple, spread, preferred_element_type=jnp.float32)
+    far_terms = jnp.swapaxes(
+        far_terms.reshape(3, group_size, tiles, slot_count, halves, vec_count), 2, 3
+    ).reshape(3, group_size, slot_count, rank_width, vec_count)
+    row_mask = keep_mask[:, :, :, None].astype(jnp.float32)
+    combined = jnp.tensordot(powers, far_terms, 1) * row_mask
+    partial_far = jnp.swapaxes(jnp.sum(combined, axis=1), 1, 2).reshape(
+        group_size, vec_count * rank_width
+    )
     far_hat = butterfly_scatter(partial_far, "coef")
     far_round = far_hat.astype(jnp.bfloat16).reshape(local_count, vec_count, rank_width)
     far_part = jnp.einsum("cki,cvk->vci", leaf_basis, far_round, preferred_element_type=jnp.float32)

time: 82.2 us -> 94.6 us (1.15)
  local copies, waits for them, and re-layouts: 13.2 us -> 27.6 us
  waiting for transfers between devices: 14.6 us -> 23.8 us
  blocking collectives: 6.18 us -> 0 us
  starting transfers between devices: 25.3 us -> 20 us
  other arithmetic: 10.3 us -> 11.9 us
  matrix products: 9.79 us -> 8.33 us
    transpose x0 -> x2, local copies, waits for them, and re-layouts: none -> 7.83 us  [the longest x1 6.32 us: on_device(): jnp.swapaxes(far_terms.reshape(3, group_size, tiles, slot_count, halves,...]
    ppermute x5, starting transfers between devices: 8.32 us -> 1.91 us  [butterfly_sum(): block = block + lax.ppermute(block, axes, route)]
    all_gather x1 -> x0, blocking collectives: 6.18 us -> none  [on_device(): grouped = lax.all_gather(own_rows, 'coef', axis=1, tiled=True)]
    ppermute x5, waiting for transfers between devices: 8.65 us -> 14.8 us  [butterfly_sum(): block = block + lax.ppermute(block, axes, route)]
    ppermute x4 -> x5, starting transfers between devices: 10 us -> 14.1 us  [butterfly_gather(): other = lax.ppermute(block, axes, route)]
    reshape x3 -> x4, local copies, waits for them, and re-layouts: 5.81 us -> 9.63 us  [the longest x1 5.26 us: on_device(): far_terms = jnp.swapaxes(far_terms.reshape(3, group_size, tiles, slot_cou...]
    another operation x0 -> x2, local copies, waits for them, and re-layouts: none -> 2.59 us  [on_device(): spread = jnp.tile(jnp.swapaxes(sources, 2, 3), (1, 1, halves, 1))]
    concatenate x2 -> x0, local copies, waits for them, and re-layouts: 2.22 us -> none  [group_reach(): return jnp.concatenate(pieces, axis=0)]
  transfers between devices with their start and end apart: 13 -> 14, of which waited for: 7 -> 9; matrix products, arithmetic and copies ran while one was open for 18% -> 15% of each run, Pallas kernels for 0% -> 0%
where the time goes in v2:
time: 94.6 us; the launch traced here: 93.9 us
  local copies, waits for them, and re-layouts  27.6 us (29%)
  waiting for transfers between devices  23.8 us (25%)
  starting transfers between devices  20 us (21%)
  other arithmetic  11.9 us (13%)
  matrix products  8.33 us (9%)
  between operations  2.26 us (2%)
    ppermute x5, waiting for transfers between devices, butterfly_sum(): block = block + lax.ppermute(block, axes, route)  14.8 us
    ppermute x5, starting transfers between devices, butterfly_gather(): other = lax.ppermute(block, axes, route)  14.1 us
    transpose x1, local copies, waits for them, and re-layouts, on_device(): jnp.swapaxes(far_terms.reshape(3, group_size, tiles, slot_count, halves,...  6.32 us
    ppermute x5, waiting for transfers between devices, butterfly_gather(): other = lax.ppermute(block, axes, route)  5.54 us
    reshape x1, local copies, waits for them, and re-layouts, on_device(): far_terms = jnp.swapaxes(far_terms.reshape(3, group_size, tiles, slot_cou...  5.26 us
    reshape x1, local copies, waits for them, and re-layouts, on_device(): coupling.reshape(3, group_size, slot_count, tiles, lane_width)  4.18 us
    ppermute x2, waiting for transfers between devices, butterfly_scatter(): parts = keep + lax.ppermute(give, axis, route)  3.49 us
    unnamed x14, local copies, waits for them, and re-layouts  2.76 us
  transfers between devices with their start and end apart: 14, of which 9 were waited for; matrix products, arithmetic and copies ran while one was open for 15% of the time, Pallas kernels for 0%

profile of v2, /device:TPU:0, one launch (start us, length us, event | category | flops | bytes accessed | tf_op | source)
XLA Modules:
  0.0 93.9 jit_solution(5849828932691118526)
XLA Ops:
  1.6 2.5 %collective-permute-start.12 = (bf16[16,512]{1,0:T(8,128)(2,1)S(1)}, bf16[16,512]{1,0:T(8,128)(2,1)S(1)}, u32[]{:S(2)}, u32[]{:S(2)}) collective-permute-start(bf16[16,512]{1,0:T(8,128)(2,1)S(1)} %convert_element_type.24), channel_id=1, source_target_pairs={{0,1},{1,2},{2,3},{3,4},{4,5},{5,6},{6,7},{7,8},{8,9},{9,10},{10,1... | collective-permute-start | bytes 49160 | tf_op jit(solution)/shard_map/ppermute | solution.py:18
  4.1 1.3 %collective-permute-start.13 = (bf16[16,512]{1,0:T(8,128)(2,1)S(1)}, bf16[16,512]{1,0:T(8,128)(2,1)S(1)}, u32[]{:S(2)}, u32[]{:S(2)}) collective-permute-start(bf16[16,512]{1,0:T(8,128)(2,1)S(1)} %convert_element_type.24), channel_id=1, source_target_pairs={{1,0},{2,1},{3,2},{4,3},{5,4},{6,5},{7,6},{8,7},{9,8},{10,9},{11,1... | collective-permute-start | bytes 49160 | tf_op jit(solution)/shard_map/ppermute | solution.py:21
  6.5 3.2 %collective-permute-start.5 = (bf16[4,1024]{1,0:T(4,128)(2,1)S(1)}, bf16[4,1024]{1,0:T(4,128)(2,1)S(1)}, u32[]{:S(2)}, u32[]{:S(2)}) collective-permute-start(bf16[4,1024]{1,0:T(4,128)(2,1)S(1)} %reshape.197), channel_id=1, source_target_pairs={{0,1},{1,0},{2,3},{3,2},{4,5},{5,4},{6,7},{7,6},{8,9},{9,8},{10,11... | collective-permute-start | bytes 24584 | tf_op jit(solution)/shard_map/ppermute | solution.py:56
  14.1 1.7 %collective-permute-start.6 = (bf16[8,1024]{1,0:T(8,128)(2,1)S(1)}, bf16[8,1024]{1,0:T(8,128)(2,1)S(1)}, u32[]{:S(2)}, u32[]{:S(2)}) collective-permute-start(bf16[8,1024]{1,0:T(8,128)(2,1)S(1)} %maximum_select_fusion.4), channel_id=1, source_target_pairs={{0,2},{1,3},{2,0},{3,1},{4,6},{5,7},{6,4},{7,5},{8,10},{9,11},{10,... | collective-permute-start | bytes 49160 | tf_op jit(solution)/shard_map/ppermute | solution.py:56
  15.9 2.0 %collective-permute-done.6 = bf16[8,1024]{1,0:T(8,128)(2,1)S(1)} collective-permute-done((bf16[8,1024]{1,0:T(8,128)(2,1)S(1)}, bf16[8,1024]{1,0:T(8,128)(2,1)S(1)}, u32[]{:S(2)}, u32[]{:S(2)}) %collective-permute-start.6) | collective-permute-done | bytes 16416 | tf_op jit(solution)/shard_map/ppermute | solution.py:56
  17.9 2.6 %collective-permute-start.7 = (bf16[16,1024]{1,0:T(8,128)(2,1)S(1)}, bf16[16,1024]{1,0:T(8,128)(2,1)S(1)}, u32[]{:S(2)}, u32[]{:S(2)}) collective-permute-start(bf16[16,1024]{1,0:T(8,128)(2,1)S(1)} %maximum_select_fusion.3), channel_id=1, source_target_pairs={{0,4},{1,5},{2,6},{3,7},{4,0},{5,1},{6,2},{7,3},{8,12},{9,13},{10,... | collective-permute-start | bytes 98312 | tf_op jit(solution)/shard_map/ppermute | solution.py:56
  20.6 1.9 %collective-permute-done.7 = bf16[16,1024]{1,0:T(8,128)(2,1)S(1)} collective-permute-done((bf16[16,1024]{1,0:T(8,128)(2,1)S(1)}, bf16[16,1024]{1,0:T(8,128)(2,1)S(1)}, u32[]{:S(2)}, u32[]{:S(2)}) %collective-permute-start.7) | collective-permute-done | bytes 32800 | tf_op jit(solution)/shard_map/ppermute | solution.py:56
  22.5 3.0 %collective-permute-start.8 = (bf16[32,1024]{1,0:T(8,128)(2,1)S(1)}, bf16[32,1024]{1,0:T(8,128)(2,1)S(1)}, u32[]{:S(2)}, u32[]{:S(2)}) collective-permute-start(bf16[32,1024]{1,0:T(8,128)(2,1)S(1)} %maximum_select_fusion.2), channel_id=1, source_target_pairs={{0,8},{1,9},{2,10},{3,11},{4,12},{5,13},{6,14},{7,15},{8,0},{9,1},... | collective-permute-start | bytes 196616 | tf_op jit(solution)/shard_map/ppermute | solution.py:56
  26.1 1.6 %collective-permute-done.8 = bf16[32,1024]{1,0:T(8,128)(2,1)S(1)} collective-permute-done((bf16[32,1024]{1,0:T(8,128)(2,1)S(1)}, bf16[32,1024]{1,0:T(8,128)(2,1)S(1)}, u32[]{:S(2)}, u32[]{:S(2)}) %collective-permute-start.8) | collective-permute-done | bytes 65568 | tf_op jit(solution)/shard_map/ppermute | solution.py:56
  27.8 3.5 %collective-permute-start.9 = (bf16[64,1024]{1,0:T(8,128)(2,1)S(1)}, bf16[64,1024]{1,0:T(8,128)(2,1)}, u32[]{:S(2)}, u32[]{:S(2)}) collective-permute-start(bf16[64,1024]{1,0:T(8,128)(2,1)S(1)} %maximum_select_fusion.1), channel_id=1, source_target_pairs={{0,16},{1,17},{2,18},{3,19},{4,20},{5,21},{6,22},{7,23},{8,24},{9,... | collective-permute-start | bytes 393224 | tf_op jit(solution)/shard_map/ppermute | solution.py:56
  31.9 4.2 %reshape.199 = bf16[3,16,4,32,128]{4,3,2,1,0:T(8,128)(2,1)} reshape(bf16[3,16,4,4096]{3,2,1,0:T(4,128)(2,1)} %param.16) | data formatting | bytes 3145728 | tf_op jit(solution)/shard_map/reshape | solution.py:132
  41.0 1.3 %tile.8 = bf16[16,4,2,64,16]{3,2,4,1,0:T(2,128)(2,1)} broadcast(bf16[16,4,64,16]{2,3,1,0:T(8,128)(2,1)S(1)} %select_bitcast_fusion), dimensions={0,1,3,4} | broadcast | bytes 393216 | tf_op jit(solution)/shard_map/tile | solution.py:124
  42.3 1.3 %tile.9 = bf16[16,4,128,16]{2,3,1,0:T(8,128)(2,1)S(1)} reshape(bf16[16,4,2,64,16]{3,2,4,1,0:T(2,128)(2,1)} %tile.8) | data formatting | bytes 524288 | tf_op jit(solution)/shard_map/tile | solution.py:124
  45.8 1.5 %copy.40 = bf16[3,16,32,128]{2,3,1,0:T(8,128)(2,1)} copy(bf16[3,16,32,128]{3,2,0,1:T(8,128)(2,1)S(1)} %fusion.6) | data formatting | bytes 786432 | tf_op jit(solution)/shard_map/jchfL,cfLw->jchw/transpose | solution.py:133
  47.3 6.3 %copy.41 = bf16[3,16,4,32,2,16]{5,1,4,3,2,0:T(8,128)(2,1)} copy(bf16[3,16,4,32,2,16]{3,5,4,2,1,0:T(8,128)(2,1)} %bitcast.121) | data formatting | bytes 786432 | tf_op jit(solution)/shard_map/transpose | solution.py:134
  53.6 5.3 %copy.51 = bf16[3,16,4,64,16]{3,0,4,2,1:T(4,128)(2,1)} copy(bf16[3,16,4,64,16]{4,1,3,2,0:T(8,128)(2,1)} %bitcast.120) | data formatting | bytes 786432 | tf_op jit(solution)/shard_map/reshape | solution.py:136
  58.9 2.0 %fusion.32 = f32[1,16,4,64,16]{3,0,4,2,1:T(1,128)S(1)} fusion(bf16[3,16,4,64,16]{3,0,4,2,1:T(4,128)(2,1)} %copy.51, bf16[1]{0:T(256)(128)(2,1)S(6)} %mul.22, f32[1]{0:T(128)S(6)} %copy.90, bf16[1]{0:T(256)(128)(2,1)} %constant.328), kind=kOutput, calls=%fused_computation.78 | convolution fusion | flops 393234 | bytes 655368 | tf_op jit(solution)/shard_map/dot_general | solution.py:138
  61.2 1.8 %fusion.11 = bf16[3,16,4,128]{3,1,0,2:T(8,128)(2,1)S(1)} fusion(bf16[3,4,8,128,128]{4,3,2,1,0:T(8,128)(2,1)S(1)} %copy-done, bf16[16,4,8,128]{3,0,2,1:T(8,128)(2,1)} %bitcast.128, pred[4,8]{1,0:T(4,128)(4,1)S(1)} %copy-done.5), kind=kOutput, calls=%fused_computation.13 | convolution fusion | flops 50397184 | bytes 3325984 | tf_op jit(solution)/shard_map/jcnil,vcnl->jvci/dot_general | solution.py:152
  63.4 3.5 %collective-permute-done.11 = f32[1,4,1024]{2,1,0:T(4,128)S(1)} collective-permute-done((f32[1,4,1024]{2,1,0:T(4,128)S(1)}, f32[1,4,1024]{2,1,0:T(4,128)S(1)}, u32[]{:S(2)}, u32[]{:S(2)}) %collective-permute-start.11) | collective-permute-done | bytes 16416 | tf_op jit(solution)/shard_map/ppermute | solution.py:78
  69.7 3.6 %collective-permute-done.15 = f32[80,16]{0,1:T(8,128)S(1)} collective-permute-done((f32[80,16]{0,1:T(8,128)S(1)}, f32[80,16]{0,1:T(8,128)S(1)}, u32[]{:S(2)}, u32[]{:S(2)}) %collective-permute-start.15) | collective-permute-done | bytes 5152 | tf_op jit(solution)/shard_map/ppermute | solution.py:39
  74.0 3.0 %collective-permute-done.16 = f32[80,16]{0,1:T(8,128)S(1)} collective-permute-done((f32[80,16]{0,1:T(8,128)S(1)}, f32[80,16]{0,1:T(8,128)S(1)}, u32[]{:S(2)}, u32[]{:S(2)}) %collective-permute-start.16) | collective-permute-done | bytes 5152 | tf_op jit(solution)/shard_map/ppermute | solution.py:39
  78.2 2.5 %collective-permute-done.17 = f32[80,16]{0,1:T(8,128)S(1)} collective-permute-done((f32[80,16]{0,1:T(8,128)S(1)}, f32[80,16]{0,1:T(8,128)S(1)}, u32[]{:S(2)}, u32[]{:S(2)}) %collective-permute-start.17) | collective-permute-done | bytes 5152 | tf_op jit(solution)/shard_map/ppermute | solution.py:39
  80.8 4.4 %collective-permute-done.18 = f32[80,16]{0,1:T(8,128)S(1)} collective-permute-done((f32[80,16]{0,1:T(8,128)S(1)}, f32[80,16]{0,1:T(8,128)S(1)}, u32[]{:S(2)}, u32[]{:S(2)}) %collective-permute-start.18) | collective-permute-done | bytes 5152 | tf_op jit(solution)/shard_map/ppermute | solution.py:39
  88.4 1.5 %cholesky.16 = f32[16,16]{1,0:T(8,128)S(1)} custom-call(f32[16,16]{1,0:T(8,128)S(1)} %fusion.28), custom_call_target="Cholesky" | custom-call | tf_op jit(solution)/shard_map/jit(cholesky)/cholesky | solution.py:171
  (90 shorter events, 26.0 us)
Async XLA Ops:
  0.6 60.5 %copy-start = (bf16[3,4,8,128,128]{4,3,2,1,0:T(8,128)(2,1)S(1)}, bf16[3,4,8,128,128]{4,3,2,1,0:T(8,128)(2,1)}, u32[]{:S(2)}) copy-start(bf16[3,4,8,128,128]{4,3,2,1,0:T(8,128)(2,1)} %param.14) | copy-start | bytes 9437188
  1.6 35.3 %collective-permute-start.12 = (bf16[16,512]{1,0:T(8,128)(2,1)S(1)}, bf16[16,512]{1,0:T(8,128)(2,1)S(1)}, u32[]{:S(2)}, u32[]{:S(2)}) collective-permute-start(bf16[16,512]{1,0:T(8,128)(2,1)S(1)} %convert_element_type.24), channel_id=1, source_target_pairs={{0,1},{1,2},{2,3},{3,4},{4,5},{5,6},{6,7},{7,8},{8,9},{9,10},{10,1... | collective-permute-start | bytes 49160 | tf_op jit(solution)/shard_map/ppermute | solution.py:18
  4.1 32.7 %collective-permute-start.13 = (bf16[16,512]{1,0:T(8,128)(2,1)S(1)}, bf16[16,512]{1,0:T(8,128)(2,1)S(1)}, u32[]{:S(2)}, u32[]{:S(2)}) collective-permute-start(bf16[16,512]{1,0:T(8,128)(2,1)S(1)} %convert_element_type.24), channel_id=1, source_target_pairs={{1,0},{2,1},{3,2},{4,3},{5,4},{6,5},{7,6},{8,7},{9,8},{10,9},{11,1... | collective-permute-start | bytes 49160 | tf_op jit(solution)/shard_map/ppermute | solution.py:21
  6.5 7.6 %collective-permute-start.5 = (bf16[4,1024]{1,0:T(4,128)(2,1)S(1)}, bf16[4,1024]{1,0:T(4,128)(2,1)S(1)}, u32[]{:S(2)}, u32[]{:S(2)}) collective-permute-start(bf16[4,1024]{1,0:T(4,128)(2,1)S(1)} %reshape.197), channel_id=1, source_target_pairs={{0,1},{1,0},{2,3},{3,2},{4,5},{5,4},{6,7},{7,6},{8,9},{9,8},{10,11... | collective-permute-start | bytes 24584 | tf_op jit(solution)/shard_map/ppermute | solution.py:56
  14.1 3.8 %collective-permute-start.6 = (bf16[8,1024]{1,0:T(8,128)(2,1)S(1)}, bf16[8,1024]{1,0:T(8,128)(2,1)S(1)}, u32[]{:S(2)}, u32[]{:S(2)}) collective-permute-start(bf16[8,1024]{1,0:T(8,128)(2,1)S(1)} %maximum_select_fusion.4), channel_id=1, source_target_pairs={{0,2},{1,3},{2,0},{3,1},{4,6},{5,7},{6,4},{7,5},{8,10},{9,11},{10,... | collective-permute-start | bytes 49160 | tf_op jit(solution)/shard_map/ppermute | solution.py:56
  17.9 4.5 %collective-permute-start.7 = (bf16[16,1024]{1,0:T(8,128)(2,1)S(1)}, bf16[16,1024]{1,0:T(8,128)(2,1)S(1)}, u32[]{:S(2)}, u32[]{:S(2)}) collective-permute-start(bf16[16,1024]{1,0:T(8,128)(2,1)S(1)} %maximum_select_fusion.3), channel_id=1, source_target_pairs={{0,4},{1,5},{2,6},{3,7},{4,0},{5,1},{6,2},{7,3},{8,12},{9,13},{10,... | collective-permute-start | bytes 98312 | tf_op jit(solution)/shard_map/ppermute | solution.py:56
  22.5 5.3 %collective-permute-start.8 = (bf16[32,1024]{1,0:T(8,128)(2,1)S(1)}, bf16[32,1024]{1,0:T(8,128)(2,1)S(1)}, u32[]{:S(2)}, u32[]{:S(2)}) collective-permute-start(bf16[32,1024]{1,0:T(8,128)(2,1)S(1)} %maximum_select_fusion.2), channel_id=1, source_target_pairs={{0,8},{1,9},{2,10},{3,11},{4,12},{5,13},{6,14},{7,15},{8,0},{9,1},... | collective-permute-start | bytes 196616 | tf_op jit(solution)/shard_map/ppermute | solution.py:56
  27.8 10.3 %collective-permute-start.9 = (bf16[64,1024]{1,0:T(8,128)(2,1)S(1)}, bf16[64,1024]{1,0:T(8,128)(2,1)}, u32[]{:S(2)}, u32[]{:S(2)}) collective-permute-start(bf16[64,1024]{1,0:T(8,128)(2,1)S(1)} %maximum_select_fusion.1), channel_id=1, source_target_pairs={{0,16},{1,17},{2,18},{3,19},{4,20},{5,21},{6,22},{7,23},{8,24},{9,... | collective-permute-start | bytes 393224 | tf_op jit(solution)/shard_map/ppermute | solution.py:56
  43.6 1.4 %copy-start.1 = (bf16[3,16,4,32,128]{4,3,2,1,0:T(8,128)(2,1)S(1)}, bf16[3,16,4,32,128]{4,3,2,1,0:T(8,128)(2,1)}, u32[]{:S(2)}) copy-start(bf16[3,16,4,32,128]{4,3,2,1,0:T(8,128)(2,1)} %reshape.199) | copy-start | bytes 4718596
  53.6 7.2 %copy-start.4 = (f32[16,4,64]{2,1,0:T(4,128)S(1)}, f32[16,4,64]{2,1,0:T(4,128)}, u32[]{:S(2)}) copy-start(f32[16,4,64]{2,1,0:T(4,128)} %get-tuple-element.14) | copy-start | bytes 49156
  58.9 2.3 %copy-start.5 = (pred[4,8]{1,0:T(4,128)(4,1)S(1)}, pred[4,8]{1,0:T(4,128)(4,1)}, u32[]{:S(2)}) copy-start(pred[4,8]{1,0:T(4,128)(4,1)} %get-tuple-element.12) | copy-start | bytes 100
  61.0 7.2 %copy-start.2 = (f32[64,512]{1,0:T(8,128)S(1)}, f32[64,512]{1,0:T(8,128)}, u32[]{:S(2)}) copy-start(f32[64,512]{1,0:T(8,128)} %param.19) | copy-start | bytes 393220
  61.1 1.9 %collective-permute-start.10 = (f32[2,4,1024]{2,1,0:T(4,128)S(1)}, f32[2,4,1024]{2,1,0:T(4,128)S(1)}, u32[]{:S(2)}, u32[]{:S(2)}) collective-permute-start(f32[2,4,1024]{2,1,0:T(4,128)S(1)} %dynamic-slice_bitcast_fusion), channel_id=1, source_target_pairs={{0,1},{1,0},{2,3},{3,2},{4,5},{5,4},{6,7},{7,6},{8,9},{9,8},{10,11... | collective-permute-start | bytes 98312 | tf_op jit(solution)/shard_map/ppermute | solution.py:78
  63.1 3.8 %collective-permute-start.11 = (f32[1,4,1024]{2,1,0:T(4,128)S(1)}, f32[1,4,1024]{2,1,0:T(4,128)S(1)}, u32[]{:S(2)}, u32[]{:S(2)}) collective-permute-start(f32[1,4,1024]{2,1,0:T(4,128)S(1)} %constant_dynamic-slice_fusion), channel_id=1, source_target_pairs={{0,2},{1,3},{2,0},{3,1},{4,6},{5,7},{6,4},{7,5},{8,10},{9,11},{10,... | collective-permute-start | bytes 49160 | tf_op jit(solution)/shard_map/ppermute | solution.py:78
  68.5 1.2 %collective-permute-start.14 = (f32[80,16]{0,1:T(8,128)S(1)}, f32[80,16]{0,1:T(8,128)S(1)}, u32[]{:S(2)}, u32[]{:S(2)}) collective-permute-start(f32[80,16]{0,1:T(8,128)S(1)} %pad_maximum_fusion), channel_id=1, source_target_pairs={{0,1},{1,0},{2,3},{3,2},{4,5},{5,4},{6,7},{7,6},{8,9},{9,8},{10,11... | collective-permute-start | bytes 15368 | tf_op jit(solution)/shard_map/ppermute | solution.py:39
  69.7 3.7 %collective-permute-start.15 = (f32[80,16]{0,1:T(8,128)S(1)}, f32[80,16]{0,1:T(8,128)S(1)}, u32[]{:S(2)}, u32[]{:S(2)}) collective-permute-start(f32[80,16]{0,1:T(8,128)S(1)} %fusion.51), channel_id=1, source_target_pairs={{0,2},{1,3},{2,0},{3,1},{4,6},{5,7},{6,4},{7,5},{8,10},{9,11},{10,... | collective-permute-start | bytes 15368 | tf_op jit(solution)/shard_map/ppermute | solution.py:39
  73.4 3.7 %collective-permute-start.16 = (f32[80,16]{0,1:T(8,128)S(1)}, f32[80,16]{0,1:T(8,128)S(1)}, u32[]{:S(2)}, u32[]{:S(2)}) collective-permute-start(f32[80,16]{0,1:T(8,128)S(1)} %add.180), channel_id=1, source_target_pairs={{0,4},{1,5},{2,6},{3,7},{4,0},{5,1},{6,2},{7,3},{8,12},{9,13},{10,... | collective-permute-start | bytes 15368 | tf_op jit(solution)/shard_map/ppermute | solution.py:39
  77.0 3.7 %collective-permute-start.17 = (f32[80,16]{0,1:T(8,128)S(1)}, f32[80,16]{0,1:T(8,128)S(1)}, u32[]{:S(2)}, u32[]{:S(2)}) collective-permute-start(f32[80,16]{0,1:T(8,128)S(1)} %add.181), channel_id=1, source_target_pairs={{0,8},{1,9},{2,10},{3,11},{4,12},{5,13},{6,14},{7,15},{8,0},{9,1},... | collective-permute-start | bytes 15368 | tf_op jit(solution)/shard_map/ppermute | solution.py:39
  80.7 4.5 %collective-permute-start.18 = (f32[80,16]{0,1:T(8,128)S(1)}, f32[80,16]{0,1:T(8,128)S(1)}, u32[]{:S(2)}, u32[]{:S(2)}) collective-permute-start(f32[80,16]{0,1:T(8,128)S(1)} %add.182), channel_id=1, source_target_pairs={{0,16},{1,17},{2,18},{3,19},{4,20},{5,21},{6,22},{7,23},{8,24},{9,... | collective-permute-start | bytes 15368 | tf_op jit(solution)/shard_map/ppermute | solution.py:39
  85.2 8.7 %copy-start.3 = (f32[80,16]{0,1:T(8,128)}, f32[80,16]{0,1:T(8,128)S(1)}, u32[]{:S(2)}) copy-start(f32[80,16]{0,1:T(8,128)S(1)} %add.183) | copy-start | bytes 15364

commit v3 on v1

--- a/solution.py
+++ b/solution.py
@@ -91,8 +91,8 @@
     ).astype(jnp.bfloat16)
     own_rows = coarse.reshape(1, local_count, vec_count * rank_width)
     offsets = list(range(-reach_groups, reach_groups + 1))
-    grouped = lax.all_gather(own_rows, "coef", axis=1, tiled=True)
-    window = group_reach(grouped, offsets)
+    reached = group_reach(own_rows, offsets)
+    window = lax.all_gather(reached, "coef", axis=1, tiled=True)
     flat_rows = window.reshape(-1, vec_count * rank_width)
     group_pos = lax.axis_index("leaf")
     local_ids = (far_list - (group_pos - reach_groups) * group_size).reshape(-1)
@@ -130,7 +130,10 @@
     outer = summed[basis_count:]
     residue = applied - jnp.dot(coeffs.T, krylov, precision=highest)
     short_gram = (outer - jnp.dot(coeffs.T, coeffs, precision=highest)) / total_points
-    kept = jnp.diagonal(short_gram) * (64 * total_points) >= jnp.diagonal(outer)
+    eye = jnp.eye(vec_count, dtype=jnp.bool_)
+    short_diag = jnp.sum(jnp.where(eye, short_gram, 0.0), axis=0)
+    outer_diag = jnp.sum(jnp.where(eye, outer, 0.0), axis=0)
+    kept = short_diag * (64 * total_points) >= outer_diag
     def exact_gram():
         part = jnp.dot(residue, residue.T, precision=highest)
         return butterfly_sum(part, both_axes) / total_points

time: 82.2 us -> 81 us (0.985)
  local copies, waits for them, and re-layouts: 13.2 us -> 11 us
  starting transfers between devices: 25.3 us -> 26.3 us
  waiting for transfers between devices: 14.6 us -> 13.7 us
    ppermute x4, waiting for transfers between devices: 4.09 us -> 0.01 us  [shifted(): return lax.ppermute(block, axis, route)]
    concatenate x2 -> x1, local copies, waits for them, and re-layouts: 2.22 us -> 0.13 us  [group_reach(): return jnp.concatenate(pieces, axis=0)]
    ppermute x5, waiting for transfers between devices: 8.65 us -> 10.6 us  [butterfly_sum(): block = block + lax.ppermute(block, axes, route)]
    gather x2 -> x0, local copies, waits for them, and re-layouts: 1.38 us -> none  [on_device(): kept = jnp.diagonal(short_gram) * (64 * total_points) >= jnp.diagonal(outer)]
    ppermute x2, waiting for transfers between devices: 1.81 us -> 3 us  [butterfly_scatter(): parts = keep + lax.ppermute(give, axis, route)]
    ppermute x5, starting transfers between devices: 8.32 us -> 9.44 us  [butterfly_sum(): block = block + lax.ppermute(block, axes, route)]
    ppermute x2, starting transfers between devices: 2.03 us -> 0.98 us  [butterfly_scatter(): parts = keep + lax.ppermute(give, axis, route)]
    ppermute x4, starting transfers between devices: 10 us -> 11 us  [shifted(): return lax.ppermute(block, axis, route)]
  transfers between devices with their start and end apart: 13 -> 13, of which waited for: 7 -> 6; matrix products, arithmetic and copies ran while one was open for 18% -> 27% of each run, Pallas kernels for 0% -> 0%
where the time goes in v3:
time: 81 us; the launch traced here: 80.4 us
  starting transfers between devices  26.3 us (32%)
  waiting for transfers between devices  13.7 us (17%)
  local copies, waits for them, and re-layouts  11 us (14%)
  other arithmetic  10.3 us (13%)
  matrix products  10 us (12%)
  blocking collectives  6.93 us (9%)
  between operations  2.21 us (3%)
    ppermute x4, starting transfers between devices, shifted(): return lax.ppermute(block, axis, route)  11 us
    ppermute x5, waiting for transfers between devices, butterfly_sum(): block = block + lax.ppermute(block, axes, route)  10.6 us
    ppermute x5, starting transfers between devices, butterfly_sum(): block = block + lax.ppermute(block, axes, route)  9.44 us
    all_gather x1, blocking collectives, on_device(): window = lax.all_gather(reached, 'coef', axis=1, tiled=True)  6.93 us
    reshape x1, local copies, waits for them, and re-layouts, on_device(): couple = coupling.reshape(3, group_size, slot_count, rank_width, rank_width)  5.64 us
    dot_general x1, matrix products, on_device(): jnp.einsum('jcfkl,cfvl->jcfvk', couple, sources, preferred_element_type=j...  4.24 us
    ppermute x1, starting transfers between devices, extended_2(): lax.ppermute(lax.slice_in_dim(block, block.shape[dim] - width, None, axis...  3.63 us
    ppermute x2, waiting for transfers between devices, butterfly_scatter(): parts = keep + lax.ppermute(give, axis, route)  3 us
  transfers between devices with their start and end apart: 13, of which 6 were waited for; matrix products, arithmetic and copies ran while one was open for 27% of the time, Pallas kernels for 0%

profile of v3, /device:TPU:0, one launch (start us, length us, event | category | flops | bytes accessed | tf_op | source)
XLA Modules:
  0.0 80.4 jit_solution(12881620607272085304)
XLA Ops:
  1.9 5.0 %collective-permute-start.5 = (bf16[1,4,1024]{2,0,1:T(2,128)(2,1)S(1)}, bf16[1,4,1024]{2,0,1:T(2,128)(2,1)S(1)}, u32[]{:S(2)}, u32[]{:S(2)}) collective-permute-start(bf16[1,4,1024]{2,0,1:T(2,128)(2,1)S(1)} %reshape.167), channel_id=1, source_target_pairs={{0,8},{4,12},{8,16},{12,20},{16,24},{20,28},{1,9},{5,13},{9,17},{1... | collective-permute-start | bytes 24584 | tf_op jit(solution)/shard_map/ppermute | solution.py:10
  6.8 3.4 %collective-permute-start.6 = (bf16[1,4,1024]{2,0,1:T(2,128)(2,1)S(1)}, bf16[1,4,1024]{2,0,1:T(2,128)(2,1)S(1)}, u32[]{:S(2)}, u32[]{:S(2)}) collective-permute-start(bf16[1,4,1024]{2,0,1:T(2,128)(2,1)S(1)} %reshape.167), channel_id=1, source_target_pairs={{0,4},{4,8},{8,12},{12,16},{16,20},{20,24},{24,28},{1,5},{5,9},{9,... | collective-permute-start | bytes 24584 | tf_op jit(solution)/shard_map/ppermute | solution.py:10
  10.3 1.3 %collective-permute-start.7 = (bf16[1,4,1024]{2,0,1:T(2,128)(2,1)S(1)}, bf16[1,4,1024]{2,0,1:T(2,128)(2,1)S(1)}, u32[]{:S(2)}, u32[]{:S(2)}) collective-permute-start(bf16[1,4,1024]{2,0,1:T(2,128)(2,1)S(1)} %reshape.167), channel_id=1, source_target_pairs={{4,0},{8,4},{12,8},{16,12},{20,16},{24,20},{28,24},{5,1},{9,5},{13... | collective-permute-start | bytes 24584 | tf_op jit(solution)/shard_map/ppermute | solution.py:10
  11.6 1.3 %collective-permute-start.8 = (bf16[1,4,1024]{2,0,1:T(2,128)(2,1)S(1)}, bf16[1,4,1024]{2,0,1:T(2,128)(2,1)S(1)}, u32[]{:S(2)}, u32[]{:S(2)}) collective-permute-start(bf16[1,4,1024]{2,0,1:T(2,128)(2,1)S(1)} %reshape.167), channel_id=1, source_target_pairs={{8,0},{12,4},{16,8},{20,12},{24,16},{28,20},{9,1},{13,5},{17,9},{2... | collective-permute-start | bytes 24584 | tf_op jit(solution)/shard_map/ppermute | solution.py:10
  13.6 1.3 %collective-permute-start.12 = (bf16[16,512]{1,0:T(8,128)(2,1)S(1)}, bf16[16,512]{1,0:T(8,128)(2,1)}, u32[]{:S(2)}, u32[]{:S(2)}) collective-permute-start(bf16[16,512]{1,0:T(8,128)(2,1)S(1)} %convert_element_type.24), channel_id=1, source_target_pairs={{1,0},{2,1},{3,2},{4,3},{5,4},{6,5},{7,6},{8,7},{9,8},{10,9},{11,1... | collective-permute-start | bytes 49160 | tf_op jit(solution)/shard_map/ppermute | solution.py:21
  17.3 1.2 %compare_and_fusion = (pred[4,8]{1,0:T(4,128)(4,1)}, s32[4,8]{1,0:T(4,128)S(1)}) fusion(s32[4,8]{1,0:T(4,128)} %param.15, s32[]{:T(128)S(6)} %mul.29), kind=kLoop, calls=%fused_computation.63 | loop fusion | flops 224 | bytes 292 | tf_op jit(solution)/shard_map/jit(_take)/and | solution.py:116
  19.2 5.6 %reshape.139 = bf16[3,16,4,64,64]{4,3,2,1,0:T(8,128)(2,1)} reshape(bf16[3,16,4,4096]{3,2,1,0:T(4,128)(2,1)} %param.16) | data formatting | bytes 3145728 | tf_op jit(solution)/shard_map/reshape | solution.py:105
  26.2 3.6 %collective-permute-start.11 = (bf16[16,512]{1,0:T(8,128)(2,1)S(1)}, bf16[16,512]{1,0:T(8,128)(2,1)}, u32[]{:S(2)}, u32[]{:S(2)}) collective-permute-start(bf16[16,512]{1,0:T(8,128)(2,1)S(1)} %convert_element_type.24), channel_id=1, source_target_pairs={{0,1},{1,2},{2,3},{3,4},{4,5},{5,6},{6,7},{7,8},{8,9},{9,10},{10,1... | collective-permute-start | bytes 49160 | tf_op jit(solution)/shard_map/ppermute | solution.py:18
  30.0 6.9 %all_gather.3 = bf16[5,16,1024]{2,0,1:T(8,128)(2,1)S(1)} all-gather(bf16[5,4,1024]{2,0,1:T(8,128)(2,1)S(1)} %concatenate.9), channel_id=1, replica_groups=mesh['leaf'=8,'coef'=4] {'coef'}, dimensions={1}, use_global_device_ids=true | all-gather | bytes 204800 | tf_op jit(solution)/shard_map/all_gather | solution.py:95
  37.9 4.2 %fusion.6 = bf16[3,16,4,16,64]{4,3,0,2,1:T(8,128)(2,1)S(1)} fusion(bf16[3,16,4,64,64]{4,3,2,1,0:T(8,128)(2,1)} %reshape.139, bf16[16,4,16,64]{3,2,1,0:T(8,128)(2,1)S(1)} %gather.13, pred[16,4]{1,0:T(8,128)(4,1)} %copy.49, pred[16,4,64]{2,1,0:T(4,128)(4,1)} %get-tuple-element.27), kind=kOutput, calls=%fused_computation.9 | convolution fusion | flops 25296896 | bytes 2101312 | tf_op jit(solution)/shard_map/jcfkl,cfvl->jcfvk/dot_general | solution.py:106
  44.3 1.4 %gather_fusion.1 = bf16[32,16,128]{2,1,0:T(8,128)(2,1)} fusion(bf16[16,12,128]{2,0,1:T(8,128)(2,1)S(1)} %copy_bitcast_fusion, s32[1024]{0:T(1024)} %pad_clamp_fusion), kind=kCustom, calls=%fused_computation.1 | custom fusion | bytes 262272 | tf_op jit(solution)/shard_map/jit(_take)/gather | solution.py:116
  45.7 1.8 %fusion.9 = bf16[3,16,4,128]{3,1,0,2:T(8,128)(2,1)S(1)} fusion(bf16[3,4,8,128,128]{4,3,2,1,0:T(8,128)(2,1)S(1)} %copy-done, bf16[16,4,8,128]{3,0,2,1:T(8,128)(2,1)} %bitcast.94, pred[4,8]{1,0:T(4,128)(4,1)} %get-tuple-element.22), kind=kOutput, calls=%fused_computation.10 | convolution fusion | flops 50397184 | bytes 3325984 | tf_op jit(solution)/shard_map/jcnil,vcnl->jvci/dot_general | solution.py:119
  48.4 3.0 %collective-permute-done.10 = f32[1,4,1024]{2,1,0:T(4,128)S(1)} collective-permute-done((f32[1,4,1024]{2,1,0:T(4,128)S(1)}, f32[1,4,1024]{2,1,0:T(4,128)S(1)}, u32[]{:S(2)}, u32[]{:S(2)}) %collective-permute-start.10) | collective-permute-done | bytes 16416 | tf_op jit(solution)/shard_map/ppermute | solution.py:57
  52.3 1.2 %collective-permute-done.13 = f32[80,16]{1,0:T(8,128)S(1)} collective-permute-done((f32[80,16]{1,0:T(8,128)S(1)}, f32[80,16]{1,0:T(8,128)S(1)}, u32[]{:S(2)}, u32[]{:S(2)}) %collective-permute-start.13) | collective-permute-done | bytes 5152 | tf_op jit(solution)/shard_map/ppermute | solution.py:39
  54.0 3.5 %collective-permute-done.14 = f32[80,16]{1,0:T(8,128)S(1)} collective-permute-done((f32[80,16]{1,0:T(8,128)S(1)}, f32[80,16]{1,0:T(8,128)S(1)}, u32[]{:S(2)}, u32[]{:S(2)}) %collective-permute-start.14) | collective-permute-done | bytes 5152 | tf_op jit(solution)/shard_map/ppermute | solution.py:39
  57.5 3.1 %collective-permute-start.15 = (f32[80,16]{1,0:T(8,128)S(1)}, f32[80,16]{1,0:T(8,128)S(1)}, u32[]{:S(2)}, u32[]{:S(2)}) collective-permute-start(f32[80,16]{1,0:T(8,128)S(1)} %add.144), channel_id=1, source_target_pairs={{0,4},{1,5},{2,6},{3,7},{4,0},{5,1},{6,2},{7,3},{8,12},{9,13},{10,... | collective-permute-start | bytes 15368 | tf_op jit(solution)/shard_map/ppermute | solution.py:39
  60.6 2.0 %collective-permute-done.15 = f32[80,16]{1,0:T(8,128)S(1)} collective-permute-done((f32[80,16]{1,0:T(8,128)S(1)}, f32[80,16]{1,0:T(8,128)S(1)}, u32[]{:S(2)}, u32[]{:S(2)}) %collective-permute-start.15) | collective-permute-done | bytes 5152 | tf_op jit(solution)/shard_map/ppermute | solution.py:39
  62.6 2.3 %collective-permute-start.16 = (f32[80,16]{1,0:T(8,128)S(1)}, f32[80,16]{1,0:T(8,128)S(1)}, u32[]{:S(2)}, u32[]{:S(2)}) collective-permute-start(f32[80,16]{1,0:T(8,128)S(1)} %add.145), channel_id=1, source_target_pairs={{0,8},{1,9},{2,10},{3,11},{4,12},{5,13},{6,14},{7,15},{8,0},{9,1},... | collective-permute-start | bytes 15368 | tf_op jit(solution)/shard_map/ppermute | solution.py:39
  64.9 2.0 %collective-permute-done.16 = f32[80,16]{1,0:T(8,128)S(1)} collective-permute-done((f32[80,16]{1,0:T(8,128)S(1)}, f32[80,16]{1,0:T(8,128)S(1)}, u32[]{:S(2)}, u32[]{:S(2)}) %collective-permute-start.16) | collective-permute-done | bytes 5152 | tf_op jit(solution)/shard_map/ppermute | solution.py:39
  66.9 3.5 %collective-permute-start.17 = (f32[80,16]{1,0:T(8,128)S(1)}, f32[80,16]{1,0:T(8,128)S(1)}, u32[]{:S(2)}, u32[]{:S(2)}) collective-permute-start(f32[80,16]{1,0:T(8,128)S(1)} %add.146), channel_id=1, source_target_pairs={{0,16},{1,17},{2,18},{3,19},{4,20},{5,21},{6,22},{7,23},{8,24},{9,... | collective-permute-start | bytes 15368 | tf_op jit(solution)/shard_map/ppermute | solution.py:39
  70.4 2.0 %collective-permute-done.17 = f32[80,16]{1,0:T(8,128)S(1)} collective-permute-done((f32[80,16]{1,0:T(8,128)S(1)}, f32[80,16]{1,0:T(8,128)S(1)}, u32[]{:S(2)}, u32[]{:S(2)}) %collective-permute-start.17) | collective-permute-done | bytes 5152 | tf_op jit(solution)/shard_map/ppermute | solution.py:39
  74.2 1.5 %cholesky.17 = f32[16,16]{1,0:T(8,128)S(1)} custom-call(f32[16,16]{1,0:T(8,128)S(1)} %fusion.33), custom_call_target="Cholesky" | custom-call | tf_op jit(solution)/shard_map/jit(cholesky)/cholesky | solution.py:141
  76.4 1.2 %select_bitcast_fusion = (f32[1,16,16]{2,1,0:T(8,128)S(1)}, f32[16,16]{1,0:T(8,128)}) fusion(f32[16,16]{1,0:T(8,128)S(1)} %cholesky.17, pred[]{:T(512)} %compare_reduce_fusion), kind=kLoop, calls=%fused_computation.48 | loop fusion | flops 1024 | bytes 3073 | tf_op jit(solution)/shard_map/jit(_solve_triangular)/triangular_solve | solution.py:142
  77.6 1.2 %custom-call.7 = f32[1,16,16]{1,2,0:T(8,128)S(1)} custom-call(f32[1,16,16]{2,1,0:T(8,128)S(1)} %get-tuple-element.20), custom_call_target="InvertDiagBlocksLowerTriangular" | custom-call | tf_op jit(solution)/shard_map/jit(_solve_triangular)/triangular_solve | solution.py:142
  (69 shorter events, 14.6 us)
Async XLA Ops:
  0.6 45.1 %copy-start = (bf16[3,4,8,128,128]{4,3,2,1,0:T(8,128)(2,1)S(1)}, bf16[3,4,8,128,128]{4,3,2,1,0:T(8,128)(2,1)}, u32[]{:S(2)}) copy-start(bf16[3,4,8,128,128]{4,3,2,1,0:T(8,128)(2,1)} %param.14) | copy-start | bytes 9437188
  1.9 24.3 %collective-permute-start.5 = (bf16[1,4,1024]{2,0,1:T(2,128)(2,1)S(1)}, bf16[1,4,1024]{2,0,1:T(2,128)(2,1)S(1)}, u32[]{:S(2)}, u32[]{:S(2)}) collective-permute-start(bf16[1,4,1024]{2,0,1:T(2,128)(2,1)S(1)} %reshape.167), channel_id=1, source_target_pairs={{0,8},{4,12},{8,16},{12,20},{16,24},{20,28},{1,9},{5,13},{9,17},{1... | collective-permute-start | bytes 24584 | tf_op jit(solution)/shard_map/ppermute | solution.py:10
  6.8 23.0 %collective-permute-start.6 = (bf16[1,4,1024]{2,0,1:T(2,128)(2,1)S(1)}, bf16[1,4,1024]{2,0,1:T(2,128)(2,1)S(1)}, u32[]{:S(2)}, u32[]{:S(2)}) collective-permute-start(bf16[1,4,1024]{2,0,1:T(2,128)(2,1)S(1)} %reshape.167), channel_id=1, source_target_pairs={{0,4},{4,8},{8,12},{12,16},{16,20},{20,24},{24,28},{1,5},{5,9},{9,... | collective-permute-start | bytes 24584 | tf_op jit(solution)/shard_map/ppermute | solution.py:10
  10.3 19.6 %collective-permute-start.7 = (bf16[1,4,1024]{2,0,1:T(2,128)(2,1)S(1)}, bf16[1,4,1024]{2,0,1:T(2,128)(2,1)S(1)}, u32[]{:S(2)}, u32[]{:S(2)}) collective-permute-start(bf16[1,4,1024]{2,0,1:T(2,128)(2,1)S(1)} %reshape.167), channel_id=1, source_target_pairs={{4,0},{8,4},{12,8},{16,12},{20,16},{24,20},{28,24},{5,1},{9,5},{13... | collective-permute-start | bytes 24584 | tf_op jit(solution)/shard_map/ppermute | solution.py:10
  11.6 18.3 %collective-permute-start.8 = (bf16[1,4,1024]{2,0,1:T(2,128)(2,1)S(1)}, bf16[1,4,1024]{2,0,1:T(2,128)(2,1)S(1)}, u32[]{:S(2)}, u32[]{:S(2)}) collective-permute-start(bf16[1,4,1024]{2,0,1:T(2,128)(2,1)S(1)} %reshape.167), channel_id=1, source_target_pairs={{8,0},{12,4},{16,8},{20,12},{24,16},{28,20},{9,1},{13,5},{17,9},{2... | collective-permute-start | bytes 24584 | tf_op jit(solution)/shard_map/ppermute | solution.py:10
  13.6 29.9 %collective-permute-start.12 = (bf16[16,512]{1,0:T(8,128)(2,1)S(1)}, bf16[16,512]{1,0:T(8,128)(2,1)}, u32[]{:S(2)}, u32[]{:S(2)}) collective-permute-start(bf16[16,512]{1,0:T(8,128)(2,1)S(1)} %convert_element_type.24), channel_id=1, source_target_pairs={{1,0},{2,1},{3,2},{4,3},{5,4},{6,5},{7,6},{8,7},{9,8},{10,9},{11,1... | collective-permute-start | bytes 49160 | tf_op jit(solution)/shard_map/ppermute | solution.py:21
  26.2 17.4 %collective-permute-start.11 = (bf16[16,512]{1,0:T(8,128)(2,1)S(1)}, bf16[16,512]{1,0:T(8,128)(2,1)}, u32[]{:S(2)}, u32[]{:S(2)}) collective-permute-start(bf16[16,512]{1,0:T(8,128)(2,1)S(1)} %convert_element_type.24), channel_id=1, source_target_pairs={{0,1},{1,2},{2,3},{3,4},{4,5},{5,6},{6,7},{7,8},{8,9},{9,10},{10,1... | collective-permute-start | bytes 49160 | tf_op jit(solution)/shard_map/ppermute | solution.py:18
  37.9 5.0 %copy-start.3 = (f32[16,4,64]{2,1,0:T(4,128)S(1)}, f32[16,4,64]{2,1,0:T(4,128)}, u32[]{:S(2)}) copy-start(f32[16,4,64]{2,1,0:T(4,128)} %get-tuple-element.26) | copy-start | bytes 49156
  42.2 9.4 %copy-start.2 = (bf16[4,64,128]{2,1,0:T(8,128)(2,1)S(1)}, bf16[4,64,128]{2,1,0:T(8,128)(2,1)}, u32[]{:S(2)}) copy-start(bf16[4,64,128]{2,1,0:T(8,128)(2,1)} %param.13) | copy-start | bytes 196612
  42.2 9.6 %copy-start.1 = (f32[64,512]{1,0:T(8,128)S(1)}, f32[64,512]{1,0:T(8,128)}, u32[]{:S(2)}) copy-start(f32[64,512]{1,0:T(8,128)} %param.19) | copy-start | bytes 393220
  43.2 4.4 %collective-permute-start.9 = (f32[2,4,1024]{2,1,0:T(4,128)S(1)}, f32[2,4,1024]{2,1,0:T(4,128)S(1)}, u32[]{:S(2)}, u32[]{:S(2)}) collective-permute-start(f32[2,4,1024]{2,1,0:T(4,128)S(1)} %dynamic-slice_bitcast_fusion), channel_id=1, source_target_pairs={{0,1},{1,0},{2,3},{3,2},{4,5},{5,4},{6,7},{7,6},{8,9},{9,8},{10,11... | collective-permute-start | bytes 98312 | tf_op jit(solution)/shard_map/ppermute | solution.py:57
  47.6 3.8 %collective-permute-start.10 = (f32[1,4,1024]{2,1,0:T(4,128)S(1)}, f32[1,4,1024]{2,1,0:T(4,128)S(1)}, u32[]{:S(2)}, u32[]{:S(2)}) collective-permute-start(f32[1,4,1024]{2,1,0:T(4,128)S(1)} %constant_dynamic-slice_fusion), channel_id=1, source_target_pairs={{0,2},{1,3},{2,0},{3,1},{4,6},{5,7},{6,4},{7,5},{8,10},{9,11},{10,... | collective-permute-start | bytes 49160 | tf_op jit(solution)/shard_map/ppermute | solution.py:57
  52.2 1.3 %collective-permute-start.13 = (f32[80,16]{1,0:T(8,128)S(1)}, f32[80,16]{1,0:T(8,128)S(1)}, u32[]{:S(2)}, u32[]{:S(2)}) collective-permute-start(f32[80,16]{1,0:T(8,128)S(1)} %copy.63), channel_id=1, source_target_pairs={{0,1},{1,0},{2,3},{3,2},{4,5},{5,4},{6,7},{7,6},{8,9},{9,8},{10,11... | collective-permute-start | bytes 15368 | tf_op jit(solution)/shard_map/ppermute | solution.py:39
  53.5 4.0 %collective-permute-start.14 = (f32[80,16]{1,0:T(8,128)S(1)}, f32[80,16]{1,0:T(8,128)S(1)}, u32[]{:S(2)}, u32[]{:S(2)}) collective-permute-start(f32[80,16]{1,0:T(8,128)S(1)} %add.143), channel_id=1, source_target_pairs={{0,2},{1,3},{2,0},{3,1},{4,6},{5,7},{6,4},{7,5},{8,10},{9,11},{10,... | collective-permute-start | bytes 15368 | tf_op jit(solution)/shard_map/ppermute | solution.py:39
  57.5 5.0 %collective-permute-start.15 = (f32[80,16]{1,0:T(8,128)S(1)}, f32[80,16]{1,0:T(8,128)S(1)}, u32[]{:S(2)}, u32[]{:S(2)}) collective-permute-start(f32[80,16]{1,0:T(8,128)S(1)} %add.144), channel_id=1, source_target_pairs={{0,4},{1,5},{2,6},{3,7},{4,0},{5,1},{6,2},{7,3},{8,12},{9,13},{10,... | collective-permute-start | bytes 15368 | tf_op jit(solution)/shard_map/ppermute | solution.py:39
  62.6 4.3 %collective-permute-start.16 = (f32[80,16]{1,0:T(8,128)S(1)}, f32[80,16]{1,0:T(8,128)S(1)}, u32[]{:S(2)}, u32[]{:S(2)}) collective-permute-start(f32[80,16]{1,0:T(8,128)S(1)} %add.145), channel_id=1, source_target_pairs={{0,8},{1,9},{2,10},{3,11},{4,12},{5,13},{6,14},{7,15},{8,0},{9,1},... | collective-permute-start | bytes 15368 | tf_op jit(solution)/shard_map/ppermute | solution.py:39
  66.9 5.5 %collective-permute-start.17 = (f32[80,16]{1,0:T(8,128)S(1)}, f32[80,16]{1,0:T(8,128)S(1)}, u32[]{:S(2)}, u32[]{:S(2)}) collective-permute-start(f32[80,16]{1,0:T(8,128)S(1)} %add.146), channel_id=1, source_target_pairs={{0,16},{1,17},{2,18},{3,19},{4,20},{5,21},{6,22},{7,23},{8,24},{9,... | collective-permute-start | bytes 15368 | tf_op jit(solution)/shard_map/ppermute | solution.py:39

commit v4 on v3

--- a/solution.py
+++ b/solution.py
@@ -1,6 +1,8 @@
 import jax
 import jax.numpy as jnp
 from jax import lax
+from jax.experimental import pallas as pl
+from jax.experimental.pallas import tpu as pltpu
 from jax.sharding import PartitionSpec as P
 
 
@@ -67,6 +69,51 @@
         else:
             pieces.append(shifted(grouped, "leaf", -offset))
     return jnp.concatenate(pieces, axis=0)
+
+
+def chol_solve_kernel(gram_ref, residue_ref, chol_ref, block_ref):
+    left = gram_ref[...]
+    size = left.shape[0]
+    rows = lax.broadcasted_iota(jnp.int32, left.shape, 0)
+    cols = lax.broadcasted_iota(jnp.int32, left.shape, 1)
+    row_ids = lax.broadcasted_iota(jnp.int32, (size, 1), 0)
+    col_ids = lax.broadcasted_iota(jnp.int32, (1, size), 1)
+    low = jnp.zeros_like(left)
+    for step in range(size):
+        column = jnp.sum(jnp.where(cols == step, left, 0.0), axis=1, keepdims=True)
+        row = jnp.sum(jnp.where(rows == step, left, 0.0), axis=0, keepdims=True)
+        pivot = jnp.sum(jnp.where(row_ids == step, column, 0.0), axis=0, keepdims=True)
+        root = jnp.sqrt(pivot)
+        low_column = jnp.where(row_ids >= step, column / root, 0.0)
+        low_row = jnp.where(col_ids >= step, row / root, 0.0)
+        low = jnp.where(cols == step, low_column, low)
+        left = left - low_column * low_row
+    chol_ref[...] = low
+    block = residue_ref[...]
+    for step in range(size):
+        low_column = jnp.sum(jnp.where(cols == step, low, 0.0), axis=1, keepdims=True)
+        diagonal = jnp.sum(jnp.where(row_ids == step, low_column, 0.0), axis=0, keepdims=True)
+        solved = jnp.sum(jnp.where(row_ids == step, block, 0.0), axis=0, keepdims=True) / diagonal
+        block = jnp.where(
+            row_ids == step, solved, jnp.where(row_ids > step, block - low_column * solved, block)
+        )
+    block_ref[...] = block
+
+
+def chol_solve(gram_matrix, residue):
+    size, width = residue.shape
+    return pl.pallas_call(
+        chol_solve_kernel,
+        out_shape=(
+            jax.ShapeDtypeStruct((size, size), jnp.float32),
+            jax.ShapeDtypeStruct((size, width), jnp.float32),
+        ),
+        in_specs=[pl.BlockSpec(memory_space=pltpu.VMEM)] * 2,
+        out_specs=(pl.BlockSpec(memory_space=pltpu.VMEM), pl.BlockSpec(memory_space=pltpu.VMEM)),
+        cost_estimate=pl.CostEstimate(
+            flops=4 * size * size * (size + width), bytes_accessed=8 * size * (size + width), transcendentals=size
+        ),
+    )(gram_matrix, residue)
 
 
 def on_device(
@@ -96,7 +143,7 @@
     flat_rows = window.reshape(-1, vec_count * rank_width)
     group_pos = lax.axis_index("leaf")
     local_ids = (far_list - (group_pos - reach_groups) * group_size).reshape(-1)
-    sources = jnp.take(flat_rows, local_ids, axis=0).reshape(
+    sources = flat_rows.at[local_ids].get(mode="promise_in_bounds").reshape(
         group_size, slot_count, vec_count, rank_width
     )
     lane_ids = jnp.arange(rank_width, dtype=jnp.int32)
@@ -113,7 +160,7 @@
     extended = extended.reshape(vec_count, 3 * local_count, leaf_size)
     device_pos = lax.axis_index("leaf") * coef_count + lax.axis_index("coef")
     near_ids = (near_list - (device_pos - 1) * local_count).reshape(-1)
-    near_src = jnp.take(extended, near_ids, axis=1).reshape(
+    near_src = extended.at[:, near_ids].get(mode="promise_in_bounds").reshape(
         vec_count, local_count, near_count, leaf_size
     )
     near_terms = jnp.einsum(
@@ -138,8 +185,7 @@
         part = jnp.dot(residue, residue.T, precision=highest)
         return butterfly_sum(part, both_axes) / total_points
     gram_matrix = lax.cond(jnp.all(kept), lambda: short_gram, exact_gram)
-    chol_factor = jnp.linalg.cholesky(gram_matrix)
-    new_block = jax.scipy.linalg.solve_triangular(chol_factor, residue, lower=True)
+    chol_factor, new_block = chol_solve(gram_matrix, residue)
     return (new_block, coeffs, chol_factor)
 
 

time: 81 us -> 74.4 us (0.919)
  other arithmetic: 10.3 us -> 6.09 us
  Pallas kernels: 0 us -> 2.43 us
  matrix products: 10 us -> 8.14 us
  waiting for transfers between devices: 13.7 us -> 12.2 us
  local copies, waits for them, and re-layouts: 11 us -> 9.55 us
    another operation x5 -> x0, other arithmetic: 4.6 us -> none  [the longest x2 2.47 us: on_device(): jax.scipy.linalg.solve_triangular(chol_factor, residue, lower=True)]
    pallas_call x0 -> x1, Pallas kernels: none -> 2.43 us  [chol_solve(): pl.pallas_call(chol_solve_kernel, out_shape=(jax.ShapeDtypeStruct((size,...]
    and x2 -> x0, other arithmetic: 1.91 us -> none  [the longest x1 1.21 us: on_device(): jnp.take(extended, near_ids, axis=1)]
    ppermute x5, waiting for transfers between devices: 10.6 us -> 9.19 us  [butterfly_sum(): block = block + lax.ppermute(block, axes, route)]
    sub x0 -> x2, other arithmetic: none -> 1.37 us  [the longest x1 0.69 us: on_device(): local_ids = (far_list - (group_pos - reach_groups) * group_size).reshape(-1)]
    dot_general x1, matrix products: 1.84 us -> 0.92 us  [on_device(): jnp.einsum('jcnil,vcnl->jvci', near_blocks, near_src, preferred_element_t...]
    another operation x1 -> x0, matrix products: 0.86 us -> none  [on_device(): jax.scipy.linalg.solve_triangular(chol_factor, residue, lower=True)]
    gather x3 -> x2, local copies, waits for them, and re-layouts: 2.24 us -> 1.42 us  [the longest x1 0.72 us: on_device(): extended.at[:, near_ids].get(mode='promise_in_bounds')]
where the time goes in v4:
time: 74.4 us; the launch traced here: 73.7 us
  starting transfers between devices  26.2 us (35%)
  waiting for transfers between devices  12.2 us (16%)
  local copies, waits for them, and re-layouts  9.55 us (13%)
  matrix products  8.14 us (11%)
  blocking collectives  6.93 us (9%)
  other arithmetic  6.09 us (8%)
  Pallas kernels  2.43 us (3%)
  between operations  2.19 us (3%)
    ppermute x4, starting transfers between devices, shifted(): return lax.ppermute(block, axis, route)  11 us
    ppermute x5, starting transfers between devices, butterfly_sum(): block = block + lax.ppermute(block, axes, route)  9.37 us
    ppermute x5, waiting for transfers between devices, butterfly_sum(): block = block + lax.ppermute(block, axes, route)  9.19 us
    all_gather x1, blocking collectives, on_device(): window = lax.all_gather(reached, 'coef', axis=1, tiled=True)  6.93 us
    reshape x1, local copies, waits for them, and re-layouts, on_device(): couple = coupling.reshape(3, group_size, slot_count, rank_width, rank_width)  5.65 us
    dot_general x1, matrix products, on_device(): jnp.einsum('jcfkl,cfvl->jcfvk', couple, sources, preferred_element_type=j...  4.19 us
    ppermute x1, starting transfers between devices, extended_2(): lax.ppermute(lax.slice_in_dim(block, block.shape[dim] - width, None, axis...  3.63 us
    ppermute x2, waiting for transfers between devices, butterfly_scatter(): parts = keep + lax.ppermute(give, axis, route)  3 us
  transfers between devices with their start and end apart: 13, of which 6 were waited for; matrix products, arithmetic and copies ran while one was open for 27% of the time, Pallas kernels for 0%

profile of v4, /device:TPU:0, one launch (start us, length us, event | category | flops | bytes accessed | tf_op | source)
XLA Modules:
  0.0 73.7 jit_solution(10455879607463703461)
XLA Ops:
  0.6 1.1 %convolution_convert_fusion = bf16[4,16,64]{2,1,0:T(8,128)(2,1)S(1)} fusion(bf16[4,64,128]{2,1,0:T(8,128)(2,1)} %param.13, f32[16,512]{1,0:T(8,128)} %param.11), kind=kOutput, calls=%fused_computation.14 | convolution fusion | flops 1060864 | bytes 106496 | tf_op jit(solution)/shard_map/cki,vci->cvk/dot_general | solution.py:136
  1.9 5.0 %collective-permute-start.5 = (bf16[1,4,1024]{2,0,1:T(2,128)(2,1)S(1)}, bf16[1,4,1024]{2,0,1:T(2,128)(2,1)S(1)}, u32[]{:S(2)}, u32[]{:S(2)}) collective-permute-start(bf16[1,4,1024]{2,0,1:T(2,128)(2,1)S(1)} %reshape.144), channel_id=1, source_target_pairs={{0,8},{4,12},{8,16},{12,20},{16,24},{20,28},{1,9},{5,13},{9,17},{1... | collective-permute-start | bytes 24584 | tf_op jit(solution)/shard_map/ppermute | solution.py:12
  6.8 3.4 %collective-permute-start.6 = (bf16[1,4,1024]{2,0,1:T(2,128)(2,1)S(1)}, bf16[1,4,1024]{2,0,1:T(2,128)(2,1)S(1)}, u32[]{:S(2)}, u32[]{:S(2)}) collective-permute-start(bf16[1,4,1024]{2,0,1:T(2,128)(2,1)S(1)} %reshape.144), channel_id=1, source_target_pairs={{0,4},{4,8},{8,12},{12,16},{16,20},{20,24},{24,28},{1,5},{5,9},{9,... | collective-permute-start | bytes 24584 | tf_op jit(solution)/shard_map/ppermute | solution.py:12
  10.3 1.3 %collective-permute-start.7 = (bf16[1,4,1024]{2,0,1:T(2,128)(2,1)S(1)}, bf16[1,4,1024]{2,0,1:T(2,128)(2,1)S(1)}, u32[]{:S(2)}, u32[]{:S(2)}) collective-permute-start(bf16[1,4,1024]{2,0,1:T(2,128)(2,1)S(1)} %reshape.144), channel_id=1, source_target_pairs={{4,0},{8,4},{12,8},{16,12},{20,16},{24,20},{28,24},{5,1},{9,5},{13... | collective-permute-start | bytes 24584 | tf_op jit(solution)/shard_map/ppermute | solution.py:12
  11.6 1.3 %collective-permute-start.8 = (bf16[1,4,1024]{2,0,1:T(2,128)(2,1)S(1)}, bf16[1,4,1024]{2,0,1:T(2,128)(2,1)S(1)}, u32[]{:S(2)}, u32[]{:S(2)}) collective-permute-start(bf16[1,4,1024]{2,0,1:T(2,128)(2,1)S(1)} %reshape.144), channel_id=1, source_target_pairs={{8,0},{12,4},{16,8},{20,12},{24,16},{28,20},{9,1},{13,5},{17,9},{2... | collective-permute-start | bytes 24584 | tf_op jit(solution)/shard_map/ppermute | solution.py:12
  12.9 0.8 %convert_element_type.24 = bf16[16,512]{1,0:T(8,128)(2,1)S(1)} convert(f32[16,512]{1,0:T(8,128)} %param.11) | non-fusion elementwise | flops 8192 | bytes 49152 | tf_op jit(solution)/shard_map/convert_element_type | solution.py:134
  13.6 1.3 %collective-permute-start.12 = (bf16[16,512]{1,0:T(8,128)(2,1)S(1)}, bf16[16,512]{1,0:T(8,128)(2,1)}, u32[]{:S(2)}, u32[]{:S(2)}) collective-permute-start(bf16[16,512]{1,0:T(8,128)(2,1)S(1)} %convert_element_type.24), channel_id=1, source_target_pairs={{1,0},{2,1},{3,2},{4,3},{5,4},{6,5},{7,6},{8,7},{9,8},{10,9},{11,1... | collective-permute-start | bytes 49160 | tf_op jit(solution)/shard_map/ppermute | solution.py:23
  18.7 5.6 %reshape.115 = bf16[3,16,4,64,64]{4,3,2,1,0:T(8,128)(2,1)} reshape(bf16[3,16,4,4096]{3,2,1,0:T(4,128)(2,1)} %param.16) | data formatting | bytes 3145728 | tf_op jit(solution)/shard_map/reshape | solution.py:152
  25.0 3.6 %collective-permute-start.11 = (bf16[16,512]{1,0:T(8,128)(2,1)S(1)}, bf16[16,512]{1,0:T(8,128)(2,1)}, u32[]{:S(2)}, u32[]{:S(2)}) collective-permute-start(bf16[16,512]{1,0:T(8,128)(2,1)S(1)} %convert_element_type.24), channel_id=1, source_target_pairs={{0,1},{1,2},{2,3},{3,4},{4,5},{5,6},{6,7},{7,8},{8,9},{9,10},{10,1... | collective-permute-start | bytes 49160 | tf_op jit(solution)/shard_map/ppermute | solution.py:20
  28.8 6.9 %all_gather.3 = bf16[5,16,1024]{2,0,1:T(8,128)(2,1)S(1)} all-gather(bf16[5,4,1024]{2,0,1:T(8,128)(2,1)S(1)} %concatenate.9), channel_id=1, replica_groups=mesh['leaf'=8,'coef'=4] {'coef'}, dimensions={1}, use_global_device_ids=true | all-gather | bytes 204800 | tf_op jit(solution)/shard_map/all_gather | solution.py:142
  36.7 4.2 %fusion.6 = bf16[3,16,4,16,64]{4,3,0,2,1:T(8,128)(2,1)S(1)} fusion(bf16[3,16,4,64,64]{4,3,2,1,0:T(8,128)(2,1)} %reshape.115, bf16[16,4,16,64]{3,2,1,0:T(8,128)(2,1)S(1)} %reshape.114, pred[16,4,64]{2,1,0:T(4,128)(4,1)} %get-tuple-element.15), kind=kOutput, calls=%fused_computation.9 | convolution fusion | flops 25231360 | bytes 2101248 | tf_op jit(solution)/shard_map/jcfkl,cfvl->jcfvk/dot_general | solution.py:153
  40.9 0.8 %fusion.4 = f32[1,16,4,16,64]{4,0,3,2,1:T(1,128)S(1)} fusion(bf16[3,16,4,16,64]{4,3,0,2,1:T(8,128)(2,1)S(1)} %fusion.6, bf16[1]{0:T(256)(128)(2,1)S(6)} %mul.24, f32[1]{0:T(128)S(6)} %copy.94, bf16[1]{0:T(256)(128)(2,1)} %constant.134), kind=kOutput, calls=%fused_computation.7 | convolution fusion | flops 393234 | bytes 655368 | tf_op jit(solution)/shard_map/dot_general | solution.py:154
  44.4 0.9 %fusion.9 = bf16[3,16,4,128]{3,1,0,2:T(8,128)(2,1)S(1)} fusion(bf16[16,4,8,128,1]{3,0,2,4,1:T(8,128)(2,1)S(1)} %bitcast.87, bf16[3,4,8,128,128]{4,3,2,1,0:T(8,128)(2,1)S(1)} %copy-done), kind=kOutput, calls=%fused_computation.10 | convolution fusion | flops 50331648 | bytes 3325952 | tf_op jit(solution)/shard_map/jcnil,vcnl->jvci/dot_general | solution.py:166
  45.3 0.8 %bitcast_add_fusion = f32[2,4,1024]{2,1,0:T(4,128)S(1)} fusion(f32[2,4,1024]{2,1,0:T(4,128)} %collective-permute-done.9, f32[2,2,4,1024]{3,2,1,0:T(4,128)S(1)} %reshape_reshape_reshape.3, s32[]{:T(128)S(6)} %select_n.64), kind=kLoop, calls=%fused_computation.29 | loop fusion | flops 8192 | bytes 98308 | tf_op jit(solution)/shard_map/add | solution.py:59
  46.9 3.0 %collective-permute-done.10 = f32[1,4,1024]{2,1,0:T(4,128)S(1)} collective-permute-done((f32[1,4,1024]{2,1,0:T(4,128)S(1)}, f32[1,4,1024]{2,1,0:T(4,128)S(1)}, u32[]{:S(2)}, u32[]{:S(2)}) %collective-permute-start.10) | collective-permute-done | bytes 16416 | tf_op jit(solution)/shard_map/ppermute | solution.py:59
  50.6 1.2 %collective-permute-done.13 = f32[80,16]{0,1:T(8,128)S(1)} collective-permute-done((f32[80,16]{0,1:T(8,128)S(1)}, f32[80,16]{0,1:T(8,128)S(1)}, u32[]{:S(2)}, u32[]{:S(2)}) %collective-permute-start.13) | collective-permute-done | bytes 5152 | tf_op jit(solution)/shard_map/ppermute | solution.py:41
  52.4 3.1 %collective-permute-done.14 = f32[80,16]{0,1:T(8,128)S(1)} collective-permute-done((f32[80,16]{0,1:T(8,128)S(1)}, f32[80,16]{0,1:T(8,128)S(1)}, u32[]{:S(2)}, u32[]{:S(2)}) %collective-permute-start.14) | collective-permute-done | bytes 5152 | tf_op jit(solution)/shard_map/ppermute | solution.py:41
  55.5 3.1 %collective-permute-start.15 = (f32[80,16]{0,1:T(8,128)S(1)}, f32[80,16]{0,1:T(8,128)S(1)}, u32[]{:S(2)}, u32[]{:S(2)}) collective-permute-start(f32[80,16]{0,1:T(8,128)S(1)} %add.110), channel_id=1, source_target_pairs={{0,4},{1,5},{2,6},{3,7},{4,0},{5,1},{6,2},{7,3},{8,12},{9,13},{10,... | collective-permute-start | bytes 15368 | tf_op jit(solution)/shard_map/ppermute | solution.py:41
  58.6 1.6 %collective-permute-done.15 = f32[80,16]{0,1:T(8,128)S(1)} collective-permute-done((f32[80,16]{0,1:T(8,128)S(1)}, f32[80,16]{0,1:T(8,128)S(1)}, u32[]{:S(2)}, u32[]{:S(2)}) %collective-permute-start.15) | collective-permute-done | bytes 5152 | tf_op jit(solution)/shard_map/ppermute | solution.py:41
  60.2 2.3 %collective-permute-start.16 = (f32[80,16]{0,1:T(8,128)S(1)}, f32[80,16]{0,1:T(8,128)S(1)}, u32[]{:S(2)}, u32[]{:S(2)}) collective-permute-start(f32[80,16]{0,1:T(8,128)S(1)} %add.111), channel_id=1, source_target_pairs={{0,8},{1,9},{2,10},{3,11},{4,12},{5,13},{6,14},{7,15},{8,0},{9,1},... | collective-permute-start | bytes 15368 | tf_op jit(solution)/shard_map/ppermute | solution.py:41
  62.5 1.6 %collective-permute-done.16 = f32[80,16]{0,1:T(8,128)S(1)} collective-permute-done((f32[80,16]{0,1:T(8,128)S(1)}, f32[80,16]{0,1:T(8,128)S(1)}, u32[]{:S(2)}, u32[]{:S(2)}) %collective-permute-start.16) | collective-permute-done | bytes 5152 | tf_op jit(solution)/shard_map/ppermute | solution.py:41
  64.2 3.5 %collective-permute-start.17 = (f32[80,16]{0,1:T(8,128)S(1)}, f32[80,16]{0,1:T(8,128)S(1)}, u32[]{:S(2)}, u32[]{:S(2)}) collective-permute-start(f32[80,16]{0,1:T(8,128)S(1)} %add.112), channel_id=1, source_target_pairs={{0,16},{1,17},{2,18},{3,19},{4,20},{5,21},{6,22},{7,23},{8,24},{9,... | collective-permute-start | bytes 15368 | tf_op jit(solution)/shard_map/ppermute | solution.py:41
  67.6 1.6 %collective-permute-done.17 = f32[80,16]{0,1:T(8,128)S(1)} collective-permute-done((f32[80,16]{0,1:T(8,128)S(1)}, f32[80,16]{0,1:T(8,128)S(1)}, u32[]{:S(2)}, u32[]{:S(2)}) %collective-permute-start.17) | collective-permute-done | bytes 5152 | tf_op jit(solution)/shard_map/ppermute | solution.py:41
  71.3 2.4 %shard_map.112 = (f32[16,16]{1,0:T(8,128)}, f32[16,512]{1,0:T(8,128)}) custom-call(f32[16,16]{1,0:T(8,128)S(1)} %get-tuple-element.18.gram_ref, f32[16,512]{1,0:T(8,128)S(1)} %convolution_subtract_fusion.residue_ref), custom_call_target="tpu_custom_call" | custom-call | flops 540672 | bytes 67584 | tf_op jit(solution)/shard_map/pallas_call | solution.py:105
  (61 shorter events, 11.1 us)
Async XLA Ops:
  0.6 43.7 %copy-start = (bf16[3,4,8,128,128]{4,3,2,1,0:T(8,128)(2,1)S(1)}, bf16[3,4,8,128,128]{4,3,2,1,0:T(8,128)(2,1)}, u32[]{:S(2)}) copy-start(bf16[3,4,8,128,128]{4,3,2,1,0:T(8,128)(2,1)} %param.14) | copy-start | bytes 9437188
  1.9 23.1 %collective-permute-start.5 = (bf16[1,4,1024]{2,0,1:T(2,128)(2,1)S(1)}, bf16[1,4,1024]{2,0,1:T(2,128)(2,1)S(1)}, u32[]{:S(2)}, u32[]{:S(2)}) collective-permute-start(bf16[1,4,1024]{2,0,1:T(2,128)(2,1)S(1)} %reshape.144), channel_id=1, source_target_pairs={{0,8},{4,12},{8,16},{12,20},{16,24},{20,28},{1,9},{5,13},{9,17},{1... | collective-permute-start | bytes 24584 | tf_op jit(solution)/shard_map/ppermute | solution.py:12
  6.8 21.8 %collective-permute-start.6 = (bf16[1,4,1024]{2,0,1:T(2,128)(2,1)S(1)}, bf16[1,4,1024]{2,0,1:T(2,128)(2,1)S(1)}, u32[]{:S(2)}, u32[]{:S(2)}) collective-permute-start(bf16[1,4,1024]{2,0,1:T(2,128)(2,1)S(1)} %reshape.144), channel_id=1, source_target_pairs={{0,4},{4,8},{8,12},{12,16},{16,20},{20,24},{24,28},{1,5},{5,9},{9,... | collective-permute-start | bytes 24584 | tf_op jit(solution)/shard_map/ppermute | solution.py:12
  10.3 18.4 %collective-permute-start.7 = (bf16[1,4,1024]{2,0,1:T(2,128)(2,1)S(1)}, bf16[1,4,1024]{2,0,1:T(2,128)(2,1)S(1)}, u32[]{:S(2)}, u32[]{:S(2)}) collective-permute-start(bf16[1,4,1024]{2,0,1:T(2,128)(2,1)S(1)} %reshape.144), channel_id=1, source_target_pairs={{4,0},{8,4},{12,8},{16,12},{20,16},{24,20},{28,24},{5,1},{9,5},{13... | collective-permute-start | bytes 24584 | tf_op jit(solution)/shard_map/ppermute | solution.py:12
  11.6 17.1 %collective-permute-start.8 = (bf16[1,4,1024]{2,0,1:T(2,128)(2,1)S(1)}, bf16[1,4,1024]{2,0,1:T(2,128)(2,1)S(1)}, u32[]{:S(2)}, u32[]{:S(2)}) collective-permute-start(bf16[1,4,1024]{2,0,1:T(2,128)(2,1)S(1)} %reshape.144), channel_id=1, source_target_pairs={{8,0},{12,4},{16,8},{20,12},{24,16},{28,20},{9,1},{13,5},{17,9},{2... | collective-permute-start | bytes 24584 | tf_op jit(solution)/shard_map/ppermute | solution.py:12
  13.6 29.2 %collective-permute-start.12 = (bf16[16,512]{1,0:T(8,128)(2,1)S(1)}, bf16[16,512]{1,0:T(8,128)(2,1)}, u32[]{:S(2)}, u32[]{:S(2)}) collective-permute-start(bf16[16,512]{1,0:T(8,128)(2,1)S(1)} %convert_element_type.24), channel_id=1, source_target_pairs={{1,0},{2,1},{3,2},{4,3},{5,4},{6,5},{7,6},{8,7},{9,8},{10,9},{11,1... | collective-permute-start | bytes 49160 | tf_op jit(solution)/shard_map/ppermute | solution.py:23
  25.0 17.9 %collective-permute-start.11 = (bf16[16,512]{1,0:T(8,128)(2,1)S(1)}, bf16[16,512]{1,0:T(8,128)(2,1)}, u32[]{:S(2)}, u32[]{:S(2)}) collective-permute-start(bf16[16,512]{1,0:T(8,128)(2,1)S(1)} %convert_element_type.24), channel_id=1, source_target_pairs={{0,1},{1,2},{2,3},{3,4},{4,5},{5,6},{6,7},{7,8},{8,9},{9,10},{10,1... | collective-permute-start | bytes 49160 | tf_op jit(solution)/shard_map/ppermute | solution.py:20
  36.7 5.0 %copy-start.4 = (f32[16,4,64]{2,1,0:T(4,128)S(1)}, f32[16,4,64]{2,1,0:T(4,128)}, u32[]{:S(2)}) copy-start(f32[16,4,64]{2,1,0:T(4,128)} %get-tuple-element.14) | copy-start | bytes 49156
  40.9 9.4 %copy-start.1 = (f32[64,512]{1,0:T(8,128)S(1)}, f32[64,512]{1,0:T(8,128)}, u32[]{:S(2)}) copy-start(f32[64,512]{1,0:T(8,128)} %param.19) | copy-start | bytes 393220
  42.5 2.8 %collective-permute-start.9 = (f32[2,4,1024]{2,1,0:T(4,128)}, f32[2,4,1024]{2,1,0:T(4,128)}, u32[]{:S(2)}, u32[]{:S(2)}) collective-permute-start(f32[2,4,1024]{2,1,0:T(4,128)} %dynamic-slice_bitcast_fusion), channel_id=1, source_target_pairs={{0,1},{1,0},{2,3},{3,2},{4,5},{5,4},{6,7},{7,6},{8,9},{9,8},{10,11... | collective-permute-start | bytes 98312 | tf_op jit(solution)/shard_map/ppermute | solution.py:59
  44.4 5.7 %copy-start.3 = (bf16[4,64,128]{2,1,0:T(8,128)(2,1)S(1)}, bf16[4,64,128]{2,1,0:T(8,128)(2,1)}, u32[]{:S(2)}) copy-start(bf16[4,64,128]{2,1,0:T(8,128)(2,1)} %param.13) | copy-start | bytes 196612
  46.1 3.8 %collective-permute-start.10 = (f32[1,4,1024]{2,1,0:T(4,128)S(1)}, f32[1,4,1024]{2,1,0:T(4,128)S(1)}, u32[]{:S(2)}, u32[]{:S(2)}) collective-permute-start(f32[1,4,1024]{2,1,0:T(4,128)S(1)} %constant_dynamic-slice_fusion), channel_id=1, source_target_pairs={{0,2},{1,3},{2,0},{3,1},{4,6},{5,7},{6,4},{7,5},{8,10},{9,11},{10,... | collective-permute-start | bytes 49160 | tf_op jit(solution)/shard_map/ppermute | solution.py:59
  50.6 1.2 %collective-permute-start.13 = (f32[80,16]{0,1:T(8,128)S(1)}, f32[80,16]{0,1:T(8,128)S(1)}, u32[]{:S(2)}, u32[]{:S(2)}) collective-permute-start(f32[80,16]{0,1:T(8,128)S(1)} %pad_maximum_fusion), channel_id=1, source_target_pairs={{0,1},{1,0},{2,3},{3,2},{4,5},{5,4},{6,7},{7,6},{8,9},{9,8},{10,11... | collective-permute-start | bytes 15368 | tf_op jit(solution)/shard_map/ppermute | solution.py:41
  51.9 3.7 %collective-permute-start.14 = (f32[80,16]{0,1:T(8,128)S(1)}, f32[80,16]{0,1:T(8,128)S(1)}, u32[]{:S(2)}, u32[]{:S(2)}) collective-permute-start(f32[80,16]{0,1:T(8,128)S(1)} %fusion.44), channel_id=1, source_target_pairs={{0,2},{1,3},{2,0},{3,1},{4,6},{5,7},{6,4},{7,5},{8,10},{9,11},{10,... | collective-permute-start | bytes 15368 | tf_op jit(solution)/shard_map/ppermute | solution.py:41
  55.5 4.7 %collective-permute-start.15 = (f32[80,16]{0,1:T(8,128)S(1)}, f32[80,16]{0,1:T(8,128)S(1)}, u32[]{:S(2)}, u32[]{:S(2)}) collective-permute-start(f32[80,16]{0,1:T(8,128)S(1)} %add.110), channel_id=1, source_target_pairs={{0,4},{1,5},{2,6},{3,7},{4,0},{5,1},{6,2},{7,3},{8,12},{9,13},{10,... | collective-permute-start | bytes 15368 | tf_op jit(solution)/shard_map/ppermute | solution.py:41
  60.2 3.9 %collective-permute-start.16 = (f32[80,16]{0,1:T(8,128)S(1)}, f32[80,16]{0,1:T(8,128)S(1)}, u32[]{:S(2)}, u32[]{:S(2)}) collective-permute-start(f32[80,16]{0,1:T(8,128)S(1)} %add.111), channel_id=1, source_target_pairs={{0,8},{1,9},{2,10},{3,11},{4,12},{5,13},{6,14},{7,15},{8,0},{9,1},... | collective-permute-start | bytes 15368 | tf_op jit(solution)/shard_map/ppermute | solution.py:41
  64.2 5.1 %collective-permute-start.17 = (f32[80,16]{0,1:T(8,128)S(1)}, f32[80,16]{0,1:T(8,128)S(1)}, u32[]{:S(2)}, u32[]{:S(2)}) collective-permute-start(f32[80,16]{0,1:T(8,128)S(1)} %add.112), channel_id=1, source_target_pairs={{0,16},{1,17},{2,18},{3,19},{4,20},{5,21},{6,22},{7,23},{8,24},{9,... | collective-permute-start | bytes 15368 | tf_op jit(solution)/shard_map/ppermute | solution.py:41
  69.3 4.4 %copy-start.2 = (f32[80,16]{0,1:T(8,128)}, f32[80,16]{0,1:T(8,128)S(1)}, u32[]{:S(2)}) copy-start(f32[80,16]{0,1:T(8,128)S(1)} %add.113) | copy-start | bytes 15364

commit v5 on v4

--- a/solution.py
+++ b/solution.py
@@ -139,13 +139,20 @@
     own_rows = coarse.reshape(1, local_count, vec_count * rank_width)
     offsets = list(range(-reach_groups, reach_groups + 1))
     reached = group_reach(own_rows, offsets)
-    window = lax.all_gather(reached, "coef", axis=1, tiled=True)
-    flat_rows = window.reshape(-1, vec_count * rank_width)
+    reach_width = len(offsets) * vec_count * rank_width
+    own_vectors = jnp.swapaxes(by_cluster, 0, 1).reshape(local_count, vec_count * leaf_size)
+    packed = jnp.concatenate(
+        [jnp.swapaxes(reached, 0, 1).reshape(local_count, reach_width), own_vectors], axis=1
+    )
+    gathered = lax.all_gather(packed, "coef", axis=0, tiled=True)
+    flat_rows = gathered[:, :reach_width].reshape(group_size * len(offsets), vec_count * rank_width)
     group_pos = lax.axis_index("leaf")
-    local_ids = (far_list - (group_pos - reach_groups) * group_size).reshape(-1)
-    sources = flat_rows.at[local_ids].get(mode="promise_in_bounds").reshape(
-        group_size, slot_count, vec_count, rank_width
-    )
+    source_group = far_list // group_size - (group_pos - reach_groups)
+    local_ids = ((far_list % group_size) * len(offsets) + source_group).reshape(-1)
+    picks = (local_ids[:, None] == jnp.arange(flat_rows.shape[0], dtype=jnp.int32)[None, :])
+    sources = jnp.dot(
+        picks.astype(jnp.bfloat16), flat_rows, preferred_element_type=jnp.float32
+    ).astype(jnp.bfloat16).reshape(group_size, slot_count, vec_count, rank_width)
     lane_ids = jnp.arange(rank_width, dtype=jnp.int32)
     keep_mask = lane_ids[None, None, :] < far_rank[:, :, None]
     sources = jnp.where(keep_mask[:, :, None, :], sources, jnp.zeros((), jnp.bfloat16))
@@ -156,13 +163,23 @@
     far_hat = butterfly_scatter(partial_far, "coef")
     far_round = far_hat.astype(jnp.bfloat16).reshape(local_count, vec_count, rank_width)
     far_part = jnp.einsum("cki,cvk->vci", leaf_basis, far_round, preferred_element_type=jnp.float32)
-    extended = extended_2(rounded, ((("leaf", "coef"), 1),), local_count * leaf_size)
-    extended = extended.reshape(vec_count, 3 * local_count, leaf_size)
-    device_pos = lax.axis_index("leaf") * coef_count + lax.axis_index("coef")
-    near_ids = (near_list - (device_pos - 1) * local_count).reshape(-1)
-    near_src = extended.at[:, near_ids].get(mode="promise_in_bounds").reshape(
-        vec_count, local_count, near_count, leaf_size
-    )
+    edge_route = []
+    for group in range(leaf_count - 1):
+        last = group * coef_count + coef_count - 1
+        edge_route += [(last, last + 1), (last + 1, last)]
+    edge_rows = lax.ppermute(own_vectors, ("leaf", "coef"), edge_route)
+    table = jnp.concatenate([edge_rows, gathered[:, reach_width:]], axis=0).reshape(
+        local_count + group_size, vec_count, leaf_size
+    )
+    coef_pos = lax.axis_index("coef")
+    group_first = group_pos * group_size
+    edge_first = jnp.where(coef_pos == 0, group_first - local_count, group_first + group_size)
+    in_group = near_list // group_size == group_pos
+    near_ids = jnp.where(in_group, local_count + near_list - group_first, near_list - edge_first)
+    near_picks = (near_ids[:, :, None] == jnp.arange(table.shape[0], dtype=jnp.int32)[None, None, :])
+    near_src = jnp.einsum(
+        "cnr,rvl->vcnl", near_picks.astype(jnp.bfloat16), table, preferred_element_type=jnp.float32
+    ).astype(jnp.bfloat16)
     near_terms = jnp.einsum(
         "jcnil,vcnl->jvci", near_blocks, near_src, preferred_element_type=jnp.float32
     )

time: 74.4 us -> 78.4 us (1.054)
  starting transfers between devices: 26.2 us -> 20 us
  local copies, waits for them, and re-layouts: 9.55 us -> 12.4 us
  matrix products: 8.14 us -> 10.7 us
  waiting for transfers between devices: 12.2 us -> 14.7 us
  blocking collectives: 6.93 us -> 9.19 us
    ppermute x5, starting transfers between devices: 9.37 us -> 4.96 us  [butterfly_sum(): block = block + lax.ppermute(block, axes, route)]
    ppermute x2 -> x1, starting transfers between devices: 4.91 us -> 1.26 us  [on_device(): edge_rows = lax.ppermute(own_vectors, ('leaf', 'coef'), edge_route)]
    ppermute x5, waiting for transfers between devices: 9.19 us -> 11.7 us  [butterfly_sum(): block = block + lax.ppermute(block, axes, route)]
    all_gather x1, blocking collectives: 6.93 us -> 9.19 us  [on_device(): gathered = lax.all_gather(packed, 'coef', axis=0, tiled=True)]
    reshape x3, local copies, waits for them, and re-layouts: 0.35 us -> 2.19 us  [the longest x1 1.12 us: on_device(): sources = jnp.dot(picks.astype(jnp.bfloat16), flat_rows, preferred_elemen...]
    ppermute x4, starting transfers between devices: 11 us -> 12.7 us  [shifted(): return lax.ppermute(block, axis, route)]
    dot_general x0 -> x2, matrix products: none -> 1.73 us  [the longest x1 1.51 us: on_device(): jnp.dot(picks.astype(jnp.bfloat16), flat_rows, preferred_element_type=jnp...]
    gather x2 -> x0, local copies, waits for them, and re-layouts: 1.42 us -> none  [the longest x1 0.72 us: on_device(): extended.at[:, near_ids].get(mode='promise_in_bounds')]
  transfers between devices with their start and end apart: 13 -> 12, of which waited for: 6 -> 6; matrix products, arithmetic and copies ran while one was open for 27% -> 32% of each run, Pallas kernels for 0% -> 0%
where the time goes in v5:
time: 78.4 us; the launch traced here: 77.7 us
  starting transfers between devices  20 us (26%)
  waiting for transfers between devices  14.7 us (19%)
  local copies, waits for them, and re-layouts  12.4 us (16%)
  matrix products  10.7 us (14%)
  blocking collectives  9.19 us (12%)
  other arithmetic  6.01 us (8%)
  Pallas kernels  2.43 us (3%)
  between operations  2.23 us (3%)
    ppermute x4, starting transfers between devices, shifted(): return lax.ppermute(block, axis, route)  12.7 us
    ppermute x5, waiting for transfers between devices, butterfly_sum(): block = block + lax.ppermute(block, axes, route)  11.7 us
    all_gather x1, blocking collectives, on_device(): gathered = lax.all_gather(packed, 'coef', axis=0, tiled=True)  9.19 us
    reshape x1, local copies, waits for them, and re-layouts, on_device(): couple = coupling.reshape(3, group_size, slot_count, rank_width, rank_width)  5.63 us
    ppermute x5, starting transfers between devices, butterfly_sum(): block = block + lax.ppermute(block, axes, route)  4.96 us
    dot_general x1, matrix products, on_device(): jnp.einsum('jcfkl,cfvl->jcfvk', couple, sources, preferred_element_type=j...  4.21 us
    ppermute x2, waiting for transfers between devices, butterfly_scatter(): parts = keep + lax.ppermute(give, axis, route)  2.96 us
    pallas_call x1, Pallas kernels, chol_solve(): pl.pallas_call(chol_solve_kernel, out_shape=(jax.ShapeDtypeStruct((size,...  2.43 us
  transfers between devices with their start and end apart: 12, of which 6 were waited for; matrix products, arithmetic and copies ran while one was open for 32% of the time, Pallas kernels for 0%

profile of v5, /device:TPU:0, one launch (start us, length us, event | category | flops | bytes accessed | tf_op | source)
XLA Modules:
  0.0 77.7 jit_solution(16915102255453044622)
XLA Ops:
  0.6 1.1 %convolution_convert_fusion.2 = bf16[4,16,64]{2,1,0:T(8,128)(2,1)S(1)} fusion(bf16[4,64,128]{2,1,0:T(8,128)(2,1)} %param.13, f32[16,512]{1,0:T(8,128)} %param.11), kind=kOutput, calls=%fused_computation.15 | convolution fusion | flops 1060864 | bytes 106496 | tf_op jit(solution)/shard_map/cki,vci->cvk/dot_general | solution.py:136
  1.9 1.3 %collective-permute-start.8 = (bf16[1,4,1024]{2,1,0:T(4,128)(2,1)S(1)}, bf16[1,4,1024]{2,1,0:T(4,128)(2,1)S(1)}, u32[]{:S(2)}, u32[]{:S(2)}) collective-permute-start(bf16[1,4,1024]{2,1,0:T(4,128)(2,1)S(1)} %reshape.54), channel_id=1, source_target_pairs={{8,0},{12,4},{16,8},{20,12},{24,16},{28,20},{9,1},{13,5},{17,9},{2... | collective-permute-start | bytes 24584 | tf_op jit(solution)/shard_map/ppermute | solution.py:12
  3.2 1.3 %collective-permute-start.7 = (bf16[1,4,1024]{2,1,0:T(4,128)(2,1)S(1)}, bf16[1,4,1024]{2,1,0:T(4,128)(2,1)S(1)}, u32[]{:S(2)}, u32[]{:S(2)}) collective-permute-start(bf16[1,4,1024]{2,1,0:T(4,128)(2,1)S(1)} %reshape.54), channel_id=1, source_target_pairs={{4,0},{8,4},{12,8},{16,12},{20,16},{24,20},{28,24},{5,1},{9,5},{13... | collective-permute-start | bytes 24584 | tf_op jit(solution)/shard_map/ppermute | solution.py:12
  4.5 5.5 %collective-permute-start.6 = (bf16[1,4,1024]{2,1,0:T(4,128)(2,1)S(1)}, bf16[1,4,1024]{2,1,0:T(4,128)(2,1)S(1)}, u32[]{:S(2)}, u32[]{:S(2)}) collective-permute-start(bf16[1,4,1024]{2,1,0:T(4,128)(2,1)S(1)} %reshape.54), channel_id=1, source_target_pairs={{0,4},{4,8},{8,12},{12,16},{16,20},{20,24},{24,28},{1,5},{5,9},{9,... | collective-permute-start | bytes 24584 | tf_op jit(solution)/shard_map/ppermute | solution.py:12
  10.0 4.6 %collective-permute-start.5 = (bf16[1,4,1024]{2,1,0:T(4,128)(2,1)S(1)}, bf16[1,4,1024]{2,1,0:T(4,128)(2,1)S(1)}, u32[]{:S(2)}, u32[]{:S(2)}) collective-permute-start(bf16[1,4,1024]{2,1,0:T(4,128)(2,1)S(1)} %reshape.54), channel_id=1, source_target_pairs={{0,8},{4,12},{8,16},{12,20},{16,24},{20,28},{1,9},{5,13},{9,17},{1... | collective-permute-start | bytes 24584 | tf_op jit(solution)/shard_map/ppermute | solution.py:12
  15.4 1.3 %collective-permute-start.11 = (bf16[4,2048]{1,0:T(4,128)(2,1)S(1)}, bf16[4,2048]{1,0:T(4,128)(2,1)}, u32[]{:S(2)}, u32[]{:S(2)}) collective-permute-start(bf16[4,2048]{1,0:T(4,128)(2,1)S(1)} %bitcast.100), channel_id=1, source_target_pairs={{3,4},{4,3},{7,8},{8,7},{11,12},{12,11},{15,16},{16,15},{19,20},{2... | collective-permute-start | bytes 49160 | tf_op jit(solution)/shard_map/ppermute | solution.py:170
  18.1 1.3 %subtract_select_fusion = s32[4,8]{1,0:T(4,128)} fusion(s32[4,8]{1,0:T(4,128)} %param.15, s32[]{:T(128)S(6)} %select_n.74, s32[]{:T(128)S(6)} %mul.29, s32[]{:T(128)S(6)} %axis_index.27), kind=kLoop, calls=%fused_computation.71 | loop fusion | flops 640 | bytes 268 | tf_op jit(solution)/shard_map/jit(_where)/select_n | solution.py:178
  21.5 5.6 %reshape.59 = bf16[3,16,4,64,64]{4,3,2,1,0:T(8,128)(2,1)} reshape(bf16[3,16,4,4096]{3,2,1,0:T(4,128)(2,1)} %param.16) | data formatting | bytes 3145728 | tf_op jit(solution)/shard_map/reshape | solution.py:159
  27.2 9.2 %all-gather = bf16[4,4,7168]{2,1,0:T(4,128)(2,1)} all-gather(bf16[1,4,7168]{2,1,0:T(4,128)(2,1)S(1)} %maximum_bitcast_fusion), channel_id=1, replica_groups=mesh['leaf'=8,'coef'=4] {'coef'}, dimensions={0}, use_global_device_ids=true | all-gather | bytes 286720 | tf_op jit(solution)/shard_map/all_gather | solution.py:147
  36.4 1.0 %reshape.63 = bf16[16,7168]{1,0:T(8,128)(2,1)S(1)} reshape(bf16[4,4,7168]{2,1,0:T(4,128)(2,1)} %all-gather) | data formatting | bytes 458752
  38.2 1.1 %reshape.57 = bf16[80,1024]{1,0:T(8,128)(2,1)S(1)} reshape(bf16[16,5120]{1,0:T(8,128)(2,1)} %slice.16) | data formatting | bytes 327680 | tf_op jit(solution)/shard_map/reshape | solution.py:148
  39.2 1.5 %convolution_convert_fusion = bf16[64,1024]{1,0:T(8,128)(2,1)} fusion(bf16[80,1024]{1,0:T(8,128)(2,1)S(1)} %reshape.57, s32[64]{0:T(128)} %eq.48), kind=kOutput, calls=%fused_computation.8 | convolution fusion | flops 10556416 | bytes 295168 | tf_op jit(solution)/shard_map/dot_general | solution.py:153
  40.8 1.1 %reshape.58 = bf16[16,4,16,64]{3,2,1,0:T(8,128)(2,1)S(1)} reshape(bf16[64,1024]{1,0:T(8,128)(2,1)} %convolution_convert_fusion) | data formatting | bytes 262144 | tf_op jit(solution)/shard_map/reshape | solution.py:155
  41.9 4.2 %fusion.6 = bf16[3,16,4,16,64]{4,3,0,2,1:T(8,128)(2,1)S(1)} fusion(bf16[3,16,4,64,64]{4,3,2,1,0:T(8,128)(2,1)} %reshape.59, bf16[16,4,16,64]{3,2,1,0:T(8,128)(2,1)S(1)} %reshape.58, pred[16,4,64]{2,1,0:T(4,128)(4,1)} %get-tuple-element.15), kind=kOutput, calls=%fused_computation.7 | convolution fusion | flops 25231360 | bytes 2101248 | tf_op jit(solution)/shard_map/jcfkl,cfvl->jcfvk/dot_general | solution.py:160
  47.7 1.0 %reshape_reshape_reshape.3 = f32[2,2,4,1024]{3,2,1,0:T(4,128)S(1)} reshape(f32[16,16,64]{2,1,0:T(8,128)} %multiply_reduce_fusion) | data formatting | bytes 131072 | tf_op jit(solution)/shard_map/reshape;reshape;reshape | solution.py:55
  52.0 3.0 %collective-permute-done.10 = f32[1,4,1024]{2,1,0:T(4,128)S(1)} collective-permute-done((f32[1,4,1024]{2,1,0:T(4,128)S(1)}, f32[1,4,1024]{2,1,0:T(4,128)S(1)}, u32[]{:S(2)}, u32[]{:S(2)}) %collective-permute-start.10) | collective-permute-done | bytes 16416 | tf_op jit(solution)/shard_map/ppermute | solution.py:59
  56.5 1.2 %collective-permute-done.12 = f32[80,16]{0,1:T(8,128)S(1)} collective-permute-done((f32[80,16]{0,1:T(8,128)S(1)}, f32[80,16]{0,1:T(8,128)S(1)}, u32[]{:S(2)}, u32[]{:S(2)}) %collective-permute-start.12) | collective-permute-done | bytes 5152 | tf_op jit(solution)/shard_map/ppermute | solution.py:41
  58.3 3.1 %collective-permute-done.13 = f32[80,16]{0,1:T(8,128)S(1)} collective-permute-done((f32[80,16]{0,1:T(8,128)S(1)}, f32[80,16]{0,1:T(8,128)S(1)}, u32[]{:S(2)}, u32[]{:S(2)}) %collective-permute-start.13) | collective-permute-done | bytes 5152 | tf_op jit(solution)/shard_map/ppermute | solution.py:41
  62.0 3.0 %collective-permute-done.14 = f32[80,16]{0,1:T(8,128)S(1)} collective-permute-done((f32[80,16]{0,1:T(8,128)S(1)}, f32[80,16]{0,1:T(8,128)S(1)}, u32[]{:S(2)}, u32[]{:S(2)}) %collective-permute-start.14) | collective-permute-done | bytes 5152 | tf_op jit(solution)/shard_map/ppermute | solution.py:41
  65.0 1.6 %collective-permute-start.15 = (f32[80,16]{0,1:T(8,128)S(1)}, f32[80,16]{0,1:T(8,128)S(1)}, u32[]{:S(2)}, u32[]{:S(2)}) collective-permute-start(f32[80,16]{0,1:T(8,128)S(1)} %add.99), channel_id=1, source_target_pairs={{0,8},{1,9},{2,10},{3,11},{4,12},{5,13},{6,14},{7,15},{8,0},{9,1},... | collective-permute-start | bytes 15368 | tf_op jit(solution)/shard_map/ppermute | solution.py:41
  66.6 2.1 %collective-permute-done.15 = f32[80,16]{0,1:T(8,128)S(1)} collective-permute-done((f32[80,16]{0,1:T(8,128)S(1)}, f32[80,16]{0,1:T(8,128)S(1)}, u32[]{:S(2)}, u32[]{:S(2)}) %collective-permute-start.15) | collective-permute-done | bytes 5152 | tf_op jit(solution)/shard_map/ppermute | solution.py:41
  68.7 2.2 %collective-permute-start.16 = (f32[80,16]{0,1:T(8,128)S(1)}, f32[80,16]{0,1:T(8,128)S(1)}, u32[]{:S(2)}, u32[]{:S(2)}) collective-permute-start(f32[80,16]{0,1:T(8,128)S(1)} %add.100), channel_id=1, source_target_pairs={{0,16},{1,17},{2,18},{3,19},{4,20},{5,21},{6,22},{7,23},{8,24},{9,... | collective-permute-start | bytes 15368 | tf_op jit(solution)/shard_map/ppermute | solution.py:41
  70.9 2.4 %collective-permute-done.16 = f32[80,16]{0,1:T(8,128)S(1)} collective-permute-done((f32[80,16]{0,1:T(8,128)S(1)}, f32[80,16]{0,1:T(8,128)S(1)}, u32[]{:S(2)}, u32[]{:S(2)}) %collective-permute-start.16) | collective-permute-done | bytes 5152 | tf_op jit(solution)/shard_map/ppermute | solution.py:41
  75.3 2.4 %shard_map.112 = (f32[16,16]{1,0:T(8,128)}, f32[16,512]{1,0:T(8,128)}) custom-call(f32[16,16]{1,0:T(8,128)S(1)} %get-tuple-element.18.gram_ref, f32[16,512]{1,0:T(8,128)S(1)} %convolution_subtract_fusion.residue_ref), custom_call_target="tpu_custom_call" | custom-call | flops 540672 | bytes 67584 | tf_op jit(solution)/shard_map/pallas_call | solution.py:105
  (68 shorter events, 13.6 us)
Async XLA Ops:
  0.6 49.5 %copy-start = (bf16[3,4,8,128,128]{4,3,2,1,0:T(8,128)(2,1)S(1)}, bf16[3,4,8,128,128]{4,3,2,1,0:T(8,128)(2,1)}, u32[]{:S(2)}) copy-start(bf16[3,4,8,128,128]{4,3,2,1,0:T(8,128)(2,1)} %param.14) | copy-start | bytes 9437188
  1.9 25.3 %collective-permute-start.8 = (bf16[1,4,1024]{2,1,0:T(4,128)(2,1)S(1)}, bf16[1,4,1024]{2,1,0:T(4,128)(2,1)S(1)}, u32[]{:S(2)}, u32[]{:S(2)}) collective-permute-start(bf16[1,4,1024]{2,1,0:T(4,128)(2,1)S(1)} %reshape.54), channel_id=1, source_target_pairs={{8,0},{12,4},{16,8},{20,12},{24,16},{28,20},{9,1},{13,5},{17,9},{2... | collective-permute-start | bytes 24584 | tf_op jit(solution)/shard_map/ppermute | solution.py:12
  3.2 24.0 %collective-permute-start.7 = (bf16[1,4,1024]{2,1,0:T(4,128)(2,1)S(1)}, bf16[1,4,1024]{2,1,0:T(4,128)(2,1)S(1)}, u32[]{:S(2)}, u32[]{:S(2)}) collective-permute-start(bf16[1,4,1024]{2,1,0:T(4,128)(2,1)S(1)} %reshape.54), channel_id=1, source_target_pairs={{4,0},{8,4},{12,8},{16,12},{20,16},{24,20},{28,24},{5,1},{9,5},{13... | collective-permute-start | bytes 24584 | tf_op jit(solution)/shard_map/ppermute | solution.py:12
  4.5 22.6 %collective-permute-start.6 = (bf16[1,4,1024]{2,1,0:T(4,128)(2,1)S(1)}, bf16[1,4,1024]{2,1,0:T(4,128)(2,1)S(1)}, u32[]{:S(2)}, u32[]{:S(2)}) collective-permute-start(bf16[1,4,1024]{2,1,0:T(4,128)(2,1)S(1)} %reshape.54), channel_id=1, source_target_pairs={{0,4},{4,8},{8,12},{12,16},{16,20},{20,24},{24,28},{1,5},{5,9},{9,... | collective-permute-start | bytes 24584 | tf_op jit(solution)/shard_map/ppermute | solution.py:12
  10.0 17.1 %collective-permute-start.5 = (bf16[1,4,1024]{2,1,0:T(4,128)(2,1)S(1)}, bf16[1,4,1024]{2,1,0:T(4,128)(2,1)S(1)}, u32[]{:S(2)}, u32[]{:S(2)}) collective-permute-start(bf16[1,4,1024]{2,1,0:T(4,128)(2,1)S(1)} %reshape.54), channel_id=1, source_target_pairs={{0,8},{4,12},{8,16},{12,20},{16,24},{20,28},{1,9},{5,13},{9,17},{1... | collective-permute-start | bytes 24584 | tf_op jit(solution)/shard_map/ppermute | solution.py:12
  15.4 33.7 %collective-permute-start.11 = (bf16[4,2048]{1,0:T(4,128)(2,1)S(1)}, bf16[4,2048]{1,0:T(4,128)(2,1)}, u32[]{:S(2)}, u32[]{:S(2)}) collective-permute-start(bf16[4,2048]{1,0:T(4,128)(2,1)S(1)} %bitcast.100), channel_id=1, source_target_pairs={{3,4},{4,3},{7,8},{8,7},{11,12},{12,11},{15,16},{16,15},{19,20},{2... | collective-permute-start | bytes 49160 | tf_op jit(solution)/shard_map/ppermute | solution.py:170
  37.4 1.8 %copy-start.1 = (bf16[16,7168]{1,0:T(8,128)(2,1)}, bf16[16,7168]{1,0:T(8,128)(2,1)S(1)}, u32[]{:S(2)}) copy-start(bf16[16,7168]{1,0:T(8,128)(2,1)S(1)} %reshape.63) | copy-start | bytes 688132
  41.9 5.0 %copy-start.4 = (f32[16,4,64]{2,1,0:T(4,128)S(1)}, f32[16,4,64]{2,1,0:T(4,128)}, u32[]{:S(2)}) copy-start(f32[16,4,64]{2,1,0:T(4,128)} %get-tuple-element.14) | copy-start | bytes 49156
  41.9 7.2 %slice-start = ((bf16[16,7168]{1,0:T(8,128)(2,1)}), bf16[16,2048]{1,0:T(8,128)(2,1)S(1)}, s32[]{:S(2)}) async-start(bf16[16,7168]{1,0:T(8,128)(2,1)} %copy-done.1), calls=%async_computation | async-start | bytes 131072 | tf_op jit(solution)/shard_map/slice | solution.py:171
  46.1 3.8 %copy-start.5 = (s32[4,8]{1,0:T(4,128)S(1)}, s32[4,8]{1,0:T(4,128)}, u32[]{:S(2)}) copy-start(s32[4,8]{1,0:T(4,128)} %subtract_select_fusion) | copy-start | bytes 388
  46.9 9.3 %copy-start.2 = (f32[64,512]{1,0:T(8,128)S(1)}, f32[64,512]{1,0:T(8,128)}, u32[]{:S(2)}) copy-start(f32[64,512]{1,0:T(8,128)} %param.19) | copy-start | bytes 393220
  48.7 2.4 %collective-permute-start.9 = (f32[2,4,1024]{2,1,0:T(4,128)S(1)}, f32[2,4,1024]{2,1,0:T(4,128)S(1)}, u32[]{:S(2)}, u32[]{:S(2)}) collective-permute-start(f32[2,4,1024]{2,1,0:T(4,128)S(1)} %dynamic-slice_bitcast_fusion), channel_id=1, source_target_pairs={{0,1},{1,0},{2,3},{3,2},{4,5},{5,4},{6,7},{7,6},{8,9},{9,8},{10,11... | collective-permute-start | bytes 98312 | tf_op jit(solution)/shard_map/ppermute | solution.py:59
  51.1 3.8 %collective-permute-start.10 = (f32[1,4,1024]{2,1,0:T(4,128)S(1)}, f32[1,4,1024]{2,1,0:T(4,128)S(1)}, u32[]{:S(2)}, u32[]{:S(2)}) collective-permute-start(f32[1,4,1024]{2,1,0:T(4,128)S(1)} %constant_dynamic-slice_fusion), channel_id=1, source_target_pairs={{0,2},{1,3},{2,0},{3,1},{4,6},{5,7},{6,4},{7,5},{8,10},{9,11},{10,... | collective-permute-start | bytes 49160 | tf_op jit(solution)/shard_map/ppermute | solution.py:59
  56.5 1.2 %collective-permute-start.12 = (f32[80,16]{0,1:T(8,128)S(1)}, f32[80,16]{0,1:T(8,128)S(1)}, u32[]{:S(2)}, u32[]{:S(2)}) collective-permute-start(f32[80,16]{0,1:T(8,128)S(1)} %pad_maximum_fusion.1), channel_id=1, source_target_pairs={{0,1},{1,0},{2,3},{3,2},{4,5},{5,4},{6,7},{7,6},{8,9},{9,8},{10,11... | collective-permute-start | bytes 15368 | tf_op jit(solution)/shard_map/ppermute | solution.py:41
  57.7 3.7 %collective-permute-start.13 = (f32[80,16]{0,1:T(8,128)S(1)}, f32[80,16]{0,1:T(8,128)S(1)}, u32[]{:S(2)}, u32[]{:S(2)}) collective-permute-start(f32[80,16]{0,1:T(8,128)S(1)} %fusion.57), channel_id=1, source_target_pairs={{0,2},{1,3},{2,0},{3,1},{4,6},{5,7},{6,4},{7,5},{8,10},{9,11},{10,... | collective-permute-start | bytes 15368 | tf_op jit(solution)/shard_map/ppermute | solution.py:41
  61.4 3.7 %collective-permute-start.14 = (f32[80,16]{0,1:T(8,128)S(1)}, f32[80,16]{0,1:T(8,128)S(1)}, u32[]{:S(2)}, u32[]{:S(2)}) collective-permute-start(f32[80,16]{0,1:T(8,128)S(1)} %add.98), channel_id=1, source_target_pairs={{0,4},{1,5},{2,6},{3,7},{4,0},{5,1},{6,2},{7,3},{8,12},{9,13},{10,... | collective-permute-start | bytes 15368 | tf_op jit(solution)/shard_map/ppermute | solution.py:41
  65.0 3.7 %collective-permute-start.15 = (f32[80,16]{0,1:T(8,128)S(1)}, f32[80,16]{0,1:T(8,128)S(1)}, u32[]{:S(2)}, u32[]{:S(2)}) collective-permute-start(f32[80,16]{0,1:T(8,128)S(1)} %add.99), channel_id=1, source_target_pairs={{0,8},{1,9},{2,10},{3,11},{4,12},{5,13},{6,14},{7,15},{8,0},{9,1},... | collective-permute-start | bytes 15368 | tf_op jit(solution)/shard_map/ppermute | solution.py:41
  68.7 4.5 %collective-permute-start.16 = (f32[80,16]{0,1:T(8,128)S(1)}, f32[80,16]{0,1:T(8,128)S(1)}, u32[]{:S(2)}, u32[]{:S(2)}) collective-permute-start(f32[80,16]{0,1:T(8,128)S(1)} %add.100), channel_id=1, source_target_pairs={{0,16},{1,17},{2,18},{3,19},{4,20},{5,21},{6,22},{7,23},{8,24},{9,... | collective-permute-start | bytes 15368 | tf_op jit(solution)/shard_map/ppermute | solution.py:41
  73.3 4.4 %copy-start.3 = (f32[80,16]{0,1:T(8,128)}, f32[80,16]{0,1:T(8,128)S(1)}, u32[]{:S(2)}) copy-start(f32[80,16]{0,1:T(8,128)S(1)} %add.101) | copy-start | bytes 15364

commit v6 on v4

--- a/solution.py
+++ b/solution.py
@@ -41,6 +41,18 @@
         block = block + lax.ppermute(block, axes, route)
         distance *= 2
     return block
+
+
+def xor_gather(block, axis, dim):
+    count = lax.axis_size(axis)
+    if not is_power_of_two(count):
+        return lax.all_gather(block, axis, axis=dim, tiled=True), False
+    distance = 1
+    while distance < count:
+        route = [(i, i ^ distance) for i in range(count)]
+        block = jnp.concatenate([block, lax.ppermute(block, axis, route)], axis=dim)
+        distance *= 2
+    return block, True
 
 
 def butterfly_scatter(block, axis):
@@ -139,10 +151,15 @@
     own_rows = coarse.reshape(1, local_count, vec_count * rank_width)
     offsets = list(range(-reach_groups, reach_groups + 1))
     reached = group_reach(own_rows, offsets)
-    window = lax.all_gather(reached, "coef", axis=1, tiled=True)
+    window, xor_order = xor_gather(reached, "coef", 1)
     flat_rows = window.reshape(-1, vec_count * rank_width)
     group_pos = lax.axis_index("leaf")
-    local_ids = (far_list - (group_pos - reach_groups) * group_size).reshape(-1)
+    local_ids = far_list - (group_pos - reach_groups) * group_size
+    if xor_order:
+        in_group = local_ids % group_size
+        holder = (in_group // local_count) ^ lax.axis_index("coef")
+        local_ids = local_ids - in_group + holder * local_count + in_group % local_count
+    local_ids = local_ids.reshape(-1)
     sources = flat_rows.at[local_ids].get(mode="promise_in_bounds").reshape(
         group_size, slot_count, vec_count, rank_width
     )

time: 74.4 us -> 72.3 us (0.972)
  blocking collectives: 6.93 us -> 0 us
  starting transfers between devices: 26.2 us -> 31.7 us
  other arithmetic: 6.09 us -> 4.8 us
  waiting for transfers between devices: 12.2 us -> 11.3 us
  matrix products: 8.14 us -> 8.99 us
    all_gather x1 -> x0, blocking collectives: 6.93 us -> none  [on_device(): window = lax.all_gather(reached, 'coef', axis=1, tiled=True)]
    ppermute x0 -> x2, starting transfers between devices: none -> 3.86 us  [xor_gather(): block = jnp.concatenate([block, lax.ppermute(block, axis, route)], axis=dim)]
    ppermute x0 -> x2, waiting for transfers between devices: none -> 1.41 us  [xor_gather(): block = jnp.concatenate([block, lax.ppermute(block, axis, route)], axis=dim)]
    ppermute x5, starting transfers between devices: 9.37 us -> 10.7 us  [butterfly_sum(): block = block + lax.ppermute(block, axes, route)]
    ppermute x5, waiting for transfers between devices: 9.19 us -> 7.93 us  [butterfly_sum(): block = block + lax.ppermute(block, axes, route)]
    ppermute x2, waiting for transfers between devices: 3 us -> 1.99 us  [butterfly_scatter(): parts = keep + lax.ppermute(give, axis, route)]
    ppermute x2, starting transfers between devices: 0.92 us -> 1.9 us  [butterfly_scatter(): parts = keep + lax.ppermute(give, axis, route)]
    another operation x1, local copies, waits for them, and re-layouts: 0.11 us -> 1 us  [butterfly_scatter(): pairs = parts.reshape(parts.shape[0] // 2, 2, *parts.shape[1:])]
  transfers between devices with their start and end apart: 13 -> 15, of which waited for: 6 -> 8; matrix products, arithmetic and copies ran while one was open for 27% -> 17% of each run, Pallas kernels for 0% -> 0%
where the time goes in v6:
time: 72.3 us; the launch traced here: 71.7 us
  starting transfers between devices  31.7 us (44%)
  waiting for transfers between devices  11.3 us (16%)
  local copies, waits for them, and re-layouts  10.2 us (14%)
  matrix products  8.99 us (12%)
  other arithmetic  4.8 us (7%)
  Pallas kernels  2.43 us (3%)
  between operations  2.26 us (3%)
    ppermute x4, starting transfers between devices, shifted(): return lax.ppermute(block, axis, route)  11 us
    ppermute x5, starting transfers between devices, butterfly_sum(): block = block + lax.ppermute(block, axes, route)  10.7 us
    ppermute x5, waiting for transfers between devices, butterfly_sum(): block = block + lax.ppermute(block, axes, route)  7.93 us
    reshape x1, local copies, waits for them, and re-layouts, on_device(): couple = coupling.reshape(3, group_size, slot_count, rank_width, rank_width)  5.63 us
    dot_general x1, matrix products, on_device(): jnp.einsum('jcfkl,cfvl->jcfvk', couple, sources, preferred_element_type=j...  4.2 us
    ppermute x2, starting transfers between devices, xor_gather(): block = jnp.concatenate([block, lax.ppermute(block, axis, route)], axis=dim)  3.86 us
    ppermute x1, starting transfers between devices, extended_2(): lax.ppermute(lax.slice_in_dim(block, block.shape[dim] - width, None, axis...  3.03 us
    pallas_call x1, Pallas kernels, chol_solve(): pl.pallas_call(chol_solve_kernel, out_shape=(jax.ShapeDtypeStruct((size,...  2.43 us
  transfers between devices with their start and end apart: 15, of which 8 were waited for; matrix products, arithmetic and copies ran while one was open for 17% of the time, Pallas kernels for 0%

profile of v6, /device:TPU:0, one launch (start us, length us, event | category | flops | bytes accessed | tf_op | source)
XLA Modules:
  0.0 71.7 jit_solution(4409388996990232993)
XLA Ops:
  1.9 5.0 %collective-permute-start.5 = (bf16[1,4,1024]{2,1,0:T(4,128)(2,1)S(1)}, bf16[1,4,1024]{2,1,0:T(4,128)(2,1)S(1)}, u32[]{:S(2)}, u32[]{:S(2)}) collective-permute-start(bf16[1,4,1024]{2,1,0:T(4,128)(2,1)S(1)} %reshape.111), channel_id=1, source_target_pairs={{0,8},{4,12},{8,16},{12,20},{16,24},{20,28},{1,9},{5,13},{9,17},{1... | collective-permute-start | bytes 24584 | tf_op jit(solution)/shard_map/ppermute | solution.py:12
  6.8 3.4 %collective-permute-start.6 = (bf16[1,4,1024]{2,1,0:T(4,128)(2,1)S(1)}, bf16[1,4,1024]{2,1,0:T(4,128)(2,1)S(1)}, u32[]{:S(2)}, u32[]{:S(2)}) collective-permute-start(bf16[1,4,1024]{2,1,0:T(4,128)(2,1)S(1)} %reshape.111), channel_id=1, source_target_pairs={{0,4},{4,8},{8,12},{12,16},{16,20},{20,24},{24,28},{1,5},{5,9},{9,... | collective-permute-start | bytes 24584 | tf_op jit(solution)/shard_map/ppermute | solution.py:12
  10.3 1.3 %collective-permute-start.7 = (bf16[1,4,1024]{2,1,0:T(4,128)(2,1)S(1)}, bf16[1,4,1024]{2,1,0:T(4,128)(2,1)S(1)}, u32[]{:S(2)}, u32[]{:S(2)}) collective-permute-start(bf16[1,4,1024]{2,1,0:T(4,128)(2,1)S(1)} %reshape.111), channel_id=1, source_target_pairs={{4,0},{8,4},{12,8},{16,12},{20,16},{24,20},{28,24},{5,1},{9,5},{13... | collective-permute-start | bytes 24584 | tf_op jit(solution)/shard_map/ppermute | solution.py:12
  11.6 1.3 %collective-permute-start.8 = (bf16[1,4,1024]{2,1,0:T(4,128)(2,1)S(1)}, bf16[1,4,1024]{2,1,0:T(4,128)(2,1)S(1)}, u32[]{:S(2)}, u32[]{:S(2)}) collective-permute-start(bf16[1,4,1024]{2,1,0:T(4,128)(2,1)S(1)} %reshape.111), channel_id=1, source_target_pairs={{8,0},{12,4},{16,8},{20,12},{24,16},{28,20},{9,1},{13,5},{17,9},{2... | collective-permute-start | bytes 24584 | tf_op jit(solution)/shard_map/ppermute | solution.py:12
  13.6 1.3 %collective-permute-start.14 = (bf16[16,512]{1,0:T(8,128)(2,1)S(1)}, bf16[16,512]{1,0:T(8,128)(2,1)S(1)}, u32[]{:S(2)}, u32[]{:S(2)}) collective-permute-start(bf16[16,512]{1,0:T(8,128)(2,1)S(1)} %convert_element_type.24), channel_id=1, source_target_pairs={{1,0},{2,1},{3,2},{4,3},{5,4},{6,5},{7,6},{8,7},{9,8},{10,9},{11,1... | collective-permute-start | bytes 49160 | tf_op jit(solution)/shard_map/ppermute | solution.py:23
  18.1 3.0 %collective-permute-start.13 = (bf16[16,512]{1,0:T(8,128)(2,1)S(1)}, bf16[16,512]{1,0:T(8,128)(2,1)S(1)}, u32[]{:S(2)}, u32[]{:S(2)}) collective-permute-start(bf16[16,512]{1,0:T(8,128)(2,1)S(1)} %convert_element_type.24), channel_id=1, source_target_pairs={{0,1},{1,2},{2,3},{3,4},{4,5},{5,6},{6,7},{7,8},{8,9},{9,10},{10,1... | collective-permute-start | bytes 49160 | tf_op jit(solution)/shard_map/ppermute | solution.py:20
  21.2 1.2 %collective-permute-start.9 = (bf16[5,4,1024]{2,1,0:T(4,128)(2,1)S(1)}, bf16[5,4,1024]{2,1,0:T(4,128)(2,1)S(1)}, u32[]{:S(2)}, u32[]{:S(2)}) collective-permute-start(bf16[5,4,1024]{2,1,0:T(4,128)(2,1)S(1)} %constant_dynamic-update-slice_fusion), channel_id=1, source_target_pairs={{0,1},{1,0},{2,3},{3,2},{4,5},{5,4},{6,7},{7,6},{8,9},{9,8},{10,11... | collective-permute-start | bytes 122888 | tf_op jit(solution)/shard_map/ppermute | solution.py:53
  22.4 5.6 %reshape.115 = bf16[3,16,4,64,64]{4,3,2,1,0:T(8,128)(2,1)} reshape(bf16[3,16,4,4096]{3,2,1,0:T(4,128)(2,1)} %param.16) | data formatting | bytes 3145728 | tf_op jit(solution)/shard_map/reshape | solution.py:169
  28.8 2.7 %collective-permute-start.10 = (bf16[5,8,1024]{2,1,0:T(8,128)(2,1)S(1)}, bf16[5,8,1024]{2,1,0:T(8,128)(2,1)S(1)}, u32[]{:S(2)}, u32[]{:S(2)}) collective-permute-start(bf16[5,8,1024]{2,1,0:T(8,128)(2,1)S(1)} %pad_maximum_fusion.1), channel_id=1, source_target_pairs={{0,2},{1,3},{2,0},{3,1},{4,6},{5,7},{6,4},{7,5},{8,10},{9,11},{10,... | collective-permute-start | bytes 245768 | tf_op jit(solution)/shard_map/ppermute | solution.py:53
  31.5 1.2 %gather_fusion.1 = bf16[32,16,128]{2,1,0:T(8,128)(2,1)} fusion(bf16[16,12,128]{2,0,1:T(8,128)(2,1)S(1)} %copy_bitcast_fusion, s32[1024]{0:T(1024)S(1)} %pad_clamp_fusion), kind=kCustom, calls=%fused_computation.1 | custom fusion | bytes 262272 | tf_op jit(solution)/shard_map/gather | solution.py:180
  32.8 1.4 %collective-permute-done.10 = bf16[5,8,1024]{2,1,0:T(8,128)(2,1)S(1)} collective-permute-done((bf16[5,8,1024]{2,1,0:T(8,128)(2,1)S(1)}, bf16[5,8,1024]{2,1,0:T(8,128)(2,1)S(1)}, u32[]{:S(2)}, u32[]{:S(2)}) %collective-permute-start.10) | collective-permute-done | bytes 81952 | tf_op jit(solution)/shard_map/ppermute | solution.py:53
  35.1 4.2 %fusion.6 = bf16[3,16,4,16,64]{4,3,0,2,1:T(8,128)(2,1)S(1)} fusion(bf16[3,16,4,64,64]{4,3,2,1,0:T(8,128)(2,1)} %reshape.115, bf16[16,4,16,64]{3,2,1,0:T(8,128)(2,1)S(1)} %reshape.114, pred[16,4,64]{2,1,0:T(4,128)(4,1)S(1)} %get-tuple-element.15), kind=kOutput, calls=%fused_computation.9 | convolution fusion | flops 25231360 | bytes 2101248 | tf_op jit(solution)/shard_map/jcfkl,cfvl->jcfvk/dot_general | solution.py:170
  43.2 1.8 %collective-permute-start.12 = (f32[1,4,1024]{2,1,0:T(4,128)S(1)}, f32[1,4,1024]{2,1,0:T(4,128)S(1)}, u32[]{:S(2)}, u32[]{:S(2)}) collective-permute-start(f32[1,4,1024]{2,1,0:T(4,128)S(1)} %constant_dynamic-slice_fusion), channel_id=1, source_target_pairs={{0,2},{1,3},{2,0},{3,1},{4,6},{5,7},{6,4},{7,5},{8,10},{9,11},{10,... | collective-permute-start | bytes 49160 | tf_op jit(solution)/shard_map/ppermute | solution.py:71
  45.3 1.7 %collective-permute-done.12 = f32[1,4,1024]{2,1,0:T(4,128)S(1)} collective-permute-done((f32[1,4,1024]{2,1,0:T(4,128)S(1)}, f32[1,4,1024]{2,1,0:T(4,128)S(1)}, u32[]{:S(2)}, u32[]{:S(2)}) %collective-permute-start.12) | collective-permute-done | bytes 16416 | tf_op jit(solution)/shard_map/ppermute | solution.py:71
  48.6 1.2 %collective-permute-done.15 = f32[80,16]{0,1:T(8,128)S(1)} collective-permute-done((f32[80,16]{0,1:T(8,128)S(1)}, f32[80,16]{0,1:T(8,128)S(1)}, u32[]{:S(2)}, u32[]{:S(2)}) %collective-permute-start.15) | collective-permute-done | bytes 5152 | tf_op jit(solution)/shard_map/ppermute | solution.py:41
  49.8 1.8 %collective-permute-start.16 = (f32[80,16]{0,1:T(8,128)S(1)}, f32[80,16]{0,1:T(8,128)S(1)}, u32[]{:S(2)}, u32[]{:S(2)}) collective-permute-start(f32[80,16]{0,1:T(8,128)S(1)} %fusion.51), channel_id=1, source_target_pairs={{0,2},{1,3},{2,0},{3,1},{4,6},{5,7},{6,4},{7,5},{8,10},{9,11},{10,... | collective-permute-start | bytes 15368 | tf_op jit(solution)/shard_map/ppermute | solution.py:41
  51.6 1.9 %collective-permute-done.16 = f32[80,16]{0,1:T(8,128)S(1)} collective-permute-done((f32[80,16]{0,1:T(8,128)S(1)}, f32[80,16]{0,1:T(8,128)S(1)}, u32[]{:S(2)}, u32[]{:S(2)}) %collective-permute-start.16) | collective-permute-done | bytes 5152 | tf_op jit(solution)/shard_map/ppermute | solution.py:41
  53.5 3.1 %collective-permute-start.17 = (f32[80,16]{0,1:T(8,128)S(1)}, f32[80,16]{0,1:T(8,128)S(1)}, u32[]{:S(2)}, u32[]{:S(2)}) collective-permute-start(f32[80,16]{0,1:T(8,128)S(1)} %add.131), channel_id=1, source_target_pairs={{0,4},{1,5},{2,6},{3,7},{4,0},{5,1},{6,2},{7,3},{8,12},{9,13},{10,... | collective-permute-start | bytes 15368 | tf_op jit(solution)/shard_map/ppermute | solution.py:41
  56.5 1.6 %collective-permute-done.17 = f32[80,16]{0,1:T(8,128)S(1)} collective-permute-done((f32[80,16]{0,1:T(8,128)S(1)}, f32[80,16]{0,1:T(8,128)S(1)}, u32[]{:S(2)}, u32[]{:S(2)}) %collective-permute-start.17) | collective-permute-done | bytes 5152 | tf_op jit(solution)/shard_map/ppermute | solution.py:41
  58.2 2.4 %collective-permute-start.18 = (f32[80,16]{0,1:T(8,128)S(1)}, f32[80,16]{0,1:T(8,128)S(1)}, u32[]{:S(2)}, u32[]{:S(2)}) collective-permute-start(f32[80,16]{0,1:T(8,128)S(1)} %add.132), channel_id=1, source_target_pairs={{0,8},{1,9},{2,10},{3,11},{4,12},{5,13},{6,14},{7,15},{8,0},{9,1},... | collective-permute-start | bytes 15368 | tf_op jit(solution)/shard_map/ppermute | solution.py:41
  60.5 1.6 %collective-permute-done.18 = f32[80,16]{0,1:T(8,128)S(1)} collective-permute-done((f32[80,16]{0,1:T(8,128)S(1)}, f32[80,16]{0,1:T(8,128)S(1)}, u32[]{:S(2)}, u32[]{:S(2)}) %collective-permute-start.18) | collective-permute-done | bytes 5152 | tf_op jit(solution)/shard_map/ppermute | solution.py:41
  62.2 3.5 %collective-permute-start.19 = (f32[80,16]{0,1:T(8,128)S(1)}, f32[80,16]{0,1:T(8,128)S(1)}, u32[]{:S(2)}, u32[]{:S(2)}) collective-permute-start(f32[80,16]{0,1:T(8,128)S(1)} %add.133), channel_id=1, source_target_pairs={{0,16},{1,17},{2,18},{3,19},{4,20},{5,21},{6,22},{7,23},{8,24},{9,... | collective-permute-start | bytes 15368 | tf_op jit(solution)/shard_map/ppermute | solution.py:41
  65.6 1.6 %collective-permute-done.19 = f32[80,16]{0,1:T(8,128)S(1)} collective-permute-done((f32[80,16]{0,1:T(8,128)S(1)}, f32[80,16]{0,1:T(8,128)S(1)}, u32[]{:S(2)}, u32[]{:S(2)}) %collective-permute-start.19) | collective-permute-done | bytes 5152 | tf_op jit(solution)/shard_map/ppermute | solution.py:41
  69.3 2.4 %shard_map.112 = (f32[16,16]{1,0:T(8,128)}, f32[16,512]{1,0:T(8,128)}) custom-call(f32[16,16]{1,0:T(8,128)S(1)} %get-tuple-element.18.gram_ref, f32[16,512]{1,0:T(8,128)S(1)} %convolution_subtract_fusion.residue_ref), custom_call_target="tpu_custom_call" | custom-call | flops 540672 | bytes 67584 | tf_op jit(solution)/shard_map/pallas_call | solution.py:117
  (69 shorter events, 13.3 us)
Async XLA Ops:
  0.6 41.4 %copy-start = (bf16[3,4,8,128,128]{4,3,2,1,0:T(8,128)(2,1)S(1)}, bf16[3,4,8,128,128]{4,3,2,1,0:T(8,128)(2,1)}, u32[]{:S(2)}) copy-start(bf16[3,4,8,128,128]{4,3,2,1,0:T(8,128)(2,1)} %param.14) | copy-start | bytes 9437188
  1.9 16.2 %collective-permute-start.5 = (bf16[1,4,1024]{2,1,0:T(4,128)(2,1)S(1)}, bf16[1,4,1024]{2,1,0:T(4,128)(2,1)S(1)}, u32[]{:S(2)}, u32[]{:S(2)}) collective-permute-start(bf16[1,4,1024]{2,1,0:T(4,128)(2,1)S(1)} %reshape.111), channel_id=1, source_target_pairs={{0,8},{4,12},{8,16},{12,20},{16,24},{20,28},{1,9},{5,13},{9,17},{1... | collective-permute-start | bytes 24584 | tf_op jit(solution)/shard_map/ppermute | solution.py:12
  6.8 14.3 %collective-permute-start.6 = (bf16[1,4,1024]{2,1,0:T(4,128)(2,1)S(1)}, bf16[1,4,1024]{2,1,0:T(4,128)(2,1)S(1)}, u32[]{:S(2)}, u32[]{:S(2)}) collective-permute-start(bf16[1,4,1024]{2,1,0:T(4,128)(2,1)S(1)} %reshape.111), channel_id=1, source_target_pairs={{0,4},{4,8},{8,12},{12,16},{16,20},{20,24},{24,28},{1,5},{5,9},{9,... | collective-permute-start | bytes 24584 | tf_op jit(solution)/shard_map/ppermute | solution.py:12
  10.3 10.9 %collective-permute-start.7 = (bf16[1,4,1024]{2,1,0:T(4,128)(2,1)S(1)}, bf16[1,4,1024]{2,1,0:T(4,128)(2,1)S(1)}, u32[]{:S(2)}, u32[]{:S(2)}) collective-permute-start(bf16[1,4,1024]{2,1,0:T(4,128)(2,1)S(1)} %reshape.111), channel_id=1, source_target_pairs={{4,0},{8,4},{12,8},{16,12},{20,16},{24,20},{28,24},{5,1},{9,5},{13... | collective-permute-start | bytes 24584 | tf_op jit(solution)/shard_map/ppermute | solution.py:12
  11.6 9.6 %collective-permute-start.8 = (bf16[1,4,1024]{2,1,0:T(4,128)(2,1)S(1)}, bf16[1,4,1024]{2,1,0:T(4,128)(2,1)S(1)}, u32[]{:S(2)}, u32[]{:S(2)}) collective-permute-start(bf16[1,4,1024]{2,1,0:T(4,128)(2,1)S(1)} %reshape.111), channel_id=1, source_target_pairs={{8,0},{12,4},{16,8},{20,12},{24,16},{28,20},{9,1},{13,5},{17,9},{2... | collective-permute-start | bytes 24584 | tf_op jit(solution)/shard_map/ppermute | solution.py:12
  13.6 17.8 %collective-permute-start.14 = (bf16[16,512]{1,0:T(8,128)(2,1)S(1)}, bf16[16,512]{1,0:T(8,128)(2,1)S(1)}, u32[]{:S(2)}, u32[]{:S(2)}) collective-permute-start(bf16[16,512]{1,0:T(8,128)(2,1)S(1)} %convert_element_type.24), channel_id=1, source_target_pairs={{1,0},{2,1},{3,2},{4,3},{5,4},{6,5},{7,6},{8,7},{9,8},{10,9},{11,1... | collective-permute-start | bytes 49160 | tf_op jit(solution)/shard_map/ppermute | solution.py:23
  18.1 13.4 %collective-permute-start.13 = (bf16[16,512]{1,0:T(8,128)(2,1)S(1)}, bf16[16,512]{1,0:T(8,128)(2,1)S(1)}, u32[]{:S(2)}, u32[]{:S(2)}) collective-permute-start(bf16[16,512]{1,0:T(8,128)(2,1)S(1)} %convert_element_type.24), channel_id=1, source_target_pairs={{0,1},{1,2},{2,3},{3,4},{4,5},{5,6},{6,7},{7,8},{8,9},{9,10},{10,1... | collective-permute-start | bytes 49160 | tf_op jit(solution)/shard_map/ppermute | solution.py:20
  21.2 7.5 %collective-permute-start.9 = (bf16[5,4,1024]{2,1,0:T(4,128)(2,1)S(1)}, bf16[5,4,1024]{2,1,0:T(4,128)(2,1)S(1)}, u32[]{:S(2)}, u32[]{:S(2)}) collective-permute-start(bf16[5,4,1024]{2,1,0:T(4,128)(2,1)S(1)} %constant_dynamic-update-slice_fusion), channel_id=1, source_target_pairs={{0,1},{1,0},{2,3},{3,2},{4,5},{5,4},{6,7},{7,6},{8,9},{9,8},{10,11... | collective-permute-start | bytes 122888 | tf_op jit(solution)/shard_map/ppermute | solution.py:53
  28.8 5.4 %collective-permute-start.10 = (bf16[5,8,1024]{2,1,0:T(8,128)(2,1)S(1)}, bf16[5,8,1024]{2,1,0:T(8,128)(2,1)S(1)}, u32[]{:S(2)}, u32[]{:S(2)}) collective-permute-start(bf16[5,8,1024]{2,1,0:T(8,128)(2,1)S(1)} %pad_maximum_fusion.1), channel_id=1, source_target_pairs={{0,2},{1,3},{2,0},{3,1},{4,6},{5,7},{6,4},{7,5},{8,10},{9,11},{10,... | collective-permute-start | bytes 245768 | tf_op jit(solution)/shard_map/ppermute | solution.py:53
  35.1 5.0 %copy-start.4 = (f32[16,4,64]{2,1,0:T(4,128)S(1)}, f32[16,4,64]{2,1,0:T(4,128)}, u32[]{:S(2)}) copy-start(f32[16,4,64]{2,1,0:T(4,128)} %get-tuple-element.14) | copy-start | bytes 49156
  35.1 6.9 %copy-start.1 = (bf16[32,16,128]{2,1,0:T(8,128)(2,1)S(1)}, bf16[32,16,128]{2,1,0:T(8,128)(2,1)}, u32[]{:S(2)}) copy-start(bf16[32,16,128]{2,1,0:T(8,128)(2,1)} %gather_fusion.1) | copy-start | bytes 393220
  39.3 8.9 %copy-start.2 = (f32[64,512]{1,0:T(8,128)S(1)}, f32[64,512]{1,0:T(8,128)}, u32[]{:S(2)}) copy-start(f32[64,512]{1,0:T(8,128)} %param.19) | copy-start | bytes 393220
  41.9 1.3 %collective-permute-start.11 = (f32[2,4,1024]{2,1,0:T(4,128)S(1)}, f32[2,4,1024]{2,1,0:T(4,128)S(1)}, u32[]{:S(2)}, u32[]{:S(2)}) collective-permute-start(f32[2,4,1024]{2,1,0:T(4,128)S(1)} %dynamic-slice_bitcast_fusion), channel_id=1, source_target_pairs={{0,1},{1,0},{2,3},{3,2},{4,5},{5,4},{6,7},{7,6},{8,9},{9,8},{10,11... | collective-permute-start | bytes 98312 | tf_op jit(solution)/shard_map/ppermute | solution.py:71
  43.2 3.8 %collective-permute-start.12 = (f32[1,4,1024]{2,1,0:T(4,128)S(1)}, f32[1,4,1024]{2,1,0:T(4,128)S(1)}, u32[]{:S(2)}, u32[]{:S(2)}) collective-permute-start(f32[1,4,1024]{2,1,0:T(4,128)S(1)} %constant_dynamic-slice_fusion), channel_id=1, source_target_pairs={{0,2},{1,3},{2,0},{3,1},{4,6},{5,7},{6,4},{7,5},{8,10},{9,11},{10,... | collective-permute-start | bytes 49160 | tf_op jit(solution)/shard_map/ppermute | solution.py:71
  48.6 1.2 %collective-permute-start.15 = (f32[80,16]{0,1:T(8,128)S(1)}, f32[80,16]{0,1:T(8,128)S(1)}, u32[]{:S(2)}, u32[]{:S(2)}) collective-permute-start(f32[80,16]{0,1:T(8,128)S(1)} %pad_maximum_fusion.2), channel_id=1, source_target_pairs={{0,1},{1,0},{2,3},{3,2},{4,5},{5,4},{6,7},{7,6},{8,9},{9,8},{10,11... | collective-permute-start | bytes 15368 | tf_op jit(solution)/shard_map/ppermute | solution.py:41
  49.8 3.7 %collective-permute-start.16 = (f32[80,16]{0,1:T(8,128)S(1)}, f32[80,16]{0,1:T(8,128)S(1)}, u32[]{:S(2)}, u32[]{:S(2)}) collective-permute-start(f32[80,16]{0,1:T(8,128)S(1)} %fusion.51), channel_id=1, source_target_pairs={{0,2},{1,3},{2,0},{3,1},{4,6},{5,7},{6,4},{7,5},{8,10},{9,11},{10,... | collective-permute-start | bytes 15368 | tf_op jit(solution)/shard_map/ppermute | solution.py:41
  53.5 4.7 %collective-permute-start.17 = (f32[80,16]{0,1:T(8,128)S(1)}, f32[80,16]{0,1:T(8,128)S(1)}, u32[]{:S(2)}, u32[]{:S(2)}) collective-permute-start(f32[80,16]{0,1:T(8,128)S(1)} %add.131), channel_id=1, source_target_pairs={{0,4},{1,5},{2,6},{3,7},{4,0},{5,1},{6,2},{7,3},{8,12},{9,13},{10,... | collective-permute-start | bytes 15368 | tf_op jit(solution)/shard_map/ppermute | solution.py:41
  58.2 4.0 %collective-permute-start.18 = (f32[80,16]{0,1:T(8,128)S(1)}, f32[80,16]{0,1:T(8,128)S(1)}, u32[]{:S(2)}, u32[]{:S(2)}) collective-permute-start(f32[80,16]{0,1:T(8,128)S(1)} %add.132), channel_id=1, source_target_pairs={{0,8},{1,9},{2,10},{3,11},{4,12},{5,13},{6,14},{7,15},{8,0},{9,1},... | collective-permute-start | bytes 15368 | tf_op jit(solution)/shard_map/ppermute | solution.py:41
  62.2 5.1 %collective-permute-start.19 = (f32[80,16]{0,1:T(8,128)S(1)}, f32[80,16]{0,1:T(8,128)S(1)}, u32[]{:S(2)}, u32[]{:S(2)}) collective-permute-start(f32[80,16]{0,1:T(8,128)S(1)} %add.133), channel_id=1, source_target_pairs={{0,16},{1,17},{2,18},{3,19},{4,20},{5,21},{6,22},{7,23},{8,24},{9,... | collective-permute-start | bytes 15368 | tf_op jit(solution)/shard_map/ppermute | solution.py:41
  67.3 4.4 %copy-start.3 = (f32[80,16]{0,1:T(8,128)}, f32[80,16]{0,1:T(8,128)S(1)}, u32[]{:S(2)}) copy-start(f32[80,16]{0,1:T(8,128)S(1)} %add.134) | copy-start | bytes 15364

commit v7 on v6

--- a/solution.py
+++ b/solution.py
@@ -173,7 +173,8 @@
     far_hat = butterfly_scatter(partial_far, "coef")
     far_round = far_hat.astype(jnp.bfloat16).reshape(local_count, vec_count, rank_width)
     far_part = jnp.einsum("cki,cvk->vci", leaf_basis, far_round, preferred_element_type=jnp.float32)
-    extended = extended_2(rounded, ((("leaf", "coef"), 1),), local_count * leaf_size)
+    after_far = (partial_far[0, 0] * 0).astype(jnp.bfloat16)
+    extended = extended_2(rounded + after_far, ((("leaf", "coef"), 1),), local_count * leaf_size)
     extended = extended.reshape(vec_count, 3 * local_count, leaf_size)
     device_pos = lax.axis_index("leaf") * coef_count + lax.axis_index("coef")
     near_ids = (near_list - (device_pos - 1) * local_count).reshape(-1)

time: 72.3 us -> 75.9 us (1.050)
  waiting for transfers between devices: 11.3 us -> 14.5 us
  matrix products: 8.99 us -> 8.12 us
    ppermute x2, starting transfers between devices: 1.9 us -> 4.98 us  [butterfly_scatter(): parts = keep + lax.ppermute(give, axis, route)]
    ppermute x4, waiting for transfers between devices: 0.01 us -> 2.62 us  [shifted(): return lax.ppermute(block, axis, route)]
    ppermute x2, starting transfers between devices: 3.86 us -> 1.63 us  [xor_gather(): block = jnp.concatenate([block, lax.ppermute(block, axis, route)], axis=dim)]
    ppermute x1, starting transfers between devices: 3.03 us -> 1.49 us  [extended_2(): lax.ppermute(lax.slice_in_dim(block, block.shape[dim] - width, None, axis...]
    ppermute x2, waiting for transfers between devices: 1.41 us -> 2.71 us  [xor_gather(): block = jnp.concatenate([block, lax.ppermute(block, axis, route)], axis=dim)]
    another operation x1, local copies, waits for them, and re-layouts: 1 us -> 0.11 us  [butterfly_scatter(): pairs = parts.reshape(parts.shape[0] // 2, 2, *parts.shape[1:])]
    ppermute x5, starting transfers between devices: 10.7 us -> 11.6 us  [butterfly_sum(): block = block + lax.ppermute(block, axes, route)]
    dot_general x1, matrix products: 0.97 us -> 0.13 us  [on_device(): jnp.einsum('cki,cvk->vci', leaf_basis, far_round, preferred_element_type=...]
where the time goes in v7:
time: 75.9 us; the launch traced here: 75.3 us
  starting transfers between devices  31.9 us (42%)
  waiting for transfers between devices  14.5 us (19%)
  local copies, waits for them, and re-layouts  9.97 us (13%)
  matrix products  8.12 us (11%)
  other arithmetic  5.46 us (7%)
  between operations  2.95 us (4%)
  Pallas kernels  2.43 us (3%)
    ppermute x5, starting transfers between devices, butterfly_sum(): block = block + lax.ppermute(block, axes, route)  11.6 us
    ppermute x4, starting transfers between devices, shifted(): return lax.ppermute(block, axis, route)  11 us
    ppermute x5, waiting for transfers between devices, butterfly_sum(): block = block + lax.ppermute(block, axes, route)  7.62 us
    reshape x1, local copies, waits for them, and re-layouts, on_device(): couple = coupling.reshape(3, group_size, slot_count, rank_width, rank_width)  5.63 us
    ppermute x2, starting transfers between devices, butterfly_scatter(): parts = keep + lax.ppermute(give, axis, route)  4.98 us
    dot_general x1, matrix products, on_device(): jnp.einsum('jcfkl,cfvl->jcfvk', couple, sources, preferred_element_type=j...  4.17 us
    ppermute x2, waiting for transfers between devices, xor_gather(): block = jnp.concatenate([block, lax.ppermute(block, axis, route)], axis=dim)  2.71 us
    ppermute x4, waiting for transfers between devices, shifted(): return lax.ppermute(block, axis, route)  2.62 us
  transfers between devices with their start and end apart: 15, of which 8 were waited for; matrix products, arithmetic and copies ran while one was open for 17% of the time, Pallas kernels for 0%

profile of v7, /device:TPU:0, one launch (start us, length us, event | category | flops | bytes accessed | tf_op | source)
XLA Modules:
  0.0 75.3 jit_solution(9977615007648882672)
XLA Ops:
  1.9 5.0 %collective-permute-start.5 = (bf16[1,4,1024]{2,1,0:T(4,128)(2,1)S(1)}, bf16[1,4,1024]{2,1,0:T(4,128)(2,1)S(1)}, u32[]{:S(2)}, u32[]{:S(2)}) collective-permute-start(bf16[1,4,1024]{2,1,0:T(4,128)(2,1)S(1)} %reshape.117), channel_id=1, source_target_pairs={{0,8},{4,12},{8,16},{12,20},{16,24},{20,28},{1,9},{5,13},{9,17},{1... | collective-permute-start | bytes 24584 | tf_op jit(solution)/shard_map/ppermute | solution.py:12
  6.8 3.4 %collective-permute-start.6 = (bf16[1,4,1024]{2,1,0:T(4,128)(2,1)S(1)}, bf16[1,4,1024]{2,1,0:T(4,128)(2,1)S(1)}, u32[]{:S(2)}, u32[]{:S(2)}) collective-permute-start(bf16[1,4,1024]{2,1,0:T(4,128)(2,1)S(1)} %reshape.117), channel_id=1, source_target_pairs={{0,4},{4,8},{8,12},{12,16},{16,20},{20,24},{24,28},{1,5},{5,9},{9,... | collective-permute-start | bytes 24584 | tf_op jit(solution)/shard_map/ppermute | solution.py:12
  10.3 1.3 %collective-permute-start.7 = (bf16[1,4,1024]{2,1,0:T(4,128)(2,1)S(1)}, bf16[1,4,1024]{2,1,0:T(4,128)(2,1)S(1)}, u32[]{:S(2)}, u32[]{:S(2)}) collective-permute-start(bf16[1,4,1024]{2,1,0:T(4,128)(2,1)S(1)} %reshape.117), channel_id=1, source_target_pairs={{4,0},{8,4},{12,8},{16,12},{20,16},{24,20},{28,24},{5,1},{9,5},{13... | collective-permute-start | bytes 24584 | tf_op jit(solution)/shard_map/ppermute | solution.py:12
  11.6 1.3 %collective-permute-start.8 = (bf16[1,4,1024]{2,1,0:T(4,128)(2,1)S(1)}, bf16[1,4,1024]{2,1,0:T(4,128)(2,1)S(1)}, u32[]{:S(2)}, u32[]{:S(2)}) collective-permute-start(bf16[1,4,1024]{2,1,0:T(4,128)(2,1)S(1)} %reshape.117), channel_id=1, source_target_pairs={{8,0},{12,4},{16,8},{20,12},{24,16},{28,20},{9,1},{13,5},{17,9},{2... | collective-permute-start | bytes 24584 | tf_op jit(solution)/shard_map/ppermute | solution.py:12
  16.1 2.6 %collective-permute-done.8 = bf16[1,4,1024]{2,1,0:T(4,128)(2,1)S(1)} collective-permute-done((bf16[1,4,1024]{2,1,0:T(4,128)(2,1)S(1)}, bf16[1,4,1024]{2,1,0:T(4,128)(2,1)S(1)}, u32[]{:S(2)}, u32[]{:S(2)}) %collective-permute-start.8) | collective-permute-done | bytes 8224 | tf_op jit(solution)/shard_map/ppermute | solution.py:12
  18.9 5.6 %reshape.121 = bf16[3,16,4,64,64]{4,3,2,1,0:T(8,128)(2,1)} reshape(bf16[3,16,4,4096]{3,2,1,0:T(4,128)(2,1)} %param.16) | data formatting | bytes 3145728 | tf_op jit(solution)/shard_map/reshape | solution.py:169
  25.2 1.6 %collective-permute-start.10 = (bf16[5,8,1024]{2,1,0:T(8,128)(2,1)S(1)}, bf16[5,8,1024]{2,1,0:T(8,128)(2,1)S(1)}, u32[]{:S(2)}, u32[]{:S(2)}) collective-permute-start(bf16[5,8,1024]{2,1,0:T(8,128)(2,1)S(1)} %pad_maximum_fusion.1), channel_id=1, source_target_pairs={{0,2},{1,3},{2,0},{3,1},{4,6},{5,7},{6,4},{7,5},{8,10},{9,11},{10,... | collective-permute-start | bytes 245768 | tf_op jit(solution)/shard_map/ppermute | solution.py:53
  27.4 2.7 %collective-permute-done.10 = bf16[5,8,1024]{2,1,0:T(8,128)(2,1)S(1)} collective-permute-done((bf16[5,8,1024]{2,1,0:T(8,128)(2,1)S(1)}, bf16[5,8,1024]{2,1,0:T(8,128)(2,1)S(1)}, u32[]{:S(2)}, u32[]{:S(2)}) %collective-permute-start.10) | collective-permute-done | bytes 81952 | tf_op jit(solution)/shard_map/ppermute | solution.py:53
  31.1 4.2 %fusion.6 = bf16[3,16,4,16,64]{4,3,0,2,1:T(8,128)(2,1)S(1)} fusion(bf16[3,16,4,64,64]{4,3,2,1,0:T(8,128)(2,1)} %reshape.121, bf16[16,4,16,64]{3,2,1,0:T(8,128)(2,1)S(1)} %reshape.120, pred[16,4,64]{2,1,0:T(4,128)(4,1)S(1)} %get-tuple-element.15), kind=kOutput, calls=%fused_computation.9 | convolution fusion | flops 25231360 | bytes 2101248 | tf_op jit(solution)/shard_map/jcfkl,cfvl->jcfvk/dot_general | solution.py:170
  37.4 1.5 %collective-permute-start.13 = (bf16[16,512]{1,0:T(8,128)(2,1)S(1)}, bf16[16,512]{1,0:T(8,128)(2,1)S(1)}, u32[]{:S(2)}, u32[]{:S(2)}) collective-permute-start(bf16[16,512]{1,0:T(8,128)(2,1)S(1)} %broadcast_add_fusion), channel_id=1, source_target_pairs={{0,1},{1,2},{2,3},{3,4},{4,5},{5,6},{6,7},{7,8},{8,9},{9,10},{10,1... | collective-permute-start | bytes 49160 | tf_op jit(solution)/shard_map/ppermute | solution.py:20
  38.9 1.3 %collective-permute-start.14 = (bf16[16,512]{1,0:T(8,128)(2,1)S(1)}, bf16[16,512]{1,0:T(8,128)(2,1)}, u32[]{:S(2)}, u32[]{:S(2)}) collective-permute-start(bf16[16,512]{1,0:T(8,128)(2,1)S(1)} %broadcast_add_fusion), channel_id=1, source_target_pairs={{1,0},{2,1},{3,2},{4,3},{5,4},{6,5},{7,6},{8,7},{9,8},{10,9},{11,1... | collective-permute-start | bytes 49160 | tf_op jit(solution)/shard_map/ppermute | solution.py:23
  41.0 2.7 %collective-permute-start.11 = (f32[2,4,1024]{2,1,0:T(4,128)}, f32[2,4,1024]{2,1,0:T(4,128)}, u32[]{:S(2)}, u32[]{:S(2)}) collective-permute-start(f32[2,4,1024]{2,1,0:T(4,128)} %dynamic-slice_bitcast_fusion), channel_id=1, source_target_pairs={{0,1},{1,0},{2,3},{3,2},{4,5},{5,4},{6,7},{7,6},{8,9},{9,8},{10,11... | collective-permute-start | bytes 98312 | tf_op jit(solution)/shard_map/ppermute | solution.py:71
  46.9 2.3 %collective-permute-start.12 = (f32[1,4,1024]{2,1,0:T(4,128)S(1)}, f32[1,4,1024]{2,1,0:T(4,128)S(1)}, u32[]{:S(2)}, u32[]{:S(2)}) collective-permute-start(f32[1,4,1024]{2,1,0:T(4,128)S(1)} %constant_dynamic-slice_fusion), channel_id=1, source_target_pairs={{0,2},{1,3},{2,0},{3,1},{4,6},{5,7},{6,4},{7,5},{8,10},{9,11},{10,... | collective-permute-start | bytes 49160 | tf_op jit(solution)/shard_map/ppermute | solution.py:71
  49.4 1.5 %collective-permute-done.12 = f32[1,4,1024]{2,1,0:T(4,128)S(1)} collective-permute-done((f32[1,4,1024]{2,1,0:T(4,128)S(1)}, f32[1,4,1024]{2,1,0:T(4,128)S(1)}, u32[]{:S(2)}, u32[]{:S(2)}) %collective-permute-start.12) | collective-permute-done | bytes 16416 | tf_op jit(solution)/shard_map/ppermute | solution.py:71
  51.6 1.3 %collective-permute-start.15 = (f32[80,16]{0,1:T(8,128)S(1)}, f32[80,16]{0,1:T(8,128)S(1)}, u32[]{:S(2)}, u32[]{:S(2)}) collective-permute-start(f32[80,16]{0,1:T(8,128)S(1)} %pad_maximum_fusion.2), channel_id=1, source_target_pairs={{0,1},{1,0},{2,3},{3,2},{4,5},{5,4},{6,7},{7,6},{8,9},{9,8},{10,11... | collective-permute-start | bytes 15368 | tf_op jit(solution)/shard_map/ppermute | solution.py:41
  53.8 1.7 %collective-permute-start.16 = (f32[80,16]{0,1:T(8,128)S(1)}, f32[80,16]{0,1:T(8,128)S(1)}, u32[]{:S(2)}, u32[]{:S(2)}) collective-permute-start(f32[80,16]{0,1:T(8,128)S(1)} %fusion.51), channel_id=1, source_target_pairs={{0,2},{1,3},{2,0},{3,1},{4,6},{5,7},{6,4},{7,5},{8,10},{9,11},{10,... | collective-permute-start | bytes 15368 | tf_op jit(solution)/shard_map/ppermute | solution.py:41
  55.5 1.9 %collective-permute-done.16 = f32[80,16]{0,1:T(8,128)S(1)} collective-permute-done((f32[80,16]{0,1:T(8,128)S(1)}, f32[80,16]{0,1:T(8,128)S(1)}, u32[]{:S(2)}, u32[]{:S(2)}) %collective-permute-start.16) | collective-permute-done | bytes 5152 | tf_op jit(solution)/shard_map/ppermute | solution.py:41
  57.4 3.3 %collective-permute-start.17 = (f32[80,16]{0,1:T(8,128)S(1)}, f32[80,16]{0,1:T(8,128)S(1)}, u32[]{:S(2)}, u32[]{:S(2)}) collective-permute-start(f32[80,16]{0,1:T(8,128)S(1)} %add.139), channel_id=1, source_target_pairs={{0,4},{1,5},{2,6},{3,7},{4,0},{5,1},{6,2},{7,3},{8,12},{9,13},{10,... | collective-permute-start | bytes 15368 | tf_op jit(solution)/shard_map/ppermute | solution.py:41
  60.8 1.6 %collective-permute-done.17 = f32[80,16]{0,1:T(8,128)S(1)} collective-permute-done((f32[80,16]{0,1:T(8,128)S(1)}, f32[80,16]{0,1:T(8,128)S(1)}, u32[]{:S(2)}, u32[]{:S(2)}) %collective-permute-start.17) | collective-permute-done | bytes 5152 | tf_op jit(solution)/shard_map/ppermute | solution.py:41
  62.4 2.1 %collective-permute-start.18 = (f32[80,16]{0,1:T(8,128)S(1)}, f32[80,16]{0,1:T(8,128)S(1)}, u32[]{:S(2)}, u32[]{:S(2)}) collective-permute-start(f32[80,16]{0,1:T(8,128)S(1)} %add.140), channel_id=1, source_target_pairs={{0,8},{1,9},{2,10},{3,11},{4,12},{5,13},{6,14},{7,15},{8,0},{9,1},... | collective-permute-start | bytes 15368 | tf_op jit(solution)/shard_map/ppermute | solution.py:41
  64.5 1.6 %collective-permute-done.18 = f32[80,16]{0,1:T(8,128)S(1)} collective-permute-done((f32[80,16]{0,1:T(8,128)S(1)}, f32[80,16]{0,1:T(8,128)S(1)}, u32[]{:S(2)}, u32[]{:S(2)}) %collective-permute-start.18) | collective-permute-done | bytes 5152 | tf_op jit(solution)/shard_map/ppermute | solution.py:41
  66.2 3.1 %collective-permute-start.19 = (f32[80,16]{0,1:T(8,128)S(1)}, f32[80,16]{0,1:T(8,128)S(1)}, u32[]{:S(2)}, u32[]{:S(2)}) collective-permute-start(f32[80,16]{0,1:T(8,128)S(1)} %add.141), channel_id=1, source_target_pairs={{0,16},{1,17},{2,18},{3,19},{4,20},{5,21},{6,22},{7,23},{8,24},{9,... | collective-permute-start | bytes 15368 | tf_op jit(solution)/shard_map/ppermute | solution.py:41
  69.3 1.6 %collective-permute-done.19 = f32[80,16]{0,1:T(8,128)S(1)} collective-permute-done((f32[80,16]{0,1:T(8,128)S(1)}, f32[80,16]{0,1:T(8,128)S(1)}, u32[]{:S(2)}, u32[]{:S(2)}) %collective-permute-start.19) | collective-permute-done | bytes 5152 | tf_op jit(solution)/shard_map/ppermute | solution.py:41
  72.9 2.4 %shard_map.112 = (f32[16,16]{1,0:T(8,128)}, f32[16,512]{1,0:T(8,128)}) custom-call(f32[16,16]{1,0:T(8,128)S(1)} %get-tuple-element.18.gram_ref, f32[16,512]{1,0:T(8,128)S(1)} %convolution_subtract_fusion.residue_ref), custom_call_target="tpu_custom_call" | custom-call | flops 540672 | bytes 67584 | tf_op jit(solution)/shard_map/pallas_call | solution.py:117
  (73 shorter events, 14.8 us)
Async XLA Ops:
  0.6 44.5 %copy-start = (bf16[3,4,8,128,128]{4,3,2,1,0:T(8,128)(2,1)S(1)}, bf16[3,4,8,128,128]{4,3,2,1,0:T(8,128)(2,1)}, u32[]{:S(2)}) copy-start(bf16[3,4,8,128,128]{4,3,2,1,0:T(8,128)(2,1)} %param.14) | copy-start | bytes 9437188
  1.9 14.1 %collective-permute-start.5 = (bf16[1,4,1024]{2,1,0:T(4,128)(2,1)S(1)}, bf16[1,4,1024]{2,1,0:T(4,128)(2,1)S(1)}, u32[]{:S(2)}, u32[]{:S(2)}) collective-permute-start(bf16[1,4,1024]{2,1,0:T(4,128)(2,1)S(1)} %reshape.117), channel_id=1, source_target_pairs={{0,8},{4,12},{8,16},{12,20},{16,24},{20,28},{1,9},{5,13},{9,17},{1... | collective-permute-start | bytes 24584 | tf_op jit(solution)/shard_map/ppermute | solution.py:12
  6.8 9.2 %collective-permute-start.6 = (bf16[1,4,1024]{2,1,0:T(4,128)(2,1)S(1)}, bf16[1,4,1024]{2,1,0:T(4,128)(2,1)S(1)}, u32[]{:S(2)}, u32[]{:S(2)}) collective-permute-start(bf16[1,4,1024]{2,1,0:T(4,128)(2,1)S(1)} %reshape.117), channel_id=1, source_target_pairs={{0,4},{4,8},{8,12},{12,16},{16,20},{20,24},{24,28},{1,5},{5,9},{9,... | collective-permute-start | bytes 24584 | tf_op jit(solution)/shard_map/ppermute | solution.py:12
  10.3 5.8 %collective-permute-start.7 = (bf16[1,4,1024]{2,1,0:T(4,128)(2,1)S(1)}, bf16[1,4,1024]{2,1,0:T(4,128)(2,1)S(1)}, u32[]{:S(2)}, u32[]{:S(2)}) collective-permute-start(bf16[1,4,1024]{2,1,0:T(4,128)(2,1)S(1)} %reshape.117), channel_id=1, source_target_pairs={{4,0},{8,4},{12,8},{16,12},{20,16},{24,20},{28,24},{5,1},{9,5},{13... | collective-permute-start | bytes 24584 | tf_op jit(solution)/shard_map/ppermute | solution.py:12
  11.6 7.1 %collective-permute-start.8 = (bf16[1,4,1024]{2,1,0:T(4,128)(2,1)S(1)}, bf16[1,4,1024]{2,1,0:T(4,128)(2,1)S(1)}, u32[]{:S(2)}, u32[]{:S(2)}) collective-permute-start(bf16[1,4,1024]{2,1,0:T(4,128)(2,1)S(1)} %reshape.117), channel_id=1, source_target_pairs={{8,0},{12,4},{16,8},{20,12},{24,16},{28,20},{9,1},{13,5},{17,9},{2... | collective-permute-start | bytes 24584 | tf_op jit(solution)/shard_map/ppermute | solution.py:12
  18.7 6.4 %collective-permute-start.9 = (bf16[5,4,1024]{2,1,0:T(4,128)(2,1)S(1)}, bf16[5,4,1024]{2,1,0:T(4,128)(2,1)S(1)}, u32[]{:S(2)}, u32[]{:S(2)}) collective-permute-start(bf16[5,4,1024]{2,1,0:T(4,128)(2,1)S(1)} %constant_dynamic-update-slice_fusion), channel_id=1, source_target_pairs={{0,1},{1,0},{2,3},{3,2},{4,5},{5,4},{6,7},{7,6},{8,9},{9,8},{10,11... | collective-permute-start | bytes 122888 | tf_op jit(solution)/shard_map/ppermute | solution.py:53
  25.2 4.9 %collective-permute-start.10 = (bf16[5,8,1024]{2,1,0:T(8,128)(2,1)S(1)}, bf16[5,8,1024]{2,1,0:T(8,128)(2,1)S(1)}, u32[]{:S(2)}, u32[]{:S(2)}) collective-permute-start(bf16[5,8,1024]{2,1,0:T(8,128)(2,1)S(1)} %pad_maximum_fusion.1), channel_id=1, source_target_pairs={{0,2},{1,3},{2,0},{3,1},{4,6},{5,7},{6,4},{7,5},{8,10},{9,11},{10,... | collective-permute-start | bytes 245768 | tf_op jit(solution)/shard_map/ppermute | solution.py:53
  31.1 5.0 %copy-start.5 = (f32[16,4,64]{2,1,0:T(4,128)S(1)}, f32[16,4,64]{2,1,0:T(4,128)}, u32[]{:S(2)}) copy-start(f32[16,4,64]{2,1,0:T(4,128)} %get-tuple-element.14) | copy-start | bytes 49156
  31.1 6.3 %copy-start.4 = (f32[16,512]{1,0:T(8,128)S(1)}, f32[16,512]{1,0:T(8,128)}, u32[]{:S(2)}) copy-start(f32[16,512]{1,0:T(8,128)} %param.11) | copy-start | bytes 98308
  36.0 15.3 %copy-start.1 = (f32[64,512]{1,0:T(8,128)S(1)}, f32[64,512]{1,0:T(8,128)}, u32[]{:S(2)}) copy-start(f32[64,512]{1,0:T(8,128)} %param.19) | copy-start | bytes 393220
  37.4 6.2 %collective-permute-start.13 = (bf16[16,512]{1,0:T(8,128)(2,1)S(1)}, bf16[16,512]{1,0:T(8,128)(2,1)S(1)}, u32[]{:S(2)}, u32[]{:S(2)}) collective-permute-start(bf16[16,512]{1,0:T(8,128)(2,1)S(1)} %broadcast_add_fusion), channel_id=1, source_target_pairs={{0,1},{1,2},{2,3},{3,4},{4,5},{5,6},{6,7},{7,8},{8,9},{9,10},{10,1... | collective-permute-start | bytes 49160 | tf_op jit(solution)/shard_map/ppermute | solution.py:20
  38.9 4.7 %collective-permute-start.14 = (bf16[16,512]{1,0:T(8,128)(2,1)S(1)}, bf16[16,512]{1,0:T(8,128)(2,1)}, u32[]{:S(2)}, u32[]{:S(2)}) collective-permute-start(bf16[16,512]{1,0:T(8,128)(2,1)S(1)} %broadcast_add_fusion), channel_id=1, source_target_pairs={{1,0},{2,1},{3,2},{4,3},{5,4},{6,5},{7,6},{8,7},{9,8},{10,9},{11,1... | collective-permute-start | bytes 49160 | tf_op jit(solution)/shard_map/ppermute | solution.py:23
  41.0 5.1 %collective-permute-start.11 = (f32[2,4,1024]{2,1,0:T(4,128)}, f32[2,4,1024]{2,1,0:T(4,128)}, u32[]{:S(2)}, u32[]{:S(2)}) collective-permute-start(f32[2,4,1024]{2,1,0:T(4,128)} %dynamic-slice_bitcast_fusion), channel_id=1, source_target_pairs={{0,1},{1,0},{2,3},{3,2},{4,5},{5,4},{6,7},{7,6},{8,9},{9,8},{10,11... | collective-permute-start | bytes 98312 | tf_op jit(solution)/shard_map/ppermute | solution.py:71
  45.1 5.9 %copy-start.3 = (bf16[4,64,128]{2,1,0:T(8,128)(2,1)S(1)}, bf16[4,64,128]{2,1,0:T(8,128)(2,1)}, u32[]{:S(2)}) copy-start(bf16[4,64,128]{2,1,0:T(8,128)(2,1)} %param.13) | copy-start | bytes 196612
  46.9 4.0 %collective-permute-start.12 = (f32[1,4,1024]{2,1,0:T(4,128)S(1)}, f32[1,4,1024]{2,1,0:T(4,128)S(1)}, u32[]{:S(2)}, u32[]{:S(2)}) collective-permute-start(f32[1,4,1024]{2,1,0:T(4,128)S(1)} %constant_dynamic-slice_fusion), channel_id=1, source_target_pairs={{0,2},{1,3},{2,0},{3,1},{4,6},{5,7},{6,4},{7,5},{8,10},{9,11},{10,... | collective-permute-start | bytes 49160 | tf_op jit(solution)/shard_map/ppermute | solution.py:71
  51.6 2.1 %collective-permute-start.15 = (f32[80,16]{0,1:T(8,128)S(1)}, f32[80,16]{0,1:T(8,128)S(1)}, u32[]{:S(2)}, u32[]{:S(2)}) collective-permute-start(f32[80,16]{0,1:T(8,128)S(1)} %pad_maximum_fusion.2), channel_id=1, source_target_pairs={{0,1},{1,0},{2,3},{3,2},{4,5},{5,4},{6,7},{7,6},{8,9},{9,8},{10,11... | collective-permute-start | bytes 15368 | tf_op jit(solution)/shard_map/ppermute | solution.py:41
  53.8 3.7 %collective-permute-start.16 = (f32[80,16]{0,1:T(8,128)S(1)}, f32[80,16]{0,1:T(8,128)S(1)}, u32[]{:S(2)}, u32[]{:S(2)}) collective-permute-start(f32[80,16]{0,1:T(8,128)S(1)} %fusion.51), channel_id=1, source_target_pairs={{0,2},{1,3},{2,0},{3,1},{4,6},{5,7},{6,4},{7,5},{8,10},{9,11},{10,... | collective-permute-start | bytes 15368 | tf_op jit(solution)/shard_map/ppermute | solution.py:41
  57.4 5.0 %collective-permute-start.17 = (f32[80,16]{0,1:T(8,128)S(1)}, f32[80,16]{0,1:T(8,128)S(1)}, u32[]{:S(2)}, u32[]{:S(2)}) collective-permute-start(f32[80,16]{0,1:T(8,128)S(1)} %add.139), channel_id=1, source_target_pairs={{0,4},{1,5},{2,6},{3,7},{4,0},{5,1},{6,2},{7,3},{8,12},{9,13},{10,... | collective-permute-start | bytes 15368 | tf_op jit(solution)/shard_map/ppermute | solution.py:41
  62.4 3.8 %collective-permute-start.18 = (f32[80,16]{0,1:T(8,128)S(1)}, f32[80,16]{0,1:T(8,128)S(1)}, u32[]{:S(2)}, u32[]{:S(2)}) collective-permute-start(f32[80,16]{0,1:T(8,128)S(1)} %add.140), channel_id=1, source_target_pairs={{0,8},{1,9},{2,10},{3,11},{4,12},{5,13},{6,14},{7,15},{8,0},{9,1},... | collective-permute-start | bytes 15368 | tf_op jit(solution)/shard_map/ppermute | solution.py:41
  66.2 4.7 %collective-permute-start.19 = (f32[80,16]{0,1:T(8,128)S(1)}, f32[80,16]{0,1:T(8,128)S(1)}, u32[]{:S(2)}, u32[]{:S(2)}) collective-permute-start(f32[80,16]{0,1:T(8,128)S(1)} %add.141), channel_id=1, source_target_pairs={{0,16},{1,17},{2,18},{3,19},{4,20},{5,21},{6,22},{7,23},{8,24},{9,... | collective-permute-start | bytes 15368 | tf_op jit(solution)/shard_map/ppermute | solution.py:41
  70.9 4.4 %copy-start.2 = (f32[80,16]{0,1:T(8,128)}, f32[80,16]{0,1:T(8,128)S(1)}, u32[]{:S(2)}) copy-start(f32[80,16]{0,1:T(8,128)S(1)} %add.142) | copy-start | bytes 15364

commit v8 on v6

--- a/solution.py
+++ b/solution.py
@@ -166,10 +166,20 @@
     lane_ids = jnp.arange(rank_width, dtype=jnp.int32)
     keep_mask = lane_ids[None, None, :] < far_rank[:, :, None]
     sources = jnp.where(keep_mask[:, :, None, :], sources, jnp.zeros((), jnp.bfloat16))
-    couple = coupling.reshape(3, group_size, slot_count, rank_width, rank_width)
-    far_terms = jnp.einsum("jcfkl,cfvl->jcfvk", couple, sources, preferred_element_type=jnp.float32)
-    combined = jnp.tensordot(powers, far_terms, 1) * keep_mask[:, :, None, :].astype(jnp.float32)
-    partial_far = jnp.sum(combined, axis=1).reshape(group_size, vec_count * rank_width)
+    row_keep = keep_mask[None, :, :, :, None].astype(jnp.float32)
+    scaled = coupling.reshape(3, group_size, slot_count, rank_width, rank_width).astype(jnp.float32)
+    scaled = scaled * powers[:, None, None, None, None] * row_keep
+    high = scaled.astype(jnp.bfloat16)
+    low = (scaled - high.astype(jnp.float32)).astype(jnp.bfloat16)
+    split_count = 2 * 3 * slot_count * rank_width
+    lhs = jnp.transpose(jnp.stack([high, low]), (2, 4, 0, 1, 3, 5)).reshape(
+        group_size, rank_width, split_count
+    )
+    rhs = jnp.broadcast_to(
+        jnp.swapaxes(sources, 2, 3)[:, None, None], (group_size, 2, 3, slot_count, rank_width, vec_count)
+    ).reshape(group_size, split_count, vec_count)
+    far_sum = jnp.einsum("ckK,cKv->cvk", lhs, rhs, preferred_element_type=jnp.float32)
+    partial_far = far_sum.reshape(group_size, vec_count * rank_width)
     far_hat = butterfly_scatter(partial_far, "coef")
     far_round = far_hat.astype(jnp.bfloat16).reshape(local_count, vec_count, rank_width)
     far_part = jnp.einsum("cki,cvk->vci", leaf_basis, far_round, preferred_element_type=jnp.float32)

time: 72.3 us -> 103 us (1.42)
  local copies, waits for them, and re-layouts: 10.2 us -> 37.5 us
  other arithmetic: 4.8 us -> 10.8 us
  matrix products: 8.99 us -> 6.26 us
    transpose x0 -> x2, local copies, waits for them, and re-layouts: none -> 10.8 us  [the longest x1 10.7 us: on_device(): jnp.transpose(jnp.stack([high, low]), (2, 4, 0, 1, 3, 5))]
    reshape x1 -> x2, local copies, waits for them, and re-layouts: 5.63 us -> 14.4 us  [the longest x1 10.6 us: on_device(): jnp.transpose(jnp.stack([high, low]), (2, 4, 0, 1, 3, 5))]
    convert_element_type x0 -> x1, local copies, waits for them, and re-layouts: none -> 5.66 us  [on_device(): coupling.reshape(3, group_size, slot_count, rank_width, rank_width)]
    transpose x0 -> x2, other arithmetic: none -> 4.08 us  [the longest x1 4.03 us: on_device(): jnp.transpose(jnp.stack([high, low]), (2, 4, 0, 1, 3, 5))]
    convert_element_type x1 -> x2, other arithmetic: 0.7 us -> 3.96 us  [the longest x1 3.88 us: on_device(): high = scaled.astype(jnp.bfloat16)]
    dot_general x2 -> x1, matrix products: 4.96 us -> 3.07 us  [on_device(): jnp.einsum('ckK,cKv->cvk', lhs, rhs, preferred_element_type=jnp.float32)]
    broadcast_in_dim x0 -> x1, local copies, waits for them, and re-layouts: none -> 1.56 us  [on_device(): jnp.broadcast_to(jnp.swapaxes(sources, 2, 3)[:, None, None], (group_size,...]
  transfers between devices with their start and end apart: 15 -> 15, of which waited for: 8 -> 8; matrix products, arithmetic and copies ran while one was open for 17% -> 39% of each run, Pallas kernels for 0% -> 0%
where the time goes in v8:
time: 103 us; the launch traced here: 102 us
  local copies, waits for them, and re-layouts  37.5 us (36%)
  starting transfers between devices  31.8 us (31%)
  waiting for transfers between devices  11.4 us (11%)
  other arithmetic  10.8 us (10%)
  matrix products  6.26 us (6%)
  Pallas kernels  2.43 us (2%)
  between operations  2.22 us (2%)
    ppermute x4, starting transfers between devices, shifted(): return lax.ppermute(block, axis, route)  11 us
    transpose x1, local copies, waits for them, and re-layouts, on_device(): jnp.transpose(jnp.stack([high, low]), (2, 4, 0, 1, 3, 5))  10.7 us
    ppermute x5, starting transfers between devices, butterfly_sum(): block = block + lax.ppermute(block, axes, route)  10.7 us
    reshape x1, local copies, waits for them, and re-layouts, on_device(): jnp.transpose(jnp.stack([high, low]), (2, 4, 0, 1, 3, 5))  10.6 us
    ppermute x5, waiting for transfers between devices, butterfly_sum(): block = block + lax.ppermute(block, axes, route)  7.93 us
    convert_element_type x1, local copies, waits for them, and re-layouts, on_device(): coupling.reshape(3, group_size, slot_count, rank_width, rank_width)  5.66 us
    transpose x1, other arithmetic, on_device(): jnp.transpose(jnp.stack([high, low]), (2, 4, 0, 1, 3, 5))  4.03 us
    convert_element_type x1, other arithmetic, on_device(): high = scaled.astype(jnp.bfloat16)  3.88 us
  transfers between devices with their start and end apart: 15, of which 8 were waited for; matrix products, arithmetic and copies ran while one was open for 39% of the time, Pallas kernels for 0%

profile of v8, /device:TPU:0, one launch (start us, length us, event | category | flops | bytes accessed | tf_op | source)
XLA Modules:
  0.0 102.4 jit_solution(17132192417054257072)
XLA Ops:
  1.9 5.0 %collective-permute-start.5 = (bf16[1,4,1024]{2,1,0:T(4,128)(2,1)S(1)}, bf16[1,4,1024]{2,1,0:T(4,128)(2,1)S(1)}, u32[]{:S(2)}, u32[]{:S(2)}) collective-permute-start(bf16[1,4,1024]{2,1,0:T(4,128)(2,1)S(1)} %reshape.153), channel_id=1, source_target_pairs={{0,8},{4,12},{8,16},{12,20},{16,24},{20,28},{1,9},{5,13},{9,17},{1... | collective-permute-start | bytes 24584 | tf_op jit(solution)/shard_map/ppermute | solution.py:12
  6.8 3.4 %collective-permute-start.6 = (bf16[1,4,1024]{2,1,0:T(4,128)(2,1)S(1)}, bf16[1,4,1024]{2,1,0:T(4,128)(2,1)S(1)}, u32[]{:S(2)}, u32[]{:S(2)}) collective-permute-start(bf16[1,4,1024]{2,1,0:T(4,128)(2,1)S(1)} %reshape.153), channel_id=1, source_target_pairs={{0,4},{4,8},{8,12},{12,16},{16,20},{20,24},{24,28},{1,5},{5,9},{9,... | collective-permute-start | bytes 24584 | tf_op jit(solution)/shard_map/ppermute | solution.py:12
  16.7 5.7 %reshape.163 = f32[1,3,16,4,64,64]{5,4,3,2,1,0:T(8,128)} reshape(bf16[3,16,4,4096]{3,2,1,0:T(4,128)(2,1)} %param.16) | data formatting | bytes 4718592 | tf_op jit(solution)/shard_map/convert_element_type | solution.py:170
  23.2 3.9 %fusion = (bf16[1,3,16,4,64,64]{5,4,3,2,1,0:T(8,128)(2,1)S(1)}, bf16[1,3,16,4,64,64]{5,4,3,2,1,0:T(8,128)(2,1)S(1)}) fusion(f32[1,3,16,4,64,64]{5,4,3,2,1,0:T(8,128)} %reshape.163, f32[16,4,64]{2,1,0:T(4,128)S(1)} %get-tuple-element.16, f32[3]{0:T(128)S(1)} %pad_maximum_fusion.3), kind=kLoop, calls=%fused_computation.6 | loop fusion | flops 4718592 | bytes 6307852 | tf_op jit(solution)/shard_map/convert_element_type | solution.py:172
  27.1 4.0 %maximum_bitcast_fusion = bf16[16,64,2,3,4,64]{5,1,4,0,3,2:T(8,128)(2,1)} fusion(bf16[1,3,16,4,64,64]{5,4,3,2,1,0:T(8,128)(2,1)S(1)} %get-tuple-element.15, bf16[1,3,16,4,64,64]{5,4,3,2,1,0:T(8,128)(2,1)S(1)} %get-tuple-element.14), kind=kLoop, calls=%fused_computation.3 | loop fusion | flops 1572864 | bytes 6291456 | tf_op jit(solution)/shard_map/transpose | solution.py:175
  31.1 3.2 %collective-permute-start.13 = (bf16[16,512]{1,0:T(8,128)(2,1)S(1)}, bf16[16,512]{1,0:T(8,128)(2,1)S(1)}, u32[]{:S(2)}, u32[]{:S(2)}) collective-permute-start(bf16[16,512]{1,0:T(8,128)(2,1)S(1)} %convert_element_type.75), channel_id=1, source_target_pairs={{0,1},{1,2},{2,3},{3,4},{4,5},{5,6},{6,7},{7,8},{8,9},{9,10},{10,1... | collective-permute-start | bytes 49160 | tf_op jit(solution)/shard_map/ppermute | solution.py:20
  35.6 10.7 %copy.44 = bf16[16,64,2,3,4,64]{5,4,3,2,1,0:T(4,128)(2,1)} copy(bf16[16,64,2,3,4,64]{5,1,4,0,3,2:T(8,128)(2,1)} %maximum_bitcast_fusion) | data formatting | bytes 6291456 | tf_op jit(solution)/shard_map/transpose | solution.py:175
  46.4 10.6 %reshape.158 = bf16[16,64,1536]{2,1,0:T(8,128)(2,1)} reshape(bf16[16,64,2,3,4,64]{5,4,3,2,1,0:T(4,128)(2,1)} %copy.44) | data formatting | bytes 6291456 | tf_op jit(solution)/shard_map/reshape | solution.py:175
  57.0 2.7 %collective-permute-start.10 = (bf16[5,8,1024]{2,1,0:T(8,128)(2,1)S(1)}, bf16[5,8,1024]{2,1,0:T(8,128)(2,1)S(1)}, u32[]{:S(2)}, u32[]{:S(2)}) collective-permute-start(bf16[5,8,1024]{2,1,0:T(8,128)(2,1)S(1)} %pad_maximum_fusion.1), channel_id=1, source_target_pairs={{0,2},{1,3},{2,0},{3,1},{4,6},{5,7},{6,4},{7,5},{8,10},{9,11},{10,... | collective-permute-start | bytes 245768 | tf_op jit(solution)/shard_map/ppermute | solution.py:53
  61.0 1.4 %collective-permute-done.10 = bf16[5,8,1024]{2,1,0:T(8,128)(2,1)S(1)} collective-permute-done((bf16[5,8,1024]{2,1,0:T(8,128)(2,1)S(1)}, bf16[5,8,1024]{2,1,0:T(8,128)(2,1)S(1)}, u32[]{:S(2)}, u32[]{:S(2)}) %collective-permute-start.10) | collective-permute-done | bytes 81952 | tf_op jit(solution)/shard_map/ppermute | solution.py:53
  63.5 1.6 %broadcast_in_dim.32 = bf16[16,2,3,4,64,16]{4,3,2,1,5,0:T(4,128)(2,1)} broadcast(bf16[16,4,64,16]{2,1,3,0:T(4,128)(2,1)S(1)} %copy.43), dimensions={0,3,4,5} | broadcast | bytes 917504 | tf_op jit(solution)/shard_map/broadcast_in_dim | solution.py:178
  65.1 3.8 %reshape.157 = bf16[16,1536,16]{1,2,0:T(8,128)(2,1)} reshape(bf16[16,2,3,4,64,16]{4,3,2,1,5,0:T(4,128)(2,1)} %broadcast_in_dim.32) | data formatting | bytes 1572864 | tf_op jit(solution)/shard_map/reshape | solution.py:180
  68.9 3.1 %fusion.29 = f32[16,16,64]{2,1,0:T(8,128)S(1)} fusion(bf16[16,1536,16]{1,2,0:T(8,128)(2,1)} %reshape.157, bf16[16,64,1536]{2,1,0:T(8,128)(2,1)} %reshape.158), kind=kOutput, calls=%fused_computation.72 | convolution fusion | flops 50331648 | bytes 3997696 | tf_op jit(solution)/shard_map/ckK,cKv->cvk/dot_general | solution.py:181
  74.8 1.8 %collective-permute-start.12 = (f32[1,4,1024]{2,1,0:T(4,128)S(1)}, f32[1,4,1024]{2,1,0:T(4,128)S(1)}, u32[]{:S(2)}, u32[]{:S(2)}) collective-permute-start(f32[1,4,1024]{2,1,0:T(4,128)S(1)} %constant_dynamic-slice_fusion), channel_id=1, source_target_pairs={{0,2},{1,3},{2,0},{3,1},{4,6},{5,7},{6,4},{7,5},{8,10},{9,11},{10,... | collective-permute-start | bytes 49160 | tf_op jit(solution)/shard_map/ppermute | solution.py:71
  76.8 1.7 %collective-permute-done.12 = f32[1,4,1024]{2,1,0:T(4,128)S(1)} collective-permute-done((f32[1,4,1024]{2,1,0:T(4,128)S(1)}, f32[1,4,1024]{2,1,0:T(4,128)S(1)}, u32[]{:S(2)}, u32[]{:S(2)}) %collective-permute-start.12) | collective-permute-done | bytes 16416 | tf_op jit(solution)/shard_map/ppermute | solution.py:71
  80.6 1.8 %collective-permute-start.16 = (f32[80,16]{0,1:T(8,128)S(1)}, f32[80,16]{0,1:T(8,128)S(1)}, u32[]{:S(2)}, u32[]{:S(2)}) collective-permute-start(f32[80,16]{0,1:T(8,128)S(1)} %fusion.46), channel_id=1, source_target_pairs={{0,2},{1,3},{2,0},{3,1},{4,6},{5,7},{6,4},{7,5},{8,10},{9,11},{10,... | collective-permute-start | bytes 15368 | tf_op jit(solution)/shard_map/ppermute | solution.py:41
  82.3 1.9 %collective-permute-done.16 = f32[80,16]{0,1:T(8,128)S(1)} collective-permute-done((f32[80,16]{0,1:T(8,128)S(1)}, f32[80,16]{0,1:T(8,128)S(1)}, u32[]{:S(2)}, u32[]{:S(2)}) %collective-permute-start.16) | collective-permute-done | bytes 5152 | tf_op jit(solution)/shard_map/ppermute | solution.py:41
  84.2 3.1 %collective-permute-start.17 = (f32[80,16]{0,1:T(8,128)S(1)}, f32[80,16]{0,1:T(8,128)S(1)}, u32[]{:S(2)}, u32[]{:S(2)}) collective-permute-start(f32[80,16]{0,1:T(8,128)S(1)} %add.131), channel_id=1, source_target_pairs={{0,4},{1,5},{2,6},{3,7},{4,0},{5,1},{6,2},{7,3},{8,12},{9,13},{10,... | collective-permute-start | bytes 15368 | tf_op jit(solution)/shard_map/ppermute | solution.py:41
  87.3 1.6 %collective-permute-done.17 = f32[80,16]{0,1:T(8,128)S(1)} collective-permute-done((f32[80,16]{0,1:T(8,128)S(1)}, f32[80,16]{0,1:T(8,128)S(1)}, u32[]{:S(2)}, u32[]{:S(2)}) %collective-permute-start.17) | collective-permute-done | bytes 5152 | tf_op jit(solution)/shard_map/ppermute | solution.py:41
  88.9 2.4 %collective-permute-start.18 = (f32[80,16]{0,1:T(8,128)S(1)}, f32[80,16]{0,1:T(8,128)S(1)}, u32[]{:S(2)}, u32[]{:S(2)}) collective-permute-start(f32[80,16]{0,1:T(8,128)S(1)} %add.132), channel_id=1, source_target_pairs={{0,8},{1,9},{2,10},{3,11},{4,12},{5,13},{6,14},{7,15},{8,0},{9,1},... | collective-permute-start | bytes 15368 | tf_op jit(solution)/shard_map/ppermute | solution.py:41
  91.3 1.6 %collective-permute-done.18 = f32[80,16]{0,1:T(8,128)S(1)} collective-permute-done((f32[80,16]{0,1:T(8,128)S(1)}, f32[80,16]{0,1:T(8,128)S(1)}, u32[]{:S(2)}, u32[]{:S(2)}) %collective-permute-start.18) | collective-permute-done | bytes 5152 | tf_op jit(solution)/shard_map/ppermute | solution.py:41
  92.9 3.5 %collective-permute-start.19 = (f32[80,16]{0,1:T(8,128)S(1)}, f32[80,16]{0,1:T(8,128)S(1)}, u32[]{:S(2)}, u32[]{:S(2)}) collective-permute-start(f32[80,16]{0,1:T(8,128)S(1)} %add.133), channel_id=1, source_target_pairs={{0,16},{1,17},{2,18},{3,19},{4,20},{5,21},{6,22},{7,23},{8,24},{9,... | collective-permute-start | bytes 15368 | tf_op jit(solution)/shard_map/ppermute | solution.py:41
  96.4 1.6 %collective-permute-done.19 = f32[80,16]{0,1:T(8,128)S(1)} collective-permute-done((f32[80,16]{0,1:T(8,128)S(1)}, f32[80,16]{0,1:T(8,128)S(1)}, u32[]{:S(2)}, u32[]{:S(2)}) %collective-permute-start.19) | collective-permute-done | bytes 5152 | tf_op jit(solution)/shard_map/ppermute | solution.py:41
  100.0 2.4 %shard_map.112 = (f32[16,16]{1,0:T(8,128)}, f32[16,512]{1,0:T(8,128)}) custom-call(f32[16,16]{1,0:T(8,128)S(1)} %get-tuple-element.20.gram_ref, f32[16,512]{1,0:T(8,128)S(1)} %convolution_subtract_fusion.residue_ref), custom_call_target="tpu_custom_call" | custom-call | flops 540672 | bytes 67584 | tf_op jit(solution)/shard_map/pallas_call | solution.py:117
  (80 shorter events, 17.9 us)
Async XLA Ops:
  0.6 72.9 %copy-start = (bf16[3,4,8,128,128]{4,3,2,1,0:T(8,128)(2,1)S(1)}, bf16[3,4,8,128,128]{4,3,2,1,0:T(8,128)(2,1)}, u32[]{:S(2)}) copy-start(bf16[3,4,8,128,128]{4,3,2,1,0:T(8,128)(2,1)} %param.14) | copy-start | bytes 9437188
  1.9 29.2 %collective-permute-start.5 = (bf16[1,4,1024]{2,1,0:T(4,128)(2,1)S(1)}, bf16[1,4,1024]{2,1,0:T(4,128)(2,1)S(1)}, u32[]{:S(2)}, u32[]{:S(2)}) collective-permute-start(bf16[1,4,1024]{2,1,0:T(4,128)(2,1)S(1)} %reshape.153), channel_id=1, source_target_pairs={{0,8},{4,12},{8,16},{12,20},{16,24},{20,28},{1,9},{5,13},{9,17},{1... | collective-permute-start | bytes 24584 | tf_op jit(solution)/shard_map/ppermute | solution.py:12
  6.8 27.5 %collective-permute-start.6 = (bf16[1,4,1024]{2,1,0:T(4,128)(2,1)S(1)}, bf16[1,4,1024]{2,1,0:T(4,128)(2,1)S(1)}, u32[]{:S(2)}, u32[]{:S(2)}) collective-permute-start(bf16[1,4,1024]{2,1,0:T(4,128)(2,1)S(1)} %reshape.153), channel_id=1, source_target_pairs={{0,4},{4,8},{8,12},{12,16},{16,20},{20,24},{24,28},{1,5},{5,9},{9,... | collective-permute-start | bytes 24584 | tf_op jit(solution)/shard_map/ppermute | solution.py:12
  10.3 24.1 %collective-permute-start.7 = (bf16[1,4,1024]{2,1,0:T(4,128)(2,1)S(1)}, bf16[1,4,1024]{2,1,0:T(4,128)(2,1)S(1)}, u32[]{:S(2)}, u32[]{:S(2)}) collective-permute-start(bf16[1,4,1024]{2,1,0:T(4,128)(2,1)S(1)} %reshape.153), channel_id=1, source_target_pairs={{4,0},{8,4},{12,8},{16,12},{20,16},{24,20},{28,24},{5,1},{9,5},{13... | collective-permute-start | bytes 24584 | tf_op jit(solution)/shard_map/ppermute | solution.py:12
  11.6 22.9 %collective-permute-start.8 = (bf16[1,4,1024]{2,1,0:T(4,128)(2,1)S(1)}, bf16[1,4,1024]{2,1,0:T(4,128)(2,1)S(1)}, u32[]{:S(2)}, u32[]{:S(2)}) collective-permute-start(bf16[1,4,1024]{2,1,0:T(4,128)(2,1)S(1)} %reshape.153), channel_id=1, source_target_pairs={{8,0},{12,4},{16,8},{20,12},{24,16},{28,20},{9,1},{13,5},{17,9},{2... | collective-permute-start | bytes 24584 | tf_op jit(solution)/shard_map/ppermute | solution.py:12
  13.6 46.1 %collective-permute-start.14 = (bf16[16,512]{1,0:T(8,128)(2,1)S(1)}, bf16[16,512]{1,0:T(8,128)(2,1)S(1)}, u32[]{:S(2)}, u32[]{:S(2)}) collective-permute-start(bf16[16,512]{1,0:T(8,128)(2,1)S(1)} %convert_element_type.75), channel_id=1, source_target_pairs={{1,0},{2,1},{3,2},{4,3},{5,4},{6,5},{7,6},{8,7},{9,8},{10,9},{11,1... | collective-permute-start | bytes 49160 | tf_op jit(solution)/shard_map/ppermute | solution.py:23
  16.7 6.3 %copy-start.6 = (s32[4,8]{1,0:T(4,128)S(1)}, s32[4,8]{1,0:T(4,128)}, u32[]{:S(2)}) copy-start(s32[4,8]{1,0:T(4,128)} %param.15) | copy-start | bytes 388
  31.1 28.6 %collective-permute-start.13 = (bf16[16,512]{1,0:T(8,128)(2,1)S(1)}, bf16[16,512]{1,0:T(8,128)(2,1)S(1)}, u32[]{:S(2)}, u32[]{:S(2)}) collective-permute-start(bf16[16,512]{1,0:T(8,128)(2,1)S(1)} %convert_element_type.75), channel_id=1, source_target_pairs={{0,1},{1,2},{2,3},{3,4},{4,5},{5,6},{6,7},{7,8},{8,9},{9,10},{10,1... | collective-permute-start | bytes 49160 | tf_op jit(solution)/shard_map/ppermute | solution.py:20
  34.5 22.5 %collective-permute-start.9 = (bf16[5,4,1024]{2,1,0:T(4,128)(2,1)S(1)}, bf16[5,4,1024]{2,1,0:T(4,128)(2,1)S(1)}, u32[]{:S(2)}, u32[]{:S(2)}) collective-permute-start(bf16[5,4,1024]{2,1,0:T(4,128)(2,1)S(1)} %constant_dynamic-update-slice_fusion), channel_id=1, source_target_pairs={{0,1},{1,0},{2,3},{3,2},{4,5},{5,4},{6,7},{7,6},{8,9},{9,8},{10,11... | collective-permute-start | bytes 122888 | tf_op jit(solution)/shard_map/ppermute | solution.py:53
  57.0 5.3 %collective-permute-start.10 = (bf16[5,8,1024]{2,1,0:T(8,128)(2,1)S(1)}, bf16[5,8,1024]{2,1,0:T(8,128)(2,1)S(1)}, u32[]{:S(2)}, u32[]{:S(2)}) collective-permute-start(bf16[5,8,1024]{2,1,0:T(8,128)(2,1)S(1)} %pad_maximum_fusion.1), channel_id=1, source_target_pairs={{0,2},{1,3},{2,0},{3,1},{4,6},{5,7},{6,4},{7,5},{8,10},{9,11},{10,... | collective-permute-start | bytes 245768 | tf_op jit(solution)/shard_map/ppermute | solution.py:53
  65.1 8.4 %copy-start.1 = (bf16[32,16,128]{2,1,0:T(8,128)(2,1)S(1)}, bf16[32,16,128]{2,1,0:T(8,128)(2,1)}, u32[]{:S(2)}) copy-start(bf16[32,16,128]{2,1,0:T(8,128)(2,1)} %gather_fusion.1) | copy-start | bytes 393220
  68.9 10.1 %copy-start.2 = (f32[64,512]{1,0:T(8,128)S(1)}, f32[64,512]{1,0:T(8,128)}, u32[]{:S(2)}) copy-start(f32[64,512]{1,0:T(8,128)} %param.19) | copy-start | bytes 393220
  72.7 2.0 %copy-start.4 = (f32[2,2,4,1024]{3,2,1,0:T(4,128)S(1)}, f32[2,2,4,1024]{3,2,1,0:T(4,128)}, u32[]{:S(2)}) copy-start(f32[2,2,4,1024]{3,2,1,0:T(4,128)} %reshape_reshape_reshape.3) | copy-start | bytes 196612
  72.7 6.0 %copy-start.5 = (bf16[4,64,128]{2,1,0:T(8,128)(2,1)S(1)}, bf16[4,64,128]{2,1,0:T(8,128)(2,1)}, u32[]{:S(2)}) copy-start(bf16[4,64,128]{2,1,0:T(8,128)(2,1)} %param.13) | copy-start | bytes 196612
  73.5 1.2 %collective-permute-start.11 = (f32[2,4,1024]{2,1,0:T(4,128)S(1)}, f32[2,4,1024]{2,1,0:T(4,128)S(1)}, u32[]{:S(2)}, u32[]{:S(2)}) collective-permute-start(f32[2,4,1024]{2,1,0:T(4,128)S(1)} %dynamic-slice_bitcast_fusion), channel_id=1, source_target_pairs={{0,1},{1,0},{2,3},{3,2},{4,5},{5,4},{6,7},{7,6},{8,9},{9,8},{10,11... | collective-permute-start | bytes 98312 | tf_op jit(solution)/shard_map/ppermute | solution.py:71
  74.8 3.8 %collective-permute-start.12 = (f32[1,4,1024]{2,1,0:T(4,128)S(1)}, f32[1,4,1024]{2,1,0:T(4,128)S(1)}, u32[]{:S(2)}, u32[]{:S(2)}) collective-permute-start(f32[1,4,1024]{2,1,0:T(4,128)S(1)} %constant_dynamic-slice_fusion), channel_id=1, source_target_pairs={{0,2},{1,3},{2,0},{3,1},{4,6},{5,7},{6,4},{7,5},{8,10},{9,11},{10,... | collective-permute-start | bytes 49160 | tf_op jit(solution)/shard_map/ppermute | solution.py:71
  79.3 1.2 %collective-permute-start.15 = (f32[80,16]{0,1:T(8,128)S(1)}, f32[80,16]{0,1:T(8,128)S(1)}, u32[]{:S(2)}, u32[]{:S(2)}) collective-permute-start(f32[80,16]{0,1:T(8,128)S(1)} %pad_maximum_fusion.2), channel_id=1, source_target_pairs={{0,1},{1,0},{2,3},{3,2},{4,5},{5,4},{6,7},{7,6},{8,9},{9,8},{10,11... | collective-permute-start | bytes 15368 | tf_op jit(solution)/shard_map/ppermute | solution.py:41
  80.6 3.7 %collective-permute-start.16 = (f32[80,16]{0,1:T(8,128)S(1)}, f32[80,16]{0,1:T(8,128)S(1)}, u32[]{:S(2)}, u32[]{:S(2)}) collective-permute-start(f32[80,16]{0,1:T(8,128)S(1)} %fusion.46), channel_id=1, source_target_pairs={{0,2},{1,3},{2,0},{3,1},{4,6},{5,7},{6,4},{7,5},{8,10},{9,11},{10,... | collective-permute-start | bytes 15368 | tf_op jit(solution)/shard_map/ppermute | solution.py:41
  84.2 4.7 %collective-permute-start.17 = (f32[80,16]{0,1:T(8,128)S(1)}, f32[80,16]{0,1:T(8,128)S(1)}, u32[]{:S(2)}, u32[]{:S(2)}) collective-permute-start(f32[80,16]{0,1:T(8,128)S(1)} %add.131), channel_id=1, source_target_pairs={{0,4},{1,5},{2,6},{3,7},{4,0},{5,1},{6,2},{7,3},{8,12},{9,13},{10,... | collective-permute-start | bytes 15368 | tf_op jit(solution)/shard_map/ppermute | solution.py:41
  88.9 4.0 %collective-permute-start.18 = (f32[80,16]{0,1:T(8,128)S(1)}, f32[80,16]{0,1:T(8,128)S(1)}, u32[]{:S(2)}, u32[]{:S(2)}) collective-permute-start(f32[80,16]{0,1:T(8,128)S(1)} %add.132), channel_id=1, source_target_pairs={{0,8},{1,9},{2,10},{3,11},{4,12},{5,13},{6,14},{7,15},{8,0},{9,1},... | collective-permute-start | bytes 15368 | tf_op jit(solution)/shard_map/ppermute | solution.py:41
  92.9 5.1 %collective-permute-start.19 = (f32[80,16]{0,1:T(8,128)S(1)}, f32[80,16]{0,1:T(8,128)S(1)}, u32[]{:S(2)}, u32[]{:S(2)}) collective-permute-start(f32[80,16]{0,1:T(8,128)S(1)} %add.133), channel_id=1, source_target_pairs={{0,16},{1,17},{2,18},{3,19},{4,20},{5,21},{6,22},{7,23},{8,24},{9,... | collective-permute-start | bytes 15368 | tf_op jit(solution)/shard_map/ppermute | solution.py:41
  98.0 4.4 %copy-start.3 = (f32[80,16]{0,1:T(8,128)}, f32[80,16]{0,1:T(8,128)S(1)}, u32[]{:S(2)}) copy-start(f32[80,16]{0,1:T(8,128)S(1)} %add.134) | copy-start | bytes 15364

commit v9 on v6

--- a/solution.py
+++ b/solution.py
@@ -149,17 +149,18 @@
         "cki,vci->cvk", leaf_basis, by_cluster, preferred_element_type=jnp.float32
     ).astype(jnp.bfloat16)
     own_rows = coarse.reshape(1, local_count, vec_count * rank_width)
-    offsets = list(range(-reach_groups, reach_groups + 1))
-    reached = group_reach(own_rows, offsets)
-    window, xor_order = xor_gather(reached, "coef", 1)
+    by_leaf, leaf_xor = xor_gather(own_rows, "leaf", 0)
+    window, coef_xor = xor_gather(by_leaf, "coef", 1)
     flat_rows = window.reshape(-1, vec_count * rank_width)
-    group_pos = lax.axis_index("leaf")
-    local_ids = far_list - (group_pos - reach_groups) * group_size
-    if xor_order:
-        in_group = local_ids % group_size
-        holder = (in_group // local_count) ^ lax.axis_index("coef")
-        local_ids = local_ids - in_group + holder * local_count + in_group % local_count
-    local_ids = local_ids.reshape(-1)
+    source_group = far_list // group_size
+    source_holder = (far_list % group_size) // local_count
+    if leaf_xor:
+        source_group = source_group ^ lax.axis_index("leaf")
+    if coef_xor:
+        source_holder = source_holder ^ lax.axis_index("coef")
+    local_ids = (
+        source_group * group_size + source_holder * local_count + far_list % local_count
+    ).reshape(-1)
     sources = flat_rows.at[local_ids].get(mode="promise_in_bounds").reshape(
         group_size, slot_count, vec_count, rank_width
     )

time: 72.3 us -> 70.4 us (0.974)
  starting transfers between devices: 31.7 us -> 20.2 us
  waiting for transfers between devices: 11.3 us -> 19.3 us
  other arithmetic: 4.8 us -> 6.64 us
    ppermute x4 -> x0, starting transfers between devices: 11 us -> none  [shifted(): return lax.ppermute(block, axis, route)]
    ppermute x5, starting transfers between devices: 10.7 us -> 5.82 us  [butterfly_sum(): block = block + lax.ppermute(block, axes, route)]
    ppermute x2 -> x5, starting transfers between devices: 3.86 us -> 8.34 us  [xor_gather(): block = jnp.concatenate([block, lax.ppermute(block, axis, route)], axis=dim)]
    ppermute x2 -> x5, waiting for transfers between devices: 1.41 us -> 5.59 us  [xor_gather(): block = jnp.concatenate([block, lax.ppermute(block, axis, route)], axis=dim)]
    ppermute x5, waiting for transfers between devices: 7.93 us -> 10.9 us  [butterfly_sum(): block = block + lax.ppermute(block, axes, route)]
    concatenate x2 -> x4, other arithmetic: 0.12 us -> 1.12 us  [xor_gather(): block = jnp.concatenate([block, lax.ppermute(block, axis, route)], axis=dim)]
    ppermute x2, starting transfers between devices: 1.9 us -> 1.04 us  [butterfly_scatter(): parts = keep + lax.ppermute(give, axis, route)]
    ppermute x2, waiting for transfers between devices: 1.99 us -> 2.85 us  [butterfly_scatter(): parts = keep + lax.ppermute(give, axis, route)]
  transfers between devices with their start and end apart: 15 -> 14, of which waited for: 8 -> 10; matrix products, arithmetic and copies ran while one was open for 17% -> 19% of each run, Pallas kernels for 0% -> 0%
where the time goes in v9:
time: 70.4 us; the launch traced here: 69.9 us
  starting transfers between devices  20.2 us (29%)
  waiting for transfers between devices  19.3 us (27%)
  local copies, waits for them, and re-layouts  10.2 us (14%)
  matrix products  8.84 us (13%)
  other arithmetic  6.64 us (9%)
  Pallas kernels  2.43 us (3%)
  between operations  2.21 us (3%)
    ppermute x5, waiting for transfers between devices, butterfly_sum(): block = block + lax.ppermute(block, axes, route)  10.9 us
    ppermute x5, starting transfers between devices, xor_gather(): block = jnp.concatenate([block, lax.ppermute(block, axis, route)], axis=dim)  8.34 us
    ppermute x5, starting transfers between devices, butterfly_sum(): block = block + lax.ppermute(block, axes, route)  5.82 us
    reshape x1, local copies, waits for them, and re-layouts, on_device(): couple = coupling.reshape(3, group_size, slot_count, rank_width, rank_width)  5.63 us
    ppermute x5, waiting for transfers between devices, xor_gather(): block = jnp.concatenate([block, lax.ppermute(block, axis, route)], axis=dim)  5.59 us
    dot_general x1, matrix products, on_device(): jnp.einsum('jcfkl,cfvl->jcfvk', couple, sources, preferred_element_type=j...  4.2 us
    ppermute x1, starting transfers between devices, extended_2(): lax.ppermute(lax.slice_in_dim(block, block.shape[dim] - width, None, axis...  3.63 us
    ppermute x2, waiting for transfers between devices, butterfly_scatter(): parts = keep + lax.ppermute(give, axis, route)  2.85 us
  transfers between devices with their start and end apart: 14, of which 10 were waited for; matrix products, arithmetic and copies ran while one was open for 19% of the time, Pallas kernels for 0%

profile of v9, /device:TPU:0, one launch (start us, length us, event | category | flops | bytes accessed | tf_op | source)
XLA Modules:
  0.0 69.9 jit_solution(4715115208092713908)
XLA Ops:
  1.6 1.4 %collective-permute-start.13 = (bf16[16,512]{1,0:T(8,128)(2,1)S(1)}, bf16[16,512]{1,0:T(8,128)(2,1)S(1)}, u32[]{:S(2)}, u32[]{:S(2)}) collective-permute-start(bf16[16,512]{1,0:T(8,128)(2,1)S(1)} %convert_element_type.24), channel_id=1, source_target_pairs={{1,0},{2,1},{3,2},{4,3},{5,4},{6,5},{7,6},{8,7},{9,8},{10,9},{11,1... | collective-permute-start | bytes 49160 | tf_op jit(solution)/shard_map/ppermute | solution.py:23
  3.0 3.6 %collective-permute-start.12 = (bf16[16,512]{1,0:T(8,128)(2,1)S(1)}, bf16[16,512]{1,0:T(8,128)(2,1)}, u32[]{:S(2)}, u32[]{:S(2)}) collective-permute-start(bf16[16,512]{1,0:T(8,128)(2,1)S(1)} %convert_element_type.24), channel_id=1, source_target_pairs={{0,1},{1,2},{2,3},{3,4},{4,5},{5,6},{6,7},{7,8},{8,9},{9,10},{10,1... | collective-permute-start | bytes 49160 | tf_op jit(solution)/shard_map/ppermute | solution.py:20
  6.6 1.0 %convolution_convert_fusion = bf16[4,16,64]{2,1,0:T(8,128)(2,1)S(1)} fusion(bf16[4,64,128]{2,1,0:T(8,128)(2,1)} %param.13, f32[16,512]{1,0:T(8,128)} %param.11), kind=kOutput, calls=%fused_computation.14 | convolution fusion | flops 1060864 | bytes 106496 | tf_op jit(solution)/shard_map/cki,vci->cvk/dot_general | solution.py:148
  7.7 2.8 %collective-permute-start.5 = (bf16[1,4,1024]{2,1,0:T(4,128)(2,1)S(1)}, bf16[1,4,1024]{2,1,0:T(4,128)(2,1)S(1)}, u32[]{:S(2)}, u32[]{:S(2)}) collective-permute-start(bf16[1,4,1024]{2,1,0:T(4,128)(2,1)S(1)} %reshape.111), channel_id=1, source_target_pairs={{0,4},{4,0},{8,12},{12,8},{16,20},{20,16},{24,28},{28,24},{1,5},{5... | collective-permute-start | bytes 24584 | tf_op jit(solution)/shard_map/ppermute | solution.py:53
  13.7 1.6 %collective-permute-start.6 = (bf16[2,4,1024]{2,1,0:T(4,128)(2,1)S(1)}, bf16[2,4,1024]{2,1,0:T(4,128)(2,1)S(1)}, u32[]{:S(2)}, u32[]{:S(2)}) collective-permute-start(bf16[2,4,1024]{2,1,0:T(4,128)(2,1)S(1)} %pad_maximum_fusion.3), channel_id=1, source_target_pairs={{0,8},{4,12},{8,0},{12,4},{16,24},{20,28},{24,16},{28,20},{1,9},{5... | collective-permute-start | bytes 49160 | tf_op jit(solution)/shard_map/ppermute | solution.py:53
  15.3 2.1 %collective-permute-done.6 = bf16[2,4,1024]{2,1,0:T(4,128)(2,1)S(1)} collective-permute-done((bf16[2,4,1024]{2,1,0:T(4,128)(2,1)S(1)}, bf16[2,4,1024]{2,1,0:T(4,128)(2,1)S(1)}, u32[]{:S(2)}, u32[]{:S(2)}) %collective-permute-start.6) | collective-permute-done | bytes 16416 | tf_op jit(solution)/shard_map/ppermute | solution.py:53
  17.5 2.7 %collective-permute-start.7 = (bf16[4,4,1024]{2,1,0:T(4,128)(2,1)S(1)}, bf16[4,4,1024]{2,1,0:T(4,128)(2,1)S(1)}, u32[]{:S(2)}, u32[]{:S(2)}) collective-permute-start(bf16[4,4,1024]{2,1,0:T(4,128)(2,1)S(1)} %pad_maximum_fusion.2), channel_id=1, source_target_pairs={{0,16},{4,20},{8,24},{12,28},{16,0},{20,4},{24,8},{28,12},{1,17},{... | collective-permute-start | bytes 98312 | tf_op jit(solution)/shard_map/ppermute | solution.py:53
  20.2 2.2 %collective-permute-done.7 = bf16[4,4,1024]{2,1,0:T(4,128)(2,1)S(1)} collective-permute-done((bf16[4,4,1024]{2,1,0:T(4,128)(2,1)S(1)}, bf16[4,4,1024]{2,1,0:T(4,128)(2,1)S(1)}, u32[]{:S(2)}, u32[]{:S(2)}) %collective-permute-start.7) | collective-permute-done | bytes 32800 | tf_op jit(solution)/shard_map/ppermute | solution.py:53
  22.5 1.2 %collective-permute-done.8 = bf16[8,4,1024]{2,1,0:T(4,128)(2,1)S(1)} collective-permute-done((bf16[8,4,1024]{2,1,0:T(4,128)(2,1)S(1)}, bf16[8,4,1024]{2,1,0:T(4,128)(2,1)S(1)}, u32[]{:S(2)}, u32[]{:S(2)}) %collective-permute-start.8) | collective-permute-done | bytes 65568 | tf_op jit(solution)/shard_map/ppermute | solution.py:53
  23.8 1.2 %collective-permute-start.9 = (bf16[8,8,1024]{2,1,0:T(8,128)(2,1)S(1)}, bf16[8,8,1024]{2,1,0:T(8,128)(2,1)}, u32[]{:S(2)}, u32[]{:S(2)}) collective-permute-start(bf16[8,8,1024]{2,1,0:T(8,128)(2,1)S(1)} %pad_maximum_fusion.1), channel_id=1, source_target_pairs={{0,2},{1,3},{2,0},{3,1},{4,6},{5,7},{6,4},{7,5},{8,10},{9,11},{10,... | collective-permute-start | bytes 393224 | tf_op jit(solution)/shard_map/ppermute | solution.py:53
  25.0 5.6 %reshape.115 = bf16[3,16,4,64,64]{4,3,2,1,0:T(8,128)(2,1)} reshape(bf16[3,16,4,4096]{3,2,1,0:T(4,128)(2,1)} %param.16) | data formatting | bytes 3145728 | tf_op jit(solution)/shard_map/reshape | solution.py:170
  32.1 1.2 %gather_fusion.1 = bf16[32,16,128]{2,1,0:T(8,128)(2,1)} fusion(bf16[16,12,128]{2,0,1:T(8,128)(2,1)S(1)} %copy_bitcast_fusion, s32[1024]{0:T(1024)S(1)} %pad_clamp_fusion), kind=kCustom, calls=%fused_computation.1 | custom fusion | bytes 262272 | tf_op jit(solution)/shard_map/gather | solution.py:181
  33.3 1.0 %pad_maximum_fusion = bf16[8,16,1024]{2,1,0:T(8,128)(2,1)S(1)} fusion(bf16[8,8,1024]{2,1,0:T(8,128)(2,1)} %collective-permute-done.9, bf16[8,4,1024]{2,1,0:T(4,128)(2,1)S(1)} %collective-permute-done.8, bf16[8,4,1024]{2,1,0:T(4,128)(2,1)S(1)} %constant_dynamic-update-slice_fusion), kind=kLoop, calls=%fused_computation.20 | loop fusion | flops 786432 | bytes 524288 | tf_op jit(solution)/shard_map/concatenate | solution.py:53
  35.2 4.2 %fusion.6 = bf16[3,16,4,16,64]{4,3,0,2,1:T(8,128)(2,1)S(1)} fusion(bf16[3,16,4,64,64]{4,3,2,1,0:T(8,128)(2,1)} %reshape.115, bf16[16,4,16,64]{3,2,1,0:T(8,128)(2,1)S(1)} %reshape.114, pred[16,4,64]{2,1,0:T(4,128)(4,1)S(1)} %get-tuple-element.15), kind=kOutput, calls=%fused_computation.9 | convolution fusion | flops 25231360 | bytes 2101248 | tf_op jit(solution)/shard_map/jcfkl,cfvl->jcfvk/dot_general | solution.py:171
  41.0 1.0 %reshape_reshape_reshape.3 = f32[2,2,4,1024]{3,2,1,0:T(4,128)S(1)} reshape(f32[16,16,64]{2,1,0:T(8,128)} %multiply_reduce_fusion) | data formatting | bytes 131072 | tf_op jit(solution)/shard_map/reshape;reshape;reshape | solution.py:67
  44.5 2.6 %collective-permute-done.11 = f32[1,4,1024]{2,1,0:T(4,128)S(1)} collective-permute-done((f32[1,4,1024]{2,1,0:T(4,128)S(1)}, f32[1,4,1024]{2,1,0:T(4,128)S(1)}, u32[]{:S(2)}, u32[]{:S(2)}) %collective-permute-start.11) | collective-permute-done | bytes 16416 | tf_op jit(solution)/shard_map/ppermute | solution.py:71
  48.7 1.2 %collective-permute-done.14 = f32[80,16]{0,1:T(8,128)S(1)} collective-permute-done((f32[80,16]{0,1:T(8,128)S(1)}, f32[80,16]{0,1:T(8,128)S(1)}, u32[]{:S(2)}, u32[]{:S(2)}) %collective-permute-start.14) | collective-permute-done | bytes 5152 | tf_op jit(solution)/shard_map/ppermute | solution.py:41
  50.8 2.7 %collective-permute-done.15 = f32[80,16]{0,1:T(8,128)S(1)} collective-permute-done((f32[80,16]{0,1:T(8,128)S(1)}, f32[80,16]{0,1:T(8,128)S(1)}, u32[]{:S(2)}, u32[]{:S(2)}) %collective-permute-start.15) | collective-permute-done | bytes 5152 | tf_op jit(solution)/shard_map/ppermute | solution.py:41
  54.1 3.1 %collective-permute-done.16 = f32[80,16]{0,1:T(8,128)S(1)} collective-permute-done((f32[80,16]{0,1:T(8,128)S(1)}, f32[80,16]{0,1:T(8,128)S(1)}, u32[]{:S(2)}, u32[]{:S(2)}) %collective-permute-start.16) | collective-permute-done | bytes 5152 | tf_op jit(solution)/shard_map/ppermute | solution.py:41
  57.2 1.6 %collective-permute-start.17 = (f32[80,16]{0,1:T(8,128)S(1)}, f32[80,16]{0,1:T(8,128)S(1)}, u32[]{:S(2)}, u32[]{:S(2)}) collective-permute-start(f32[80,16]{0,1:T(8,128)S(1)} %add.132), channel_id=1, source_target_pairs={{0,8},{1,9},{2,10},{3,11},{4,12},{5,13},{6,14},{7,15},{8,0},{9,1},... | collective-permute-start | bytes 15368 | tf_op jit(solution)/shard_map/ppermute | solution.py:41
  58.8 2.1 %collective-permute-done.17 = f32[80,16]{0,1:T(8,128)S(1)} collective-permute-done((f32[80,16]{0,1:T(8,128)S(1)}, f32[80,16]{0,1:T(8,128)S(1)}, u32[]{:S(2)}, u32[]{:S(2)}) %collective-permute-start.17) | collective-permute-done | bytes 5152 | tf_op jit(solution)/shard_map/ppermute | solution.py:41
  60.9 2.7 %collective-permute-start.18 = (f32[80,16]{0,1:T(8,128)S(1)}, f32[80,16]{0,1:T(8,128)S(1)}, u32[]{:S(2)}, u32[]{:S(2)}) collective-permute-start(f32[80,16]{0,1:T(8,128)S(1)} %add.133), channel_id=1, source_target_pairs={{0,16},{1,17},{2,18},{3,19},{4,20},{5,21},{6,22},{7,23},{8,24},{9,... | collective-permute-start | bytes 15368 | tf_op jit(solution)/shard_map/ppermute | solution.py:41
  63.6 1.8 %collective-permute-done.18 = f32[80,16]{0,1:T(8,128)S(1)} collective-permute-done((f32[80,16]{0,1:T(8,128)S(1)}, f32[80,16]{0,1:T(8,128)S(1)}, u32[]{:S(2)}, u32[]{:S(2)}) %collective-permute-start.18) | collective-permute-done | bytes 5152 | tf_op jit(solution)/shard_map/ppermute | solution.py:41
  67.4 2.4 %shard_map.112 = (f32[16,16]{1,0:T(8,128)}, f32[16,512]{1,0:T(8,128)}) custom-call(f32[16,16]{1,0:T(8,128)S(1)} %get-tuple-element.18.gram_ref, f32[16,512]{1,0:T(8,128)S(1)} %convolution_subtract_fusion.residue_ref), custom_call_target="tpu_custom_call" | custom-call | flops 540672 | bytes 67584 | tf_op jit(solution)/shard_map/pallas_call | solution.py:117
  (68 shorter events, 14.6 us)
Async XLA Ops:
  0.6 41.4 %copy-start = (bf16[3,4,8,128,128]{4,3,2,1,0:T(8,128)(2,1)S(1)}, bf16[3,4,8,128,128]{4,3,2,1,0:T(8,128)(2,1)}, u32[]{:S(2)}) copy-start(bf16[3,4,8,128,128]{4,3,2,1,0:T(8,128)(2,1)} %param.14) | copy-start | bytes 9437188
  1.6 29.7 %collective-permute-start.13 = (bf16[16,512]{1,0:T(8,128)(2,1)S(1)}, bf16[16,512]{1,0:T(8,128)(2,1)S(1)}, u32[]{:S(2)}, u32[]{:S(2)}) collective-permute-start(bf16[16,512]{1,0:T(8,128)(2,1)S(1)} %convert_element_type.24), channel_id=1, source_target_pairs={{1,0},{2,1},{3,2},{4,3},{5,4},{6,5},{7,6},{8,7},{9,8},{10,9},{11,1... | collective-permute-start | bytes 49160 | tf_op jit(solution)/shard_map/ppermute | solution.py:23
  3.0 28.3 %collective-permute-start.12 = (bf16[16,512]{1,0:T(8,128)(2,1)S(1)}, bf16[16,512]{1,0:T(8,128)(2,1)}, u32[]{:S(2)}, u32[]{:S(2)}) collective-permute-start(bf16[16,512]{1,0:T(8,128)(2,1)S(1)} %convert_element_type.24), channel_id=1, source_target_pairs={{0,1},{1,2},{2,3},{3,4},{4,5},{5,6},{6,7},{7,8},{8,9},{9,10},{10,1... | collective-permute-start | bytes 49160 | tf_op jit(solution)/shard_map/ppermute | solution.py:20
  7.7 5.9 %collective-permute-start.5 = (bf16[1,4,1024]{2,1,0:T(4,128)(2,1)S(1)}, bf16[1,4,1024]{2,1,0:T(4,128)(2,1)S(1)}, u32[]{:S(2)}, u32[]{:S(2)}) collective-permute-start(bf16[1,4,1024]{2,1,0:T(4,128)(2,1)S(1)} %reshape.111), channel_id=1, source_target_pairs={{0,4},{4,0},{8,12},{12,8},{16,20},{20,16},{24,28},{28,24},{1,5},{5... | collective-permute-start | bytes 24584 | tf_op jit(solution)/shard_map/ppermute | solution.py:53
  13.7 3.8 %collective-permute-start.6 = (bf16[2,4,1024]{2,1,0:T(4,128)(2,1)S(1)}, bf16[2,4,1024]{2,1,0:T(4,128)(2,1)S(1)}, u32[]{:S(2)}, u32[]{:S(2)}) collective-permute-start(bf16[2,4,1024]{2,1,0:T(4,128)(2,1)S(1)} %pad_maximum_fusion.3), channel_id=1, source_target_pairs={{0,8},{4,12},{8,0},{12,4},{16,24},{20,28},{24,16},{28,20},{1,9},{5... | collective-permute-start | bytes 49160 | tf_op jit(solution)/shard_map/ppermute | solution.py:53
  17.5 4.9 %collective-permute-start.7 = (bf16[4,4,1024]{2,1,0:T(4,128)(2,1)S(1)}, bf16[4,4,1024]{2,1,0:T(4,128)(2,1)S(1)}, u32[]{:S(2)}, u32[]{:S(2)}) collective-permute-start(bf16[4,4,1024]{2,1,0:T(4,128)(2,1)S(1)} %pad_maximum_fusion.2), channel_id=1, source_target_pairs={{0,16},{4,20},{8,24},{12,28},{16,0},{20,4},{24,8},{28,12},{1,17},{... | collective-permute-start | bytes 98312 | tf_op jit(solution)/shard_map/ppermute | solution.py:53
  22.4 1.3 %collective-permute-start.8 = (bf16[8,4,1024]{2,1,0:T(4,128)(2,1)S(1)}, bf16[8,4,1024]{2,1,0:T(4,128)(2,1)S(1)}, u32[]{:S(2)}, u32[]{:S(2)}) collective-permute-start(bf16[8,4,1024]{2,1,0:T(4,128)(2,1)S(1)} %constant_dynamic-update-slice_fusion), channel_id=1, source_target_pairs={{0,1},{1,0},{2,3},{3,2},{4,5},{5,4},{6,7},{7,6},{8,9},{9,8},{10,11... | collective-permute-start | bytes 196616 | tf_op jit(solution)/shard_map/ppermute | solution.py:53
  23.8 9.5 %collective-permute-start.9 = (bf16[8,8,1024]{2,1,0:T(8,128)(2,1)S(1)}, bf16[8,8,1024]{2,1,0:T(8,128)(2,1)}, u32[]{:S(2)}, u32[]{:S(2)}) collective-permute-start(bf16[8,8,1024]{2,1,0:T(8,128)(2,1)S(1)} %pad_maximum_fusion.1), channel_id=1, source_target_pairs={{0,2},{1,3},{2,0},{3,1},{4,6},{5,7},{6,4},{7,5},{8,10},{9,11},{10,... | collective-permute-start | bytes 393224 | tf_op jit(solution)/shard_map/ppermute | solution.py:53
  35.2 5.0 %copy-start.4 = (f32[16,4,64]{2,1,0:T(4,128)S(1)}, f32[16,4,64]{2,1,0:T(4,128)}, u32[]{:S(2)}) copy-start(f32[16,4,64]{2,1,0:T(4,128)} %get-tuple-element.14) | copy-start | bytes 49156
  35.2 6.8 %copy-start.1 = (bf16[32,16,128]{2,1,0:T(8,128)(2,1)S(1)}, bf16[32,16,128]{2,1,0:T(8,128)(2,1)}, u32[]{:S(2)}) copy-start(bf16[32,16,128]{2,1,0:T(8,128)(2,1)} %gather_fusion.1) | copy-start | bytes 393220
  39.4 8.9 %copy-start.2 = (f32[64,512]{1,0:T(8,128)S(1)}, f32[64,512]{1,0:T(8,128)}, u32[]{:S(2)}) copy-start(f32[64,512]{1,0:T(8,128)} %param.19) | copy-start | bytes 393220
  42.0 1.3 %collective-permute-start.10 = (f32[2,4,1024]{2,1,0:T(4,128)S(1)}, f32[2,4,1024]{2,1,0:T(4,128)S(1)}, u32[]{:S(2)}, u32[]{:S(2)}) collective-permute-start(f32[2,4,1024]{2,1,0:T(4,128)S(1)} %dynamic-slice_bitcast_fusion), channel_id=1, source_target_pairs={{0,1},{1,0},{2,3},{3,2},{4,5},{5,4},{6,7},{7,6},{8,9},{9,8},{10,11... | collective-permute-start | bytes 98312 | tf_op jit(solution)/shard_map/ppermute | solution.py:71
  43.3 3.8 %collective-permute-start.11 = (f32[1,4,1024]{2,1,0:T(4,128)S(1)}, f32[1,4,1024]{2,1,0:T(4,128)S(1)}, u32[]{:S(2)}, u32[]{:S(2)}) collective-permute-start(f32[1,4,1024]{2,1,0:T(4,128)S(1)} %constant_dynamic-slice_fusion), channel_id=1, source_target_pairs={{0,2},{1,3},{2,0},{3,1},{4,6},{5,7},{6,4},{7,5},{8,10},{9,11},{10,... | collective-permute-start | bytes 49160 | tf_op jit(solution)/shard_map/ppermute | solution.py:71
  48.6 1.2 %collective-permute-start.14 = (f32[80,16]{0,1:T(8,128)S(1)}, f32[80,16]{0,1:T(8,128)S(1)}, u32[]{:S(2)}, u32[]{:S(2)}) collective-permute-start(f32[80,16]{0,1:T(8,128)S(1)} %pad_maximum_fusion.4), channel_id=1, source_target_pairs={{0,1},{1,0},{2,3},{3,2},{4,5},{5,4},{6,7},{7,6},{8,9},{9,8},{10,11... | collective-permute-start | bytes 15368 | tf_op jit(solution)/shard_map/ppermute | solution.py:41
  49.9 3.7 %collective-permute-start.15 = (f32[80,16]{0,1:T(8,128)S(1)}, f32[80,16]{0,1:T(8,128)S(1)}, u32[]{:S(2)}, u32[]{:S(2)}) collective-permute-start(f32[80,16]{0,1:T(8,128)S(1)} %fusion.54), channel_id=1, source_target_pairs={{0,2},{1,3},{2,0},{3,1},{4,6},{5,7},{6,4},{7,5},{8,10},{9,11},{10,... | collective-permute-start | bytes 15368 | tf_op jit(solution)/shard_map/ppermute | solution.py:41
  53.6 3.7 %collective-permute-start.16 = (f32[80,16]{0,1:T(8,128)S(1)}, f32[80,16]{0,1:T(8,128)S(1)}, u32[]{:S(2)}, u32[]{:S(2)}) collective-permute-start(f32[80,16]{0,1:T(8,128)S(1)} %add.131), channel_id=1, source_target_pairs={{0,4},{1,5},{2,6},{3,7},{4,0},{5,1},{6,2},{7,3},{8,12},{9,13},{10,... | collective-permute-start | bytes 15368 | tf_op jit(solution)/shard_map/ppermute | solution.py:41
  57.2 3.7 %collective-permute-start.17 = (f32[80,16]{0,1:T(8,128)S(1)}, f32[80,16]{0,1:T(8,128)S(1)}, u32[]{:S(2)}, u32[]{:S(2)}) collective-permute-start(f32[80,16]{0,1:T(8,128)S(1)} %add.132), channel_id=1, source_target_pairs={{0,8},{1,9},{2,10},{3,11},{4,12},{5,13},{6,14},{7,15},{8,0},{9,1},... | collective-permute-start | bytes 15368 | tf_op jit(solution)/shard_map/ppermute | solution.py:41
  60.9 4.5 %collective-permute-start.18 = (f32[80,16]{0,1:T(8,128)S(1)}, f32[80,16]{0,1:T(8,128)S(1)}, u32[]{:S(2)}, u32[]{:S(2)}) collective-permute-start(f32[80,16]{0,1:T(8,128)S(1)} %add.133), channel_id=1, source_target_pairs={{0,16},{1,17},{2,18},{3,19},{4,20},{5,21},{6,22},{7,23},{8,24},{9,... | collective-permute-start | bytes 15368 | tf_op jit(solution)/shard_map/ppermute | solution.py:41
  65.4 4.4 %copy-start.3 = (f32[80,16]{0,1:T(8,128)}, f32[80,16]{0,1:T(8,128)S(1)}, u32[]{:S(2)}) copy-start(f32[80,16]{0,1:T(8,128)S(1)} %add.134) | copy-start | bytes 15364

commit v10 on v9

--- a/solution.py
+++ b/solution.py
@@ -71,6 +71,23 @@
         parts = keep + lax.ppermute(give, axis, route)
         distance *= 2
     return parts.reshape(-1, *block.shape[1:])
+
+
+def paired_halo(block, axes):
+    total = 1
+    for axis in axes:
+        total *= lax.axis_size(axis)
+    me = lax.axis_index(axes[0])
+    for axis in axes[1:]:
+        me = me * lax.axis_size(axis) + lax.axis_index(axis)
+    even_pairs = [(i, i ^ 1) for i in range(total) if (i ^ 1) < total]
+    odd_pairs = [(i, i + 1) for i in range(1, total - 1, 2)] + [(i + 1, i) for i in range(1, total - 1, 2)]
+    first = lax.ppermute(block, axes, even_pairs)
+    second = lax.ppermute(block, axes, odd_pairs)
+    is_even = me % 2 == 0
+    low = jnp.where(is_even, second, first)
+    high = jnp.where(is_even, first, second)
+    return jnp.concatenate([low, block, high], axis=1)
 
 
 def group_reach(grouped, offsets):
@@ -174,7 +191,7 @@
     far_hat = butterfly_scatter(partial_far, "coef")
     far_round = far_hat.astype(jnp.bfloat16).reshape(local_count, vec_count, rank_width)
     far_part = jnp.einsum("cki,cvk->vci", leaf_basis, far_round, preferred_element_type=jnp.float32)
-    extended = extended_2(rounded, ((("leaf", "coef"), 1),), local_count * leaf_size)
+    extended = paired_halo(rounded, ("leaf", "coef"))
     extended = extended.reshape(vec_count, 3 * local_count, leaf_size)
     device_pos = lax.axis_index("leaf") * coef_count + lax.axis_index("coef")
     near_ids = (near_list - (device_pos - 1) * local_count).reshape(-1)

time: 70.4 us -> 71.8 us (1.020)
  waiting for transfers between devices: 19.3 us -> 21.2 us
    ppermute x5, waiting for transfers between devices: 5.59 us -> 8.48 us  [xor_gather(): block = jnp.concatenate([block, lax.ppermute(block, axis, route)], axis=dim)]
    ppermute x5, starting transfers between devices: 8.34 us -> 7.45 us  [xor_gather(): block = jnp.concatenate([block, lax.ppermute(block, axis, route)], axis=dim)]
  transfers between devices with their start and end apart: 14 -> 14, of which waited for: 10 -> 11; matrix products, arithmetic and copies ran while one was open for 19% -> 17% of each run, Pallas kernels for 0% -> 0%
where the time goes in v10:
time: 71.8 us; the launch traced here: 71.3 us
  waiting for transfers between devices  21.2 us (30%)
  starting transfers between devices  20.5 us (29%)
  local copies, waits for them, and re-layouts  10.2 us (14%)
  matrix products  8.84 us (12%)
  other arithmetic  5.95 us (8%)
  Pallas kernels  2.43 us (3%)
  between operations  2.25 us (3%)
    ppermute x5, waiting for transfers between devices, butterfly_sum(): block = block + lax.ppermute(block, axes, route)  10.5 us
    ppermute x5, waiting for transfers between devices, xor_gather(): block = jnp.concatenate([block, lax.ppermute(block, axis, route)], axis=dim)  8.48 us
    ppermute x5, starting transfers between devices, xor_gather(): block = jnp.concatenate([block, lax.ppermute(block, axis, route)], axis=dim)  7.45 us
    ppermute x5, starting transfers between devices, butterfly_sum(): block = block + lax.ppermute(block, axes, route)  6.21 us
    reshape x1, local copies, waits for them, and re-layouts, on_device(): couple = coupling.reshape(3, group_size, slot_count, rank_width, rank_width)  5.63 us
    ppermute x1, starting transfers between devices, paired_halo(): first = lax.ppermute(block, axes, even_pairs)  4.39 us
    dot_general x1, matrix products, on_device(): jnp.einsum('jcfkl,cfvl->jcfvk', couple, sources, preferred_element_type=j...  4.2 us
    pallas_call x1, Pallas kernels, chol_solve(): pl.pallas_call(chol_solve_kernel, out_shape=(jax.ShapeDtypeStruct((size,...  2.43 us
  transfers between devices with their start and end apart: 14, of which 11 were waited for; matrix products, arithmetic and copies ran while one was open for 17% of the time, Pallas kernels for 0%

profile of v10, /device:TPU:0, one launch (start us, length us, event | category | flops | bytes accessed | tf_op | source)
XLA Modules:
  0.0 71.3 jit_solution(7896109540539876843)
XLA Ops:
  2.3 4.4 %collective-permute-start.13 = (bf16[16,512]{1,0:T(8,128)(2,1)S(1)}, bf16[16,512]{1,0:T(8,128)(2,1)S(1)}, u32[]{:S(2)}, u32[]{:S(2)}) collective-permute-start(bf16[16,512]{1,0:T(8,128)(2,1)S(1)} %convert_element_type.24), channel_id=1, source_target_pairs={{0,1},{1,0},{2,3},{3,2},{4,5},{5,4},{6,7},{7,6},{8,9},{9,8},{10,11... | collective-permute-start | bytes 49160 | tf_op jit(solution)/shard_map/ppermute | solution.py:85
  7.8 1.5 %collective-permute-start.5 = (bf16[1,4,1024]{2,1,0:T(4,128)(2,1)S(1)}, bf16[1,4,1024]{2,1,0:T(4,128)(2,1)S(1)}, u32[]{:S(2)}, u32[]{:S(2)}) collective-permute-start(bf16[1,4,1024]{2,1,0:T(4,128)(2,1)S(1)} %reshape.111), channel_id=1, source_target_pairs={{0,4},{4,0},{8,12},{12,8},{16,20},{20,16},{24,28},{28,24},{1,5},{5... | collective-permute-start | bytes 24584 | tf_op jit(solution)/shard_map/ppermute | solution.py:53
  12.6 5.6 %reshape.115 = bf16[3,16,4,64,64]{4,3,2,1,0:T(8,128)(2,1)} reshape(bf16[3,16,4,4096]{3,2,1,0:T(4,128)(2,1)} %param.16) | data formatting | bytes 3145728 | tf_op jit(solution)/shard_map/reshape | solution.py:187
  18.9 1.6 %collective-permute-start.6 = (bf16[2,4,1024]{2,1,0:T(4,128)(2,1)S(1)}, bf16[2,4,1024]{2,1,0:T(4,128)(2,1)S(1)}, u32[]{:S(2)}, u32[]{:S(2)}) collective-permute-start(bf16[2,4,1024]{2,1,0:T(4,128)(2,1)S(1)} %pad_maximum_fusion.3), channel_id=1, source_target_pairs={{0,8},{4,12},{8,0},{12,4},{16,24},{20,28},{24,16},{28,20},{1,9},{5... | collective-permute-start | bytes 49160 | tf_op jit(solution)/shard_map/ppermute | solution.py:53
  20.6 2.1 %collective-permute-done.6 = bf16[2,4,1024]{2,1,0:T(4,128)(2,1)S(1)} collective-permute-done((bf16[2,4,1024]{2,1,0:T(4,128)(2,1)S(1)}, bf16[2,4,1024]{2,1,0:T(4,128)(2,1)S(1)}, u32[]{:S(2)}, u32[]{:S(2)}) %collective-permute-start.6) | collective-permute-done | bytes 16416 | tf_op jit(solution)/shard_map/ppermute | solution.py:53
  22.7 2.7 %collective-permute-start.7 = (bf16[4,4,1024]{2,1,0:T(4,128)(2,1)S(1)}, bf16[4,4,1024]{2,1,0:T(4,128)(2,1)S(1)}, u32[]{:S(2)}, u32[]{:S(2)}) collective-permute-start(bf16[4,4,1024]{2,1,0:T(4,128)(2,1)S(1)} %pad_maximum_fusion.2), channel_id=1, source_target_pairs={{0,16},{4,20},{8,24},{12,28},{16,0},{20,4},{24,8},{28,12},{1,17},{... | collective-permute-start | bytes 98312 | tf_op jit(solution)/shard_map/ppermute | solution.py:53
  25.4 2.2 %collective-permute-done.7 = bf16[4,4,1024]{2,1,0:T(4,128)(2,1)S(1)} collective-permute-done((bf16[4,4,1024]{2,1,0:T(4,128)(2,1)S(1)}, bf16[4,4,1024]{2,1,0:T(4,128)(2,1)S(1)}, u32[]{:S(2)}, u32[]{:S(2)}) %collective-permute-start.7) | collective-permute-done | bytes 32800 | tf_op jit(solution)/shard_map/ppermute | solution.py:53
  27.7 1.2 %collective-permute-done.8 = bf16[8,4,1024]{2,1,0:T(4,128)(2,1)S(1)} collective-permute-done((bf16[8,4,1024]{2,1,0:T(4,128)(2,1)S(1)}, bf16[8,4,1024]{2,1,0:T(4,128)(2,1)S(1)}, u32[]{:S(2)}, u32[]{:S(2)}) %collective-permute-start.8) | collective-permute-done | bytes 65568 | tf_op jit(solution)/shard_map/ppermute | solution.py:53
  29.0 1.6 %collective-permute-start.9 = (bf16[8,8,1024]{2,1,0:T(8,128)(2,1)S(1)}, bf16[8,8,1024]{2,1,0:T(8,128)(2,1)}, u32[]{:S(2)}, u32[]{:S(2)}) collective-permute-start(bf16[8,8,1024]{2,1,0:T(8,128)(2,1)S(1)} %pad_maximum_fusion.1), channel_id=1, source_target_pairs={{0,2},{1,3},{2,0},{3,1},{4,6},{5,7},{6,4},{7,5},{8,10},{9,11},{10,... | collective-permute-start | bytes 393224 | tf_op jit(solution)/shard_map/ppermute | solution.py:53
  30.6 1.2 %gather_fusion.1 = bf16[32,16,128]{2,1,0:T(8,128)(2,1)} fusion(bf16[16,12,128]{2,0,1:T(8,128)(2,1)S(1)} %copy_bitcast_fusion, s32[1024]{0:T(1024)S(1)} %pad_clamp_fusion), kind=kCustom, calls=%fused_computation.1 | custom fusion | bytes 262272 | tf_op jit(solution)/shard_map/gather | solution.py:198
  31.9 2.9 %collective-permute-done.9 = bf16[8,8,1024]{2,1,0:T(8,128)(2,1)} collective-permute-done((bf16[8,8,1024]{2,1,0:T(8,128)(2,1)S(1)}, bf16[8,8,1024]{2,1,0:T(8,128)(2,1)}, u32[]{:S(2)}, u32[]{:S(2)}) %collective-permute-start.9) | collective-permute-done | bytes 131104 | tf_op jit(solution)/shard_map/ppermute | solution.py:53
  34.8 1.0 %pad_maximum_fusion = bf16[8,16,1024]{2,1,0:T(8,128)(2,1)S(1)} fusion(bf16[8,8,1024]{2,1,0:T(8,128)(2,1)} %collective-permute-done.9, bf16[8,4,1024]{2,1,0:T(4,128)(2,1)S(1)} %collective-permute-done.8, bf16[8,4,1024]{2,1,0:T(4,128)(2,1)S(1)} %constant_dynamic-update-slice_fusion), kind=kLoop, calls=%fused_computation.20 | loop fusion | flops 786432 | bytes 524288 | tf_op jit(solution)/shard_map/concatenate | solution.py:53
  36.7 4.2 %fusion.6 = bf16[3,16,4,16,64]{4,3,0,2,1:T(8,128)(2,1)S(1)} fusion(bf16[3,16,4,64,64]{4,3,2,1,0:T(8,128)(2,1)} %reshape.115, bf16[16,4,16,64]{3,2,1,0:T(8,128)(2,1)S(1)} %reshape.114, pred[16,4,64]{2,1,0:T(4,128)(4,1)S(1)} %get-tuple-element.17), kind=kOutput, calls=%fused_computation.9 | convolution fusion | flops 25231360 | bytes 2101248 | tf_op jit(solution)/shard_map/jcfkl,cfvl->jcfvk/dot_general | solution.py:188
  44.8 1.6 %collective-permute-start.11 = (f32[1,4,1024]{2,1,0:T(4,128)S(1)}, f32[1,4,1024]{2,1,0:T(4,128)S(1)}, u32[]{:S(2)}, u32[]{:S(2)}) collective-permute-start(f32[1,4,1024]{2,1,0:T(4,128)S(1)} %constant_dynamic-slice_fusion), channel_id=1, source_target_pairs={{0,2},{1,3},{2,0},{3,1},{4,6},{5,7},{6,4},{7,5},{8,10},{9,11},{10,... | collective-permute-start | bytes 49160 | tf_op jit(solution)/shard_map/ppermute | solution.py:71
  46.6 2.0 %collective-permute-done.11 = f32[1,4,1024]{2,1,0:T(4,128)S(1)} collective-permute-done((f32[1,4,1024]{2,1,0:T(4,128)S(1)}, f32[1,4,1024]{2,1,0:T(4,128)S(1)}, u32[]{:S(2)}, u32[]{:S(2)}) %collective-permute-start.11) | collective-permute-done | bytes 16416 | tf_op jit(solution)/shard_map/ppermute | solution.py:71
  50.1 1.2 %collective-permute-done.14 = f32[80,16]{0,1:T(8,128)S(1)} collective-permute-done((f32[80,16]{0,1:T(8,128)S(1)}, f32[80,16]{0,1:T(8,128)S(1)}, u32[]{:S(2)}, u32[]{:S(2)}) %collective-permute-start.14) | collective-permute-done | bytes 5152 | tf_op jit(solution)/shard_map/ppermute | solution.py:41
  51.4 1.5 %collective-permute-start.15 = (f32[80,16]{0,1:T(8,128)S(1)}, f32[80,16]{0,1:T(8,128)S(1)}, u32[]{:S(2)}, u32[]{:S(2)}) collective-permute-start(f32[80,16]{0,1:T(8,128)S(1)} %fusion.54), channel_id=1, source_target_pairs={{0,2},{1,3},{2,0},{3,1},{4,6},{5,7},{6,4},{7,5},{8,10},{9,11},{10,... | collective-permute-start | bytes 15368 | tf_op jit(solution)/shard_map/ppermute | solution.py:41
  52.9 2.2 %collective-permute-done.15 = f32[80,16]{0,1:T(8,128)S(1)} collective-permute-done((f32[80,16]{0,1:T(8,128)S(1)}, f32[80,16]{0,1:T(8,128)S(1)}, u32[]{:S(2)}, u32[]{:S(2)}) %collective-permute-start.15) | collective-permute-done | bytes 5152 | tf_op jit(solution)/shard_map/ppermute | solution.py:41
  55.5 3.1 %collective-permute-done.16 = f32[80,16]{0,1:T(8,128)S(1)} collective-permute-done((f32[80,16]{0,1:T(8,128)S(1)}, f32[80,16]{0,1:T(8,128)S(1)}, u32[]{:S(2)}, u32[]{:S(2)}) %collective-permute-start.16) | collective-permute-done | bytes 5152 | tf_op jit(solution)/shard_map/ppermute | solution.py:41
  58.7 1.6 %collective-permute-start.17 = (f32[80,16]{0,1:T(8,128)S(1)}, f32[80,16]{0,1:T(8,128)S(1)}, u32[]{:S(2)}, u32[]{:S(2)}) collective-permute-start(f32[80,16]{0,1:T(8,128)S(1)} %add.137), channel_id=1, source_target_pairs={{0,8},{1,9},{2,10},{3,11},{4,12},{5,13},{6,14},{7,15},{8,0},{9,1},... | collective-permute-start | bytes 15368 | tf_op jit(solution)/shard_map/ppermute | solution.py:41
  60.3 2.1 %collective-permute-done.17 = f32[80,16]{0,1:T(8,128)S(1)} collective-permute-done((f32[80,16]{0,1:T(8,128)S(1)}, f32[80,16]{0,1:T(8,128)S(1)}, u32[]{:S(2)}, u32[]{:S(2)}) %collective-permute-start.17) | collective-permute-done | bytes 5152 | tf_op jit(solution)/shard_map/ppermute | solution.py:41
  62.3 2.6 %collective-permute-start.18 = (f32[80,16]{0,1:T(8,128)S(1)}, f32[80,16]{0,1:T(8,128)S(1)}, u32[]{:S(2)}, u32[]{:S(2)}) collective-permute-start(f32[80,16]{0,1:T(8,128)S(1)} %add.138), channel_id=1, source_target_pairs={{0,16},{1,17},{2,18},{3,19},{4,20},{5,21},{6,22},{7,23},{8,24},{9,... | collective-permute-start | bytes 15368 | tf_op jit(solution)/shard_map/ppermute | solution.py:41
  65.0 1.9 %collective-permute-done.18 = f32[80,16]{0,1:T(8,128)S(1)} collective-permute-done((f32[80,16]{0,1:T(8,128)S(1)}, f32[80,16]{0,1:T(8,128)S(1)}, u32[]{:S(2)}, u32[]{:S(2)}) %collective-permute-start.18) | collective-permute-done | bytes 5152 | tf_op jit(solution)/shard_map/ppermute | solution.py:41
  68.9 2.4 %shard_map.112 = (f32[16,16]{1,0:T(8,128)}, f32[16,512]{1,0:T(8,128)}) custom-call(f32[16,16]{1,0:T(8,128)S(1)} %get-tuple-element.20.gram_ref, f32[16,512]{1,0:T(8,128)S(1)} %convolution_subtract_fusion.residue_ref), custom_call_target="tpu_custom_call" | custom-call | flops 540672 | bytes 67584 | tf_op jit(solution)/shard_map/pallas_call | solution.py:134
  (69 shorter events, 14.7 us)
Async XLA Ops:
  0.6 42.9 %copy-start = (bf16[3,4,8,128,128]{4,3,2,1,0:T(8,128)(2,1)S(1)}, bf16[3,4,8,128,128]{4,3,2,1,0:T(8,128)(2,1)}, u32[]{:S(2)}) copy-start(bf16[3,4,8,128,128]{4,3,2,1,0:T(8,128)(2,1)} %param.14) | copy-start | bytes 9437188
  1.6 29.0 %collective-permute-start.12 = (bf16[16,512]{1,0:T(8,128)(2,1)S(1)}, bf16[16,512]{1,0:T(8,128)(2,1)S(1)}, u32[]{:S(2)}, u32[]{:S(2)}) collective-permute-start(bf16[16,512]{1,0:T(8,128)(2,1)S(1)} %convert_element_type.24), channel_id=1, source_target_pairs={{1,2},{3,4},{5,6},{7,8},{9,10},{11,12},{13,14},{15,16},{17,18},{19... | collective-permute-start | bytes 49160 | tf_op jit(solution)/shard_map/ppermute | solution.py:86
  2.3 28.3 %collective-permute-start.13 = (bf16[16,512]{1,0:T(8,128)(2,1)S(1)}, bf16[16,512]{1,0:T(8,128)(2,1)S(1)}, u32[]{:S(2)}, u32[]{:S(2)}) collective-permute-start(bf16[16,512]{1,0:T(8,128)(2,1)S(1)} %convert_element_type.24), channel_id=1, source_target_pairs={{0,1},{1,0},{2,3},{3,2},{4,5},{5,4},{6,7},{7,6},{8,9},{9,8},{10,11... | collective-permute-start | bytes 49160 | tf_op jit(solution)/shard_map/ppermute | solution.py:85
  7.8 11.0 %collective-permute-start.5 = (bf16[1,4,1024]{2,1,0:T(4,128)(2,1)S(1)}, bf16[1,4,1024]{2,1,0:T(4,128)(2,1)S(1)}, u32[]{:S(2)}, u32[]{:S(2)}) collective-permute-start(bf16[1,4,1024]{2,1,0:T(4,128)(2,1)S(1)} %reshape.111), channel_id=1, source_target_pairs={{0,4},{4,0},{8,12},{12,8},{16,20},{20,16},{24,28},{28,24},{1,5},{5... | collective-permute-start | bytes 24584 | tf_op jit(solution)/shard_map/ppermute | solution.py:53
  18.9 3.8 %collective-permute-start.6 = (bf16[2,4,1024]{2,1,0:T(4,128)(2,1)S(1)}, bf16[2,4,1024]{2,1,0:T(4,128)(2,1)S(1)}, u32[]{:S(2)}, u32[]{:S(2)}) collective-permute-start(bf16[2,4,1024]{2,1,0:T(4,128)(2,1)S(1)} %pad_maximum_fusion.3), channel_id=1, source_target_pairs={{0,8},{4,12},{8,0},{12,4},{16,24},{20,28},{24,16},{28,20},{1,9},{5... | collective-permute-start | bytes 49160 | tf_op jit(solution)/shard_map/ppermute | solution.py:53
  22.7 4.9 %collective-permute-start.7 = (bf16[4,4,1024]{2,1,0:T(4,128)(2,1)S(1)}, bf16[4,4,1024]{2,1,0:T(4,128)(2,1)S(1)}, u32[]{:S(2)}, u32[]{:S(2)}) collective-permute-start(bf16[4,4,1024]{2,1,0:T(4,128)(2,1)S(1)} %pad_maximum_fusion.2), channel_id=1, source_target_pairs={{0,16},{4,20},{8,24},{12,28},{16,0},{20,4},{24,8},{28,12},{1,17},{... | collective-permute-start | bytes 98312 | tf_op jit(solution)/shard_map/ppermute | solution.py:53
  27.7 1.3 %collective-permute-start.8 = (bf16[8,4,1024]{2,1,0:T(4,128)(2,1)S(1)}, bf16[8,4,1024]{2,1,0:T(4,128)(2,1)S(1)}, u32[]{:S(2)}, u32[]{:S(2)}) collective-permute-start(bf16[8,4,1024]{2,1,0:T(4,128)(2,1)S(1)} %constant_dynamic-update-slice_fusion), channel_id=1, source_target_pairs={{0,1},{1,0},{2,3},{3,2},{4,5},{5,4},{6,7},{7,6},{8,9},{9,8},{10,11... | collective-permute-start | bytes 196616 | tf_op jit(solution)/shard_map/ppermute | solution.py:53
  29.0 5.7 %collective-permute-start.9 = (bf16[8,8,1024]{2,1,0:T(8,128)(2,1)S(1)}, bf16[8,8,1024]{2,1,0:T(8,128)(2,1)}, u32[]{:S(2)}, u32[]{:S(2)}) collective-permute-start(bf16[8,8,1024]{2,1,0:T(8,128)(2,1)S(1)} %pad_maximum_fusion.1), channel_id=1, source_target_pairs={{0,2},{1,3},{2,0},{3,1},{4,6},{5,7},{6,4},{7,5},{8,10},{9,11},{10,... | collective-permute-start | bytes 393224 | tf_op jit(solution)/shard_map/ppermute | solution.py:53
  36.7 5.0 %copy-start.4 = (f32[16,4,64]{2,1,0:T(4,128)S(1)}, f32[16,4,64]{2,1,0:T(4,128)}, u32[]{:S(2)}) copy-start(f32[16,4,64]{2,1,0:T(4,128)} %get-tuple-element.16) | copy-start | bytes 49156
  36.7 6.9 %copy-start.1 = (bf16[32,16,128]{2,1,0:T(8,128)(2,1)S(1)}, bf16[32,16,128]{2,1,0:T(8,128)(2,1)}, u32[]{:S(2)}) copy-start(bf16[32,16,128]{2,1,0:T(8,128)(2,1)} %gather_fusion.1) | copy-start | bytes 393220
  40.9 8.9 %copy-start.2 = (f32[64,512]{1,0:T(8,128)S(1)}, f32[64,512]{1,0:T(8,128)}, u32[]{:S(2)}) copy-start(f32[64,512]{1,0:T(8,128)} %param.19) | copy-start | bytes 393220
  43.5 1.3 %collective-permute-start.10 = (f32[2,4,1024]{2,1,0:T(4,128)S(1)}, f32[2,4,1024]{2,1,0:T(4,128)S(1)}, u32[]{:S(2)}, u32[]{:S(2)}) collective-permute-start(f32[2,4,1024]{2,1,0:T(4,128)S(1)} %dynamic-slice_bitcast_fusion), channel_id=1, source_target_pairs={{0,1},{1,0},{2,3},{3,2},{4,5},{5,4},{6,7},{7,6},{8,9},{9,8},{10,11... | collective-permute-start | bytes 98312 | tf_op jit(solution)/shard_map/ppermute | solution.py:71
  44.8 3.8 %collective-permute-start.11 = (f32[1,4,1024]{2,1,0:T(4,128)S(1)}, f32[1,4,1024]{2,1,0:T(4,128)S(1)}, u32[]{:S(2)}, u32[]{:S(2)}) collective-permute-start(f32[1,4,1024]{2,1,0:T(4,128)S(1)} %constant_dynamic-slice_fusion), channel_id=1, source_target_pairs={{0,2},{1,3},{2,0},{3,1},{4,6},{5,7},{6,4},{7,5},{8,10},{9,11},{10,... | collective-permute-start | bytes 49160 | tf_op jit(solution)/shard_map/ppermute | solution.py:71
  50.1 1.2 %collective-permute-start.14 = (f32[80,16]{0,1:T(8,128)S(1)}, f32[80,16]{0,1:T(8,128)S(1)}, u32[]{:S(2)}, u32[]{:S(2)}) collective-permute-start(f32[80,16]{0,1:T(8,128)S(1)} %pad_maximum_fusion.4), channel_id=1, source_target_pairs={{0,1},{1,0},{2,3},{3,2},{4,5},{5,4},{6,7},{7,6},{8,9},{9,8},{10,11... | collective-permute-start | bytes 15368 | tf_op jit(solution)/shard_map/ppermute | solution.py:41
  51.4 3.7 %collective-permute-start.15 = (f32[80,16]{0,1:T(8,128)S(1)}, f32[80,16]{0,1:T(8,128)S(1)}, u32[]{:S(2)}, u32[]{:S(2)}) collective-permute-start(f32[80,16]{0,1:T(8,128)S(1)} %fusion.54), channel_id=1, source_target_pairs={{0,2},{1,3},{2,0},{3,1},{4,6},{5,7},{6,4},{7,5},{8,10},{9,11},{10,... | collective-permute-start | bytes 15368 | tf_op jit(solution)/shard_map/ppermute | solution.py:41
  55.0 3.7 %collective-permute-start.16 = (f32[80,16]{0,1:T(8,128)S(1)}, f32[80,16]{0,1:T(8,128)S(1)}, u32[]{:S(2)}, u32[]{:S(2)}) collective-permute-start(f32[80,16]{0,1:T(8,128)S(1)} %add.136), channel_id=1, source_target_pairs={{0,4},{1,5},{2,6},{3,7},{4,0},{5,1},{6,2},{7,3},{8,12},{9,13},{10,... | collective-permute-start | bytes 15368 | tf_op jit(solution)/shard_map/ppermute | solution.py:41
  58.7 3.7 %collective-permute-start.17 = (f32[80,16]{0,1:T(8,128)S(1)}, f32[80,16]{0,1:T(8,128)S(1)}, u32[]{:S(2)}, u32[]{:S(2)}) collective-permute-start(f32[80,16]{0,1:T(8,128)S(1)} %add.137), channel_id=1, source_target_pairs={{0,8},{1,9},{2,10},{3,11},{4,12},{5,13},{6,14},{7,15},{8,0},{9,1},... | collective-permute-start | bytes 15368 | tf_op jit(solution)/shard_map/ppermute | solution.py:41
  62.3 4.5 %collective-permute-start.18 = (f32[80,16]{0,1:T(8,128)S(1)}, f32[80,16]{0,1:T(8,128)S(1)}, u32[]{:S(2)}, u32[]{:S(2)}) collective-permute-start(f32[80,16]{0,1:T(8,128)S(1)} %add.138), channel_id=1, source_target_pairs={{0,16},{1,17},{2,18},{3,19},{4,20},{5,21},{6,22},{7,23},{8,24},{9,... | collective-permute-start | bytes 15368 | tf_op jit(solution)/shard_map/ppermute | solution.py:41
  66.9 4.4 %copy-start.3 = (f32[80,16]{0,1:T(8,128)}, f32[80,16]{0,1:T(8,128)S(1)}, u32[]{:S(2)}) copy-start(f32[80,16]{0,1:T(8,128)S(1)} %add.139) | copy-start | bytes 15364

commit v11 on v9

--- a/solution.py
+++ b/solution.py
@@ -60,17 +60,17 @@
     if not is_power_of_two(count):
         return lax.psum_scatter(block, axis, scatter_dimension=0, tiled=True)
     me = lax.axis_index(axis)
-    parts = block.reshape(count, -1, *block.shape[1:])
-    distance = 1
-    while distance < count:
+    parts = block
+    distance = count // 2
+    while distance >= 1:
+        halves = parts.reshape(2, parts.shape[0] // 2, *parts.shape[1:])
         bit = (me // distance) % 2
-        pairs = parts.reshape(parts.shape[0] // 2, 2, *parts.shape[1:])
-        keep = lax.dynamic_index_in_dim(pairs, bit, axis=1, keepdims=False)
-        give = lax.dynamic_index_in_dim(pairs, 1 - bit, axis=1, keepdims=False)
+        keep = lax.dynamic_index_in_dim(halves, bit, axis=0, keepdims=False)
+        give = lax.dynamic_index_in_dim(halves, 1 - bit, axis=0, keepdims=False)
         route = [(i, i ^ distance) for i in range(count)]
         parts = keep + lax.ppermute(give, axis, route)
-        distance *= 2
-    return parts.reshape(-1, *block.shape[1:])
+        distance //= 2
+    return parts
 
 
 def group_reach(grouped, offsets):

time: 70.4 us -> 70.6 us (level)
  waiting for transfers between devices: 19.3 us -> 17.7 us
  matrix products: 8.84 us -> 10.3 us
    ppermute x2, waiting for transfers between devices: 2.85 us -> 1.58 us  [butterfly_scatter(): parts = keep + lax.ppermute(give, axis, route)]
    dot_general x1, matrix products: 0.23 us -> 1.03 us  [on_device(): near_part = jnp.tensordot(powers, near_terms, 1)]
  transfers between devices with their start and end apart: 14 -> 14, of which waited for: 10 -> 10; matrix products, arithmetic and copies ran while one was open for 19% -> 21% of each run, Pallas kernels for 0% -> 0%
where the time goes in v11:
time: 70.6 us; the launch traced here: 70 us
  starting transfers between devices  20.6 us (29%)
  waiting for transfers between devices  17.7 us (25%)
  matrix products  10.3 us (15%)
  local copies, waits for them, and re-layouts  10.2 us (14%)
  other arithmetic  6.64 us (9%)
  Pallas kernels  2.43 us (3%)
  between operations  2.18 us (3%)
    ppermute x5, waiting for transfers between devices, butterfly_sum(): block = block + lax.ppermute(block, axes, route)  10.5 us
    ppermute x5, starting transfers between devices, xor_gather(): block = jnp.concatenate([block, lax.ppermute(block, axis, route)], axis=dim)  8.34 us
    ppermute x5, starting transfers between devices, butterfly_sum(): block = block + lax.ppermute(block, axes, route)  6.19 us
    reshape x1, local copies, waits for them, and re-layouts, on_device(): couple = coupling.reshape(3, group_size, slot_count, rank_width, rank_width)  5.63 us
    ppermute x5, waiting for transfers between devices, xor_gather(): block = jnp.concatenate([block, lax.ppermute(block, axis, route)], axis=dim)  5.59 us
    dot_general x1, matrix products, on_device(): jnp.einsum('jcfkl,cfvl->jcfvk', couple, sources, preferred_element_type=j...  4.2 us
    ppermute x1, starting transfers between devices, extended_2(): lax.ppermute(lax.slice_in_dim(block, block.shape[dim] - width, None, axis...  3.63 us
    pallas_call x1, Pallas kernels, chol_solve(): pl.pallas_call(chol_solve_kernel, out_shape=(jax.ShapeDtypeStruct((size,...  2.43 us
  transfers between devices with their start and end apart: 14, of which 10 were waited for; matrix products, arithmetic and copies ran while one was open for 21% of the time, Pallas kernels for 0%

profile of v11, /device:TPU:0, one launch (start us, length us, event | category | flops | bytes accessed | tf_op | source)
XLA Modules:
  0.0 70.0 jit_solution(16062818244939410891)
XLA Ops:
  1.6 1.4 %collective-permute-start.13 = (bf16[16,512]{1,0:T(8,128)(2,1)S(1)}, bf16[16,512]{1,0:T(8,128)(2,1)S(1)}, u32[]{:S(2)}, u32[]{:S(2)}) collective-permute-start(bf16[16,512]{1,0:T(8,128)(2,1)S(1)} %convert_element_type.20), channel_id=1, source_target_pairs={{1,0},{2,1},{3,2},{4,3},{5,4},{6,5},{7,6},{8,7},{9,8},{10,9},{11,1... | collective-permute-start | bytes 49160 | tf_op jit(solution)/shard_map/ppermute | solution.py:23
  3.0 3.6 %collective-permute-start.12 = (bf16[16,512]{1,0:T(8,128)(2,1)S(1)}, bf16[16,512]{1,0:T(8,128)(2,1)}, u32[]{:S(2)}, u32[]{:S(2)}) collective-permute-start(bf16[16,512]{1,0:T(8,128)(2,1)S(1)} %convert_element_type.20), channel_id=1, source_target_pairs={{0,1},{1,2},{2,3},{3,4},{4,5},{5,6},{6,7},{7,8},{8,9},{9,10},{10,1... | collective-permute-start | bytes 49160 | tf_op jit(solution)/shard_map/ppermute | solution.py:20
  7.7 2.8 %collective-permute-start.5 = (bf16[1,4,1024]{2,1,0:T(4,128)(2,1)S(1)}, bf16[1,4,1024]{2,1,0:T(4,128)(2,1)S(1)}, u32[]{:S(2)}, u32[]{:S(2)}) collective-permute-start(bf16[1,4,1024]{2,1,0:T(4,128)(2,1)S(1)} %reshape.108), channel_id=1, source_target_pairs={{0,4},{4,0},{8,12},{12,8},{16,20},{20,16},{24,28},{28,24},{1,5},{5... | collective-permute-start | bytes 24584 | tf_op jit(solution)/shard_map/ppermute | solution.py:53
  13.7 1.6 %collective-permute-start.6 = (bf16[2,4,1024]{2,1,0:T(4,128)(2,1)S(1)}, bf16[2,4,1024]{2,1,0:T(4,128)(2,1)S(1)}, u32[]{:S(2)}, u32[]{:S(2)}) collective-permute-start(bf16[2,4,1024]{2,1,0:T(4,128)(2,1)S(1)} %pad_maximum_fusion.3), channel_id=1, source_target_pairs={{0,8},{4,12},{8,0},{12,4},{16,24},{20,28},{24,16},{28,20},{1,9},{5... | collective-permute-start | bytes 49160 | tf_op jit(solution)/shard_map/ppermute | solution.py:53
  15.3 2.1 %collective-permute-done.6 = bf16[2,4,1024]{2,1,0:T(4,128)(2,1)S(1)} collective-permute-done((bf16[2,4,1024]{2,1,0:T(4,128)(2,1)S(1)}, bf16[2,4,1024]{2,1,0:T(4,128)(2,1)S(1)}, u32[]{:S(2)}, u32[]{:S(2)}) %collective-permute-start.6) | collective-permute-done | bytes 16416 | tf_op jit(solution)/shard_map/ppermute | solution.py:53
  17.5 2.7 %collective-permute-start.7 = (bf16[4,4,1024]{2,1,0:T(4,128)(2,1)S(1)}, bf16[4,4,1024]{2,1,0:T(4,128)(2,1)S(1)}, u32[]{:S(2)}, u32[]{:S(2)}) collective-permute-start(bf16[4,4,1024]{2,1,0:T(4,128)(2,1)S(1)} %pad_maximum_fusion.2), channel_id=1, source_target_pairs={{0,16},{4,20},{8,24},{12,28},{16,0},{20,4},{24,8},{28,12},{1,17},{... | collective-permute-start | bytes 98312 | tf_op jit(solution)/shard_map/ppermute | solution.py:53
  20.2 2.2 %collective-permute-done.7 = bf16[4,4,1024]{2,1,0:T(4,128)(2,1)S(1)} collective-permute-done((bf16[4,4,1024]{2,1,0:T(4,128)(2,1)S(1)}, bf16[4,4,1024]{2,1,0:T(4,128)(2,1)S(1)}, u32[]{:S(2)}, u32[]{:S(2)}) %collective-permute-start.7) | collective-permute-done | bytes 32800 | tf_op jit(solution)/shard_map/ppermute | solution.py:53
  22.5 1.2 %collective-permute-done.8 = bf16[8,4,1024]{2,1,0:T(4,128)(2,1)S(1)} collective-permute-done((bf16[8,4,1024]{2,1,0:T(4,128)(2,1)S(1)}, bf16[8,4,1024]{2,1,0:T(4,128)(2,1)S(1)}, u32[]{:S(2)}, u32[]{:S(2)}) %collective-permute-start.8) | collective-permute-done | bytes 65568 | tf_op jit(solution)/shard_map/ppermute | solution.py:53
  23.8 1.2 %collective-permute-start.9 = (bf16[8,8,1024]{2,1,0:T(8,128)(2,1)S(1)}, bf16[8,8,1024]{2,1,0:T(8,128)(2,1)}, u32[]{:S(2)}, u32[]{:S(2)}) collective-permute-start(bf16[8,8,1024]{2,1,0:T(8,128)(2,1)S(1)} %pad_maximum_fusion.1), channel_id=1, source_target_pairs={{0,2},{1,3},{2,0},{3,1},{4,6},{5,7},{6,4},{7,5},{8,10},{9,11},{10,... | collective-permute-start | bytes 393224 | tf_op jit(solution)/shard_map/ppermute | solution.py:53
  25.0 5.6 %reshape.112 = bf16[3,16,4,64,64]{4,3,2,1,0:T(8,128)(2,1)} reshape(bf16[3,16,4,4096]{3,2,1,0:T(4,128)(2,1)} %param.16) | data formatting | bytes 3145728 | tf_op jit(solution)/shard_map/reshape | solution.py:170
  32.1 1.2 %gather_fusion.1 = bf16[32,16,128]{2,1,0:T(8,128)(2,1)} fusion(bf16[16,12,128]{2,0,1:T(8,128)(2,1)S(1)} %copy_bitcast_fusion, s32[1024]{0:T(1024)S(1)} %pad_clamp_fusion), kind=kCustom, calls=%fused_computation.1 | custom fusion | bytes 262272 | tf_op jit(solution)/shard_map/gather | solution.py:181
  33.3 1.0 %pad_maximum_fusion = bf16[8,16,1024]{2,1,0:T(8,128)(2,1)S(1)} fusion(bf16[8,8,1024]{2,1,0:T(8,128)(2,1)} %collective-permute-done.9, bf16[8,4,1024]{2,1,0:T(4,128)(2,1)S(1)} %collective-permute-done.8, bf16[8,4,1024]{2,1,0:T(4,128)(2,1)S(1)} %constant_dynamic-update-slice_fusion), kind=kLoop, calls=%fused_computation.20 | loop fusion | flops 786432 | bytes 524288 | tf_op jit(solution)/shard_map/concatenate | solution.py:53
  35.2 4.2 %fusion.6 = bf16[3,16,4,16,64]{4,3,0,2,1:T(8,128)(2,1)S(1)} fusion(bf16[3,16,4,64,64]{4,3,2,1,0:T(8,128)(2,1)} %reshape.112, bf16[16,4,16,64]{3,2,1,0:T(8,128)(2,1)S(1)} %reshape.111, pred[16,4,64]{2,1,0:T(4,128)(4,1)S(1)} %get-tuple-element.15), kind=kOutput, calls=%fused_computation.9 | convolution fusion | flops 25231360 | bytes 2101248 | tf_op jit(solution)/shard_map/jcfkl,cfvl->jcfvk/dot_general | solution.py:171
  41.0 1.0 %reshape_reshape.3 = f32[2,8,1024]{2,1,0:T(8,128)S(1)} reshape(f32[16,16,64]{2,1,0:T(8,128)} %multiply_reduce_fusion) | data formatting | bytes 131072 | tf_op jit(solution)/shard_map/reshape;reshape | solution.py:66
  42.9 1.6 %fusion.9 = bf16[3,16,4,128]{3,1,0,2:T(8,128)(2,1)} fusion(bf16[16,4,8,128,1]{3,0,2,4,1:T(8,128)(2,1)S(1)} %bitcast.93, bf16[3,4,8,128,128]{4,3,2,1,0:T(8,128)(2,1)S(1)} %copy-done), kind=kOutput, calls=%fused_computation.10 | convolution fusion | flops 50331648 | bytes 3325952 | tf_op jit(solution)/shard_map/jcnil,vcnl->jvci/dot_general | solution.py:184
  44.5 1.4 %collective-permute-done.10 = f32[8,1024]{1,0:T(8,128)S(1)} collective-permute-done((f32[8,1024]{1,0:T(8,128)S(1)}, f32[8,1024]{1,0:T(8,128)S(1)}, u32[]{:S(2)}, u32[]{:S(2)}) %collective-permute-start.10) | collective-permute-done | bytes 32800 | tf_op jit(solution)/shard_map/ppermute | solution.py:71
  46.1 1.0 %fusion.17 = f32[1,16,4,128]{3,0,2,1:T(1,128)S(1)} fusion(bf16[3,16,4,128]{3,1,0,2:T(8,128)(2,1)} %fusion.9, bf16[1]{0:T(256)(128)(2,1)S(6)} %mul.29, f32[1]{0:T(128)S(6)} %copy.76, bf16[1]{0:T(256)(128)(2,1)} %constant.214), kind=kOutput, calls=%fused_computation.25 | convolution fusion | flops 49170 | bytes 81928 | tf_op jit(solution)/shard_map/dot_general | solution.py:187
  51.0 2.7 %collective-permute-done.15 = f32[80,16]{0,1:T(8,128)S(1)} collective-permute-done((f32[80,16]{0,1:T(8,128)S(1)}, f32[80,16]{0,1:T(8,128)S(1)}, u32[]{:S(2)}, u32[]{:S(2)}) %collective-permute-start.15) | collective-permute-done | bytes 5152 | tf_op jit(solution)/shard_map/ppermute | solution.py:41
  54.3 3.1 %collective-permute-done.16 = f32[80,16]{0,1:T(8,128)S(1)} collective-permute-done((f32[80,16]{0,1:T(8,128)S(1)}, f32[80,16]{0,1:T(8,128)S(1)}, u32[]{:S(2)}, u32[]{:S(2)}) %collective-permute-start.16) | collective-permute-done | bytes 5152 | tf_op jit(solution)/shard_map/ppermute | solution.py:41
  57.4 1.6 %collective-permute-start.17 = (f32[80,16]{0,1:T(8,128)S(1)}, f32[80,16]{0,1:T(8,128)S(1)}, u32[]{:S(2)}, u32[]{:S(2)}) collective-permute-start(f32[80,16]{0,1:T(8,128)S(1)} %add.132), channel_id=1, source_target_pairs={{0,8},{1,9},{2,10},{3,11},{4,12},{5,13},{6,14},{7,15},{8,0},{9,1},... | collective-permute-start | bytes 15368 | tf_op jit(solution)/shard_map/ppermute | solution.py:41
  59.0 2.1 %collective-permute-done.17 = f32[80,16]{0,1:T(8,128)S(1)} collective-permute-done((f32[80,16]{0,1:T(8,128)S(1)}, f32[80,16]{0,1:T(8,128)S(1)}, u32[]{:S(2)}, u32[]{:S(2)}) %collective-permute-start.17) | collective-permute-done | bytes 5152 | tf_op jit(solution)/shard_map/ppermute | solution.py:41
  61.0 2.7 %collective-permute-start.18 = (f32[80,16]{0,1:T(8,128)S(1)}, f32[80,16]{0,1:T(8,128)S(1)}, u32[]{:S(2)}, u32[]{:S(2)}) collective-permute-start(f32[80,16]{0,1:T(8,128)S(1)} %add.133), channel_id=1, source_target_pairs={{0,16},{1,17},{2,18},{3,19},{4,20},{5,21},{6,22},{7,23},{8,24},{9,... | collective-permute-start | bytes 15368 | tf_op jit(solution)/shard_map/ppermute | solution.py:41
  63.8 1.8 %collective-permute-done.18 = f32[80,16]{0,1:T(8,128)S(1)} collective-permute-done((f32[80,16]{0,1:T(8,128)S(1)}, f32[80,16]{0,1:T(8,128)S(1)}, u32[]{:S(2)}, u32[]{:S(2)}) %collective-permute-start.18) | collective-permute-done | bytes 5152 | tf_op jit(solution)/shard_map/ppermute | solution.py:41
  67.6 2.4 %shard_map.112 = (f32[16,16]{1,0:T(8,128)}, f32[16,512]{1,0:T(8,128)}) custom-call(f32[16,16]{1,0:T(8,128)S(1)} %get-tuple-element.18.gram_ref, f32[16,512]{1,0:T(8,128)S(1)} %convolution_subtract_fusion.residue_ref), custom_call_target="tpu_custom_call" | custom-call | flops 540672 | bytes 67584 | tf_op jit(solution)/shard_map/pallas_call | solution.py:117
  (69 shorter events, 15.5 us)
Async XLA Ops:
  0.6 42.3 %copy-start = (bf16[3,4,8,128,128]{4,3,2,1,0:T(8,128)(2,1)S(1)}, bf16[3,4,8,128,128]{4,3,2,1,0:T(8,128)(2,1)}, u32[]{:S(2)}) copy-start(bf16[3,4,8,128,128]{4,3,2,1,0:T(8,128)(2,1)} %param.14) | copy-start | bytes 9437188
  1.6 29.7 %collective-permute-start.13 = (bf16[16,512]{1,0:T(8,128)(2,1)S(1)}, bf16[16,512]{1,0:T(8,128)(2,1)S(1)}, u32[]{:S(2)}, u32[]{:S(2)}) collective-permute-start(bf16[16,512]{1,0:T(8,128)(2,1)S(1)} %convert_element_type.20), channel_id=1, source_target_pairs={{1,0},{2,1},{3,2},{4,3},{5,4},{6,5},{7,6},{8,7},{9,8},{10,9},{11,1... | collective-permute-start | bytes 49160 | tf_op jit(solution)/shard_map/ppermute | solution.py:23
  3.0 28.3 %collective-permute-start.12 = (bf16[16,512]{1,0:T(8,128)(2,1)S(1)}, bf16[16,512]{1,0:T(8,128)(2,1)}, u32[]{:S(2)}, u32[]{:S(2)}) collective-permute-start(bf16[16,512]{1,0:T(8,128)(2,1)S(1)} %convert_element_type.20), channel_id=1, source_target_pairs={{0,1},{1,2},{2,3},{3,4},{4,5},{5,6},{6,7},{7,8},{8,9},{9,10},{10,1... | collective-permute-start | bytes 49160 | tf_op jit(solution)/shard_map/ppermute | solution.py:20
  7.7 5.9 %collective-permute-start.5 = (bf16[1,4,1024]{2,1,0:T(4,128)(2,1)S(1)}, bf16[1,4,1024]{2,1,0:T(4,128)(2,1)S(1)}, u32[]{:S(2)}, u32[]{:S(2)}) collective-permute-start(bf16[1,4,1024]{2,1,0:T(4,128)(2,1)S(1)} %reshape.108), channel_id=1, source_target_pairs={{0,4},{4,0},{8,12},{12,8},{16,20},{20,16},{24,28},{28,24},{1,5},{5... | collective-permute-start | bytes 24584 | tf_op jit(solution)/shard_map/ppermute | solution.py:53
  13.7 3.8 %collective-permute-start.6 = (bf16[2,4,1024]{2,1,0:T(4,128)(2,1)S(1)}, bf16[2,4,1024]{2,1,0:T(4,128)(2,1)S(1)}, u32[]{:S(2)}, u32[]{:S(2)}) collective-permute-start(bf16[2,4,1024]{2,1,0:T(4,128)(2,1)S(1)} %pad_maximum_fusion.3), channel_id=1, source_target_pairs={{0,8},{4,12},{8,0},{12,4},{16,24},{20,28},{24,16},{28,20},{1,9},{5... | collective-permute-start | bytes 49160 | tf_op jit(solution)/shard_map/ppermute | solution.py:53
  17.5 4.9 %collective-permute-start.7 = (bf16[4,4,1024]{2,1,0:T(4,128)(2,1)S(1)}, bf16[4,4,1024]{2,1,0:T(4,128)(2,1)S(1)}, u32[]{:S(2)}, u32[]{:S(2)}) collective-permute-start(bf16[4,4,1024]{2,1,0:T(4,128)(2,1)S(1)} %pad_maximum_fusion.2), channel_id=1, source_target_pairs={{0,16},{4,20},{8,24},{12,28},{16,0},{20,4},{24,8},{28,12},{1,17},{... | collective-permute-start | bytes 98312 | tf_op jit(solution)/shard_map/ppermute | solution.py:53
  22.4 1.3 %collective-permute-start.8 = (bf16[8,4,1024]{2,1,0:T(4,128)(2,1)S(1)}, bf16[8,4,1024]{2,1,0:T(4,128)(2,1)S(1)}, u32[]{:S(2)}, u32[]{:S(2)}) collective-permute-start(bf16[8,4,1024]{2,1,0:T(4,128)(2,1)S(1)} %constant_dynamic-update-slice_fusion), channel_id=1, source_target_pairs={{0,1},{1,0},{2,3},{3,2},{4,5},{5,4},{6,7},{7,6},{8,9},{9,8},{10,11... | collective-permute-start | bytes 196616 | tf_op jit(solution)/shard_map/ppermute | solution.py:53
  23.8 9.5 %collective-permute-start.9 = (bf16[8,8,1024]{2,1,0:T(8,128)(2,1)S(1)}, bf16[8,8,1024]{2,1,0:T(8,128)(2,1)}, u32[]{:S(2)}, u32[]{:S(2)}) collective-permute-start(bf16[8,8,1024]{2,1,0:T(8,128)(2,1)S(1)} %pad_maximum_fusion.1), channel_id=1, source_target_pairs={{0,2},{1,3},{2,0},{3,1},{4,6},{5,7},{6,4},{7,5},{8,10},{9,11},{10,... | collective-permute-start | bytes 393224 | tf_op jit(solution)/shard_map/ppermute | solution.py:53
  35.2 5.0 %copy-start.4 = (f32[16,4,64]{2,1,0:T(4,128)S(1)}, f32[16,4,64]{2,1,0:T(4,128)}, u32[]{:S(2)}) copy-start(f32[16,4,64]{2,1,0:T(4,128)} %get-tuple-element.14) | copy-start | bytes 49156
  35.2 7.7 %copy-start.1 = (bf16[32,16,128]{2,1,0:T(8,128)(2,1)S(1)}, bf16[32,16,128]{2,1,0:T(8,128)(2,1)}, u32[]{:S(2)}) copy-start(bf16[32,16,128]{2,1,0:T(8,128)(2,1)} %gather_fusion.1) | copy-start | bytes 393220
  39.4 9.0 %copy-start.2 = (f32[64,512]{1,0:T(8,128)S(1)}, f32[64,512]{1,0:T(8,128)}, u32[]{:S(2)}) copy-start(f32[64,512]{1,0:T(8,128)} %param.19) | copy-start | bytes 393220
  42.0 4.0 %collective-permute-start.10 = (f32[8,1024]{1,0:T(8,128)S(1)}, f32[8,1024]{1,0:T(8,128)S(1)}, u32[]{:S(2)}, u32[]{:S(2)}) collective-permute-start(f32[8,1024]{1,0:T(8,128)S(1)} %dynamic-slice_bitcast_fusion), channel_id=1, source_target_pairs={{0,2},{1,3},{2,0},{3,1},{4,6},{5,7},{6,4},{7,5},{8,10},{9,11},{10,... | collective-permute-start | bytes 98312 | tf_op jit(solution)/shard_map/ppermute | solution.py:71
  46.0 1.2 %collective-permute-start.11 = (f32[4,1024]{1,0:T(4,128)S(1)}, f32[4,1024]{1,0:T(4,128)S(1)}, u32[]{:S(2)}, u32[]{:S(2)}) collective-permute-start(f32[4,1024]{1,0:T(4,128)S(1)} %dynamic-slice_bitcast_fusion.1), channel_id=1, source_target_pairs={{0,1},{1,0},{2,3},{3,2},{4,5},{5,4},{6,7},{7,6},{8,9},{9,8},{10,11... | collective-permute-start | bytes 49160 | tf_op jit(solution)/shard_map/ppermute | solution.py:71
  48.8 1.2 %collective-permute-start.14 = (f32[80,16]{0,1:T(8,128)S(1)}, f32[80,16]{0,1:T(8,128)S(1)}, u32[]{:S(2)}, u32[]{:S(2)}) collective-permute-start(f32[80,16]{0,1:T(8,128)S(1)} %pad_maximum_fusion.4), channel_id=1, source_target_pairs={{0,1},{1,0},{2,3},{3,2},{4,5},{5,4},{6,7},{7,6},{8,9},{9,8},{10,11... | collective-permute-start | bytes 15368 | tf_op jit(solution)/shard_map/ppermute | solution.py:41
  50.1 3.7 %collective-permute-start.15 = (f32[80,16]{0,1:T(8,128)S(1)}, f32[80,16]{0,1:T(8,128)S(1)}, u32[]{:S(2)}, u32[]{:S(2)}) collective-permute-start(f32[80,16]{0,1:T(8,128)S(1)} %fusion.55), channel_id=1, source_target_pairs={{0,2},{1,3},{2,0},{3,1},{4,6},{5,7},{6,4},{7,5},{8,10},{9,11},{10,... | collective-permute-start | bytes 15368 | tf_op jit(solution)/shard_map/ppermute | solution.py:41
  53.7 3.7 %collective-permute-start.16 = (f32[80,16]{0,1:T(8,128)S(1)}, f32[80,16]{0,1:T(8,128)S(1)}, u32[]{:S(2)}, u32[]{:S(2)}) collective-permute-start(f32[80,16]{0,1:T(8,128)S(1)} %add.131), channel_id=1, source_target_pairs={{0,4},{1,5},{2,6},{3,7},{4,0},{5,1},{6,2},{7,3},{8,12},{9,13},{10,... | collective-permute-start | bytes 15368 | tf_op jit(solution)/shard_map/ppermute | solution.py:41
  57.4 3.7 %collective-permute-start.17 = (f32[80,16]{0,1:T(8,128)S(1)}, f32[80,16]{0,1:T(8,128)S(1)}, u32[]{:S(2)}, u32[]{:S(2)}) collective-permute-start(f32[80,16]{0,1:T(8,128)S(1)} %add.132), channel_id=1, source_target_pairs={{0,8},{1,9},{2,10},{3,11},{4,12},{5,13},{6,14},{7,15},{8,0},{9,1},... | collective-permute-start | bytes 15368 | tf_op jit(solution)/shard_map/ppermute | solution.py:41
  61.0 4.5 %collective-permute-start.18 = (f32[80,16]{0,1:T(8,128)S(1)}, f32[80,16]{0,1:T(8,128)S(1)}, u32[]{:S(2)}, u32[]{:S(2)}) collective-permute-start(f32[80,16]{0,1:T(8,128)S(1)} %add.133), channel_id=1, source_target_pairs={{0,16},{1,17},{2,18},{3,19},{4,20},{5,21},{6,22},{7,23},{8,24},{9,... | collective-permute-start | bytes 15368 | tf_op jit(solution)/shard_map/ppermute | solution.py:41
  65.6 4.4 %copy-start.3 = (f32[80,16]{0,1:T(8,128)}, f32[80,16]{0,1:T(8,128)S(1)}, u32[]{:S(2)}) copy-start(f32[80,16]{0,1:T(8,128)S(1)} %add.134) | copy-start | bytes 15364

commit v12 on v11

--- a/solution.py
+++ b/solution.py
@@ -168,9 +168,9 @@
     keep_mask = lane_ids[None, None, :] < far_rank[:, :, None]
     sources = jnp.where(keep_mask[:, :, None, :], sources, jnp.zeros((), jnp.bfloat16))
     couple = coupling.reshape(3, group_size, slot_count, rank_width, rank_width)
-    far_terms = jnp.einsum("jcfkl,cfvl->jcfvk", couple, sources, preferred_element_type=jnp.float32)
-    combined = jnp.tensordot(powers, far_terms, 1) * keep_mask[:, :, None, :].astype(jnp.float32)
-    partial_far = jnp.sum(combined, axis=1).reshape(group_size, vec_count * rank_width)
+    far_terms = jnp.einsum("cfvl,jcfkl->cfvjk", sources, couple, preferred_element_type=jnp.float32)
+    weights = powers[None, None, None, :, None] * keep_mask[:, :, None, None, :].astype(jnp.float32)
+    partial_far = jnp.sum(far_terms * weights, axis=(1, 3)).reshape(group_size, vec_count * rank_width)
     far_hat = butterfly_scatter(partial_far, "coef")
     far_round = far_hat.astype(jnp.bfloat16).reshape(local_count, vec_count, rank_width)
     far_part = jnp.einsum("cki,cvk->vci", leaf_basis, far_round, preferred_element_type=jnp.float32)

time: 70.6 us -> 70.3 us (level)
  starting transfers between devices: 20.6 us -> 22.7 us
  other arithmetic: 6.64 us -> 5.4 us
  matrix products: 10.3 us -> 9.37 us
  waiting for transfers between devices: 17.7 us -> 16.8 us
    ppermute x5, starting transfers between devices: 8.34 us -> 10.8 us  [xor_gather(): block = jnp.concatenate([block, lax.ppermute(block, axis, route)], axis=dim)]
    ppermute x1, starting transfers between devices: 3.63 us -> 2.52 us  [extended_2(): lax.ppermute(lax.slice_in_dim(block, block.shape[dim] - width, None, axis...]
    dot_general x1, matrix products: 0.97 us -> 0.13 us  [on_device(): jnp.einsum('cki,cvk->vci', leaf_basis, far_round, preferred_element_type=...]
    mul x0 -> x1, other arithmetic: none -> 0.74 us  [on_device(): powers[None, None, None, :, None]]
    reduce_sum x1 -> x0, other arithmetic: 0.73 us -> none  [on_device(): jnp.sum(combined, axis=1).reshape(group_size, vec_count * rank_width)]
    reshape x1, other arithmetic: 0.73 us -> 0.01 us  [on_device(): extended = extended.reshape(vec_count, 3 * local_count, leaf_size)]
    reshape x1, local copies, waits for them, and re-layouts: 0.18 us -> 0.89 us  [on_device(): flat_rows.at[local_ids].get(mode='promise_in_bounds')]
    dot_general x2 -> x1, matrix products: 4.96 us -> 4.9 us  [on_device(): jnp.einsum('cfvl,jcfkl->cfvjk', sources, couple, preferred_element_type=j...]
  transfers between devices with their start and end apart: 14 -> 14, of which waited for: 10 -> 10; matrix products, arithmetic and copies ran while one was open for 21% -> 20% of each run, Pallas kernels for 0% -> 0%
where the time goes in v12:
time: 70.3 us; the launch traced here: 69.8 us
  starting transfers between devices  22.7 us (32%)
  waiting for transfers between devices  16.8 us (24%)
  local copies, waits for them, and re-layouts  10.9 us (16%)
  matrix products  9.37 us (13%)
  other arithmetic  5.4 us (8%)
  Pallas kernels  2.43 us (3%)
  between operations  2.13 us (3%)
    ppermute x5, starting transfers between devices, xor_gather(): block = jnp.concatenate([block, lax.ppermute(block, axis, route)], axis=dim)  10.8 us
    ppermute x5, waiting for transfers between devices, butterfly_sum(): block = block + lax.ppermute(block, axes, route)  10.2 us
    ppermute x5, starting transfers between devices, butterfly_sum(): block = block + lax.ppermute(block, axes, route)  6.57 us
    reshape x1, local copies, waits for them, and re-layouts, on_device(): couple = coupling.reshape(3, group_size, slot_count, rank_width, rank_width)  5.63 us
    ppermute x5, waiting for transfers between devices, xor_gather(): block = jnp.concatenate([block, lax.ppermute(block, axis, route)], axis=dim)  5.59 us
    dot_general x1, matrix products, on_device(): jnp.einsum('cfvl,jcfkl->cfvjk', sources, couple, preferred_element_type=j...  4.9 us
    ppermute x1, starting transfers between devices, extended_2(): lax.ppermute(lax.slice_in_dim(block, block.shape[dim] - width, None, axis...  2.52 us
    pallas_call x1, Pallas kernels, chol_solve(): pl.pallas_call(chol_solve_kernel, out_shape=(jax.ShapeDtypeStruct((size,...  2.43 us
  transfers between devices with their start and end apart: 14, of which 10 were waited for; matrix products, arithmetic and copies ran while one was open for 20% of the time, Pallas kernels for 0%

profile of v12, /device:TPU:0, one launch (start us, length us, event | category | flops | bytes accessed | tf_op | source)
XLA Modules:
  0.0 69.8 jit_solution(9634526655710139591)
XLA Ops:
  1.6 2.5 %collective-permute-start.12 = (bf16[16,512]{1,0:T(8,128)(2,1)S(1)}, bf16[16,512]{1,0:T(8,128)(2,1)S(1)}, u32[]{:S(2)}, u32[]{:S(2)}) collective-permute-start(bf16[16,512]{1,0:T(8,128)(2,1)S(1)} %convert_element_type.20), channel_id=1, source_target_pairs={{0,1},{1,2},{2,3},{3,4},{4,5},{5,6},{6,7},{7,8},{8,9},{9,10},{10,1... | collective-permute-start | bytes 49160 | tf_op jit(solution)/shard_map/ppermute | solution.py:20
  4.1 1.3 %collective-permute-start.13 = (bf16[16,512]{1,0:T(8,128)(2,1)S(1)}, bf16[16,512]{1,0:T(8,128)(2,1)S(1)}, u32[]{:S(2)}, u32[]{:S(2)}) collective-permute-start(bf16[16,512]{1,0:T(8,128)(2,1)S(1)} %convert_element_type.20), channel_id=1, source_target_pairs={{1,0},{2,1},{3,2},{4,3},{5,4},{6,5},{7,6},{8,7},{9,8},{10,9},{11,1... | collective-permute-start | bytes 49160 | tf_op jit(solution)/shard_map/ppermute | solution.py:23
  6.5 5.8 %collective-permute-start.5 = (bf16[1,4,1024]{2,1,0:T(4,128)(2,1)S(1)}, bf16[1,4,1024]{2,1,0:T(4,128)(2,1)S(1)}, u32[]{:S(2)}, u32[]{:S(2)}) collective-permute-start(bf16[1,4,1024]{2,1,0:T(4,128)(2,1)S(1)} %reshape.117), channel_id=1, source_target_pairs={{0,4},{4,0},{8,12},{12,8},{16,20},{20,16},{24,28},{28,24},{1,5},{5... | collective-permute-start | bytes 24584 | tf_op jit(solution)/shard_map/ppermute | solution.py:53
  16.3 1.6 %collective-permute-start.6 = (bf16[2,4,1024]{2,1,0:T(4,128)(2,1)S(1)}, bf16[2,4,1024]{2,1,0:T(4,128)(2,1)S(1)}, u32[]{:S(2)}, u32[]{:S(2)}) collective-permute-start(bf16[2,4,1024]{2,1,0:T(4,128)(2,1)S(1)} %pad_maximum_fusion.3), channel_id=1, source_target_pairs={{0,8},{4,12},{8,0},{12,4},{16,24},{20,28},{24,16},{28,20},{1,9},{5... | collective-permute-start | bytes 49160 | tf_op jit(solution)/shard_map/ppermute | solution.py:53
  17.9 2.1 %collective-permute-done.6 = bf16[2,4,1024]{2,1,0:T(4,128)(2,1)S(1)} collective-permute-done((bf16[2,4,1024]{2,1,0:T(4,128)(2,1)S(1)}, bf16[2,4,1024]{2,1,0:T(4,128)(2,1)S(1)}, u32[]{:S(2)}, u32[]{:S(2)}) %collective-permute-start.6) | collective-permute-done | bytes 16416 | tf_op jit(solution)/shard_map/ppermute | solution.py:53
  20.1 2.7 %collective-permute-start.7 = (bf16[4,4,1024]{2,1,0:T(4,128)(2,1)S(1)}, bf16[4,4,1024]{2,1,0:T(4,128)(2,1)S(1)}, u32[]{:S(2)}, u32[]{:S(2)}) collective-permute-start(bf16[4,4,1024]{2,1,0:T(4,128)(2,1)S(1)} %pad_maximum_fusion.2), channel_id=1, source_target_pairs={{0,16},{4,20},{8,24},{12,28},{16,0},{20,4},{24,8},{28,12},{1,17},{... | collective-permute-start | bytes 98312 | tf_op jit(solution)/shard_map/ppermute | solution.py:53
  22.8 2.2 %collective-permute-done.7 = bf16[4,4,1024]{2,1,0:T(4,128)(2,1)S(1)} collective-permute-done((bf16[4,4,1024]{2,1,0:T(4,128)(2,1)S(1)}, bf16[4,4,1024]{2,1,0:T(4,128)(2,1)S(1)}, u32[]{:S(2)}, u32[]{:S(2)}) %collective-permute-start.7) | collective-permute-done | bytes 32800 | tf_op jit(solution)/shard_map/ppermute | solution.py:53
  25.1 1.2 %collective-permute-done.8 = bf16[8,4,1024]{2,1,0:T(4,128)(2,1)S(1)} collective-permute-done((bf16[8,4,1024]{2,1,0:T(4,128)(2,1)S(1)}, bf16[8,4,1024]{2,1,0:T(4,128)(2,1)S(1)}, u32[]{:S(2)}, u32[]{:S(2)}) %collective-permute-start.8) | collective-permute-done | bytes 65568 | tf_op jit(solution)/shard_map/ppermute | solution.py:53
  27.1 5.6 %reshape.121 = bf16[3,16,4,64,64]{4,3,2,1,0:T(8,128)(2,1)} reshape(bf16[3,16,4,4096]{3,2,1,0:T(4,128)(2,1)} %param.16) | data formatting | bytes 3145728 | tf_op jit(solution)/shard_map/reshape | solution.py:170
  32.7 1.2 %gather_fusion.1 = bf16[32,16,128]{2,1,0:T(8,128)(2,1)} fusion(bf16[16,12,128]{2,0,1:T(8,128)(2,1)S(1)} %copy_bitcast_fusion, s32[1024]{0:T(1024)S(1)} %pad_clamp_fusion), kind=kCustom, calls=%fused_computation.1 | custom fusion | bytes 262272 | tf_op jit(solution)/shard_map/gather | solution.py:181
  34.0 1.0 %pad_maximum_fusion = bf16[8,16,1024]{2,1,0:T(8,128)(2,1)S(1)} fusion(bf16[8,8,1024]{2,1,0:T(8,128)(2,1)} %collective-permute-done.9, bf16[8,4,1024]{2,1,0:T(4,128)(2,1)S(1)} %collective-permute-done.8, bf16[8,4,1024]{2,1,0:T(4,128)(2,1)S(1)} %constant_dynamic-update-slice_fusion), kind=kLoop, calls=%fused_computation.16 | loop fusion | flops 786432 | bytes 524288 | tf_op jit(solution)/shard_map/concatenate | solution.py:53
  36.6 4.9 %multiply_reduce_fusion = f32[16,16,64]{2,1,0:T(8,128)} fusion(bf16[3,16,4,64,64]{4,3,2,1,0:T(8,128)(2,1)} %reshape.121, f32[16,4,3,64]{3,2,1,0:T(4,128)} %broadcast_multiply_fusion, bf16[16,4,16,64]{3,2,1,0:T(8,128)(2,1)} %reshape.120, pred[16,4,64]{2,1,0:T(4,128)(4,1)S(1)} %get-tuple-element.14), kind=kOutput, calls=%fused_computation.7 | convolution fusion | flops 25608192 | bytes 1822720 | tf_op jit(solution)/shard_map/cfvl,jcfkl->cfvjk/dot_general | solution.py:171
  41.5 1.0 %reshape_reshape.3 = f32[2,8,1024]{2,1,0:T(8,128)S(1)} reshape(f32[16,16,64]{2,1,0:T(8,128)} %multiply_reduce_fusion) | data formatting | bytes 131072 | tf_op jit(solution)/shard_map/reshape;reshape | solution.py:66
  42.5 1.5 %collective-permute-start.10 = (f32[8,1024]{1,0:T(8,128)S(1)}, f32[8,1024]{1,0:T(8,128)S(1)}, u32[]{:S(2)}, u32[]{:S(2)}) collective-permute-start(f32[8,1024]{1,0:T(8,128)S(1)} %dynamic-slice_bitcast_fusion), channel_id=1, source_target_pairs={{0,2},{1,3},{2,0},{3,1},{4,6},{5,7},{6,4},{7,5},{8,10},{9,11},{10,... | collective-permute-start | bytes 98312 | tf_op jit(solution)/shard_map/ppermute | solution.py:71
  44.1 1.6 %fusion = bf16[4,16,3,128,1]{3,1,4,2,0:T(8,128)(2,1)} fusion(bf16[16,4,8,128,1]{3,0,2,4,1:T(8,128)(2,1)S(1)} %bitcast.93, bf16[3,4,8,128,128]{4,3,2,1,0:T(8,128)(2,1)S(1)} %copy-done), kind=kOutput, calls=%fused_computation.3 | convolution fusion | flops 50331648 | bytes 3325952 | tf_op jit(solution)/shard_map/jcnil,vcnl->jvci/dot_general | solution.py:184
  46.6 1.0 %fusion.11 = f32[1,16,4,128]{3,0,2,1:T(1,128)S(1)} fusion(bf16[4,16,3,128,1]{3,1,4,2,0:T(8,128)(2,1)} %fusion, f32[1]{0:T(128)S(6)} %mul.49, f32[1]{0:T(128)S(6)} %copy.66, f32[1]{0:T(128)} %constant.122.clone.1), kind=kOutput, calls=%fused_computation.21 | convolution fusion | flops 49158 | bytes 81932 | tf_op jit(solution)/shard_map/dot_general | solution.py:187
  49.8 1.4 %collective-permute-start.15 = (f32[80,16]{0,1:T(8,128)S(1)}, f32[80,16]{0,1:T(8,128)S(1)}, u32[]{:S(2)}, u32[]{:S(2)}) collective-permute-start(f32[80,16]{0,1:T(8,128)S(1)} %fusion.53), channel_id=1, source_target_pairs={{0,2},{1,3},{2,0},{3,1},{4,6},{5,7},{6,4},{7,5},{8,10},{9,11},{10,... | collective-permute-start | bytes 15368 | tf_op jit(solution)/shard_map/ppermute | solution.py:41
  51.3 2.2 %collective-permute-done.15 = f32[80,16]{0,1:T(8,128)S(1)} collective-permute-done((f32[80,16]{0,1:T(8,128)S(1)}, f32[80,16]{0,1:T(8,128)S(1)}, u32[]{:S(2)}, u32[]{:S(2)}) %collective-permute-start.15) | collective-permute-done | bytes 5152 | tf_op jit(solution)/shard_map/ppermute | solution.py:41
  54.0 3.1 %collective-permute-done.16 = f32[80,16]{0,1:T(8,128)S(1)} collective-permute-done((f32[80,16]{0,1:T(8,128)S(1)}, f32[80,16]{0,1:T(8,128)S(1)}, u32[]{:S(2)}, u32[]{:S(2)}) %collective-permute-start.16) | collective-permute-done | bytes 5152 | tf_op jit(solution)/shard_map/ppermute | solution.py:41
  57.1 1.6 %collective-permute-start.17 = (f32[80,16]{0,1:T(8,128)S(1)}, f32[80,16]{0,1:T(8,128)S(1)}, u32[]{:S(2)}, u32[]{:S(2)}) collective-permute-start(f32[80,16]{0,1:T(8,128)S(1)} %add.132), channel_id=1, source_target_pairs={{0,8},{1,9},{2,10},{3,11},{4,12},{5,13},{6,14},{7,15},{8,0},{9,1},... | collective-permute-start | bytes 15368 | tf_op jit(solution)/shard_map/ppermute | solution.py:41
  58.7 2.1 %collective-permute-done.17 = f32[80,16]{0,1:T(8,128)S(1)} collective-permute-done((f32[80,16]{0,1:T(8,128)S(1)}, f32[80,16]{0,1:T(8,128)S(1)}, u32[]{:S(2)}, u32[]{:S(2)}) %collective-permute-start.17) | collective-permute-done | bytes 5152 | tf_op jit(solution)/shard_map/ppermute | solution.py:41
  60.8 2.6 %collective-permute-start.18 = (f32[80,16]{0,1:T(8,128)S(1)}, f32[80,16]{0,1:T(8,128)S(1)}, u32[]{:S(2)}, u32[]{:S(2)}) collective-permute-start(f32[80,16]{0,1:T(8,128)S(1)} %add.133), channel_id=1, source_target_pairs={{0,16},{1,17},{2,18},{3,19},{4,20},{5,21},{6,22},{7,23},{8,24},{9,... | collective-permute-start | bytes 15368 | tf_op jit(solution)/shard_map/ppermute | solution.py:41
  63.4 1.9 %collective-permute-done.18 = f32[80,16]{0,1:T(8,128)S(1)} collective-permute-done((f32[80,16]{0,1:T(8,128)S(1)}, f32[80,16]{0,1:T(8,128)S(1)}, u32[]{:S(2)}, u32[]{:S(2)}) %collective-permute-start.18) | collective-permute-done | bytes 5152 | tf_op jit(solution)/shard_map/ppermute | solution.py:41
  67.4 2.4 %shard_map.112 = (f32[16,16]{1,0:T(8,128)}, f32[16,512]{1,0:T(8,128)}) custom-call(f32[16,16]{1,0:T(8,128)S(1)} %get-tuple-element.18.gram_ref, f32[16,512]{1,0:T(8,128)S(1)} %convolution_subtract_fusion.residue_ref), custom_call_target="tpu_custom_call" | custom-call | flops 540672 | bytes 67584 | tf_op jit(solution)/shard_map/pallas_call | solution.py:117
  (69 shorter events, 13.0 us)
Async XLA Ops:
  0.6 43.4 %copy-start = (bf16[3,4,8,128,128]{4,3,2,1,0:T(8,128)(2,1)S(1)}, bf16[3,4,8,128,128]{4,3,2,1,0:T(8,128)(2,1)}, u32[]{:S(2)}) copy-start(bf16[3,4,8,128,128]{4,3,2,1,0:T(8,128)(2,1)} %param.14) | copy-start | bytes 9437188
  1.6 31.2 %collective-permute-start.12 = (bf16[16,512]{1,0:T(8,128)(2,1)S(1)}, bf16[16,512]{1,0:T(8,128)(2,1)S(1)}, u32[]{:S(2)}, u32[]{:S(2)}) collective-permute-start(bf16[16,512]{1,0:T(8,128)(2,1)S(1)} %convert_element_type.20), channel_id=1, source_target_pairs={{0,1},{1,2},{2,3},{3,4},{4,5},{5,6},{6,7},{7,8},{8,9},{9,10},{10,1... | collective-permute-start | bytes 49160 | tf_op jit(solution)/shard_map/ppermute | solution.py:20
  4.1 28.6 %collective-permute-start.13 = (bf16[16,512]{1,0:T(8,128)(2,1)S(1)}, bf16[16,512]{1,0:T(8,128)(2,1)S(1)}, u32[]{:S(2)}, u32[]{:S(2)}) collective-permute-start(bf16[16,512]{1,0:T(8,128)(2,1)S(1)} %convert_element_type.20), channel_id=1, source_target_pairs={{1,0},{2,1},{3,2},{4,3},{5,4},{6,5},{7,6},{8,7},{9,8},{10,9},{11,1... | collective-permute-start | bytes 49160 | tf_op jit(solution)/shard_map/ppermute | solution.py:23
  6.5 9.8 %collective-permute-start.5 = (bf16[1,4,1024]{2,1,0:T(4,128)(2,1)S(1)}, bf16[1,4,1024]{2,1,0:T(4,128)(2,1)S(1)}, u32[]{:S(2)}, u32[]{:S(2)}) collective-permute-start(bf16[1,4,1024]{2,1,0:T(4,128)(2,1)S(1)} %reshape.117), channel_id=1, source_target_pairs={{0,4},{4,0},{8,12},{12,8},{16,20},{20,16},{24,28},{28,24},{1,5},{5... | collective-permute-start | bytes 24584 | tf_op jit(solution)/shard_map/ppermute | solution.py:53
  16.3 3.8 %collective-permute-start.6 = (bf16[2,4,1024]{2,1,0:T(4,128)(2,1)S(1)}, bf16[2,4,1024]{2,1,0:T(4,128)(2,1)S(1)}, u32[]{:S(2)}, u32[]{:S(2)}) collective-permute-start(bf16[2,4,1024]{2,1,0:T(4,128)(2,1)S(1)} %pad_maximum_fusion.3), channel_id=1, source_target_pairs={{0,8},{4,12},{8,0},{12,4},{16,24},{20,28},{24,16},{28,20},{1,9},{5... | collective-permute-start | bytes 49160 | tf_op jit(solution)/shard_map/ppermute | solution.py:53
  20.1 4.9 %collective-permute-start.7 = (bf16[4,4,1024]{2,1,0:T(4,128)(2,1)S(1)}, bf16[4,4,1024]{2,1,0:T(4,128)(2,1)S(1)}, u32[]{:S(2)}, u32[]{:S(2)}) collective-permute-start(bf16[4,4,1024]{2,1,0:T(4,128)(2,1)S(1)} %pad_maximum_fusion.2), channel_id=1, source_target_pairs={{0,16},{4,20},{8,24},{12,28},{16,0},{20,4},{24,8},{28,12},{1,17},{... | collective-permute-start | bytes 98312 | tf_op jit(solution)/shard_map/ppermute | solution.py:53
  25.0 1.3 %collective-permute-start.8 = (bf16[8,4,1024]{2,1,0:T(4,128)(2,1)S(1)}, bf16[8,4,1024]{2,1,0:T(4,128)(2,1)S(1)}, u32[]{:S(2)}, u32[]{:S(2)}) collective-permute-start(bf16[8,4,1024]{2,1,0:T(4,128)(2,1)S(1)} %constant_dynamic-update-slice_fusion), channel_id=1, source_target_pairs={{0,1},{1,0},{2,3},{3,2},{4,5},{5,4},{6,7},{7,6},{8,9},{9,8},{10,11... | collective-permute-start | bytes 196616 | tf_op jit(solution)/shard_map/ppermute | solution.py:53
  26.4 7.5 %collective-permute-start.9 = (bf16[8,8,1024]{2,1,0:T(8,128)(2,1)S(1)}, bf16[8,8,1024]{2,1,0:T(8,128)(2,1)}, u32[]{:S(2)}, u32[]{:S(2)}) collective-permute-start(bf16[8,8,1024]{2,1,0:T(8,128)(2,1)S(1)} %pad_maximum_fusion.1), channel_id=1, source_target_pairs={{0,2},{1,3},{2,0},{3,1},{4,6},{5,7},{6,4},{7,5},{8,10},{9,11},{10,... | collective-permute-start | bytes 393224 | tf_op jit(solution)/shard_map/ppermute | solution.py:53
  35.7 8.4 %copy-start.1 = (bf16[32,16,128]{2,1,0:T(8,128)(2,1)S(1)}, bf16[32,16,128]{2,1,0:T(8,128)(2,1)}, u32[]{:S(2)}) copy-start(bf16[32,16,128]{2,1,0:T(8,128)(2,1)} %gather_fusion.1) | copy-start | bytes 393220
  36.6 11.3 %copy-start.4 = (bf16[4,64,128]{2,1,0:T(8,128)(2,1)S(1)}, bf16[4,64,128]{2,1,0:T(8,128)(2,1)}, u32[]{:S(2)}) copy-start(bf16[4,64,128]{2,1,0:T(8,128)(2,1)} %param.13) | copy-start | bytes 196612
  41.5 6.7 %copy-start.2 = (f32[64,512]{1,0:T(8,128)S(1)}, f32[64,512]{1,0:T(8,128)}, u32[]{:S(2)}) copy-start(f32[64,512]{1,0:T(8,128)} %param.19) | copy-start | bytes 393220
  42.5 4.0 %collective-permute-start.10 = (f32[8,1024]{1,0:T(8,128)S(1)}, f32[8,1024]{1,0:T(8,128)S(1)}, u32[]{:S(2)}, u32[]{:S(2)}) collective-permute-start(f32[8,1024]{1,0:T(8,128)S(1)} %dynamic-slice_bitcast_fusion), channel_id=1, source_target_pairs={{0,2},{1,3},{2,0},{3,1},{4,6},{5,7},{6,4},{7,5},{8,10},{9,11},{10,... | collective-permute-start | bytes 98312 | tf_op jit(solution)/shard_map/ppermute | solution.py:71
  46.6 1.2 %collective-permute-start.11 = (f32[4,1024]{1,0:T(4,128)S(1)}, f32[4,1024]{1,0:T(4,128)S(1)}, u32[]{:S(2)}, u32[]{:S(2)}) collective-permute-start(f32[4,1024]{1,0:T(4,128)S(1)} %dynamic-slice_bitcast_fusion.1), channel_id=1, source_target_pairs={{0,1},{1,0},{2,3},{3,2},{4,5},{5,4},{6,7},{7,6},{8,9},{9,8},{10,11... | collective-permute-start | bytes 49160 | tf_op jit(solution)/shard_map/ppermute | solution.py:71
  48.5 1.2 %collective-permute-start.14 = (f32[80,16]{0,1:T(8,128)S(1)}, f32[80,16]{0,1:T(8,128)S(1)}, u32[]{:S(2)}, u32[]{:S(2)}) collective-permute-start(f32[80,16]{0,1:T(8,128)S(1)} %pad_maximum_fusion.4), channel_id=1, source_target_pairs={{0,1},{1,0},{2,3},{3,2},{4,5},{5,4},{6,7},{7,6},{8,9},{9,8},{10,11... | collective-permute-start | bytes 15368 | tf_op jit(solution)/shard_map/ppermute | solution.py:41
  49.8 3.7 %collective-permute-start.15 = (f32[80,16]{0,1:T(8,128)S(1)}, f32[80,16]{0,1:T(8,128)S(1)}, u32[]{:S(2)}, u32[]{:S(2)}) collective-permute-start(f32[80,16]{0,1:T(8,128)S(1)} %fusion.53), channel_id=1, source_target_pairs={{0,2},{1,3},{2,0},{3,1},{4,6},{5,7},{6,4},{7,5},{8,10},{9,11},{10,... | collective-permute-start | bytes 15368 | tf_op jit(solution)/shard_map/ppermute | solution.py:41
  53.5 3.7 %collective-permute-start.16 = (f32[80,16]{0,1:T(8,128)S(1)}, f32[80,16]{0,1:T(8,128)S(1)}, u32[]{:S(2)}, u32[]{:S(2)}) collective-permute-start(f32[80,16]{0,1:T(8,128)S(1)} %add.131), channel_id=1, source_target_pairs={{0,4},{1,5},{2,6},{3,7},{4,0},{5,1},{6,2},{7,3},{8,12},{9,13},{10,... | collective-permute-start | bytes 15368 | tf_op jit(solution)/shard_map/ppermute | solution.py:41
  57.1 3.7 %collective-permute-start.17 = (f32[80,16]{0,1:T(8,128)S(1)}, f32[80,16]{0,1:T(8,128)S(1)}, u32[]{:S(2)}, u32[]{:S(2)}) collective-permute-start(f32[80,16]{0,1:T(8,128)S(1)} %add.132), channel_id=1, source_target_pairs={{0,8},{1,9},{2,10},{3,11},{4,12},{5,13},{6,14},{7,15},{8,0},{9,1},... | collective-permute-start | bytes 15368 | tf_op jit(solution)/shard_map/ppermute | solution.py:41
  60.8 4.5 %collective-permute-start.18 = (f32[80,16]{0,1:T(8,128)S(1)}, f32[80,16]{0,1:T(8,128)S(1)}, u32[]{:S(2)}, u32[]{:S(2)}) collective-permute-start(f32[80,16]{0,1:T(8,128)S(1)} %add.133), channel_id=1, source_target_pairs={{0,16},{1,17},{2,18},{3,19},{4,20},{5,21},{6,22},{7,23},{8,24},{9,... | collective-permute-start | bytes 15368 | tf_op jit(solution)/shard_map/ppermute | solution.py:41
  65.3 4.4 %copy-start.3 = (f32[80,16]{0,1:T(8,128)}, f32[80,16]{0,1:T(8,128)S(1)}, u32[]{:S(2)}) copy-start(f32[80,16]{0,1:T(8,128)S(1)} %add.134) | copy-start | bytes 15364

commit v13 on v12

--- a/solution.py
+++ b/solution.py
@@ -170,7 +170,7 @@
     couple = coupling.reshape(3, group_size, slot_count, rank_width, rank_width)
     far_terms = jnp.einsum("cfvl,jcfkl->cfvjk", sources, couple, preferred_element_type=jnp.float32)
     weights = powers[None, None, None, :, None] * keep_mask[:, :, None, None, :].astype(jnp.float32)
-    partial_far = jnp.sum(far_terms * weights, axis=(1, 3)).reshape(group_size, vec_count * rank_width)
+    partial_far = jnp.sum(far_terms * weights, axis=(1, 3))
     far_hat = butterfly_scatter(partial_far, "coef")
     far_round = far_hat.astype(jnp.bfloat16).reshape(local_count, vec_count, rank_width)
     far_part = jnp.einsum("cki,cvk->vci", leaf_basis, far_round, preferred_element_type=jnp.float32)

time: 70.3 us -> 69.5 us (0.989)
  matrix products: 9.37 us -> 7.35 us
  waiting for transfers between devices: 16.8 us -> 18.2 us
  other arithmetic: 5.4 us -> 6.59 us
  local copies, waits for them, and re-layouts: 10.9 us -> 9.88 us
    ppermute x2, waiting for transfers between devices: 1.05 us -> 2.87 us  [butterfly_scatter(): parts = keep + lax.ppermute(give, axis, route)]
    another operation x1 -> x0, local copies, waits for them, and re-layouts: 1.03 us -> none  [butterfly_scatter(): halves = parts.reshape(2, parts.shape[0] // 2, *parts.shape[1:])]
    dot_general x1, matrix products: 1.03 us -> 0.23 us  [on_device(): near_part = jnp.tensordot(powers, near_terms, 1)]
where the time goes in v13:
time: 69.5 us; the launch traced here: 69.1 us
  starting transfers between devices  22.5 us (32%)
  waiting for transfers between devices  18.2 us (26%)
  local copies, waits for them, and re-layouts  9.88 us (14%)
  matrix products  7.35 us (11%)
  other arithmetic  6.59 us (9%)
  Pallas kernels  2.43 us (3%)
  between operations  2.1 us (3%)
    ppermute x5, starting transfers between devices, xor_gather(): block = jnp.concatenate([block, lax.ppermute(block, axis, route)], axis=dim)  10.8 us
    ppermute x5, waiting for transfers between devices, butterfly_sum(): block = block + lax.ppermute(block, axes, route)  10.3 us
    ppermute x5, starting transfers between devices, butterfly_sum(): block = block + lax.ppermute(block, axes, route)  6.35 us
    reshape x1, local copies, waits for them, and re-layouts, on_device(): couple = coupling.reshape(3, group_size, slot_count, rank_width, rank_width)  5.63 us
    ppermute x5, waiting for transfers between devices, xor_gather(): block = jnp.concatenate([block, lax.ppermute(block, axis, route)], axis=dim)  5.01 us
    dot_general x1, matrix products, on_device(): jnp.einsum('cfvl,jcfkl->cfvjk', sources, couple, preferred_element_type=j...  4.31 us
    ppermute x2, waiting for transfers between devices, butterfly_scatter(): parts = keep + lax.ppermute(give, axis, route)  2.87 us
    ppermute x1, starting transfers between devices, extended_2(): lax.ppermute(lax.slice_in_dim(block, block.shape[dim] - width, None, axis...  2.52 us
  transfers between devices with their start and end apart: 14, of which 10 were waited for; matrix products, arithmetic and copies ran while one was open for 20% of the time, Pallas kernels for 0%

profile of v13, /device:TPU:0, one launch (start us, length us, event | category | flops | bytes accessed | tf_op | source)
XLA Modules:
  0.0 69.1 jit_solution(8421976550088218078)
XLA Ops:
  1.6 2.5 %collective-permute-start.12 = (bf16[16,512]{1,0:T(8,128)(2,1)S(1)}, bf16[16,512]{1,0:T(8,128)(2,1)S(1)}, u32[]{:S(2)}, u32[]{:S(2)}) collective-permute-start(bf16[16,512]{1,0:T(8,128)(2,1)S(1)} %convert_element_type.20), channel_id=1, source_target_pairs={{0,1},{1,2},{2,3},{3,4},{4,5},{5,6},{6,7},{7,8},{8,9},{9,10},{10,1... | collective-permute-start | bytes 49160 | tf_op jit(solution)/shard_map/ppermute | solution.py:20
  4.1 1.3 %collective-permute-start.13 = (bf16[16,512]{1,0:T(8,128)(2,1)S(1)}, bf16[16,512]{1,0:T(8,128)(2,1)S(1)}, u32[]{:S(2)}, u32[]{:S(2)}) collective-permute-start(bf16[16,512]{1,0:T(8,128)(2,1)S(1)} %convert_element_type.20), channel_id=1, source_target_pairs={{1,0},{2,1},{3,2},{4,3},{5,4},{6,5},{7,6},{8,7},{9,8},{10,9},{11,1... | collective-permute-start | bytes 49160 | tf_op jit(solution)/shard_map/ppermute | solution.py:23
  5.4 1.0 %convolution_convert_fusion = bf16[4,16,64]{2,1,0:T(8,128)(2,1)S(1)} fusion(bf16[4,64,128]{2,1,0:T(8,128)(2,1)} %param.13, f32[16,512]{1,0:T(8,128)} %param.11), kind=kOutput, calls=%fused_computation.11 | convolution fusion | flops 1060864 | bytes 106496 | tf_op jit(solution)/shard_map/cki,vci->cvk/dot_general | solution.py:148
  6.5 5.8 %collective-permute-start.5 = (bf16[1,4,1024]{2,1,0:T(4,128)(2,1)S(1)}, bf16[1,4,1024]{2,1,0:T(4,128)(2,1)S(1)}, u32[]{:S(2)}, u32[]{:S(2)}) collective-permute-start(bf16[1,4,1024]{2,1,0:T(4,128)(2,1)S(1)} %reshape.117), channel_id=1, source_target_pairs={{0,4},{4,0},{8,12},{12,8},{16,20},{20,16},{24,28},{28,24},{1,5},{5... | collective-permute-start | bytes 24584 | tf_op jit(solution)/shard_map/ppermute | solution.py:53
  16.9 1.6 %collective-permute-start.6 = (bf16[2,4,1024]{2,1,0:T(4,128)(2,1)S(1)}, bf16[2,4,1024]{2,1,0:T(4,128)(2,1)S(1)}, u32[]{:S(2)}, u32[]{:S(2)}) collective-permute-start(bf16[2,4,1024]{2,1,0:T(4,128)(2,1)S(1)} %pad_maximum_fusion.3), channel_id=1, source_target_pairs={{0,8},{4,12},{8,0},{12,4},{16,24},{20,28},{24,16},{28,20},{1,9},{5... | collective-permute-start | bytes 49160 | tf_op jit(solution)/shard_map/ppermute | solution.py:53
  18.5 2.1 %collective-permute-done.6 = bf16[2,4,1024]{2,1,0:T(4,128)(2,1)S(1)} collective-permute-done((bf16[2,4,1024]{2,1,0:T(4,128)(2,1)S(1)}, bf16[2,4,1024]{2,1,0:T(4,128)(2,1)S(1)}, u32[]{:S(2)}, u32[]{:S(2)}) %collective-permute-start.6) | collective-permute-done | bytes 16416 | tf_op jit(solution)/shard_map/ppermute | solution.py:53
  20.7 2.7 %collective-permute-start.7 = (bf16[4,4,1024]{2,1,0:T(4,128)(2,1)S(1)}, bf16[4,4,1024]{2,1,0:T(4,128)(2,1)S(1)}, u32[]{:S(2)}, u32[]{:S(2)}) collective-permute-start(bf16[4,4,1024]{2,1,0:T(4,128)(2,1)S(1)} %pad_maximum_fusion.2), channel_id=1, source_target_pairs={{0,16},{4,20},{8,24},{12,28},{16,0},{20,4},{24,8},{28,12},{1,17},{... | collective-permute-start | bytes 98312 | tf_op jit(solution)/shard_map/ppermute | solution.py:53
  23.4 2.2 %collective-permute-done.7 = bf16[4,4,1024]{2,1,0:T(4,128)(2,1)S(1)} collective-permute-done((bf16[4,4,1024]{2,1,0:T(4,128)(2,1)S(1)}, bf16[4,4,1024]{2,1,0:T(4,128)(2,1)S(1)}, u32[]{:S(2)}, u32[]{:S(2)}) %collective-permute-start.7) | collective-permute-done | bytes 32800 | tf_op jit(solution)/shard_map/ppermute | solution.py:53
  27.7 5.6 %reshape.121 = bf16[3,16,4,64,64]{4,3,2,1,0:T(8,128)(2,1)} reshape(bf16[3,16,4,4096]{3,2,1,0:T(4,128)(2,1)} %param.16) | data formatting | bytes 3145728 | tf_op jit(solution)/shard_map/reshape | solution.py:170
  33.3 1.2 %gather_fusion.1 = bf16[32,16,128]{2,1,0:T(8,128)(2,1)} fusion(bf16[16,12,128]{2,0,1:T(8,128)(2,1)S(1)} %copy_bitcast_fusion, s32[1024]{0:T(1024)S(1)} %pad_clamp_fusion), kind=kCustom, calls=%fused_computation.1 | custom fusion | bytes 262272 | tf_op jit(solution)/shard_map/gather | solution.py:181
  34.5 1.0 %pad_maximum_fusion = bf16[8,16,1024]{2,1,0:T(8,128)(2,1)S(1)} fusion(bf16[8,8,1024]{2,1,0:T(8,128)(2,1)} %collective-permute-done.9, bf16[8,4,1024]{2,1,0:T(4,128)(2,1)S(1)} %collective-permute-done.8, bf16[8,4,1024]{2,1,0:T(4,128)(2,1)S(1)} %constant_dynamic-update-slice_fusion), kind=kLoop, calls=%fused_computation.16 | loop fusion | flops 786432 | bytes 524288 | tf_op jit(solution)/shard_map/concatenate | solution.py:53
  37.3 4.3 %multiply_reduce_fusion = f32[16,16,64]{2,1,0:T(8,128)S(1)} fusion(bf16[3,16,4,64,64]{4,3,2,1,0:T(8,128)(2,1)} %reshape.121, f32[16,4,3,64]{3,2,1,0:T(4,128)} %broadcast_multiply_fusion, bf16[16,4,16,64]{3,2,1,0:T(8,128)(2,1)} %reshape.120, pred[16,4,64]{2,1,0:T(4,128)(4,1)} %get-tuple-element.14), kind=kOutput, calls=%fused_computation.7 | convolution fusion | flops 25608192 | bytes 1822720 | tf_op jit(solution)/shard_map/cfvl,jcfkl->cfvjk/dot_general | solution.py:171
  41.6 1.5 %collective-permute-start.10 = (f32[8,16,64]{2,1,0:T(8,128)S(1)}, f32[8,16,64]{2,1,0:T(8,128)S(1)}, u32[]{:S(2)}, u32[]{:S(2)}) collective-permute-start(f32[8,16,64]{2,1,0:T(8,128)S(1)} %dynamic-slice_bitcast_fusion), channel_id=1, source_target_pairs={{0,2},{1,3},{2,0},{3,1},{4,6},{5,7},{6,4},{7,5},{8,10},{9,11},{10,... | collective-permute-start | bytes 98312 | tf_op jit(solution)/shard_map/ppermute | solution.py:71
  44.1 1.9 %collective-permute-done.10 = f32[8,16,64]{2,1,0:T(8,128)S(1)} collective-permute-done((f32[8,16,64]{2,1,0:T(8,128)S(1)}, f32[8,16,64]{2,1,0:T(8,128)S(1)}, u32[]{:S(2)}, u32[]{:S(2)}) %collective-permute-start.10) | collective-permute-done | bytes 32800 | tf_op jit(solution)/shard_map/ppermute | solution.py:71
  46.3 1.0 %collective-permute-done.11 = f32[4,16,64]{2,1,0:T(8,128)S(1)} collective-permute-done((f32[4,16,64]{2,1,0:T(8,128)S(1)}, f32[4,16,64]{2,1,0:T(8,128)S(1)}, u32[]{:S(2)}, u32[]{:S(2)}) %collective-permute-start.11) | collective-permute-done | bytes 16416 | tf_op jit(solution)/shard_map/ppermute | solution.py:71
  48.1 1.0 %collective-permute-done.14 = f32[80,16]{0,1:T(8,128)S(1)} collective-permute-done((f32[80,16]{0,1:T(8,128)S(1)}, f32[80,16]{0,1:T(8,128)S(1)}, u32[]{:S(2)}, u32[]{:S(2)}) %collective-permute-start.14) | collective-permute-done | bytes 5152 | tf_op jit(solution)/shard_map/ppermute | solution.py:41
  49.1 1.4 %collective-permute-start.15 = (f32[80,16]{0,1:T(8,128)S(1)}, f32[80,16]{0,1:T(8,128)S(1)}, u32[]{:S(2)}, u32[]{:S(2)}) collective-permute-start(f32[80,16]{0,1:T(8,128)S(1)} %fusion.54), channel_id=1, source_target_pairs={{0,2},{1,3},{2,0},{3,1},{4,6},{5,7},{6,4},{7,5},{8,10},{9,11},{10,... | collective-permute-start | bytes 15368 | tf_op jit(solution)/shard_map/ppermute | solution.py:41
  50.6 2.2 %collective-permute-done.15 = f32[80,16]{0,1:T(8,128)S(1)} collective-permute-done((f32[80,16]{0,1:T(8,128)S(1)}, f32[80,16]{0,1:T(8,128)S(1)}, u32[]{:S(2)}, u32[]{:S(2)}) %collective-permute-start.15) | collective-permute-done | bytes 5152 | tf_op jit(solution)/shard_map/ppermute | solution.py:41
  53.4 3.1 %collective-permute-done.16 = f32[80,16]{0,1:T(8,128)S(1)} collective-permute-done((f32[80,16]{0,1:T(8,128)S(1)}, f32[80,16]{0,1:T(8,128)S(1)}, u32[]{:S(2)}, u32[]{:S(2)}) %collective-permute-start.16) | collective-permute-done | bytes 5152 | tf_op jit(solution)/shard_map/ppermute | solution.py:41
  56.5 1.6 %collective-permute-start.17 = (f32[80,16]{0,1:T(8,128)S(1)}, f32[80,16]{0,1:T(8,128)S(1)}, u32[]{:S(2)}, u32[]{:S(2)}) collective-permute-start(f32[80,16]{0,1:T(8,128)S(1)} %add.132), channel_id=1, source_target_pairs={{0,8},{1,9},{2,10},{3,11},{4,12},{5,13},{6,14},{7,15},{8,0},{9,1},... | collective-permute-start | bytes 15368 | tf_op jit(solution)/shard_map/ppermute | solution.py:41
  58.0 2.1 %collective-permute-done.17 = f32[80,16]{0,1:T(8,128)S(1)} collective-permute-done((f32[80,16]{0,1:T(8,128)S(1)}, f32[80,16]{0,1:T(8,128)S(1)}, u32[]{:S(2)}, u32[]{:S(2)}) %collective-permute-start.17) | collective-permute-done | bytes 5152 | tf_op jit(solution)/shard_map/ppermute | solution.py:41
  60.1 2.6 %collective-permute-start.18 = (f32[80,16]{0,1:T(8,128)S(1)}, f32[80,16]{0,1:T(8,128)S(1)}, u32[]{:S(2)}, u32[]{:S(2)}) collective-permute-start(f32[80,16]{0,1:T(8,128)S(1)} %add.133), channel_id=1, source_target_pairs={{0,16},{1,17},{2,18},{3,19},{4,20},{5,21},{6,22},{7,23},{8,24},{9,... | collective-permute-start | bytes 15368 | tf_op jit(solution)/shard_map/ppermute | solution.py:41
  62.7 1.9 %collective-permute-done.18 = f32[80,16]{0,1:T(8,128)S(1)} collective-permute-done((f32[80,16]{0,1:T(8,128)S(1)}, f32[80,16]{0,1:T(8,128)S(1)}, u32[]{:S(2)}, u32[]{:S(2)}) %collective-permute-start.18) | collective-permute-done | bytes 5152 | tf_op jit(solution)/shard_map/ppermute | solution.py:41
  66.7 2.4 %shard_map.112 = (f32[16,16]{1,0:T(8,128)}, f32[16,512]{1,0:T(8,128)}) custom-call(f32[16,16]{1,0:T(8,128)S(1)} %get-tuple-element.18.gram_ref, f32[16,512]{1,0:T(8,128)S(1)} %convolution_subtract_fusion.residue_ref), custom_call_target="tpu_custom_call" | custom-call | flops 540672 | bytes 67584 | tf_op jit(solution)/shard_map/pallas_call | solution.py:117
  (65 shorter events, 12.9 us)
Async XLA Ops:
  0.6 42.5 %copy-start = (bf16[3,4,8,128,128]{4,3,2,1,0:T(8,128)(2,1)S(1)}, bf16[3,4,8,128,128]{4,3,2,1,0:T(8,128)(2,1)}, u32[]{:S(2)}) copy-start(bf16[3,4,8,128,128]{4,3,2,1,0:T(8,128)(2,1)} %param.14) | copy-start | bytes 9437188
  1.6 31.7 %collective-permute-start.12 = (bf16[16,512]{1,0:T(8,128)(2,1)S(1)}, bf16[16,512]{1,0:T(8,128)(2,1)S(1)}, u32[]{:S(2)}, u32[]{:S(2)}) collective-permute-start(bf16[16,512]{1,0:T(8,128)(2,1)S(1)} %convert_element_type.20), channel_id=1, source_target_pairs={{0,1},{1,2},{2,3},{3,4},{4,5},{5,6},{6,7},{7,8},{8,9},{9,10},{10,1... | collective-permute-start | bytes 49160 | tf_op jit(solution)/shard_map/ppermute | solution.py:20
  4.1 29.2 %collective-permute-start.13 = (bf16[16,512]{1,0:T(8,128)(2,1)S(1)}, bf16[16,512]{1,0:T(8,128)(2,1)S(1)}, u32[]{:S(2)}, u32[]{:S(2)}) collective-permute-start(bf16[16,512]{1,0:T(8,128)(2,1)S(1)} %convert_element_type.20), channel_id=1, source_target_pairs={{1,0},{2,1},{3,2},{4,3},{5,4},{6,5},{7,6},{8,7},{9,8},{10,9},{11,1... | collective-permute-start | bytes 49160 | tf_op jit(solution)/shard_map/ppermute | solution.py:23
  6.5 10.4 %collective-permute-start.5 = (bf16[1,4,1024]{2,1,0:T(4,128)(2,1)S(1)}, bf16[1,4,1024]{2,1,0:T(4,128)(2,1)S(1)}, u32[]{:S(2)}, u32[]{:S(2)}) collective-permute-start(bf16[1,4,1024]{2,1,0:T(4,128)(2,1)S(1)} %reshape.117), channel_id=1, source_target_pairs={{0,4},{4,0},{8,12},{12,8},{16,20},{20,16},{24,28},{28,24},{1,5},{5... | collective-permute-start | bytes 24584 | tf_op jit(solution)/shard_map/ppermute | solution.py:53
  16.9 3.8 %collective-permute-start.6 = (bf16[2,4,1024]{2,1,0:T(4,128)(2,1)S(1)}, bf16[2,4,1024]{2,1,0:T(4,128)(2,1)S(1)}, u32[]{:S(2)}, u32[]{:S(2)}) collective-permute-start(bf16[2,4,1024]{2,1,0:T(4,128)(2,1)S(1)} %pad_maximum_fusion.3), channel_id=1, source_target_pairs={{0,8},{4,12},{8,0},{12,4},{16,24},{20,28},{24,16},{28,20},{1,9},{5... | collective-permute-start | bytes 49160 | tf_op jit(solution)/shard_map/ppermute | solution.py:53
  20.7 4.9 %collective-permute-start.7 = (bf16[4,4,1024]{2,1,0:T(4,128)(2,1)S(1)}, bf16[4,4,1024]{2,1,0:T(4,128)(2,1)S(1)}, u32[]{:S(2)}, u32[]{:S(2)}) collective-permute-start(bf16[4,4,1024]{2,1,0:T(4,128)(2,1)S(1)} %pad_maximum_fusion.2), channel_id=1, source_target_pairs={{0,16},{4,20},{8,24},{12,28},{16,0},{20,4},{24,8},{28,12},{1,17},{... | collective-permute-start | bytes 98312 | tf_op jit(solution)/shard_map/ppermute | solution.py:53
  25.6 1.3 %collective-permute-start.8 = (bf16[8,4,1024]{2,1,0:T(4,128)(2,1)S(1)}, bf16[8,4,1024]{2,1,0:T(4,128)(2,1)S(1)}, u32[]{:S(2)}, u32[]{:S(2)}) collective-permute-start(bf16[8,4,1024]{2,1,0:T(4,128)(2,1)S(1)} %constant_dynamic-update-slice_fusion), channel_id=1, source_target_pairs={{0,1},{1,0},{2,3},{3,2},{4,5},{5,4},{6,7},{7,6},{8,9},{9,8},{10,11... | collective-permute-start | bytes 196616 | tf_op jit(solution)/shard_map/ppermute | solution.py:53
  27.0 7.5 %collective-permute-start.9 = (bf16[8,8,1024]{2,1,0:T(8,128)(2,1)S(1)}, bf16[8,8,1024]{2,1,0:T(8,128)(2,1)}, u32[]{:S(2)}, u32[]{:S(2)}) collective-permute-start(bf16[8,8,1024]{2,1,0:T(8,128)(2,1)S(1)} %pad_maximum_fusion.1), channel_id=1, source_target_pairs={{0,2},{1,3},{2,0},{3,1},{4,6},{5,7},{6,4},{7,5},{8,10},{9,11},{10,... | collective-permute-start | bytes 393224 | tf_op jit(solution)/shard_map/ppermute | solution.py:53
  36.4 6.8 %copy-start.1 = (bf16[32,16,128]{2,1,0:T(8,128)(2,1)S(1)}, bf16[32,16,128]{2,1,0:T(8,128)(2,1)}, u32[]{:S(2)}) copy-start(bf16[32,16,128]{2,1,0:T(8,128)(2,1)} %gather_fusion.1) | copy-start | bytes 393220
  37.3 10.0 %copy-start.4 = (bf16[4,64,128]{2,1,0:T(8,128)(2,1)S(1)}, bf16[4,64,128]{2,1,0:T(8,128)(2,1)}, u32[]{:S(2)}) copy-start(bf16[4,64,128]{2,1,0:T(8,128)(2,1)} %param.13) | copy-start | bytes 196612
  37.3 10.3 %copy-start.2 = (f32[64,512]{1,0:T(8,128)S(1)}, f32[64,512]{1,0:T(8,128)}, u32[]{:S(2)}) copy-start(f32[64,512]{1,0:T(8,128)} %param.19) | copy-start | bytes 393220
  41.6 4.3 %collective-permute-start.10 = (f32[8,16,64]{2,1,0:T(8,128)S(1)}, f32[8,16,64]{2,1,0:T(8,128)S(1)}, u32[]{:S(2)}, u32[]{:S(2)}) collective-permute-start(f32[8,16,64]{2,1,0:T(8,128)S(1)} %dynamic-slice_bitcast_fusion), channel_id=1, source_target_pairs={{0,2},{1,3},{2,0},{3,1},{4,6},{5,7},{6,4},{7,5},{8,10},{9,11},{10,... | collective-permute-start | bytes 98312 | tf_op jit(solution)/shard_map/ppermute | solution.py:71
  46.0 1.3 %collective-permute-start.11 = (f32[4,16,64]{2,1,0:T(8,128)S(1)}, f32[4,16,64]{2,1,0:T(8,128)S(1)}, u32[]{:S(2)}, u32[]{:S(2)}) collective-permute-start(f32[4,16,64]{2,1,0:T(8,128)S(1)} %dynamic-slice_bitcast_fusion.1), channel_id=1, source_target_pairs={{0,1},{1,0},{2,3},{3,2},{4,5},{5,4},{6,7},{7,6},{8,9},{9,8},{10,11... | collective-permute-start | bytes 49160 | tf_op jit(solution)/shard_map/ppermute | solution.py:71
  47.9 1.2 %collective-permute-start.14 = (f32[80,16]{0,1:T(8,128)S(1)}, f32[80,16]{0,1:T(8,128)S(1)}, u32[]{:S(2)}, u32[]{:S(2)}) collective-permute-start(f32[80,16]{0,1:T(8,128)S(1)} %pad_maximum_fusion.4), channel_id=1, source_target_pairs={{0,1},{1,0},{2,3},{3,2},{4,5},{5,4},{6,7},{7,6},{8,9},{9,8},{10,11... | collective-permute-start | bytes 15368 | tf_op jit(solution)/shard_map/ppermute | solution.py:41
  49.1 3.7 %collective-permute-start.15 = (f32[80,16]{0,1:T(8,128)S(1)}, f32[80,16]{0,1:T(8,128)S(1)}, u32[]{:S(2)}, u32[]{:S(2)}) collective-permute-start(f32[80,16]{0,1:T(8,128)S(1)} %fusion.54), channel_id=1, source_target_pairs={{0,2},{1,3},{2,0},{3,1},{4,6},{5,7},{6,4},{7,5},{8,10},{9,11},{10,... | collective-permute-start | bytes 15368 | tf_op jit(solution)/shard_map/ppermute | solution.py:41
  52.8 3.7 %collective-permute-start.16 = (f32[80,16]{0,1:T(8,128)S(1)}, f32[80,16]{0,1:T(8,128)S(1)}, u32[]{:S(2)}, u32[]{:S(2)}) collective-permute-start(f32[80,16]{0,1:T(8,128)S(1)} %add.131), channel_id=1, source_target_pairs={{0,4},{1,5},{2,6},{3,7},{4,0},{5,1},{6,2},{7,3},{8,12},{9,13},{10,... | collective-permute-start | bytes 15368 | tf_op jit(solution)/shard_map/ppermute | solution.py:41
  56.5 3.7 %collective-permute-start.17 = (f32[80,16]{0,1:T(8,128)S(1)}, f32[80,16]{0,1:T(8,128)S(1)}, u32[]{:S(2)}, u32[]{:S(2)}) collective-permute-start(f32[80,16]{0,1:T(8,128)S(1)} %add.132), channel_id=1, source_target_pairs={{0,8},{1,9},{2,10},{3,11},{4,12},{5,13},{6,14},{7,15},{8,0},{9,1},... | collective-permute-start | bytes 15368 | tf_op jit(solution)/shard_map/ppermute | solution.py:41
  60.1 4.5 %collective-permute-start.18 = (f32[80,16]{0,1:T(8,128)S(1)}, f32[80,16]{0,1:T(8,128)S(1)}, u32[]{:S(2)}, u32[]{:S(2)}) collective-permute-start(f32[80,16]{0,1:T(8,128)S(1)} %add.133), channel_id=1, source_target_pairs={{0,16},{1,17},{2,18},{3,19},{4,20},{5,21},{6,22},{7,23},{8,24},{9,... | collective-permute-start | bytes 15368 | tf_op jit(solution)/shard_map/ppermute | solution.py:41
  64.7 4.4 %copy-start.3 = (f32[80,16]{0,1:T(8,128)}, f32[80,16]{0,1:T(8,128)S(1)}, u32[]{:S(2)}) copy-start(f32[80,16]{0,1:T(8,128)S(1)} %add.134) | copy-start | bytes 15364

commit v14 on v13

--- a/solution.py
+++ b/solution.py
@@ -1,3 +1,5 @@
+import functools
+
 import jax
 import jax.numpy as jnp
 from jax import lax
@@ -83,8 +85,7 @@
     return jnp.concatenate(pieces, axis=0)
 
 
-def chol_solve_kernel(gram_ref, residue_ref, chol_ref, block_ref):
-    left = gram_ref[...]
+def cholesky_and_solve(left, block):
     size = left.shape[0]
     rows = lax.broadcasted_iota(jnp.int32, left.shape, 0)
     cols = lax.broadcasted_iota(jnp.int32, left.shape, 1)
@@ -100,8 +101,6 @@
         low_row = jnp.where(col_ids >= step, row / root, 0.0)
         low = jnp.where(cols == step, low_column, low)
         left = left - low_column * low_row
-    chol_ref[...] = low
-    block = residue_ref[...]
     for step in range(size):
         low_column = jnp.sum(jnp.where(cols == step, low, 0.0), axis=1, keepdims=True)
         diagonal = jnp.sum(jnp.where(row_ids == step, low_column, 0.0), axis=0, keepdims=True)
@@ -109,6 +108,32 @@
         block = jnp.where(
             row_ids == step, solved, jnp.where(row_ids > step, block - low_column * solved, block)
         )
+    return low, block
+
+
+def chol_solve_kernel(gram_ref, residue_ref, chol_ref, block_ref):
+    low, block = cholesky_and_solve(gram_ref[...], residue_ref[...])
+    chol_ref[...] = low
+    block_ref[...] = block
+
+
+def fast_tail_kernel(scale, coeffs_ref, outer_ref, applied_ref, krylov_ref, chol_ref, block_ref, flag_ref):
+    highest = lax.Precision.HIGHEST
+    coeffs_t = coeffs_ref[...]
+    outer = outer_ref[...]
+    residue = applied_ref[...] - jnp.dot(coeffs_t, krylov_ref[...], precision=highest)
+    overlap = lax.dot_general(coeffs_t, coeffs_t, (((1,), (1,)), ((), ())), precision=highest)
+    short = outer - overlap
+    size = short.shape[0]
+    rows = lax.broadcasted_iota(jnp.int32, short.shape, 0)
+    cols = lax.broadcasted_iota(jnp.int32, short.shape, 1)
+    on_diagonal = rows == cols
+    short_diag = jnp.sum(jnp.where(on_diagonal, short, 0.0), axis=0, keepdims=True)
+    outer_diag = jnp.sum(jnp.where(on_diagonal, outer, 0.0), axis=0, keepdims=True)
+    failed = jnp.sum(jnp.where(short_diag * 64.0 >= outer_diag, 0.0, 1.0), axis=1, keepdims=True)
+    flag_ref[...] = jnp.broadcast_to(failed, flag_ref.shape)
+    low, block = cholesky_and_solve(short * scale, residue)
+    chol_ref[...] = low
     block_ref[...] = block
 
 
@@ -126,6 +151,26 @@
             flops=4 * size * size * (size + width), bytes_accessed=8 * size * (size + width), transcendentals=size
         ),
     )(gram_matrix, residue)
+
+
+def fast_tail(coeffs_t, outer, applied, krylov, scale):
+    size, width = applied.shape
+    vmem = pl.BlockSpec(memory_space=pltpu.VMEM)
+    return pl.pallas_call(
+        functools.partial(fast_tail_kernel, scale),
+        out_shape=(
+            jax.ShapeDtypeStruct((size, size), jnp.float32),
+            jax.ShapeDtypeStruct((size, width), jnp.float32),
+            jax.ShapeDtypeStruct((8, 128), jnp.float32),
+        ),
+        in_specs=[vmem] * 4,
+        out_specs=(vmem, vmem, vmem),
+        cost_estimate=pl.CostEstimate(
+            flops=4 * size * width * (size + krylov.shape[0]),
+            bytes_accessed=4 * (krylov.size + 3 * applied.size),
+            transcendentals=size,
+        ),
+    )(coeffs_t, outer, applied, krylov)
 
 
 def on_device(
@@ -193,17 +238,16 @@
     summed = butterfly_sum(jnp.concatenate([proj_part, self_part], axis=0), both_axes)
     coeffs = summed[:basis_count]
     outer = summed[basis_count:]
-    residue = applied - jnp.dot(coeffs.T, krylov, precision=highest)
-    short_gram = (outer - jnp.dot(coeffs.T, coeffs, precision=highest)) / total_points
-    eye = jnp.eye(vec_count, dtype=jnp.bool_)
-    short_diag = jnp.sum(jnp.where(eye, short_gram, 0.0), axis=0)
-    outer_diag = jnp.sum(jnp.where(eye, outer, 0.0), axis=0)
-    kept = short_diag * (64 * total_points) >= outer_diag
-    def exact_gram():
+    chol_fast, block_fast, failed = fast_tail(
+        coeffs.T, outer, applied, krylov, 1.0 / total_points
+    )
+    def exact_path():
+        residue = applied - jnp.dot(coeffs.T, krylov, precision=highest)
         part = jnp.dot(residue, residue.T, precision=highest)
-        return butterfly_sum(part, both_axes) / total_points
-    gram_matrix = lax.cond(jnp.all(kept), lambda: short_gram, exact_gram)
-    chol_factor, new_block = chol_solve(gram_matrix, residue)
+        return chol_solve(butterfly_sum(part, both_axes) / total_points, residue)
+    chol_factor, new_block = lax.cond(
+        failed[0, 0] > 0, exact_path, lambda: (chol_fast, block_fast)
+    )
     return (new_block, coeffs, chol_factor)
 
 

time: 69.5 us -> 73.2 us (1.053)
  local copies, waits for them, and re-layouts: 9.88 us -> 13 us
  other arithmetic: 6.59 us -> 4.52 us
  waiting for transfers between devices: 18.2 us -> 20 us
  Pallas kernels: 2.43 us -> 3.33 us
    slice x0 -> x3, local copies, waits for them, and re-layouts: none -> 1.85 us  [the longest x1 1.25 us: on_device(): failed[0, 0] > 0]
    ppermute x5, waiting for transfers between devices: 10.3 us -> 11.5 us  [butterfly_sum(): block = block + lax.ppermute(block, axes, route)]
    pallas_call x1, Pallas kernels: 2.43 us -> 3.33 us  [fast_tail(): pl.pallas_call(functools.partial(fast_tail_kernel, scale), out_shape=(jax...]
    unnamed x14 -> x13, local copies, waits for them, and re-layouts: 0.82 us -> 1.49 us
  transfers between devices with their start and end apart: 14 -> 14, of which waited for: 10 -> 10; matrix products, arithmetic and copies ran while one was open for 20% -> 17% of each run, Pallas kernels for 0% -> 0%
where the time goes in v14:
time: 73.2 us; the launch traced here: 72.7 us
  starting transfers between devices  22.8 us (31%)
  waiting for transfers between devices  20 us (27%)
  local copies, waits for them, and re-layouts  13 us (18%)
  matrix products  6.86 us (9%)
  other arithmetic  4.52 us (6%)
  Pallas kernels  3.33 us (5%)
  between operations  2.15 us (3%)
    ppermute x5, waiting for transfers between devices, butterfly_sum(): block = block + lax.ppermute(block, axes, route)  11.5 us
    ppermute x5, starting transfers between devices, xor_gather(): block = jnp.concatenate([block, lax.ppermute(block, axis, route)], axis=dim)  10.8 us
    ppermute x5, starting transfers between devices, butterfly_sum(): block = block + lax.ppermute(block, axes, route)  6.65 us
    reshape x1, local copies, waits for them, and re-layouts, on_device(): couple = coupling.reshape(3, group_size, slot_count, rank_width, rank_width)  5.65 us
    ppermute x5, waiting for transfers between devices, xor_gather(): block = jnp.concatenate([block, lax.ppermute(block, axis, route)], axis=dim)  5.59 us
    dot_general x1, matrix products, on_device(): jnp.einsum('cfvl,jcfkl->cfvjk', sources, couple, preferred_element_type=j...  4.25 us
    pallas_call x1, Pallas kernels, fast_tail(): pl.pallas_call(functools.partial(fast_tail_kernel, scale), out_shape=(jax...  3.33 us
    ppermute x2, waiting for transfers between devices, butterfly_scatter(): parts = keep + lax.ppermute(give, axis, route)  2.87 us
  transfers between devices with their start and end apart: 14, of which 10 were waited for; matrix products, arithmetic and copies ran while one was open for 17% of the time, Pallas kernels for 0%

profile of v14, /device:TPU:0, one launch (start us, length us, event | category | flops | bytes accessed | tf_op | source)
XLA Modules:
  0.0 72.7 jit_solution(15225197562936389714)
XLA Ops:
  1.6 2.5 %collective-permute-start.12 = (bf16[16,512]{1,0:T(8,128)(2,1)S(1)}, bf16[16,512]{1,0:T(8,128)(2,1)S(1)}, u32[]{:S(2)}, u32[]{:S(2)}) collective-permute-start(bf16[16,512]{1,0:T(8,128)(2,1)S(1)} %convert_element_type.23), channel_id=1, source_target_pairs={{0,1},{1,2},{2,3},{3,4},{4,5},{5,6},{6,7},{7,8},{8,9},{9,10},{10,1... | collective-permute-start | bytes 49160 | tf_op jit(solution)/shard_map/ppermute | solution.py:22
  4.1 1.3 %collective-permute-start.13 = (bf16[16,512]{1,0:T(8,128)(2,1)S(1)}, bf16[16,512]{1,0:T(8,128)(2,1)S(1)}, u32[]{:S(2)}, u32[]{:S(2)}) collective-permute-start(bf16[16,512]{1,0:T(8,128)(2,1)S(1)} %convert_element_type.23), channel_id=1, source_target_pairs={{1,0},{2,1},{3,2},{4,3},{5,4},{6,5},{7,6},{8,7},{9,8},{10,9},{11,1... | collective-permute-start | bytes 49160 | tf_op jit(solution)/shard_map/ppermute | solution.py:25
  6.5 5.8 %collective-permute-start.5 = (bf16[1,4,1024]{2,1,0:T(4,128)(2,1)S(1)}, bf16[1,4,1024]{2,1,0:T(4,128)(2,1)S(1)}, u32[]{:S(2)}, u32[]{:S(2)}) collective-permute-start(bf16[1,4,1024]{2,1,0:T(4,128)(2,1)S(1)} %reshape.121), channel_id=1, source_target_pairs={{0,4},{4,0},{8,12},{12,8},{16,20},{20,16},{24,28},{28,24},{1,5},{5... | collective-permute-start | bytes 24584 | tf_op jit(solution)/shard_map/ppermute | solution.py:55
  16.3 1.6 %collective-permute-start.6 = (bf16[2,4,1024]{2,1,0:T(4,128)(2,1)S(1)}, bf16[2,4,1024]{2,1,0:T(4,128)(2,1)S(1)}, u32[]{:S(2)}, u32[]{:S(2)}) collective-permute-start(bf16[2,4,1024]{2,1,0:T(4,128)(2,1)S(1)} %pad_maximum_fusion.3), channel_id=1, source_target_pairs={{0,8},{4,12},{8,0},{12,4},{16,24},{20,28},{24,16},{28,20},{1,9},{5... | collective-permute-start | bytes 49160 | tf_op jit(solution)/shard_map/ppermute | solution.py:55
  18.0 2.1 %collective-permute-done.6 = bf16[2,4,1024]{2,1,0:T(4,128)(2,1)S(1)} collective-permute-done((bf16[2,4,1024]{2,1,0:T(4,128)(2,1)S(1)}, bf16[2,4,1024]{2,1,0:T(4,128)(2,1)S(1)}, u32[]{:S(2)}, u32[]{:S(2)}) %collective-permute-start.6) | collective-permute-done | bytes 16416 | tf_op jit(solution)/shard_map/ppermute | solution.py:55
  20.1 2.7 %collective-permute-start.7 = (bf16[4,4,1024]{2,1,0:T(4,128)(2,1)S(1)}, bf16[4,4,1024]{2,1,0:T(4,128)(2,1)S(1)}, u32[]{:S(2)}, u32[]{:S(2)}) collective-permute-start(bf16[4,4,1024]{2,1,0:T(4,128)(2,1)S(1)} %pad_maximum_fusion.2), channel_id=1, source_target_pairs={{0,16},{4,20},{8,24},{12,28},{16,0},{20,4},{24,8},{28,12},{1,17},{... | collective-permute-start | bytes 98312 | tf_op jit(solution)/shard_map/ppermute | solution.py:55
  22.8 2.2 %collective-permute-done.7 = bf16[4,4,1024]{2,1,0:T(4,128)(2,1)S(1)} collective-permute-done((bf16[4,4,1024]{2,1,0:T(4,128)(2,1)S(1)}, bf16[4,4,1024]{2,1,0:T(4,128)(2,1)S(1)}, u32[]{:S(2)}, u32[]{:S(2)}) %collective-permute-start.7) | collective-permute-done | bytes 32800 | tf_op jit(solution)/shard_map/ppermute | solution.py:55
  25.1 1.2 %collective-permute-done.8 = bf16[8,4,1024]{2,1,0:T(4,128)(2,1)S(1)} collective-permute-done((bf16[8,4,1024]{2,1,0:T(4,128)(2,1)S(1)}, bf16[8,4,1024]{2,1,0:T(4,128)(2,1)S(1)}, u32[]{:S(2)}, u32[]{:S(2)}) %collective-permute-start.8) | collective-permute-done | bytes 65568 | tf_op jit(solution)/shard_map/ppermute | solution.py:55
  27.1 5.6 %reshape.125 = bf16[3,16,4,64,64]{4,3,2,1,0:T(8,128)(2,1)} reshape(bf16[3,16,4,4096]{3,2,1,0:T(4,128)(2,1)} %param.16) | data formatting | bytes 3145728 | tf_op jit(solution)/shard_map/reshape | solution.py:215
  32.8 1.2 %gather_fusion.1 = bf16[32,16,128]{2,1,0:T(8,128)(2,1)} fusion(bf16[16,12,128]{2,0,1:T(8,128)(2,1)S(1)} %copy_bitcast_fusion, s32[1024]{0:T(1024)S(1)} %pad_clamp_fusion), kind=kCustom, calls=%fused_computation.1 | custom fusion | bytes 262272 | tf_op jit(solution)/shard_map/gather | solution.py:226
  34.0 1.0 %pad_maximum_fusion = bf16[8,16,1024]{2,1,0:T(8,128)(2,1)S(1)} fusion(bf16[8,8,1024]{2,1,0:T(8,128)(2,1)} %collective-permute-done.9, bf16[8,4,1024]{2,1,0:T(4,128)(2,1)S(1)} %collective-permute-done.8, bf16[8,4,1024]{2,1,0:T(4,128)(2,1)S(1)} %constant_dynamic-update-slice_fusion), kind=kLoop, calls=%fused_computation.15 | loop fusion | flops 786432 | bytes 524288 | tf_op jit(solution)/shard_map/concatenate | solution.py:55
  36.6 4.3 %multiply_reduce_fusion = f32[16,16,64]{2,1,0:T(8,128)S(1)} fusion(bf16[3,16,4,64,64]{4,3,2,1,0:T(8,128)(2,1)} %reshape.125, f32[16,4,3,64]{3,2,1,0:T(4,128)} %broadcast_multiply_fusion, bf16[16,4,16,64]{3,2,1,0:T(8,128)(2,1)} %reshape.124, pred[16,4,64]{2,1,0:T(4,128)(4,1)S(1)} %get-tuple-element.46), kind=kOutput, calls=%fused_computation.8 | convolution fusion | flops 25608192 | bytes 1822720 | tf_op jit(solution)/shard_map/cfvl,jcfkl->cfvjk/dot_general | solution.py:216
  40.9 1.5 %collective-permute-start.10 = (f32[8,16,64]{2,1,0:T(8,128)S(1)}, f32[8,16,64]{2,1,0:T(8,128)S(1)}, u32[]{:S(2)}, u32[]{:S(2)}) collective-permute-start(f32[8,16,64]{2,1,0:T(8,128)S(1)} %dynamic-slice_bitcast_fusion), channel_id=1, source_target_pairs={{0,2},{1,3},{2,0},{3,1},{4,6},{5,7},{6,4},{7,5},{8,10},{9,11},{10,... | collective-permute-start | bytes 98312 | tf_op jit(solution)/shard_map/ppermute | solution.py:73
  43.3 1.9 %collective-permute-done.10 = f32[8,16,64]{2,1,0:T(8,128)S(1)} collective-permute-done((f32[8,16,64]{2,1,0:T(8,128)S(1)}, f32[8,16,64]{2,1,0:T(8,128)S(1)}, u32[]{:S(2)}, u32[]{:S(2)}) %collective-permute-start.10) | collective-permute-done | bytes 32800 | tf_op jit(solution)/shard_map/ppermute | solution.py:73
  47.5 1.1 %collective-permute-done.14 = f32[80,16]{1,0:T(8,128)S(1)} collective-permute-done((f32[80,16]{1,0:T(8,128)S(1)}, f32[80,16]{1,0:T(8,128)S(1)}, u32[]{:S(2)}, u32[]{:S(2)}) %collective-permute-start.14) | collective-permute-done | bytes 5152 | tf_op jit(solution)/shard_map/ppermute | solution.py:43
  48.6 1.4 %collective-permute-start.15 = (f32[80,16]{1,0:T(8,128)S(1)}, f32[80,16]{1,0:T(8,128)S(1)}, u32[]{:S(2)}, u32[]{:S(2)}) collective-permute-start(f32[80,16]{1,0:T(8,128)S(1)} %add.130), channel_id=1, source_target_pairs={{0,2},{1,3},{2,0},{3,1},{4,6},{5,7},{6,4},{7,5},{8,10},{9,11},{10,... | collective-permute-start | bytes 15368 | tf_op jit(solution)/shard_map/ppermute | solution.py:43
  50.0 2.6 %collective-permute-done.15 = f32[80,16]{1,0:T(8,128)S(1)} collective-permute-done((f32[80,16]{1,0:T(8,128)S(1)}, f32[80,16]{1,0:T(8,128)S(1)}, u32[]{:S(2)}, u32[]{:S(2)}) %collective-permute-start.15) | collective-permute-done | bytes 5152 | tf_op jit(solution)/shard_map/ppermute | solution.py:43
  53.1 3.4 %collective-permute-done.16 = f32[80,16]{1,0:T(8,128)S(1)} collective-permute-done((f32[80,16]{1,0:T(8,128)S(1)}, f32[80,16]{1,0:T(8,128)S(1)}, u32[]{:S(2)}, u32[]{:S(2)}) %collective-permute-start.16) | collective-permute-done | bytes 5152 | tf_op jit(solution)/shard_map/ppermute | solution.py:43
  56.6 1.6 %collective-permute-start.17 = (f32[80,16]{1,0:T(8,128)S(1)}, f32[80,16]{1,0:T(8,128)S(1)}, u32[]{:S(2)}, u32[]{:S(2)}) collective-permute-start(f32[80,16]{1,0:T(8,128)S(1)} %add.132), channel_id=1, source_target_pairs={{0,8},{1,9},{2,10},{3,11},{4,12},{5,13},{6,14},{7,15},{8,0},{9,1},... | collective-permute-start | bytes 15368 | tf_op jit(solution)/shard_map/ppermute | solution.py:43
  58.2 2.4 %collective-permute-done.17 = f32[80,16]{1,0:T(8,128)S(1)} collective-permute-done((f32[80,16]{1,0:T(8,128)S(1)}, f32[80,16]{1,0:T(8,128)S(1)}, u32[]{:S(2)}, u32[]{:S(2)}) %collective-permute-start.17) | collective-permute-done | bytes 5152 | tf_op jit(solution)/shard_map/ppermute | solution.py:43
  60.6 2.9 %collective-permute-start.18 = (f32[80,16]{1,0:T(8,128)S(1)}, f32[80,16]{1,0:T(8,128)S(1)}, u32[]{:S(2)}, u32[]{:S(2)}) collective-permute-start(f32[80,16]{1,0:T(8,128)S(1)} %add.133), channel_id=1, source_target_pairs={{0,16},{1,17},{2,18},{3,19},{4,20},{5,21},{6,22},{7,23},{8,24},{9,... | collective-permute-start | bytes 15368 | tf_op jit(solution)/shard_map/ppermute | solution.py:43
  63.4 2.0 %collective-permute-done.18 = f32[80,16]{1,0:T(8,128)S(1)} collective-permute-done((f32[80,16]{1,0:T(8,128)S(1)}, f32[80,16]{1,0:T(8,128)S(1)}, u32[]{:S(2)}, u32[]{:S(2)}) %collective-permute-start.18) | collective-permute-done | bytes 5152 | tf_op jit(solution)/shard_map/ppermute | solution.py:43
  67.4 3.3 %shard_map.112 = (f32[16,16]{1,0:T(8,128)}, f32[16,512]{1,0:T(8,128)}, f32[8,128]{1,0:T(8,128)}) custom-call(f32[16,64]{1,0:T(8,128)} %copy.42.coeffs_ref, f32[16,16]{1,0:T(8,128)} %slice.17.outer_ref, f32[16,512]{1,0:T(8,128)S(1)} %copy_bitcast_fusion.1.applied_ref, f32[64,512]{1,0:T(8,128)S(1)} %copy-done.1), custom_call_target="tpu_custom_call" | custom-call | flops 2621440 | bytes 229376 | tf_op jit(solution)/shard_map/pallas_call | solution.py:159
  70.8 1.3 %slice.11 = f32[1,1]{1,0:T(1,128)} slice(f32[8,128]{1,0:T(8,128)} %get-tuple-element.21), slice={[0:1], [0:1]} | slice | bytes 8 | tf_op jit(solution)/shard_map/slice | solution.py:249
  (65 shorter events, 13.5 us)
Async XLA Ops:
  0.6 41.8 %copy-start = (bf16[3,4,8,128,128]{4,3,2,1,0:T(8,128)(2,1)S(1)}, bf16[3,4,8,128,128]{4,3,2,1,0:T(8,128)(2,1)}, u32[]{:S(2)}) copy-start(bf16[3,4,8,128,128]{4,3,2,1,0:T(8,128)(2,1)} %param.14) | copy-start | bytes 9437188
  1.6 31.2 %collective-permute-start.12 = (bf16[16,512]{1,0:T(8,128)(2,1)S(1)}, bf16[16,512]{1,0:T(8,128)(2,1)S(1)}, u32[]{:S(2)}, u32[]{:S(2)}) collective-permute-start(bf16[16,512]{1,0:T(8,128)(2,1)S(1)} %convert_element_type.23), channel_id=1, source_target_pairs={{0,1},{1,2},{2,3},{3,4},{4,5},{5,6},{6,7},{7,8},{8,9},{9,10},{10,1... | collective-permute-start | bytes 49160 | tf_op jit(solution)/shard_map/ppermute | solution.py:22
  4.1 28.7 %collective-permute-start.13 = (bf16[16,512]{1,0:T(8,128)(2,1)S(1)}, bf16[16,512]{1,0:T(8,128)(2,1)S(1)}, u32[]{:S(2)}, u32[]{:S(2)}) collective-permute-start(bf16[16,512]{1,0:T(8,128)(2,1)S(1)} %convert_element_type.23), channel_id=1, source_target_pairs={{1,0},{2,1},{3,2},{4,3},{5,4},{6,5},{7,6},{8,7},{9,8},{10,9},{11,1... | collective-permute-start | bytes 49160 | tf_op jit(solution)/shard_map/ppermute | solution.py:25
  6.5 9.8 %collective-permute-start.5 = (bf16[1,4,1024]{2,1,0:T(4,128)(2,1)S(1)}, bf16[1,4,1024]{2,1,0:T(4,128)(2,1)S(1)}, u32[]{:S(2)}, u32[]{:S(2)}) collective-permute-start(bf16[1,4,1024]{2,1,0:T(4,128)(2,1)S(1)} %reshape.121), channel_id=1, source_target_pairs={{0,4},{4,0},{8,12},{12,8},{16,20},{20,16},{24,28},{28,24},{1,5},{5... | collective-permute-start | bytes 24584 | tf_op jit(solution)/shard_map/ppermute | solution.py:55
  16.3 3.8 %collective-permute-start.6 = (bf16[2,4,1024]{2,1,0:T(4,128)(2,1)S(1)}, bf16[2,4,1024]{2,1,0:T(4,128)(2,1)S(1)}, u32[]{:S(2)}, u32[]{:S(2)}) collective-permute-start(bf16[2,4,1024]{2,1,0:T(4,128)(2,1)S(1)} %pad_maximum_fusion.3), channel_id=1, source_target_pairs={{0,8},{4,12},{8,0},{12,4},{16,24},{20,28},{24,16},{28,20},{1,9},{5... | collective-permute-start | bytes 49160 | tf_op jit(solution)/shard_map/ppermute | solution.py:55
  20.1 4.9 %collective-permute-start.7 = (bf16[4,4,1024]{2,1,0:T(4,128)(2,1)S(1)}, bf16[4,4,1024]{2,1,0:T(4,128)(2,1)S(1)}, u32[]{:S(2)}, u32[]{:S(2)}) collective-permute-start(bf16[4,4,1024]{2,1,0:T(4,128)(2,1)S(1)} %pad_maximum_fusion.2), channel_id=1, source_target_pairs={{0,16},{4,20},{8,24},{12,28},{16,0},{20,4},{24,8},{28,12},{1,17},{... | collective-permute-start | bytes 98312 | tf_op jit(solution)/shard_map/ppermute | solution.py:55
  25.0 1.3 %collective-permute-start.8 = (bf16[8,4,1024]{2,1,0:T(4,128)(2,1)S(1)}, bf16[8,4,1024]{2,1,0:T(4,128)(2,1)S(1)}, u32[]{:S(2)}, u32[]{:S(2)}) collective-permute-start(bf16[8,4,1024]{2,1,0:T(4,128)(2,1)S(1)} %constant_dynamic-update-slice_fusion), channel_id=1, source_target_pairs={{0,1},{1,0},{2,3},{3,2},{4,5},{5,4},{6,7},{7,6},{8,9},{9,8},{10,11... | collective-permute-start | bytes 196616 | tf_op jit(solution)/shard_map/ppermute | solution.py:55
  26.4 7.6 %collective-permute-start.9 = (bf16[8,8,1024]{2,1,0:T(8,128)(2,1)S(1)}, bf16[8,8,1024]{2,1,0:T(8,128)(2,1)}, u32[]{:S(2)}, u32[]{:S(2)}) collective-permute-start(bf16[8,8,1024]{2,1,0:T(8,128)(2,1)S(1)} %pad_maximum_fusion.1), channel_id=1, source_target_pairs={{0,2},{1,3},{2,0},{3,1},{4,6},{5,7},{6,4},{7,5},{8,10},{9,11},{10,... | collective-permute-start | bytes 393224 | tf_op jit(solution)/shard_map/ppermute | solution.py:55
  35.7 6.7 %copy-start.2 = (bf16[32,16,128]{2,1,0:T(8,128)(2,1)S(1)}, bf16[32,16,128]{2,1,0:T(8,128)(2,1)}, u32[]{:S(2)}) copy-start(bf16[32,16,128]{2,1,0:T(8,128)(2,1)} %gather_fusion.1) | copy-start | bytes 393220
  36.6 9.9 %copy-start.4 = (bf16[4,64,128]{2,1,0:T(8,128)(2,1)S(1)}, bf16[4,64,128]{2,1,0:T(8,128)(2,1)}, u32[]{:S(2)}) copy-start(bf16[4,64,128]{2,1,0:T(8,128)(2,1)} %param.13) | copy-start | bytes 196612
  36.6 10.2 %copy-start.1 = (f32[64,512]{1,0:T(8,128)S(1)}, f32[64,512]{1,0:T(8,128)}, u32[]{:S(2)}) copy-start(f32[64,512]{1,0:T(8,128)} %krylov_ref.1) | copy-start | bytes 393220
  40.9 4.3 %collective-permute-start.10 = (f32[8,16,64]{2,1,0:T(8,128)S(1)}, f32[8,16,64]{2,1,0:T(8,128)S(1)}, u32[]{:S(2)}, u32[]{:S(2)}) collective-permute-start(f32[8,16,64]{2,1,0:T(8,128)S(1)} %dynamic-slice_bitcast_fusion), channel_id=1, source_target_pairs={{0,2},{1,3},{2,0},{3,1},{4,6},{5,7},{6,4},{7,5},{8,10},{9,11},{10,... | collective-permute-start | bytes 98312 | tf_op jit(solution)/shard_map/ppermute | solution.py:73
  45.3 1.3 %collective-permute-start.11 = (f32[4,16,64]{2,1,0:T(8,128)S(1)}, f32[4,16,64]{2,1,0:T(8,128)S(1)}, u32[]{:S(2)}, u32[]{:S(2)}) collective-permute-start(f32[4,16,64]{2,1,0:T(8,128)S(1)} %dynamic-slice_bitcast_fusion.1), channel_id=1, source_target_pairs={{0,1},{1,0},{2,3},{3,2},{4,5},{5,4},{6,7},{7,6},{8,9},{9,8},{10,11... | collective-permute-start | bytes 49160 | tf_op jit(solution)/shard_map/ppermute | solution.py:73
  47.3 1.3 %collective-permute-start.14 = (f32[80,16]{1,0:T(8,128)S(1)}, f32[80,16]{1,0:T(8,128)S(1)}, u32[]{:S(2)}, u32[]{:S(2)}) collective-permute-start(f32[80,16]{1,0:T(8,128)S(1)} %copy.41), channel_id=1, source_target_pairs={{0,1},{1,0},{2,3},{3,2},{4,5},{5,4},{6,7},{7,6},{8,9},{9,8},{10,11... | collective-permute-start | bytes 15368 | tf_op jit(solution)/shard_map/ppermute | solution.py:43
  48.6 4.0 %collective-permute-start.15 = (f32[80,16]{1,0:T(8,128)S(1)}, f32[80,16]{1,0:T(8,128)S(1)}, u32[]{:S(2)}, u32[]{:S(2)}) collective-permute-start(f32[80,16]{1,0:T(8,128)S(1)} %add.130), channel_id=1, source_target_pairs={{0,2},{1,3},{2,0},{3,1},{4,6},{5,7},{6,4},{7,5},{8,10},{9,11},{10,... | collective-permute-start | bytes 15368 | tf_op jit(solution)/shard_map/ppermute | solution.py:43
  52.6 4.0 %collective-permute-start.16 = (f32[80,16]{1,0:T(8,128)S(1)}, f32[80,16]{1,0:T(8,128)S(1)}, u32[]{:S(2)}, u32[]{:S(2)}) collective-permute-start(f32[80,16]{1,0:T(8,128)S(1)} %add.131), channel_id=1, source_target_pairs={{0,4},{1,5},{2,6},{3,7},{4,0},{5,1},{6,2},{7,3},{8,12},{9,13},{10,... | collective-permute-start | bytes 15368 | tf_op jit(solution)/shard_map/ppermute | solution.py:43
  56.6 4.0 %collective-permute-start.17 = (f32[80,16]{1,0:T(8,128)S(1)}, f32[80,16]{1,0:T(8,128)S(1)}, u32[]{:S(2)}, u32[]{:S(2)}) collective-permute-start(f32[80,16]{1,0:T(8,128)S(1)} %add.132), channel_id=1, source_target_pairs={{0,8},{1,9},{2,10},{3,11},{4,12},{5,13},{6,14},{7,15},{8,0},{9,1},... | collective-permute-start | bytes 15368 | tf_op jit(solution)/shard_map/ppermute | solution.py:43
  60.6 4.9 %collective-permute-start.18 = (f32[80,16]{1,0:T(8,128)S(1)}, f32[80,16]{1,0:T(8,128)S(1)}, u32[]{:S(2)}, u32[]{:S(2)}) collective-permute-start(f32[80,16]{1,0:T(8,128)S(1)} %add.133), channel_id=1, source_target_pairs={{0,16},{1,17},{2,18},{3,19},{4,20},{5,21},{6,22},{7,23},{8,24},{9,... | collective-permute-start | bytes 15368 | tf_op jit(solution)/shard_map/ppermute | solution.py:43

commit v15 on v13

--- a/solution.py
+++ b/solution.py
@@ -47,12 +47,22 @@
     count = lax.axis_size(axis)
     if not is_power_of_two(count):
         return lax.all_gather(block, axis, axis=dim, tiled=True), False
-    distance = 1
-    while distance < count:
+    distance = count // 2
+    while distance >= 1:
         route = [(i, i ^ distance) for i in range(count)]
         block = jnp.concatenate([block, lax.ppermute(block, axis, route)], axis=dim)
-        distance *= 2
+        distance //= 2
     return block, True
+
+
+def xor_position(difference, count):
+    position = jnp.zeros_like(difference)
+    distance, place = count // 2, 1
+    while distance >= 1:
+        position = position + ((difference // distance) % 2) * place
+        distance //= 2
+        place *= 2
+    return position
 
 
 def butterfly_scatter(block, axis):
@@ -155,9 +165,9 @@
     source_group = far_list // group_size
     source_holder = (far_list % group_size) // local_count
     if leaf_xor:
-        source_group = source_group ^ lax.axis_index("leaf")
+        source_group = xor_position(source_group ^ lax.axis_index("leaf"), leaf_count)
     if coef_xor:
-        source_holder = source_holder ^ lax.axis_index("coef")
+        source_holder = xor_position(source_holder ^ lax.axis_index("coef"), coef_count)
     local_ids = (
         source_group * group_size + source_holder * local_count + far_list % local_count
     ).reshape(-1)

time: 69.5 us -> 73.3 us (1.055)
  waiting for transfers between devices: 18.2 us -> 27.5 us
  starting transfers between devices: 22.5 us -> 16.9 us
    ppermute x5, waiting for transfers between devices: 5.01 us -> 9.09 us  [xor_gather(): block = jnp.concatenate([block, lax.ppermute(block, axis, route)], axis=dim)]
    ppermute x5, starting transfers between devices: 6.35 us -> 2.68 us  [butterfly_sum(): block = block + lax.ppermute(block, axes, route)]
    ppermute x5, waiting for transfers between devices: 10.3 us -> 14 us  [butterfly_sum(): block = block + lax.ppermute(block, axes, route)]
    ppermute x2, waiting for transfers between devices: 2.87 us -> 4.44 us  [butterfly_scatter(): parts = keep + lax.ppermute(give, axis, route)]
    ppermute x2, starting transfers between devices: 1.57 us -> 0.14 us  [butterfly_scatter(): parts = keep + lax.ppermute(give, axis, route)]
  transfers between devices with their start and end apart: 14 -> 14, of which waited for: 10 -> 10; matrix products, arithmetic and copies ran while one was open for 20% -> 19% of each run, Pallas kernels for 0% -> 0%
where the time goes in v15:
time: 73.3 us; the launch traced here: 72.9 us
  waiting for transfers between devices  27.5 us (38%)
  starting transfers between devices  16.9 us (23%)
  local copies, waits for them, and re-layouts  9.89 us (13%)
  matrix products  7.35 us (10%)
  other arithmetic  6.6 us (9%)
  Pallas kernels  2.43 us (3%)
  between operations  2.18 us (3%)
    ppermute x5, waiting for transfers between devices, butterfly_sum(): block = block + lax.ppermute(block, axes, route)  14 us
    ppermute x5, starting transfers between devices, xor_gather(): block = jnp.concatenate([block, lax.ppermute(block, axis, route)], axis=dim)  10.2 us
    ppermute x5, waiting for transfers between devices, xor_gather(): block = jnp.concatenate([block, lax.ppermute(block, axis, route)], axis=dim)  9.09 us
    reshape x1, local copies, waits for them, and re-layouts, on_device(): couple = coupling.reshape(3, group_size, slot_count, rank_width, rank_width)  5.64 us
    ppermute x2, waiting for transfers between devices, butterfly_scatter(): parts = keep + lax.ppermute(give, axis, route)  4.44 us
    dot_general x1, matrix products, on_device(): jnp.einsum('cfvl,jcfkl->cfvjk', sources, couple, preferred_element_type=j...  4.31 us
    ppermute x5, starting transfers between devices, butterfly_sum(): block = block + lax.ppermute(block, axes, route)  2.68 us
    ppermute x1, starting transfers between devices, extended_2(): lax.ppermute(lax.slice_in_dim(block, block.shape[dim] - width, None, axis...  2.52 us
  transfers between devices with their start and end apart: 14, of which 10 were waited for; matrix products, arithmetic and copies ran while one was open for 19% of the time, Pallas kernels for 0%

profile of v15, /device:TPU:0, one launch (start us, length us, event | category | flops | bytes accessed | tf_op | source)
XLA Modules:
  0.0 72.9 jit_solution(5564366457286948604)
XLA Ops:
  0.6 0.9 %convert_element_type.20 = bf16[16,512]{1,0:T(8,128)(2,1)S(1)} convert(f32[16,512]{1,0:T(8,128)} %param.11) | non-fusion elementwise | flops 8192 | bytes 49152 | tf_op jit(solution)/shard_map/convert_element_type | solution.py:156
  1.6 2.5 %collective-permute-start.12 = (bf16[16,512]{1,0:T(8,128)(2,1)S(1)}, bf16[16,512]{1,0:T(8,128)(2,1)S(1)}, u32[]{:S(2)}, u32[]{:S(2)}) collective-permute-start(bf16[16,512]{1,0:T(8,128)(2,1)S(1)} %convert_element_type.20), channel_id=1, source_target_pairs={{0,1},{1,2},{2,3},{3,4},{4,5},{5,6},{6,7},{7,8},{8,9},{9,10},{10,1... | collective-permute-start | bytes 49160 | tf_op jit(solution)/shard_map/ppermute | solution.py:20
  4.1 1.3 %collective-permute-start.13 = (bf16[16,512]{1,0:T(8,128)(2,1)S(1)}, bf16[16,512]{1,0:T(8,128)(2,1)S(1)}, u32[]{:S(2)}, u32[]{:S(2)}) collective-permute-start(bf16[16,512]{1,0:T(8,128)(2,1)S(1)} %convert_element_type.20), channel_id=1, source_target_pairs={{1,0},{2,1},{3,2},{4,3},{5,4},{6,5},{7,6},{8,7},{9,8},{10,9},{11,1... | collective-permute-start | bytes 49160 | tf_op jit(solution)/shard_map/ppermute | solution.py:23
  5.4 1.0 %convolution_convert_fusion = bf16[4,16,64]{2,1,0:T(8,128)(2,1)S(1)} fusion(bf16[4,64,128]{2,1,0:T(8,128)(2,1)} %param.13, f32[16,512]{1,0:T(8,128)} %param.11), kind=kOutput, calls=%fused_computation.11 | convolution fusion | flops 1060864 | bytes 106496 | tf_op jit(solution)/shard_map/cki,vci->cvk/dot_general | solution.py:158
  6.5 7.7 %collective-permute-start.5 = (bf16[1,4,1024]{2,1,0:T(4,128)(2,1)S(1)}, bf16[1,4,1024]{2,1,0:T(4,128)(2,1)S(1)}, u32[]{:S(2)}, u32[]{:S(2)}) collective-permute-start(bf16[1,4,1024]{2,1,0:T(4,128)(2,1)S(1)} %reshape.117), channel_id=1, source_target_pairs={{0,16},{4,20},{8,24},{12,28},{16,0},{20,4},{24,8},{28,12},{1,17},{... | collective-permute-start | bytes 24584 | tf_op jit(solution)/shard_map/ppermute | solution.py:53
  18.9 1.6 %collective-permute-start.6 = (bf16[2,4,1024]{2,1,0:T(4,128)(2,1)S(1)}, bf16[2,4,1024]{2,1,0:T(4,128)(2,1)S(1)}, u32[]{:S(2)}, u32[]{:S(2)}) collective-permute-start(bf16[2,4,1024]{2,1,0:T(4,128)(2,1)S(1)} %pad_maximum_fusion.3), channel_id=1, source_target_pairs={{0,8},{4,12},{8,0},{12,4},{16,24},{20,28},{24,16},{28,20},{1,9},{5... | collective-permute-start | bytes 49160 | tf_op jit(solution)/shard_map/ppermute | solution.py:53
  20.5 2.1 %collective-permute-done.6 = bf16[2,4,1024]{2,1,0:T(4,128)(2,1)S(1)} collective-permute-done((bf16[2,4,1024]{2,1,0:T(4,128)(2,1)S(1)}, bf16[2,4,1024]{2,1,0:T(4,128)(2,1)S(1)}, u32[]{:S(2)}, u32[]{:S(2)}) %collective-permute-start.6) | collective-permute-done | bytes 16416 | tf_op jit(solution)/shard_map/ppermute | solution.py:53
  23.4 3.3 %collective-permute-done.7 = bf16[4,4,1024]{2,1,0:T(4,128)(2,1)S(1)} collective-permute-done((bf16[4,4,1024]{2,1,0:T(4,128)(2,1)S(1)}, bf16[4,4,1024]{2,1,0:T(4,128)(2,1)S(1)}, u32[]{:S(2)}, u32[]{:S(2)}) %collective-permute-start.7) | collective-permute-done | bytes 32800 | tf_op jit(solution)/shard_map/ppermute | solution.py:53
  27.4 3.7 %collective-permute-done.8 = bf16[8,4,1024]{2,1,0:T(4,128)(2,1)S(1)} collective-permute-done((bf16[8,4,1024]{2,1,0:T(4,128)(2,1)S(1)}, bf16[8,4,1024]{2,1,0:T(4,128)(2,1)S(1)}, u32[]{:S(2)}, u32[]{:S(2)}) %collective-permute-start.8) | collective-permute-done | bytes 65568 | tf_op jit(solution)/shard_map/ppermute | solution.py:53
  31.2 5.6 %reshape.121 = bf16[3,16,4,64,64]{4,3,2,1,0:T(8,128)(2,1)} reshape(bf16[3,16,4,4096]{3,2,1,0:T(4,128)(2,1)} %param.16) | data formatting | bytes 3145728 | tf_op jit(solution)/shard_map/reshape | solution.py:180
  36.9 1.2 %gather_fusion.1 = bf16[32,16,128]{2,1,0:T(8,128)(2,1)} fusion(bf16[16,12,128]{2,0,1:T(8,128)(2,1)S(1)} %copy_bitcast_fusion, s32[1024]{0:T(1024)S(1)} %pad_clamp_fusion), kind=kCustom, calls=%fused_computation.1 | custom fusion | bytes 262272 | tf_op jit(solution)/shard_map/gather | solution.py:191
  38.1 1.0 %pad_maximum_fusion = bf16[8,16,1024]{2,1,0:T(8,128)(2,1)S(1)} fusion(bf16[8,8,1024]{2,1,0:T(8,128)(2,1)} %collective-permute-done.9, bf16[8,4,1024]{2,1,0:T(4,128)(2,1)S(1)} %collective-permute-done.8, bf16[8,4,1024]{2,1,0:T(4,128)(2,1)S(1)} %constant_dynamic-update-slice_fusion), kind=kLoop, calls=%fused_computation.16 | loop fusion | flops 786432 | bytes 524288 | tf_op jit(solution)/shard_map/concatenate | solution.py:53
  40.0 0.9 %reshape.120 = bf16[16,4,16,64]{3,2,1,0:T(8,128)(2,1)} reshape(bf16[64,1024]{1,0:T(8,128)(2,1)S(1)} %gather_fusion) | data formatting | bytes 262144 | tf_op jit(solution)/shard_map/reshape | solution.py:174
  40.9 4.3 %multiply_reduce_fusion = f32[16,16,64]{2,1,0:T(8,128)S(1)} fusion(bf16[3,16,4,64,64]{4,3,2,1,0:T(8,128)(2,1)} %reshape.121, f32[16,4,3,64]{3,2,1,0:T(4,128)} %broadcast_multiply_fusion, bf16[16,4,16,64]{3,2,1,0:T(8,128)(2,1)} %reshape.120, pred[16,4,64]{2,1,0:T(4,128)(4,1)} %get-tuple-element.14), kind=kOutput, calls=%fused_computation.7 | convolution fusion | flops 25608192 | bytes 1822720 | tf_op jit(solution)/shard_map/cfvl,jcfkl->cfvjk/dot_general | solution.py:181
  45.3 0.9 %fusion = bf16[4,16,3,128,1]{3,1,4,2,0:T(8,128)(2,1)S(1)} fusion(bf16[16,4,8,128,1]{3,0,2,4,1:T(8,128)(2,1)S(1)} %bitcast.95, bf16[3,4,8,128,128]{4,3,2,1,0:T(8,128)(2,1)S(1)} %copy-done), kind=kOutput, calls=%fused_computation.3 | convolution fusion | flops 50331648 | bytes 3325952 | tf_op jit(solution)/shard_map/jcnil,vcnl->jvci/dot_general | solution.py:194
  46.2 3.5 %collective-permute-done.10 = f32[8,16,64]{2,1,0:T(8,128)S(1)} collective-permute-done((f32[8,16,64]{2,1,0:T(8,128)S(1)}, f32[8,16,64]{2,1,0:T(8,128)S(1)}, u32[]{:S(2)}, u32[]{:S(2)}) %collective-permute-start.10) | collective-permute-done | bytes 32800 | tf_op jit(solution)/shard_map/ppermute | solution.py:81
  50.1 1.0 %collective-permute-done.11 = f32[4,16,64]{2,1,0:T(8,128)S(1)} collective-permute-done((f32[4,16,64]{2,1,0:T(8,128)S(1)}, f32[4,16,64]{2,1,0:T(8,128)S(1)}, u32[]{:S(2)}, u32[]{:S(2)}) %collective-permute-start.11) | collective-permute-done | bytes 16416 | tf_op jit(solution)/shard_map/ppermute | solution.py:81
  51.8 1.0 %collective-permute-done.14 = f32[80,16]{0,1:T(8,128)S(1)} collective-permute-done((f32[80,16]{0,1:T(8,128)S(1)}, f32[80,16]{0,1:T(8,128)S(1)}, u32[]{:S(2)}, u32[]{:S(2)}) %collective-permute-start.14) | collective-permute-done | bytes 5152 | tf_op jit(solution)/shard_map/ppermute | solution.py:41
  53.2 3.4 %collective-permute-done.15 = f32[80,16]{0,1:T(8,128)S(1)} collective-permute-done((f32[80,16]{0,1:T(8,128)S(1)}, f32[80,16]{0,1:T(8,128)S(1)}, u32[]{:S(2)}, u32[]{:S(2)}) %collective-permute-start.15) | collective-permute-done | bytes 5152 | tf_op jit(solution)/shard_map/ppermute | solution.py:41
  57.2 3.0 %collective-permute-done.16 = f32[80,16]{0,1:T(8,128)S(1)} collective-permute-done((f32[80,16]{0,1:T(8,128)S(1)}, f32[80,16]{0,1:T(8,128)S(1)}, u32[]{:S(2)}, u32[]{:S(2)}) %collective-permute-start.16) | collective-permute-done | bytes 5152 | tf_op jit(solution)/shard_map/ppermute | solution.py:41
  60.2 1.6 %collective-permute-start.17 = (f32[80,16]{0,1:T(8,128)S(1)}, f32[80,16]{0,1:T(8,128)S(1)}, u32[]{:S(2)}, u32[]{:S(2)}) collective-permute-start(f32[80,16]{0,1:T(8,128)S(1)} %add.174), channel_id=1, source_target_pairs={{0,8},{1,9},{2,10},{3,11},{4,12},{5,13},{6,14},{7,15},{8,0},{9,1},... | collective-permute-start | bytes 15368 | tf_op jit(solution)/shard_map/ppermute | solution.py:41
  61.8 2.1 %collective-permute-done.17 = f32[80,16]{0,1:T(8,128)S(1)} collective-permute-done((f32[80,16]{0,1:T(8,128)S(1)}, f32[80,16]{0,1:T(8,128)S(1)}, u32[]{:S(2)}, u32[]{:S(2)}) %collective-permute-start.17) | collective-permute-done | bytes 5152 | tf_op jit(solution)/shard_map/ppermute | solution.py:41
  63.9 4.5 %collective-permute-done.18 = f32[80,16]{0,1:T(8,128)S(1)} collective-permute-done((f32[80,16]{0,1:T(8,128)S(1)}, f32[80,16]{0,1:T(8,128)S(1)}, u32[]{:S(2)}, u32[]{:S(2)}) %collective-permute-start.18) | collective-permute-done | bytes 5152 | tf_op jit(solution)/shard_map/ppermute | solution.py:41
  70.4 2.4 %shard_map.112 = (f32[16,16]{1,0:T(8,128)}, f32[16,512]{1,0:T(8,128)}) custom-call(f32[16,16]{1,0:T(8,128)S(1)} %get-tuple-element.18.gram_ref, f32[16,512]{1,0:T(8,128)S(1)} %convolution_subtract_fusion.residue_ref), custom_call_target="tpu_custom_call" | custom-call | flops 540672 | bytes 67584 | tf_op jit(solution)/shard_map/pallas_call | solution.py:127
  (65 shorter events, 10.1 us)
Async XLA Ops:
  0.6 44.7 %copy-start = (bf16[3,4,8,128,128]{4,3,2,1,0:T(8,128)(2,1)S(1)}, bf16[3,4,8,128,128]{4,3,2,1,0:T(8,128)(2,1)}, u32[]{:S(2)}) copy-start(bf16[3,4,8,128,128]{4,3,2,1,0:T(8,128)(2,1)} %param.14) | copy-start | bytes 9437188
  1.6 35.3 %collective-permute-start.12 = (bf16[16,512]{1,0:T(8,128)(2,1)S(1)}, bf16[16,512]{1,0:T(8,128)(2,1)S(1)}, u32[]{:S(2)}, u32[]{:S(2)}) collective-permute-start(bf16[16,512]{1,0:T(8,128)(2,1)S(1)} %convert_element_type.20), channel_id=1, source_target_pairs={{0,1},{1,2},{2,3},{3,4},{4,5},{5,6},{6,7},{7,8},{8,9},{9,10},{10,1... | collective-permute-start | bytes 49160 | tf_op jit(solution)/shard_map/ppermute | solution.py:20
  4.1 32.8 %collective-permute-start.13 = (bf16[16,512]{1,0:T(8,128)(2,1)S(1)}, bf16[16,512]{1,0:T(8,128)(2,1)S(1)}, u32[]{:S(2)}, u32[]{:S(2)}) collective-permute-start(bf16[16,512]{1,0:T(8,128)(2,1)S(1)} %convert_element_type.20), channel_id=1, source_target_pairs={{1,0},{2,1},{3,2},{4,3},{5,4},{6,5},{7,6},{8,7},{9,8},{10,9},{11,1... | collective-permute-start | bytes 49160 | tf_op jit(solution)/shard_map/ppermute | solution.py:23
  6.5 12.4 %collective-permute-start.5 = (bf16[1,4,1024]{2,1,0:T(4,128)(2,1)S(1)}, bf16[1,4,1024]{2,1,0:T(4,128)(2,1)S(1)}, u32[]{:S(2)}, u32[]{:S(2)}) collective-permute-start(bf16[1,4,1024]{2,1,0:T(4,128)(2,1)S(1)} %reshape.117), channel_id=1, source_target_pairs={{0,16},{4,20},{8,24},{12,28},{16,0},{20,4},{24,8},{28,12},{1,17},{... | collective-permute-start | bytes 24584 | tf_op jit(solution)/shard_map/ppermute | solution.py:53
  18.9 3.8 %collective-permute-start.6 = (bf16[2,4,1024]{2,1,0:T(4,128)(2,1)S(1)}, bf16[2,4,1024]{2,1,0:T(4,128)(2,1)S(1)}, u32[]{:S(2)}, u32[]{:S(2)}) collective-permute-start(bf16[2,4,1024]{2,1,0:T(4,128)(2,1)S(1)} %pad_maximum_fusion.3), channel_id=1, source_target_pairs={{0,8},{4,12},{8,0},{12,4},{16,24},{20,28},{24,16},{28,20},{1,9},{5... | collective-permute-start | bytes 49160 | tf_op jit(solution)/shard_map/ppermute | solution.py:53
  22.7 4.0 %collective-permute-start.7 = (bf16[4,4,1024]{2,1,0:T(4,128)(2,1)S(1)}, bf16[4,4,1024]{2,1,0:T(4,128)(2,1)S(1)}, u32[]{:S(2)}, u32[]{:S(2)}) collective-permute-start(bf16[4,4,1024]{2,1,0:T(4,128)(2,1)S(1)} %pad_maximum_fusion.2), channel_id=1, source_target_pairs={{0,4},{4,0},{8,12},{12,8},{16,20},{20,16},{24,28},{28,24},{1,5},{5... | collective-permute-start | bytes 98312 | tf_op jit(solution)/shard_map/ppermute | solution.py:53
  26.7 4.3 %collective-permute-start.8 = (bf16[8,4,1024]{2,1,0:T(4,128)(2,1)S(1)}, bf16[8,4,1024]{2,1,0:T(4,128)(2,1)S(1)}, u32[]{:S(2)}, u32[]{:S(2)}) collective-permute-start(bf16[8,4,1024]{2,1,0:T(4,128)(2,1)S(1)} %constant_dynamic-update-slice_fusion), channel_id=1, source_target_pairs={{0,2},{1,3},{2,0},{3,1},{4,6},{5,7},{6,4},{7,5},{8,10},{9,11},{10,... | collective-permute-start | bytes 196616 | tf_op jit(solution)/shard_map/ppermute | solution.py:53
  31.1 7.0 %collective-permute-start.9 = (bf16[8,8,1024]{2,1,0:T(8,128)(2,1)S(1)}, bf16[8,8,1024]{2,1,0:T(8,128)(2,1)}, u32[]{:S(2)}, u32[]{:S(2)}) collective-permute-start(bf16[8,8,1024]{2,1,0:T(8,128)(2,1)S(1)} %pad_maximum_fusion.1), channel_id=1, source_target_pairs={{0,1},{1,0},{2,3},{3,2},{4,5},{5,4},{6,7},{7,6},{8,9},{9,8},{10,11... | collective-permute-start | bytes 393224 | tf_op jit(solution)/shard_map/ppermute | solution.py:53
  40.0 5.3 %copy-start.1 = (bf16[32,16,128]{2,1,0:T(8,128)(2,1)S(1)}, bf16[32,16,128]{2,1,0:T(8,128)(2,1)}, u32[]{:S(2)}) copy-start(bf16[32,16,128]{2,1,0:T(8,128)(2,1)} %gather_fusion.1) | copy-start | bytes 393220
  40.9 10.2 %copy-start.4 = (bf16[4,64,128]{2,1,0:T(8,128)(2,1)S(1)}, bf16[4,64,128]{2,1,0:T(8,128)(2,1)}, u32[]{:S(2)}) copy-start(bf16[4,64,128]{2,1,0:T(8,128)(2,1)} %param.13) | copy-start | bytes 196612
  40.9 10.5 %copy-start.2 = (f32[64,512]{1,0:T(8,128)S(1)}, f32[64,512]{1,0:T(8,128)}, u32[]{:S(2)}) copy-start(f32[64,512]{1,0:T(8,128)} %param.19) | copy-start | bytes 393220
  45.2 4.5 %collective-permute-start.10 = (f32[8,16,64]{2,1,0:T(8,128)S(1)}, f32[8,16,64]{2,1,0:T(8,128)S(1)}, u32[]{:S(2)}, u32[]{:S(2)}) collective-permute-start(f32[8,16,64]{2,1,0:T(8,128)S(1)} %dynamic-slice_bitcast_fusion), channel_id=1, source_target_pairs={{0,2},{1,3},{2,0},{3,1},{4,6},{5,7},{6,4},{7,5},{8,10},{9,11},{10,... | collective-permute-start | bytes 98312 | tf_op jit(solution)/shard_map/ppermute | solution.py:81
  49.8 1.3 %collective-permute-start.11 = (f32[4,16,64]{2,1,0:T(8,128)S(1)}, f32[4,16,64]{2,1,0:T(8,128)S(1)}, u32[]{:S(2)}, u32[]{:S(2)}) collective-permute-start(f32[4,16,64]{2,1,0:T(8,128)S(1)} %dynamic-slice_bitcast_fusion.1), channel_id=1, source_target_pairs={{0,1},{1,0},{2,3},{3,2},{4,5},{5,4},{6,7},{7,6},{8,9},{9,8},{10,11... | collective-permute-start | bytes 49160 | tf_op jit(solution)/shard_map/ppermute | solution.py:81
  51.6 1.2 %collective-permute-start.14 = (f32[80,16]{0,1:T(8,128)S(1)}, f32[80,16]{0,1:T(8,128)S(1)}, u32[]{:S(2)}, u32[]{:S(2)}) collective-permute-start(f32[80,16]{0,1:T(8,128)S(1)} %pad_maximum_fusion.4), channel_id=1, source_target_pairs={{0,1},{1,0},{2,3},{3,2},{4,5},{5,4},{6,7},{7,6},{8,9},{9,8},{10,11... | collective-permute-start | bytes 15368 | tf_op jit(solution)/shard_map/ppermute | solution.py:41
  52.9 3.7 %collective-permute-start.15 = (f32[80,16]{0,1:T(8,128)S(1)}, f32[80,16]{0,1:T(8,128)S(1)}, u32[]{:S(2)}, u32[]{:S(2)}) collective-permute-start(f32[80,16]{0,1:T(8,128)S(1)} %fusion.64), channel_id=1, source_target_pairs={{0,2},{1,3},{2,0},{3,1},{4,6},{5,7},{6,4},{7,5},{8,10},{9,11},{10,... | collective-permute-start | bytes 15368 | tf_op jit(solution)/shard_map/ppermute | solution.py:41
  56.6 3.7 %collective-permute-start.16 = (f32[80,16]{0,1:T(8,128)S(1)}, f32[80,16]{0,1:T(8,128)S(1)}, u32[]{:S(2)}, u32[]{:S(2)}) collective-permute-start(f32[80,16]{0,1:T(8,128)S(1)} %add.173), channel_id=1, source_target_pairs={{0,4},{1,5},{2,6},{3,7},{4,0},{5,1},{6,2},{7,3},{8,12},{9,13},{10,... | collective-permute-start | bytes 15368 | tf_op jit(solution)/shard_map/ppermute | solution.py:41
  60.2 3.7 %collective-permute-start.17 = (f32[80,16]{0,1:T(8,128)S(1)}, f32[80,16]{0,1:T(8,128)S(1)}, u32[]{:S(2)}, u32[]{:S(2)}) collective-permute-start(f32[80,16]{0,1:T(8,128)S(1)} %add.174), channel_id=1, source_target_pairs={{0,8},{1,9},{2,10},{3,11},{4,12},{5,13},{6,14},{7,15},{8,0},{9,1},... | collective-permute-start | bytes 15368 | tf_op jit(solution)/shard_map/ppermute | solution.py:41
  63.9 4.5 %collective-permute-start.18 = (f32[80,16]{0,1:T(8,128)S(1)}, f32[80,16]{0,1:T(8,128)S(1)}, u32[]{:S(2)}, u32[]{:S(2)}) collective-permute-start(f32[80,16]{0,1:T(8,128)S(1)} %add.175), channel_id=1, source_target_pairs={{0,16},{1,17},{2,18},{3,19},{4,20},{5,21},{6,22},{7,23},{8,24},{9,... | collective-permute-start | bytes 15368 | tf_op jit(solution)/shard_map/ppermute | solution.py:41
  68.4 4.4 %copy-start.3 = (f32[80,16]{0,1:T(8,128)}, f32[80,16]{0,1:T(8,128)S(1)}, u32[]{:S(2)}) copy-start(f32[80,16]{0,1:T(8,128)S(1)} %add.176) | copy-start | bytes 15364

commit v16 on v15

--- a/solution.py
+++ b/solution.py
@@ -43,15 +43,20 @@
     return block
 
 
-def xor_gather(block, axis, dim):
+def xor_gather(block, axis, dim, descending=False):
     count = lax.axis_size(axis)
     if not is_power_of_two(count):
         return lax.all_gather(block, axis, axis=dim, tiled=True), False
-    distance = count // 2
-    while distance >= 1:
+    distances = []
+    distance = 1
+    while distance < count:
+        distances.append(distance)
+        distance *= 2
+    if descending:
+        distances.reverse()
+    for distance in distances:
         route = [(i, i ^ distance) for i in range(count)]
         block = jnp.concatenate([block, lax.ppermute(block, axis, route)], axis=dim)
-        distance //= 2
     return block, True
 
 
@@ -160,12 +165,12 @@
     ).astype(jnp.bfloat16)
     own_rows = coarse.reshape(1, local_count, vec_count * rank_width)
     by_leaf, leaf_xor = xor_gather(own_rows, "leaf", 0)
-    window, coef_xor = xor_gather(by_leaf, "coef", 1)
+    window, coef_xor = xor_gather(by_leaf, "coef", 1, descending=True)
     flat_rows = window.reshape(-1, vec_count * rank_width)
     source_group = far_list // group_size
     source_holder = (far_list % group_size) // local_count
     if leaf_xor:
-        source_group = xor_position(source_group ^ lax.axis_index("leaf"), leaf_count)
+        source_group = source_group ^ lax.axis_index("leaf")
     if coef_xor:
         source_holder = xor_position(source_holder ^ lax.axis_index("coef"), coef_count)
     local_ids = (

time: 73.3 us -> 72.2 us (0.985)
  waiting for transfers between devices: 27.5 us -> 22 us
  starting transfers between devices: 16.9 us -> 21.4 us
    ppermute x5, starting transfers between devices: 2.68 us -> 6.03 us  [butterfly_sum(): block = block + lax.ppermute(block, axes, route)]
    ppermute x5, waiting for transfers between devices: 14 us -> 10.7 us  [butterfly_sum(): block = block + lax.ppermute(block, axes, route)]
    ppermute x5, waiting for transfers between devices: 9.09 us -> 7.44 us  [xor_gather(): block = jnp.concatenate([block, lax.ppermute(block, axis, route)], axis=dim)]
where the time goes in v16:
time: 72.2 us; the launch traced here: 71.8 us
  waiting for transfers between devices  22 us (30%)
  starting transfers between devices  21.4 us (30%)
  local copies, waits for them, and re-layouts  9.89 us (14%)
  matrix products  7.35 us (10%)
  other arithmetic  6.6 us (9%)
  Pallas kernels  2.43 us (3%)
  between operations  2.15 us (3%)
    ppermute x5, starting transfers between devices, xor_gather(): block = jnp.concatenate([block, lax.ppermute(block, axis, route)], axis=dim)  10.8 us
    ppermute x5, waiting for transfers between devices, butterfly_sum(): block = block + lax.ppermute(block, axes, route)  10.7 us
    ppermute x5, waiting for transfers between devices, xor_gather(): block = jnp.concatenate([block, lax.ppermute(block, axis, route)], axis=dim)  7.44 us
    ppermute x5, starting transfers between devices, butterfly_sum(): block = block + lax.ppermute(block, axes, route)  6.03 us
    reshape x1, local copies, waits for them, and re-layouts, on_device(): couple = coupling.reshape(3, group_size, slot_count, rank_width, rank_width)  5.64 us
    dot_general x1, matrix products, on_device(): jnp.einsum('cfvl,jcfkl->cfvjk', sources, couple, preferred_element_type=j...  4.31 us
    ppermute x2, waiting for transfers between devices, butterfly_scatter(): parts = keep + lax.ppermute(give, axis, route)  3.88 us
    ppermute x1, starting transfers between devices, extended_2(): lax.ppermute(lax.slice_in_dim(block, block.shape[dim] - width, None, axis...  2.52 us
  transfers between devices with their start and end apart: 14, of which 10 were waited for; matrix products, arithmetic and copies ran while one was open for 19% of the time, Pallas kernels for 0%

profile of v16, /device:TPU:0, one launch (start us, length us, event | category | flops | bytes accessed | tf_op | source)
XLA Modules:
  0.0 71.8 jit_solution(10272247638010903680)
XLA Ops:
  1.6 2.5 %collective-permute-start.12 = (bf16[16,512]{1,0:T(8,128)(2,1)S(1)}, bf16[16,512]{1,0:T(8,128)(2,1)S(1)}, u32[]{:S(2)}, u32[]{:S(2)}) collective-permute-start(bf16[16,512]{1,0:T(8,128)(2,1)S(1)} %convert_element_type.20), channel_id=1, source_target_pairs={{0,1},{1,2},{2,3},{3,4},{4,5},{5,6},{6,7},{7,8},{8,9},{9,10},{10,1... | collective-permute-start | bytes 49160 | tf_op jit(solution)/shard_map/ppermute | solution.py:20
  4.1 1.3 %collective-permute-start.13 = (bf16[16,512]{1,0:T(8,128)(2,1)S(1)}, bf16[16,512]{1,0:T(8,128)(2,1)S(1)}, u32[]{:S(2)}, u32[]{:S(2)}) collective-permute-start(bf16[16,512]{1,0:T(8,128)(2,1)S(1)} %convert_element_type.20), channel_id=1, source_target_pairs={{1,0},{2,1},{3,2},{4,3},{5,4},{6,5},{7,6},{8,7},{9,8},{10,9},{11,1... | collective-permute-start | bytes 49160 | tf_op jit(solution)/shard_map/ppermute | solution.py:23
  5.4 1.0 %convolution_convert_fusion = bf16[4,16,64]{2,1,0:T(8,128)(2,1)S(1)} fusion(bf16[4,64,128]{2,1,0:T(8,128)(2,1)} %param.13, f32[16,512]{1,0:T(8,128)} %param.11), kind=kOutput, calls=%fused_computation.11 | convolution fusion | flops 1060864 | bytes 106496 | tf_op jit(solution)/shard_map/cki,vci->cvk/dot_general | solution.py:163
  6.5 5.8 %collective-permute-start.5 = (bf16[1,4,1024]{2,1,0:T(4,128)(2,1)S(1)}, bf16[1,4,1024]{2,1,0:T(4,128)(2,1)S(1)}, u32[]{:S(2)}, u32[]{:S(2)}) collective-permute-start(bf16[1,4,1024]{2,1,0:T(4,128)(2,1)S(1)} %reshape.117), channel_id=1, source_target_pairs={{0,4},{4,0},{8,12},{12,8},{16,20},{20,16},{24,28},{28,24},{1,5},{5... | collective-permute-start | bytes 24584 | tf_op jit(solution)/shard_map/ppermute | solution.py:59
  16.9 1.6 %collective-permute-start.6 = (bf16[2,4,1024]{2,1,0:T(4,128)(2,1)S(1)}, bf16[2,4,1024]{2,1,0:T(4,128)(2,1)S(1)}, u32[]{:S(2)}, u32[]{:S(2)}) collective-permute-start(bf16[2,4,1024]{2,1,0:T(4,128)(2,1)S(1)} %pad_maximum_fusion.3), channel_id=1, source_target_pairs={{0,8},{4,12},{8,0},{12,4},{16,24},{20,28},{24,16},{28,20},{1,9},{5... | collective-permute-start | bytes 49160 | tf_op jit(solution)/shard_map/ppermute | solution.py:59
  18.5 2.1 %collective-permute-done.6 = bf16[2,4,1024]{2,1,0:T(4,128)(2,1)S(1)} collective-permute-done((bf16[2,4,1024]{2,1,0:T(4,128)(2,1)S(1)}, bf16[2,4,1024]{2,1,0:T(4,128)(2,1)S(1)}, u32[]{:S(2)}, u32[]{:S(2)}) %collective-permute-start.6) | collective-permute-done | bytes 16416 | tf_op jit(solution)/shard_map/ppermute | solution.py:59
  20.7 2.7 %collective-permute-start.7 = (bf16[4,4,1024]{2,1,0:T(4,128)(2,1)S(1)}, bf16[4,4,1024]{2,1,0:T(4,128)(2,1)S(1)}, u32[]{:S(2)}, u32[]{:S(2)}) collective-permute-start(bf16[4,4,1024]{2,1,0:T(4,128)(2,1)S(1)} %pad_maximum_fusion.2), channel_id=1, source_target_pairs={{0,16},{4,20},{8,24},{12,28},{16,0},{20,4},{24,8},{28,12},{1,17},{... | collective-permute-start | bytes 98312 | tf_op jit(solution)/shard_map/ppermute | solution.py:59
  23.4 2.2 %collective-permute-done.7 = bf16[4,4,1024]{2,1,0:T(4,128)(2,1)S(1)} collective-permute-done((bf16[4,4,1024]{2,1,0:T(4,128)(2,1)S(1)}, bf16[4,4,1024]{2,1,0:T(4,128)(2,1)S(1)}, u32[]{:S(2)}, u32[]{:S(2)}) %collective-permute-start.7) | collective-permute-done | bytes 32800 | tf_op jit(solution)/shard_map/ppermute | solution.py:59
  26.9 3.1 %collective-permute-done.8 = bf16[8,4,1024]{2,1,0:T(4,128)(2,1)S(1)} collective-permute-done((bf16[8,4,1024]{2,1,0:T(4,128)(2,1)S(1)}, bf16[8,4,1024]{2,1,0:T(4,128)(2,1)S(1)}, u32[]{:S(2)}, u32[]{:S(2)}) %collective-permute-start.8) | collective-permute-done | bytes 65568 | tf_op jit(solution)/shard_map/ppermute | solution.py:59
  30.2 5.6 %reshape.121 = bf16[3,16,4,64,64]{4,3,2,1,0:T(8,128)(2,1)} reshape(bf16[3,16,4,4096]{3,2,1,0:T(4,128)(2,1)} %param.16) | data formatting | bytes 3145728 | tf_op jit(solution)/shard_map/reshape | solution.py:185
  35.8 1.2 %gather_fusion.1 = bf16[32,16,128]{2,1,0:T(8,128)(2,1)} fusion(bf16[16,12,128]{2,0,1:T(8,128)(2,1)S(1)} %copy_bitcast_fusion, s32[1024]{0:T(1024)S(1)} %pad_clamp_fusion), kind=kCustom, calls=%fused_computation.1 | custom fusion | bytes 262272 | tf_op jit(solution)/shard_map/gather | solution.py:196
  37.0 1.0 %pad_maximum_fusion = bf16[8,16,1024]{2,1,0:T(8,128)(2,1)S(1)} fusion(bf16[8,8,1024]{2,1,0:T(8,128)(2,1)} %collective-permute-done.9, bf16[8,4,1024]{2,1,0:T(4,128)(2,1)S(1)} %collective-permute-done.8, bf16[8,4,1024]{2,1,0:T(4,128)(2,1)S(1)} %constant_dynamic-update-slice_fusion), kind=kLoop, calls=%fused_computation.16 | loop fusion | flops 786432 | bytes 524288 | tf_op jit(solution)/shard_map/concatenate | solution.py:59
  39.8 4.3 %multiply_reduce_fusion = f32[16,16,64]{2,1,0:T(8,128)S(1)} fusion(bf16[3,16,4,64,64]{4,3,2,1,0:T(8,128)(2,1)} %reshape.121, f32[16,4,3,64]{3,2,1,0:T(4,128)} %broadcast_multiply_fusion, bf16[16,4,16,64]{3,2,1,0:T(8,128)(2,1)} %reshape.120, pred[16,4,64]{2,1,0:T(4,128)(4,1)} %get-tuple-element.14), kind=kOutput, calls=%fused_computation.7 | convolution fusion | flops 25608192 | bytes 1822720 | tf_op jit(solution)/shard_map/cfvl,jcfkl->cfvjk/dot_general | solution.py:186
  45.7 2.9 %collective-permute-done.10 = f32[8,16,64]{2,1,0:T(8,128)S(1)} collective-permute-done((f32[8,16,64]{2,1,0:T(8,128)S(1)}, f32[8,16,64]{2,1,0:T(8,128)S(1)}, u32[]{:S(2)}, u32[]{:S(2)}) %collective-permute-start.10) | collective-permute-done | bytes 32800 | tf_op jit(solution)/shard_map/ppermute | solution.py:86
  49.0 1.0 %collective-permute-done.11 = f32[4,16,64]{2,1,0:T(8,128)S(1)} collective-permute-done((f32[4,16,64]{2,1,0:T(8,128)S(1)}, f32[4,16,64]{2,1,0:T(8,128)S(1)}, u32[]{:S(2)}, u32[]{:S(2)}) %collective-permute-start.11) | collective-permute-done | bytes 16416 | tf_op jit(solution)/shard_map/ppermute | solution.py:86
  50.7 1.0 %collective-permute-done.14 = f32[80,16]{0,1:T(8,128)S(1)} collective-permute-done((f32[80,16]{0,1:T(8,128)S(1)}, f32[80,16]{0,1:T(8,128)S(1)}, u32[]{:S(2)}, u32[]{:S(2)}) %collective-permute-start.14) | collective-permute-done | bytes 5152 | tf_op jit(solution)/shard_map/ppermute | solution.py:41
  52.4 3.1 %collective-permute-done.15 = f32[80,16]{0,1:T(8,128)S(1)} collective-permute-done((f32[80,16]{0,1:T(8,128)S(1)}, f32[80,16]{0,1:T(8,128)S(1)}, u32[]{:S(2)}, u32[]{:S(2)}) %collective-permute-start.15) | collective-permute-done | bytes 5152 | tf_op jit(solution)/shard_map/ppermute | solution.py:41
  55.5 1.1 %collective-permute-start.16 = (f32[80,16]{0,1:T(8,128)S(1)}, f32[80,16]{0,1:T(8,128)S(1)}, u32[]{:S(2)}, u32[]{:S(2)}) collective-permute-start(f32[80,16]{0,1:T(8,128)S(1)} %add.147), channel_id=1, source_target_pairs={{0,4},{1,5},{2,6},{3,7},{4,0},{5,1},{6,2},{7,3},{8,12},{9,13},{10,... | collective-permute-start | bytes 15368 | tf_op jit(solution)/shard_map/ppermute | solution.py:41
  56.6 2.6 %collective-permute-done.16 = f32[80,16]{0,1:T(8,128)S(1)} collective-permute-done((f32[80,16]{0,1:T(8,128)S(1)}, f32[80,16]{0,1:T(8,128)S(1)}, u32[]{:S(2)}, u32[]{:S(2)}) %collective-permute-start.16) | collective-permute-done | bytes 5152 | tf_op jit(solution)/shard_map/ppermute | solution.py:41
  59.1 1.6 %collective-permute-start.17 = (f32[80,16]{0,1:T(8,128)S(1)}, f32[80,16]{0,1:T(8,128)S(1)}, u32[]{:S(2)}, u32[]{:S(2)}) collective-permute-start(f32[80,16]{0,1:T(8,128)S(1)} %add.148), channel_id=1, source_target_pairs={{0,8},{1,9},{2,10},{3,11},{4,12},{5,13},{6,14},{7,15},{8,0},{9,1},... | collective-permute-start | bytes 15368 | tf_op jit(solution)/shard_map/ppermute | solution.py:41
  60.7 2.1 %collective-permute-done.17 = f32[80,16]{0,1:T(8,128)S(1)} collective-permute-done((f32[80,16]{0,1:T(8,128)S(1)}, f32[80,16]{0,1:T(8,128)S(1)}, u32[]{:S(2)}, u32[]{:S(2)}) %collective-permute-start.17) | collective-permute-done | bytes 5152 | tf_op jit(solution)/shard_map/ppermute | solution.py:41
  62.8 2.6 %collective-permute-start.18 = (f32[80,16]{0,1:T(8,128)S(1)}, f32[80,16]{0,1:T(8,128)S(1)}, u32[]{:S(2)}, u32[]{:S(2)}) collective-permute-start(f32[80,16]{0,1:T(8,128)S(1)} %add.149), channel_id=1, source_target_pairs={{0,16},{1,17},{2,18},{3,19},{4,20},{5,21},{6,22},{7,23},{8,24},{9,... | collective-permute-start | bytes 15368 | tf_op jit(solution)/shard_map/ppermute | solution.py:41
  65.4 1.9 %collective-permute-done.18 = f32[80,16]{0,1:T(8,128)S(1)} collective-permute-done((f32[80,16]{0,1:T(8,128)S(1)}, f32[80,16]{0,1:T(8,128)S(1)}, u32[]{:S(2)}, u32[]{:S(2)}) %collective-permute-start.18) | collective-permute-done | bytes 5152 | tf_op jit(solution)/shard_map/ppermute | solution.py:41
  69.4 2.4 %shard_map.112 = (f32[16,16]{1,0:T(8,128)}, f32[16,512]{1,0:T(8,128)}) custom-call(f32[16,16]{1,0:T(8,128)S(1)} %get-tuple-element.18.gram_ref, f32[16,512]{1,0:T(8,128)S(1)} %convolution_subtract_fusion.residue_ref), custom_call_target="tpu_custom_call" | custom-call | flops 540672 | bytes 67584 | tf_op jit(solution)/shard_map/pallas_call | solution.py:132
  (65 shorter events, 13.0 us)
Async XLA Ops:
  0.6 44.2 %copy-start = (bf16[3,4,8,128,128]{4,3,2,1,0:T(8,128)(2,1)S(1)}, bf16[3,4,8,128,128]{4,3,2,1,0:T(8,128)(2,1)}, u32[]{:S(2)}) copy-start(bf16[3,4,8,128,128]{4,3,2,1,0:T(8,128)(2,1)} %param.14) | copy-start | bytes 9437188
  1.6 34.2 %collective-permute-start.12 = (bf16[16,512]{1,0:T(8,128)(2,1)S(1)}, bf16[16,512]{1,0:T(8,128)(2,1)S(1)}, u32[]{:S(2)}, u32[]{:S(2)}) collective-permute-start(bf16[16,512]{1,0:T(8,128)(2,1)S(1)} %convert_element_type.20), channel_id=1, source_target_pairs={{0,1},{1,2},{2,3},{3,4},{4,5},{5,6},{6,7},{7,8},{8,9},{9,10},{10,1... | collective-permute-start | bytes 49160 | tf_op jit(solution)/shard_map/ppermute | solution.py:20
  4.1 31.7 %collective-permute-start.13 = (bf16[16,512]{1,0:T(8,128)(2,1)S(1)}, bf16[16,512]{1,0:T(8,128)(2,1)S(1)}, u32[]{:S(2)}, u32[]{:S(2)}) collective-permute-start(bf16[16,512]{1,0:T(8,128)(2,1)S(1)} %convert_element_type.20), channel_id=1, source_target_pairs={{1,0},{2,1},{3,2},{4,3},{5,4},{6,5},{7,6},{8,7},{9,8},{10,9},{11,1... | collective-permute-start | bytes 49160 | tf_op jit(solution)/shard_map/ppermute | solution.py:23
  6.5 10.4 %collective-permute-start.5 = (bf16[1,4,1024]{2,1,0:T(4,128)(2,1)S(1)}, bf16[1,4,1024]{2,1,0:T(4,128)(2,1)S(1)}, u32[]{:S(2)}, u32[]{:S(2)}) collective-permute-start(bf16[1,4,1024]{2,1,0:T(4,128)(2,1)S(1)} %reshape.117), channel_id=1, source_target_pairs={{0,4},{4,0},{8,12},{12,8},{16,20},{20,16},{24,28},{28,24},{1,5},{5... | collective-permute-start | bytes 24584 | tf_op jit(solution)/shard_map/ppermute | solution.py:59
  16.9 3.8 %collective-permute-start.6 = (bf16[2,4,1024]{2,1,0:T(4,128)(2,1)S(1)}, bf16[2,4,1024]{2,1,0:T(4,128)(2,1)S(1)}, u32[]{:S(2)}, u32[]{:S(2)}) collective-permute-start(bf16[2,4,1024]{2,1,0:T(4,128)(2,1)S(1)} %pad_maximum_fusion.3), channel_id=1, source_target_pairs={{0,8},{4,12},{8,0},{12,4},{16,24},{20,28},{24,16},{28,20},{1,9},{5... | collective-permute-start | bytes 49160 | tf_op jit(solution)/shard_map/ppermute | solution.py:59
  20.7 4.9 %collective-permute-start.7 = (bf16[4,4,1024]{2,1,0:T(4,128)(2,1)S(1)}, bf16[4,4,1024]{2,1,0:T(4,128)(2,1)S(1)}, u32[]{:S(2)}, u32[]{:S(2)}) collective-permute-start(bf16[4,4,1024]{2,1,0:T(4,128)(2,1)S(1)} %pad_maximum_fusion.2), channel_id=1, source_target_pairs={{0,16},{4,20},{8,24},{12,28},{16,0},{20,4},{24,8},{28,12},{1,17},{... | collective-permute-start | bytes 98312 | tf_op jit(solution)/shard_map/ppermute | solution.py:59
  25.6 4.3 %collective-permute-start.8 = (bf16[8,4,1024]{2,1,0:T(4,128)(2,1)S(1)}, bf16[8,4,1024]{2,1,0:T(4,128)(2,1)S(1)}, u32[]{:S(2)}, u32[]{:S(2)}) collective-permute-start(bf16[8,4,1024]{2,1,0:T(4,128)(2,1)S(1)} %constant_dynamic-update-slice_fusion), channel_id=1, source_target_pairs={{0,2},{1,3},{2,0},{3,1},{4,6},{5,7},{6,4},{7,5},{8,10},{9,11},{10,... | collective-permute-start | bytes 196616 | tf_op jit(solution)/shard_map/ppermute | solution.py:59
  30.0 7.0 %collective-permute-start.9 = (bf16[8,8,1024]{2,1,0:T(8,128)(2,1)S(1)}, bf16[8,8,1024]{2,1,0:T(8,128)(2,1)}, u32[]{:S(2)}, u32[]{:S(2)}) collective-permute-start(bf16[8,8,1024]{2,1,0:T(8,128)(2,1)S(1)} %pad_maximum_fusion.1), channel_id=1, source_target_pairs={{0,1},{1,0},{2,3},{3,2},{4,5},{5,4},{6,7},{7,6},{8,9},{9,8},{10,11... | collective-permute-start | bytes 393224 | tf_op jit(solution)/shard_map/ppermute | solution.py:59
  38.9 5.9 %copy-start.1 = (bf16[32,16,128]{2,1,0:T(8,128)(2,1)S(1)}, bf16[32,16,128]{2,1,0:T(8,128)(2,1)}, u32[]{:S(2)}) copy-start(bf16[32,16,128]{2,1,0:T(8,128)(2,1)} %gather_fusion.1) | copy-start | bytes 393220
  39.8 10.2 %copy-start.4 = (bf16[4,64,128]{2,1,0:T(8,128)(2,1)S(1)}, bf16[4,64,128]{2,1,0:T(8,128)(2,1)}, u32[]{:S(2)}) copy-start(bf16[4,64,128]{2,1,0:T(8,128)(2,1)} %param.13) | copy-start | bytes 196612
  39.8 10.5 %copy-start.2 = (f32[64,512]{1,0:T(8,128)S(1)}, f32[64,512]{1,0:T(8,128)}, u32[]{:S(2)}) copy-start(f32[64,512]{1,0:T(8,128)} %param.19) | copy-start | bytes 393220
  44.1 4.5 %collective-permute-start.10 = (f32[8,16,64]{2,1,0:T(8,128)S(1)}, f32[8,16,64]{2,1,0:T(8,128)S(1)}, u32[]{:S(2)}, u32[]{:S(2)}) collective-permute-start(f32[8,16,64]{2,1,0:T(8,128)S(1)} %dynamic-slice_bitcast_fusion), channel_id=1, source_target_pairs={{0,2},{1,3},{2,0},{3,1},{4,6},{5,7},{6,4},{7,5},{8,10},{9,11},{10,... | collective-permute-start | bytes 98312 | tf_op jit(solution)/shard_map/ppermute | solution.py:86
  48.7 1.3 %collective-permute-start.11 = (f32[4,16,64]{2,1,0:T(8,128)S(1)}, f32[4,16,64]{2,1,0:T(8,128)S(1)}, u32[]{:S(2)}, u32[]{:S(2)}) collective-permute-start(f32[4,16,64]{2,1,0:T(8,128)S(1)} %dynamic-slice_bitcast_fusion.1), channel_id=1, source_target_pairs={{0,1},{1,0},{2,3},{3,2},{4,5},{5,4},{6,7},{7,6},{8,9},{9,8},{10,11... | collective-permute-start | bytes 49160 | tf_op jit(solution)/shard_map/ppermute | solution.py:86
  50.6 1.2 %collective-permute-start.14 = (f32[80,16]{0,1:T(8,128)S(1)}, f32[80,16]{0,1:T(8,128)S(1)}, u32[]{:S(2)}, u32[]{:S(2)}) collective-permute-start(f32[80,16]{0,1:T(8,128)S(1)} %pad_maximum_fusion.4), channel_id=1, source_target_pairs={{0,1},{1,0},{2,3},{3,2},{4,5},{5,4},{6,7},{7,6},{8,9},{9,8},{10,11... | collective-permute-start | bytes 15368 | tf_op jit(solution)/shard_map/ppermute | solution.py:41
  51.8 3.7 %collective-permute-start.15 = (f32[80,16]{0,1:T(8,128)S(1)}, f32[80,16]{0,1:T(8,128)S(1)}, u32[]{:S(2)}, u32[]{:S(2)}) collective-permute-start(f32[80,16]{0,1:T(8,128)S(1)} %fusion.58), channel_id=1, source_target_pairs={{0,2},{1,3},{2,0},{3,1},{4,6},{5,7},{6,4},{7,5},{8,10},{9,11},{10,... | collective-permute-start | bytes 15368 | tf_op jit(solution)/shard_map/ppermute | solution.py:41
  55.5 3.7 %collective-permute-start.16 = (f32[80,16]{0,1:T(8,128)S(1)}, f32[80,16]{0,1:T(8,128)S(1)}, u32[]{:S(2)}, u32[]{:S(2)}) collective-permute-start(f32[80,16]{0,1:T(8,128)S(1)} %add.147), channel_id=1, source_target_pairs={{0,4},{1,5},{2,6},{3,7},{4,0},{5,1},{6,2},{7,3},{8,12},{9,13},{10,... | collective-permute-start | bytes 15368 | tf_op jit(solution)/shard_map/ppermute | solution.py:41
  59.1 3.7 %collective-permute-start.17 = (f32[80,16]{0,1:T(8,128)S(1)}, f32[80,16]{0,1:T(8,128)S(1)}, u32[]{:S(2)}, u32[]{:S(2)}) collective-permute-start(f32[80,16]{0,1:T(8,128)S(1)} %add.148), channel_id=1, source_target_pairs={{0,8},{1,9},{2,10},{3,11},{4,12},{5,13},{6,14},{7,15},{8,0},{9,1},... | collective-permute-start | bytes 15368 | tf_op jit(solution)/shard_map/ppermute | solution.py:41
  62.8 4.5 %collective-permute-start.18 = (f32[80,16]{0,1:T(8,128)S(1)}, f32[80,16]{0,1:T(8,128)S(1)}, u32[]{:S(2)}, u32[]{:S(2)}) collective-permute-start(f32[80,16]{0,1:T(8,128)S(1)} %add.149), channel_id=1, source_target_pairs={{0,16},{1,17},{2,18},{3,19},{4,20},{5,21},{6,22},{7,23},{8,24},{9,... | collective-permute-start | bytes 15368 | tf_op jit(solution)/shard_map/ppermute | solution.py:41
  67.3 4.4 %copy-start.3 = (f32[80,16]{0,1:T(8,128)}, f32[80,16]{0,1:T(8,128)S(1)}, u32[]{:S(2)}) copy-start(f32[80,16]{0,1:T(8,128)S(1)} %add.150) | copy-start | bytes 15364

commit v17 on v13

--- a/solution.py
+++ b/solution.py
@@ -43,14 +43,17 @@
     return block
 
 
-def xor_gather(block, axis, dim):
+def xor_gather(block, axis, dim, arrived=None):
     count = lax.axis_size(axis)
     if not is_power_of_two(count):
         return lax.all_gather(block, axis, axis=dim, tiled=True), False
     distance = 1
     while distance < count:
         route = [(i, i ^ distance) for i in range(count)]
-        block = jnp.concatenate([block, lax.ppermute(block, axis, route)], axis=dim)
+        other = lax.ppermute(block, axis, route)
+        if arrived is not None and not arrived:
+            arrived.append(other)
+        block = jnp.concatenate([block, other], axis=dim)
         distance *= 2
     return block, True
 
@@ -149,7 +152,13 @@
         "cki,vci->cvk", leaf_basis, by_cluster, preferred_element_type=jnp.float32
     ).astype(jnp.bfloat16)
     own_rows = coarse.reshape(1, local_count, vec_count * rank_width)
-    by_leaf, leaf_xor = xor_gather(own_rows, "leaf", 0)
+    arrived = []
+    by_leaf, leaf_xor = xor_gather(own_rows, "leaf", 0, arrived)
+    if arrived:
+        later = (arrived[0][0, 0, 0] * 0).astype(jnp.int32)
+        far_list = far_list + later
+        far_rank = far_rank + later
+        near_list = near_list + later
     window, coef_xor = xor_gather(by_leaf, "coef", 1)
     flat_rows = window.reshape(-1, vec_count * rank_width)
     source_group = far_list // group_size

time: 69.5 us -> 70.7 us (1.017)
  waiting for transfers between devices: 18.2 us -> 22.5 us
  starting transfers between devices: 22.5 us -> 20.2 us
  other arithmetic: 6.59 us -> 5.23 us
  between operations: 2.1 us -> 2.83 us
    ppermute x5, waiting for transfers between devices: 5.01 us -> 7.01 us  [xor_gather(): other = lax.ppermute(block, axis, route)]
    ppermute x5, waiting for transfers between devices: 10.3 us -> 11.8 us  [butterfly_sum(): block = block + lax.ppermute(block, axes, route)]
    ppermute x5, starting transfers between devices: 6.35 us -> 4.86 us  [butterfly_sum(): block = block + lax.ppermute(block, axes, route)]
    ppermute x2, starting transfers between devices: 1.57 us -> 0.73 us  [butterfly_scatter(): parts = keep + lax.ppermute(give, axis, route)]
    ppermute x2, waiting for transfers between devices: 2.87 us -> 3.71 us  [butterfly_scatter(): parts = keep + lax.ppermute(give, axis, route)]
    unnamed x14 -> x19, local copies, waits for them, and re-layouts: 0.82 us -> 0.08 us
  transfers between devices with their start and end apart: 14 -> 14, of which waited for: 10 -> 10; matrix products, arithmetic and copies ran while one was open for 20% -> 17% of each run, Pallas kernels for 0% -> 0%
where the time goes in v17:
time: 70.7 us; the launch traced here: 70.3 us
  waiting for transfers between devices  22.5 us (32%)
  starting transfers between devices  20.2 us (29%)
  local copies, waits for them, and re-layouts  9.72 us (14%)
  matrix products  7.35 us (10%)
  other arithmetic  5.23 us (7%)
  between operations  2.83 us (4%)
  Pallas kernels  2.43 us (3%)
    ppermute x5, waiting for transfers between devices, butterfly_sum(): block = block + lax.ppermute(block, axes, route)  11.8 us
    ppermute x5, starting transfers between devices, xor_gather(): other = lax.ppermute(block, axis, route)  10.8 us
    ppermute x5, waiting for transfers between devices, xor_gather(): other = lax.ppermute(block, axis, route)  7.01 us
    reshape x1, local copies, waits for them, and re-layouts, on_device(): couple = coupling.reshape(3, group_size, slot_count, rank_width, rank_width)  5.63 us
    ppermute x5, starting transfers between devices, butterfly_sum(): block = block + lax.ppermute(block, axes, route)  4.86 us
    dot_general x1, matrix products, on_device(): jnp.einsum('cfvl,jcfkl->cfvjk', sources, couple, preferred_element_type=j...  4.31 us
    ppermute x2, waiting for transfers between devices, butterfly_scatter(): parts = keep + lax.ppermute(give, axis, route)  3.71 us
    ppermute x1, starting transfers between devices, extended_2(): lax.ppermute(lax.slice_in_dim(block, block.shape[dim] - width, None, axis...  2.52 us
  transfers between devices with their start and end apart: 14, of which 10 were waited for; matrix products, arithmetic and copies ran while one was open for 17% of the time, Pallas kernels for 0%

profile of v17, /device:TPU:0, one launch (start us, length us, event | category | flops | bytes accessed | tf_op | source)
XLA Modules:
  0.0 70.3 jit_solution(2733589150040781673)
XLA Ops:
  0.7 0.9 %convert_element_type.26 = bf16[16,512]{1,0:T(8,128)(2,1)S(1)} convert(f32[16,512]{1,0:T(8,128)} %param.11) | non-fusion elementwise | flops 8192 | bytes 49152 | tf_op jit(solution)/shard_map/convert_element_type | solution.py:149
  1.6 2.5 %collective-permute-start.12 = (bf16[16,512]{1,0:T(8,128)(2,1)S(1)}, bf16[16,512]{1,0:T(8,128)(2,1)S(1)}, u32[]{:S(2)}, u32[]{:S(2)}) collective-permute-start(bf16[16,512]{1,0:T(8,128)(2,1)S(1)} %convert_element_type.26), channel_id=1, source_target_pairs={{0,1},{1,2},{2,3},{3,4},{4,5},{5,6},{6,7},{7,8},{8,9},{9,10},{10,1... | collective-permute-start | bytes 49160 | tf_op jit(solution)/shard_map/ppermute | solution.py:20
  4.1 1.3 %collective-permute-start.13 = (bf16[16,512]{1,0:T(8,128)(2,1)S(1)}, bf16[16,512]{1,0:T(8,128)(2,1)S(1)}, u32[]{:S(2)}, u32[]{:S(2)}) collective-permute-start(bf16[16,512]{1,0:T(8,128)(2,1)S(1)} %convert_element_type.26), channel_id=1, source_target_pairs={{1,0},{2,1},{3,2},{4,3},{5,4},{6,5},{7,6},{8,7},{9,8},{10,9},{11,1... | collective-permute-start | bytes 49160 | tf_op jit(solution)/shard_map/ppermute | solution.py:23
  5.4 1.0 %convolution_convert_fusion = bf16[4,16,64]{2,1,0:T(8,128)(2,1)S(1)} fusion(bf16[4,64,128]{2,1,0:T(8,128)(2,1)} %param.13, f32[16,512]{1,0:T(8,128)} %param.11), kind=kOutput, calls=%fused_computation.11 | convolution fusion | flops 1060864 | bytes 106496 | tf_op jit(solution)/shard_map/cki,vci->cvk/dot_general | solution.py:151
  6.5 5.8 %collective-permute-start.5 = (bf16[1,4,1024]{2,1,0:T(4,128)(2,1)S(1)}, bf16[1,4,1024]{2,1,0:T(4,128)(2,1)S(1)}, u32[]{:S(2)}, u32[]{:S(2)}) collective-permute-start(bf16[1,4,1024]{2,1,0:T(4,128)(2,1)S(1)} %reshape.121), channel_id=1, source_target_pairs={{0,4},{4,0},{8,12},{12,8},{16,20},{20,16},{24,28},{28,24},{1,5},{5... | collective-permute-start | bytes 24584 | tf_op jit(solution)/shard_map/ppermute | solution.py:53
  13.0 5.6 %reshape.125 = bf16[3,16,4,64,64]{4,3,2,1,0:T(8,128)(2,1)} reshape(bf16[3,16,4,4096]{3,2,1,0:T(4,128)(2,1)} %param.16) | data formatting | bytes 3145728 | tf_op jit(solution)/shard_map/reshape | solution.py:179
  18.7 1.6 %collective-permute-start.6 = (bf16[2,4,1024]{2,1,0:T(4,128)(2,1)S(1)}, bf16[2,4,1024]{2,1,0:T(4,128)(2,1)S(1)}, u32[]{:S(2)}, u32[]{:S(2)}) collective-permute-start(bf16[2,4,1024]{2,1,0:T(4,128)(2,1)S(1)} %pad_maximum_fusion.3), channel_id=1, source_target_pairs={{0,8},{4,12},{8,0},{12,4},{16,24},{20,28},{24,16},{28,20},{1,9},{5... | collective-permute-start | bytes 49160 | tf_op jit(solution)/shard_map/ppermute | solution.py:53
  23.4 2.7 %collective-permute-start.7 = (bf16[4,4,1024]{2,1,0:T(4,128)(2,1)S(1)}, bf16[4,4,1024]{2,1,0:T(4,128)(2,1)S(1)}, u32[]{:S(2)}, u32[]{:S(2)}) collective-permute-start(bf16[4,4,1024]{2,1,0:T(4,128)(2,1)S(1)} %pad_maximum_fusion.2), channel_id=1, source_target_pairs={{0,16},{4,20},{8,24},{12,28},{16,0},{20,4},{24,8},{28,12},{1,17},{... | collective-permute-start | bytes 98312 | tf_op jit(solution)/shard_map/ppermute | solution.py:53
  26.1 2.6 %collective-permute-done.7 = bf16[4,4,1024]{2,1,0:T(4,128)(2,1)S(1)} collective-permute-done((bf16[4,4,1024]{2,1,0:T(4,128)(2,1)S(1)}, bf16[4,4,1024]{2,1,0:T(4,128)(2,1)S(1)}, u32[]{:S(2)}, u32[]{:S(2)}) %collective-permute-start.7) | collective-permute-done | bytes 32800 | tf_op jit(solution)/shard_map/ppermute | solution.py:53
  30.7 1.2 %gather_fusion.1 = bf16[32,16,128]{2,1,0:T(8,128)(2,1)} fusion(bf16[16,12,128]{2,0,1:T(8,128)(2,1)S(1)} %copy_bitcast_fusion, s32[1024]{0:T(1024)S(1)} %pad_clamp_fusion), kind=kCustom, calls=%fused_computation.1 | custom fusion | bytes 262272 | tf_op jit(solution)/shard_map/gather | solution.py:190
  32.0 3.8 %collective-permute-done.9 = bf16[8,8,1024]{2,1,0:T(8,128)(2,1)} collective-permute-done((bf16[8,8,1024]{2,1,0:T(8,128)(2,1)S(1)}, bf16[8,8,1024]{2,1,0:T(8,128)(2,1)}, u32[]{:S(2)}, u32[]{:S(2)}) %collective-permute-start.9) | collective-permute-done | bytes 131104 | tf_op jit(solution)/shard_map/ppermute | solution.py:53
  35.8 1.0 %pad_maximum_fusion = bf16[8,16,1024]{2,1,0:T(8,128)(2,1)S(1)} fusion(bf16[8,8,1024]{2,1,0:T(8,128)(2,1)} %collective-permute-done.9, bf16[8,4,1024]{2,1,0:T(4,128)(2,1)S(1)} %collective-permute-done.8, bf16[8,4,1024]{2,1,0:T(4,128)(2,1)S(1)} %constant_dynamic-update-slice_fusion), kind=kLoop, calls=%fused_computation.16 | loop fusion | flops 786432 | bytes 524288 | tf_op jit(solution)/shard_map/concatenate | solution.py:56
  38.5 4.3 %multiply_reduce_fusion = f32[16,16,64]{2,1,0:T(8,128)S(1)} fusion(bf16[3,16,4,64,64]{4,3,2,1,0:T(8,128)(2,1)} %reshape.125, f32[16,4,3,64]{3,2,1,0:T(4,128)} %broadcast_multiply_fusion, bf16[16,4,16,64]{3,2,1,0:T(8,128)(2,1)} %reshape.124, pred[16,4,64]{2,1,0:T(4,128)(4,1)} %get-tuple-element.14), kind=kOutput, calls=%fused_computation.7 | convolution fusion | flops 25608192 | bytes 1822720 | tf_op jit(solution)/shard_map/cfvl,jcfkl->cfvjk/dot_general | solution.py:180
  43.5 0.9 %fusion = bf16[4,16,3,128,1]{3,1,4,2,0:T(8,128)(2,1)S(1)} fusion(bf16[16,4,8,128,1]{3,0,2,4,1:T(8,128)(2,1)S(1)} %bitcast.97, bf16[3,4,8,128,128]{4,3,2,1,0:T(8,128)(2,1)S(1)} %copy-done), kind=kOutput, calls=%fused_computation.3 | convolution fusion | flops 50331648 | bytes 3325952 | tf_op jit(solution)/shard_map/jcnil,vcnl->jvci/dot_general | solution.py:193
  44.4 2.7 %collective-permute-done.10 = f32[8,16,64]{2,1,0:T(8,128)S(1)} collective-permute-done((f32[8,16,64]{2,1,0:T(8,128)S(1)}, f32[8,16,64]{2,1,0:T(8,128)S(1)}, u32[]{:S(2)}, u32[]{:S(2)}) %collective-permute-start.10) | collective-permute-done | bytes 32800 | tf_op jit(solution)/shard_map/ppermute | solution.py:74
  47.5 1.0 %collective-permute-done.11 = f32[4,16,64]{2,1,0:T(8,128)S(1)} collective-permute-done((f32[4,16,64]{2,1,0:T(8,128)S(1)}, f32[4,16,64]{2,1,0:T(8,128)S(1)}, u32[]{:S(2)}, u32[]{:S(2)}) %collective-permute-start.11) | collective-permute-done | bytes 16416 | tf_op jit(solution)/shard_map/ppermute | solution.py:74
  49.3 1.0 %collective-permute-done.14 = f32[80,16]{0,1:T(8,128)S(1)} collective-permute-done((f32[80,16]{0,1:T(8,128)S(1)}, f32[80,16]{0,1:T(8,128)S(1)}, u32[]{:S(2)}, u32[]{:S(2)}) %collective-permute-start.14) | collective-permute-done | bytes 5152 | tf_op jit(solution)/shard_map/ppermute | solution.py:41
  51.0 3.1 %collective-permute-done.15 = f32[80,16]{0,1:T(8,128)S(1)} collective-permute-done((f32[80,16]{0,1:T(8,128)S(1)}, f32[80,16]{0,1:T(8,128)S(1)}, u32[]{:S(2)}, u32[]{:S(2)}) %collective-permute-start.15) | collective-permute-done | bytes 5152 | tf_op jit(solution)/shard_map/ppermute | solution.py:41
  54.0 1.4 %collective-permute-start.16 = (f32[80,16]{0,1:T(8,128)S(1)}, f32[80,16]{0,1:T(8,128)S(1)}, u32[]{:S(2)}, u32[]{:S(2)}) collective-permute-start(f32[80,16]{0,1:T(8,128)S(1)} %add.152), channel_id=1, source_target_pairs={{0,4},{1,5},{2,6},{3,7},{4,0},{5,1},{6,2},{7,3},{8,12},{9,13},{10,... | collective-permute-start | bytes 15368 | tf_op jit(solution)/shard_map/ppermute | solution.py:41
  55.4 2.2 %collective-permute-done.16 = f32[80,16]{0,1:T(8,128)S(1)} collective-permute-done((f32[80,16]{0,1:T(8,128)S(1)}, f32[80,16]{0,1:T(8,128)S(1)}, u32[]{:S(2)}, u32[]{:S(2)}) %collective-permute-start.16) | collective-permute-done | bytes 5152 | tf_op jit(solution)/shard_map/ppermute | solution.py:41
  58.1 3.2 %collective-permute-done.17 = f32[80,16]{0,1:T(8,128)S(1)} collective-permute-done((f32[80,16]{0,1:T(8,128)S(1)}, f32[80,16]{0,1:T(8,128)S(1)}, u32[]{:S(2)}, u32[]{:S(2)}) %collective-permute-start.17) | collective-permute-done | bytes 5152 | tf_op jit(solution)/shard_map/ppermute | solution.py:41
  61.3 2.2 %collective-permute-start.18 = (f32[80,16]{0,1:T(8,128)S(1)}, f32[80,16]{0,1:T(8,128)S(1)}, u32[]{:S(2)}, u32[]{:S(2)}) collective-permute-start(f32[80,16]{0,1:T(8,128)S(1)} %add.154), channel_id=1, source_target_pairs={{0,16},{1,17},{2,18},{3,19},{4,20},{5,21},{6,22},{7,23},{8,24},{9,... | collective-permute-start | bytes 15368 | tf_op jit(solution)/shard_map/ppermute | solution.py:41
  63.6 2.3 %collective-permute-done.18 = f32[80,16]{0,1:T(8,128)S(1)} collective-permute-done((f32[80,16]{0,1:T(8,128)S(1)}, f32[80,16]{0,1:T(8,128)S(1)}, u32[]{:S(2)}, u32[]{:S(2)}) %collective-permute-start.18) | collective-permute-done | bytes 5152 | tf_op jit(solution)/shard_map/ppermute | solution.py:41
  67.9 2.4 %shard_map.112 = (f32[16,16]{1,0:T(8,128)}, f32[16,512]{1,0:T(8,128)}) custom-call(f32[16,16]{1,0:T(8,128)S(1)} %get-tuple-element.20.gram_ref, f32[16,512]{1,0:T(8,128)S(1)} %convolution_subtract_fusion.residue_ref), custom_call_target="tpu_custom_call" | custom-call | flops 540672 | bytes 67584 | tf_op jit(solution)/shard_map/pallas_call | solution.py:120
  (72 shorter events, 10.7 us)
Async XLA Ops:
  0.6 42.9 %copy-start = (bf16[3,4,8,128,128]{4,3,2,1,0:T(8,128)(2,1)S(1)}, bf16[3,4,8,128,128]{4,3,2,1,0:T(8,128)(2,1)}, u32[]{:S(2)}) copy-start(bf16[3,4,8,128,128]{4,3,2,1,0:T(8,128)(2,1)} %param.14) | copy-start | bytes 9437188
  0.6 20.9 %copy-start.5 = (s32[16,4]{0,1:T(4,128)S(1)}, s32[16,4]{0,1:T(4,128)}, u32[]{:S(2)}) copy-start(s32[16,4]{0,1:T(4,128)} %param.17) | copy-start | bytes 772
  0.7 20.9 %copy-start.6 = (s32[16,4]{0,1:T(4,128)S(1)}, s32[16,4]{0,1:T(4,128)}, u32[]{:S(2)}) copy-start(s32[16,4]{0,1:T(4,128)} %param.18) | copy-start | bytes 772
  0.7 21.8 %copy-start.7 = (s32[4,8]{1,0:T(4,128)S(1)}, s32[4,8]{1,0:T(4,128)}, u32[]{:S(2)}) copy-start(s32[4,8]{1,0:T(4,128)} %param.15) | copy-start | bytes 388
  1.6 29.1 %collective-permute-start.12 = (bf16[16,512]{1,0:T(8,128)(2,1)S(1)}, bf16[16,512]{1,0:T(8,128)(2,1)S(1)}, u32[]{:S(2)}, u32[]{:S(2)}) collective-permute-start(bf16[16,512]{1,0:T(8,128)(2,1)S(1)} %convert_element_type.26), channel_id=1, source_target_pairs={{0,1},{1,2},{2,3},{3,4},{4,5},{5,6},{6,7},{7,8},{8,9},{9,10},{10,1... | collective-permute-start | bytes 49160 | tf_op jit(solution)/shard_map/ppermute | solution.py:20
  4.1 26.6 %collective-permute-start.13 = (bf16[16,512]{1,0:T(8,128)(2,1)S(1)}, bf16[16,512]{1,0:T(8,128)(2,1)S(1)}, u32[]{:S(2)}, u32[]{:S(2)}) collective-permute-start(bf16[16,512]{1,0:T(8,128)(2,1)S(1)} %convert_element_type.26), channel_id=1, source_target_pairs={{1,0},{2,1},{3,2},{4,3},{5,4},{6,5},{7,6},{8,7},{9,8},{10,9},{11,1... | collective-permute-start | bytes 49160 | tf_op jit(solution)/shard_map/ppermute | solution.py:23
  6.5 12.1 %collective-permute-start.5 = (bf16[1,4,1024]{2,1,0:T(4,128)(2,1)S(1)}, bf16[1,4,1024]{2,1,0:T(4,128)(2,1)S(1)}, u32[]{:S(2)}, u32[]{:S(2)}) collective-permute-start(bf16[1,4,1024]{2,1,0:T(4,128)(2,1)S(1)} %reshape.121), channel_id=1, source_target_pairs={{0,4},{4,0},{8,12},{12,8},{16,20},{20,16},{24,28},{28,24},{1,5},{5... | collective-permute-start | bytes 24584 | tf_op jit(solution)/shard_map/ppermute | solution.py:53
  18.7 4.7 %collective-permute-start.6 = (bf16[2,4,1024]{2,1,0:T(4,128)(2,1)S(1)}, bf16[2,4,1024]{2,1,0:T(4,128)(2,1)S(1)}, u32[]{:S(2)}, u32[]{:S(2)}) collective-permute-start(bf16[2,4,1024]{2,1,0:T(4,128)(2,1)S(1)} %pad_maximum_fusion.3), channel_id=1, source_target_pairs={{0,8},{4,12},{8,0},{12,4},{16,24},{20,28},{24,16},{28,20},{1,9},{5... | collective-permute-start | bytes 49160 | tf_op jit(solution)/shard_map/ppermute | solution.py:53
  23.4 5.2 %collective-permute-start.7 = (bf16[4,4,1024]{2,1,0:T(4,128)(2,1)S(1)}, bf16[4,4,1024]{2,1,0:T(4,128)(2,1)S(1)}, u32[]{:S(2)}, u32[]{:S(2)}) collective-permute-start(bf16[4,4,1024]{2,1,0:T(4,128)(2,1)S(1)} %pad_maximum_fusion.2), channel_id=1, source_target_pairs={{0,16},{4,20},{8,24},{12,28},{16,0},{20,4},{24,8},{28,12},{1,17},{... | collective-permute-start | bytes 98312 | tf_op jit(solution)/shard_map/ppermute | solution.py:53
  28.6 1.3 %collective-permute-start.8 = (bf16[8,4,1024]{2,1,0:T(4,128)(2,1)S(1)}, bf16[8,4,1024]{2,1,0:T(4,128)(2,1)S(1)}, u32[]{:S(2)}, u32[]{:S(2)}) collective-permute-start(bf16[8,4,1024]{2,1,0:T(4,128)(2,1)S(1)} %constant_dynamic-update-slice_fusion), channel_id=1, source_target_pairs={{0,1},{1,0},{2,3},{3,2},{4,5},{5,4},{6,7},{7,6},{8,9},{9,8},{10,11... | collective-permute-start | bytes 196616 | tf_op jit(solution)/shard_map/ppermute | solution.py:53
  30.0 5.7 %collective-permute-start.9 = (bf16[8,8,1024]{2,1,0:T(8,128)(2,1)S(1)}, bf16[8,8,1024]{2,1,0:T(8,128)(2,1)}, u32[]{:S(2)}, u32[]{:S(2)}) collective-permute-start(bf16[8,8,1024]{2,1,0:T(8,128)(2,1)S(1)} %pad_maximum_fusion.1), channel_id=1, source_target_pairs={{0,2},{1,3},{2,0},{3,1},{4,6},{5,7},{6,4},{7,5},{8,10},{9,11},{10,... | collective-permute-start | bytes 393224 | tf_op jit(solution)/shard_map/ppermute | solution.py:53
  37.6 5.9 %copy-start.1 = (bf16[32,16,128]{2,1,0:T(8,128)(2,1)S(1)}, bf16[32,16,128]{2,1,0:T(8,128)(2,1)}, u32[]{:S(2)}) copy-start(bf16[32,16,128]{2,1,0:T(8,128)(2,1)} %gather_fusion.1) | copy-start | bytes 393220
  38.5 10.0 %copy-start.4 = (bf16[4,64,128]{2,1,0:T(8,128)(2,1)S(1)}, bf16[4,64,128]{2,1,0:T(8,128)(2,1)}, u32[]{:S(2)}) copy-start(bf16[4,64,128]{2,1,0:T(8,128)(2,1)} %param.13) | copy-start | bytes 196612
  38.5 10.3 %copy-start.2 = (f32[64,512]{1,0:T(8,128)S(1)}, f32[64,512]{1,0:T(8,128)}, u32[]{:S(2)}) copy-start(f32[64,512]{1,0:T(8,128)} %param.19) | copy-start | bytes 393220
  42.8 4.3 %collective-permute-start.10 = (f32[8,16,64]{2,1,0:T(8,128)S(1)}, f32[8,16,64]{2,1,0:T(8,128)S(1)}, u32[]{:S(2)}, u32[]{:S(2)}) collective-permute-start(f32[8,16,64]{2,1,0:T(8,128)S(1)} %dynamic-slice_bitcast_fusion), channel_id=1, source_target_pairs={{0,2},{1,3},{2,0},{3,1},{4,6},{5,7},{6,4},{7,5},{8,10},{9,11},{10,... | collective-permute-start | bytes 98312 | tf_op jit(solution)/shard_map/ppermute | solution.py:74
  47.2 1.3 %collective-permute-start.11 = (f32[4,16,64]{2,1,0:T(8,128)S(1)}, f32[4,16,64]{2,1,0:T(8,128)S(1)}, u32[]{:S(2)}, u32[]{:S(2)}) collective-permute-start(f32[4,16,64]{2,1,0:T(8,128)S(1)} %dynamic-slice_bitcast_fusion.1), channel_id=1, source_target_pairs={{0,1},{1,0},{2,3},{3,2},{4,5},{5,4},{6,7},{7,6},{8,9},{9,8},{10,11... | collective-permute-start | bytes 49160 | tf_op jit(solution)/shard_map/ppermute | solution.py:74
  49.1 1.2 %collective-permute-start.14 = (f32[80,16]{0,1:T(8,128)S(1)}, f32[80,16]{0,1:T(8,128)S(1)}, u32[]{:S(2)}, u32[]{:S(2)}) collective-permute-start(f32[80,16]{0,1:T(8,128)S(1)} %pad_maximum_fusion.4), channel_id=1, source_target_pairs={{0,1},{1,0},{2,3},{3,2},{4,5},{5,4},{6,7},{7,6},{8,9},{9,8},{10,11... | collective-permute-start | bytes 15368 | tf_op jit(solution)/shard_map/ppermute | solution.py:41
  50.4 3.7 %collective-permute-start.15 = (f32[80,16]{0,1:T(8,128)S(1)}, f32[80,16]{0,1:T(8,128)S(1)}, u32[]{:S(2)}, u32[]{:S(2)}) collective-permute-start(f32[80,16]{0,1:T(8,128)S(1)} %fusion.54), channel_id=1, source_target_pairs={{0,2},{1,3},{2,0},{3,1},{4,6},{5,7},{6,4},{7,5},{8,10},{9,11},{10,... | collective-permute-start | bytes 15368 | tf_op jit(solution)/shard_map/ppermute | solution.py:41
  54.0 3.7 %collective-permute-start.16 = (f32[80,16]{0,1:T(8,128)S(1)}, f32[80,16]{0,1:T(8,128)S(1)}, u32[]{:S(2)}, u32[]{:S(2)}) collective-permute-start(f32[80,16]{0,1:T(8,128)S(1)} %add.152), channel_id=1, source_target_pairs={{0,4},{1,5},{2,6},{3,7},{4,0},{5,1},{6,2},{7,3},{8,12},{9,13},{10,... | collective-permute-start | bytes 15368 | tf_op jit(solution)/shard_map/ppermute | solution.py:41
  57.7 3.7 %collective-permute-start.17 = (f32[80,16]{0,1:T(8,128)S(1)}, f32[80,16]{0,1:T(8,128)S(1)}, u32[]{:S(2)}, u32[]{:S(2)}) collective-permute-start(f32[80,16]{0,1:T(8,128)S(1)} %add.153), channel_id=1, source_target_pairs={{0,8},{1,9},{2,10},{3,11},{4,12},{5,13},{6,14},{7,15},{8,0},{9,1},... | collective-permute-start | bytes 15368 | tf_op jit(solution)/shard_map/ppermute | solution.py:41
  61.3 4.5 %collective-permute-start.18 = (f32[80,16]{0,1:T(8,128)S(1)}, f32[80,16]{0,1:T(8,128)S(1)}, u32[]{:S(2)}, u32[]{:S(2)}) collective-permute-start(f32[80,16]{0,1:T(8,128)S(1)} %add.154), channel_id=1, source_target_pairs={{0,16},{1,17},{2,18},{3,19},{4,20},{5,21},{6,22},{7,23},{8,24},{9,... | collective-permute-start | bytes 15368 | tf_op jit(solution)/shard_map/ppermute | solution.py:41
  65.9 4.4 %copy-start.3 = (f32[80,16]{0,1:T(8,128)}, f32[80,16]{0,1:T(8,128)S(1)}, u32[]{:S(2)}) copy-start(f32[80,16]{0,1:T(8,128)S(1)} %add.155) | copy-start | bytes 15364

commit v18 on v13

--- a/solution.py
+++ b/solution.py
@@ -167,10 +167,25 @@
     lane_ids = jnp.arange(rank_width, dtype=jnp.int32)
     keep_mask = lane_ids[None, None, :] < far_rank[:, :, None]
     sources = jnp.where(keep_mask[:, :, None, :], sources, jnp.zeros((), jnp.bfloat16))
-    couple = coupling.reshape(3, group_size, slot_count, rank_width, rank_width)
-    far_terms = jnp.einsum("cfvl,jcfkl->cfvjk", sources, couple, preferred_element_type=jnp.float32)
-    weights = powers[None, None, None, :, None] * keep_mask[:, :, None, None, :].astype(jnp.float32)
-    partial_far = jnp.sum(far_terms * weights, axis=(1, 3))
+    lane_width = 128
+    halves = lane_width // rank_width
+    tiles = rank_width // halves
+    lane_half = jnp.arange(lane_width, dtype=jnp.int32) // rank_width
+    spread = jnp.where(
+        (lane_half[:, None] == jnp.arange(halves, dtype=jnp.int32)[None, :])[None, None, :, :, None],
+        jnp.tile(jnp.swapaxes(sources, 2, 3), (1, 1, halves, 1))[:, :, :, None, :],
+        jnp.zeros((), jnp.bfloat16),
+    ).reshape(group_size, slot_count, lane_width, halves * vec_count)
+    spread = jnp.broadcast_to(spread[None], (3, *spread.shape))
+    couple = coupling.reshape(3, group_size, slot_count, tiles, lane_width)
+    far_terms = jnp.einsum("jcfhL,jcfLw->jcfhw", couple, spread, preferred_element_type=jnp.float32)
+    far_terms = far_terms.reshape(3, group_size, slot_count, tiles, halves, vec_count)
+    weights = powers[:, None, None, None, None, None] * keep_mask.reshape(
+        1, group_size, slot_count, tiles, halves, 1
+    ).astype(jnp.float32)
+    partial_far = jnp.transpose(
+        jnp.sum(far_terms * weights, axis=(0, 2)), (0, 3, 1, 2)
+    ).reshape(group_size, vec_count, rank_width)
     far_hat = butterfly_scatter(partial_far, "coef")
     far_round = far_hat.astype(jnp.bfloat16).reshape(local_count, vec_count, rank_width)
     far_part = jnp.einsum("cki,cvk->vci", leaf_basis, far_round, preferred_element_type=jnp.float32)

time: 69.5 us -> 77.1 us (1.11)
  local copies, waits for them, and re-layouts: 9.88 us -> 15 us
  matrix products: 7.35 us -> 9.52 us
  waiting for transfers between devices: 18.2 us -> 17.4 us
    dynamic_slice x0 -> x3, local copies, waits for them, and re-layouts: none -> 3.58 us  [the longest x2 1.9 us: butterfly_scatter(): keep = lax.dynamic_index_in_dim(halves, bit, axis=0, keepdims=False)]
    another operation x0 -> x2, local copies, waits for them, and re-layouts: none -> 2.62 us  [on_device(): jnp.tile(jnp.swapaxes(sources, 2, 3), (1, 1, halves, 1))[:, :, :, None, :]]
    dot_general x1, matrix products: 4.31 us -> 2.39 us  [on_device(): jnp.einsum('jcfhL,jcfLw->jcfhw', couple, spread, preferred_element_type=j...]
    reshape x1, local copies, waits for them, and re-layouts: 5.63 us -> 4.19 us  [on_device(): couple = coupling.reshape(3, group_size, slot_count, tiles, lane_width)]
    ppermute x2, waiting for transfers between devices: 2.87 us -> 1.62 us  [butterfly_scatter(): parts = keep + lax.ppermute(give, axis, route)]
    transpose x0 -> x1, local copies, waits for them, and re-layouts: none -> 1.21 us  [on_device(): jnp.transpose(jnp.sum(far_terms * weights, axis=(0, 2)), (0, 3, 1, 2))]
    dot_general x1, matrix products: 0.19 us -> 1.11 us  [on_device(): proj_part = jnp.dot(krylov, applied.T, precision=highest)]
    dot_general x1, matrix products: 0.18 us -> 1.09 us  [on_device(): residue = applied - jnp.dot(coeffs.T, krylov, precision=highest)]
  transfers between devices with their start and end apart: 14 -> 14, of which waited for: 10 -> 10; matrix products, arithmetic and copies ran while one was open for 20% -> 18% of each run, Pallas kernels for 0% -> 0%
where the time goes in v18:
time: 77.1 us; the launch traced here: 76.4 us
  starting transfers between devices  22.6 us (29%)
  waiting for transfers between devices  17.4 us (23%)
  local copies, waits for them, and re-layouts  15 us (19%)
  matrix products  9.52 us (12%)
  other arithmetic  7.25 us (9%)
  Pallas kernels  2.43 us (3%)
  between operations  2.15 us (3%)
    ppermute x5, starting transfers between devices, xor_gather(): block = jnp.concatenate([block, lax.ppermute(block, axis, route)], axis=dim)  10.8 us
    ppermute x5, waiting for transfers between devices, butterfly_sum(): block = block + lax.ppermute(block, axes, route)  10.2 us
    ppermute x5, starting transfers between devices, butterfly_sum(): block = block + lax.ppermute(block, axes, route)  6.53 us
    ppermute x5, waiting for transfers between devices, xor_gather(): block = jnp.concatenate([block, lax.ppermute(block, axis, route)], axis=dim)  5.59 us
    reshape x1, local copies, waits for them, and re-layouts, on_device(): couple = coupling.reshape(3, group_size, slot_count, tiles, lane_width)  4.19 us
    another operation x2, local copies, waits for them, and re-layouts, on_device(): jnp.tile(jnp.swapaxes(sources, 2, 3), (1, 1, halves, 1))[:, :, :, None, :]  2.62 us
    ppermute x1, starting transfers between devices, extended_2(): lax.ppermute(lax.slice_in_dim(block, block.shape[dim] - width, None, axis...  2.52 us
    pallas_call x1, Pallas kernels, chol_solve(): pl.pallas_call(chol_solve_kernel, out_shape=(jax.ShapeDtypeStruct((size,...  2.43 us
  transfers between devices with their start and end apart: 14, of which 10 were waited for; matrix products, arithmetic and copies ran while one was open for 18% of the time, Pallas kernels for 0%

profile of v18, /device:TPU:0, one launch (start us, length us, event | category | flops | bytes accessed | tf_op | source)
XLA Modules:
  0.0 76.4 jit_solution(8952656819780754541)
XLA Ops:
  1.6 2.5 %collective-permute-start.12 = (bf16[16,512]{1,0:T(8,128)(2,1)S(1)}, bf16[16,512]{1,0:T(8,128)(2,1)S(1)}, u32[]{:S(2)}, u32[]{:S(2)}) collective-permute-start(bf16[16,512]{1,0:T(8,128)(2,1)S(1)} %convert_element_type.20), channel_id=1, source_target_pairs={{0,1},{1,2},{2,3},{3,4},{4,5},{5,6},{6,7},{7,8},{8,9},{9,10},{10,1... | collective-permute-start | bytes 49160 | tf_op jit(solution)/shard_map/ppermute | solution.py:20
  4.1 1.3 %collective-permute-start.13 = (bf16[16,512]{1,0:T(8,128)(2,1)S(1)}, bf16[16,512]{1,0:T(8,128)(2,1)}, u32[]{:S(2)}, u32[]{:S(2)}) collective-permute-start(bf16[16,512]{1,0:T(8,128)(2,1)S(1)} %convert_element_type.20), channel_id=1, source_target_pairs={{1,0},{2,1},{3,2},{4,3},{5,4},{6,5},{7,6},{8,7},{9,8},{10,9},{11,1... | collective-permute-start | bytes 49160 | tf_op jit(solution)/shard_map/ppermute | solution.py:23
  6.5 5.8 %collective-permute-start.5 = (bf16[1,4,1024]{2,1,0:T(4,128)(2,1)S(1)}, bf16[1,4,1024]{2,1,0:T(4,128)(2,1)S(1)}, u32[]{:S(2)}, u32[]{:S(2)}) collective-permute-start(bf16[1,4,1024]{2,1,0:T(4,128)(2,1)S(1)} %reshape.167), channel_id=1, source_target_pairs={{0,4},{4,0},{8,12},{12,8},{16,20},{20,16},{24,28},{28,24},{1,5},{5... | collective-permute-start | bytes 24584 | tf_op jit(solution)/shard_map/ppermute | solution.py:53
  16.5 1.6 %collective-permute-start.6 = (bf16[2,4,1024]{2,1,0:T(4,128)(2,1)S(1)}, bf16[2,4,1024]{2,1,0:T(4,128)(2,1)S(1)}, u32[]{:S(2)}, u32[]{:S(2)}) collective-permute-start(bf16[2,4,1024]{2,1,0:T(4,128)(2,1)S(1)} %pad_maximum_fusion.3), channel_id=1, source_target_pairs={{0,8},{4,12},{8,0},{12,4},{16,24},{20,28},{24,16},{28,20},{1,9},{5... | collective-permute-start | bytes 49160 | tf_op jit(solution)/shard_map/ppermute | solution.py:53
  18.2 2.1 %collective-permute-done.6 = bf16[2,4,1024]{2,1,0:T(4,128)(2,1)S(1)} collective-permute-done((bf16[2,4,1024]{2,1,0:T(4,128)(2,1)S(1)}, bf16[2,4,1024]{2,1,0:T(4,128)(2,1)S(1)}, u32[]{:S(2)}, u32[]{:S(2)}) %collective-permute-start.6) | collective-permute-done | bytes 16416 | tf_op jit(solution)/shard_map/ppermute | solution.py:53
  20.3 2.7 %collective-permute-start.7 = (bf16[4,4,1024]{2,1,0:T(4,128)(2,1)S(1)}, bf16[4,4,1024]{2,1,0:T(4,128)(2,1)S(1)}, u32[]{:S(2)}, u32[]{:S(2)}) collective-permute-start(bf16[4,4,1024]{2,1,0:T(4,128)(2,1)S(1)} %pad_maximum_fusion.2), channel_id=1, source_target_pairs={{0,16},{4,20},{8,24},{12,28},{16,0},{20,4},{24,8},{28,12},{1,17},{... | collective-permute-start | bytes 98312 | tf_op jit(solution)/shard_map/ppermute | solution.py:53
  23.0 2.2 %collective-permute-done.7 = bf16[4,4,1024]{2,1,0:T(4,128)(2,1)S(1)} collective-permute-done((bf16[4,4,1024]{2,1,0:T(4,128)(2,1)S(1)}, bf16[4,4,1024]{2,1,0:T(4,128)(2,1)S(1)}, u32[]{:S(2)}, u32[]{:S(2)}) %collective-permute-start.7) | collective-permute-done | bytes 32800 | tf_op jit(solution)/shard_map/ppermute | solution.py:53
  27.3 4.2 %reshape.171 = bf16[3,16,4,32,128]{4,3,2,1,0:T(8,128)(2,1)} reshape(bf16[3,16,4,4096]{3,2,1,0:T(4,128)(2,1)} %param.16) | data formatting | bytes 3145728 | tf_op jit(solution)/shard_map/reshape | solution.py:180
  35.4 1.3 %tile.8 = bf16[16,4,2,64,16]{3,2,4,1,0:T(2,128)(2,1)} broadcast(bf16[16,4,64,16]{2,3,1,0:T(8,128)(2,1)S(1)} %select_bitcast_fusion), dimensions={0,1,3,4} | broadcast | bytes 393216 | tf_op jit(solution)/shard_map/tile | solution.py:176
  36.7 1.4 %tile.9 = bf16[16,4,128,16]{2,3,1,0:T(8,128)(2,1)S(1)} reshape(bf16[16,4,2,64,16]{3,2,4,1,0:T(2,128)(2,1)} %tile.8) | data formatting | bytes 524288 | tf_op jit(solution)/shard_map/tile | solution.py:176
  38.1 2.4 %fusion = f32[16,32,32]{1,2,0:T(8,128)S(1)} fusion(bf16[3,16,4,32,128]{4,3,2,1,0:T(8,128)(2,1)} %reshape.171, f32[3,16,4,32,2]{3,4,2,1,0:T(2,128)} %broadcast_multiply_fusion, bf16[16,4,128,32]{2,3,1,0:T(8,128)(2,1)S(1)} %bitcast_select_fusion), kind=kOutput, calls=%fused_computation.4 | convolution fusion | flops 50708480 | bytes 2211840 | tf_op jit(solution)/shard_map/jcfhL,jcfLw->jcfhw/dot_general | solution.py:181
  41.7 1.8 %constant_dynamic-slice_fusion.1 = (f32[1,8,16,64]{2,1,0,3:T(8,128)S(1)}, f32[1,8,16,64]{2,1,0,3:T(8,128)}) fusion(f32[2,8,16,64]{2,1,0,3:T(8,128)} %bitcast.106, s32[]{:T(128)S(6)} %select_n.106, s32[]{:T(128)S(6)} %select_n.107), kind=kLoop, calls=%fused_computation.80 | loop fusion | bytes 131080 | tf_op jit(solution)/shard_map/jit(dynamic_index_in_dim)/dynamic_slice | solution.py:68
  43.5 1.7 %copy.44 = f32[1,8,16,64]{3,2,1,0:T(8,128)} copy(f32[1,8,16,64]{2,1,0,3:T(8,128)} %get-tuple-element.15) | data formatting | bytes 65536 | tf_op jit(solution)/shard_map/jit(dynamic_index_in_dim)/dynamic_slice | solution.py:69
  45.2 1.4 %collective-permute-start.10 = (f32[8,16,64]{2,1,0:T(8,128)}, f32[8,16,64]{2,1,0:T(8,128)}, u32[]{:S(2)}, u32[]{:S(2)}) collective-permute-start(f32[8,16,64]{2,1,0:T(8,128)} %bitcast.114), channel_id=1, source_target_pairs={{0,2},{1,3},{2,0},{3,1},{4,6},{5,7},{6,4},{7,5},{8,10},{9,11},{10,... | collective-permute-start | bytes 98312 | tf_op jit(solution)/shard_map/ppermute | solution.py:71
  46.6 1.6 %fusion.3 = bf16[3,16,4,128]{3,1,0,2:T(8,128)(2,1)} fusion(bf16[16,4,8,128,1]{3,0,2,4,1:T(8,128)(2,1)S(1)} %bitcast.108, bf16[3,4,8,128,128]{4,3,2,1,0:T(8,128)(2,1)S(1)} %copy-done), kind=kOutput, calls=%fused_computation.7 | convolution fusion | flops 50331648 | bytes 3325952 | tf_op jit(solution)/shard_map/jcnil,vcnl->jvci/dot_general | solution.py:199
  48.3 1.5 %collective-permute-done.10 = f32[8,16,64]{2,1,0:T(8,128)} collective-permute-done((f32[8,16,64]{2,1,0:T(8,128)}, f32[8,16,64]{2,1,0:T(8,128)}, u32[]{:S(2)}, u32[]{:S(2)}) %collective-permute-start.10) | collective-permute-done | bytes 32800 | tf_op jit(solution)/shard_map/ppermute | solution.py:71
  55.5 1.4 %collective-permute-start.15 = (f32[80,16]{0,1:T(8,128)S(1)}, f32[80,16]{0,1:T(8,128)S(1)}, u32[]{:S(2)}, u32[]{:S(2)}) collective-permute-start(f32[80,16]{0,1:T(8,128)S(1)} %fusion.49), channel_id=1, source_target_pairs={{0,2},{1,3},{2,0},{3,1},{4,6},{5,7},{6,4},{7,5},{8,10},{9,11},{10,... | collective-permute-start | bytes 15368 | tf_op jit(solution)/shard_map/ppermute | solution.py:41
  56.9 2.2 %collective-permute-done.15 = f32[80,16]{0,1:T(8,128)S(1)} collective-permute-done((f32[80,16]{0,1:T(8,128)S(1)}, f32[80,16]{0,1:T(8,128)S(1)}, u32[]{:S(2)}, u32[]{:S(2)}) %collective-permute-start.15) | collective-permute-done | bytes 5152 | tf_op jit(solution)/shard_map/ppermute | solution.py:41
  59.7 3.1 %collective-permute-done.16 = f32[80,16]{0,1:T(8,128)S(1)} collective-permute-done((f32[80,16]{0,1:T(8,128)S(1)}, f32[80,16]{0,1:T(8,128)S(1)}, u32[]{:S(2)}, u32[]{:S(2)}) %collective-permute-start.16) | collective-permute-done | bytes 5152 | tf_op jit(solution)/shard_map/ppermute | solution.py:41
  62.8 1.6 %collective-permute-start.17 = (f32[80,16]{0,1:T(8,128)S(1)}, f32[80,16]{0,1:T(8,128)S(1)}, u32[]{:S(2)}, u32[]{:S(2)}) collective-permute-start(f32[80,16]{0,1:T(8,128)S(1)} %add.138), channel_id=1, source_target_pairs={{0,8},{1,9},{2,10},{3,11},{4,12},{5,13},{6,14},{7,15},{8,0},{9,1},... | collective-permute-start | bytes 15368 | tf_op jit(solution)/shard_map/ppermute | solution.py:41
  64.4 2.1 %collective-permute-done.17 = f32[80,16]{0,1:T(8,128)S(1)} collective-permute-done((f32[80,16]{0,1:T(8,128)S(1)}, f32[80,16]{0,1:T(8,128)S(1)}, u32[]{:S(2)}, u32[]{:S(2)}) %collective-permute-start.17) | collective-permute-done | bytes 5152 | tf_op jit(solution)/shard_map/ppermute | solution.py:41
  66.5 2.6 %collective-permute-start.18 = (f32[80,16]{0,1:T(8,128)S(1)}, f32[80,16]{0,1:T(8,128)S(1)}, u32[]{:S(2)}, u32[]{:S(2)}) collective-permute-start(f32[80,16]{0,1:T(8,128)S(1)} %add.139), channel_id=1, source_target_pairs={{0,16},{1,17},{2,18},{3,19},{4,20},{5,21},{6,22},{7,23},{8,24},{9,... | collective-permute-start | bytes 15368 | tf_op jit(solution)/shard_map/ppermute | solution.py:41
  69.1 1.9 %collective-permute-done.18 = f32[80,16]{0,1:T(8,128)S(1)} collective-permute-done((f32[80,16]{0,1:T(8,128)S(1)}, f32[80,16]{0,1:T(8,128)S(1)}, u32[]{:S(2)}, u32[]{:S(2)}) %collective-permute-start.18) | collective-permute-done | bytes 5152 | tf_op jit(solution)/shard_map/ppermute | solution.py:41
  73.9 2.4 %shard_map.112 = (f32[16,16]{1,0:T(8,128)}, f32[16,512]{1,0:T(8,128)}) custom-call(f32[16,16]{1,0:T(8,128)S(1)} %get-tuple-element.18.gram_ref, f32[16,512]{1,0:T(8,128)S(1)} %convolution_subtract_fusion.residue_ref), custom_call_target="tpu_custom_call" | custom-call | flops 540672 | bytes 67584 | tf_op jit(solution)/shard_map/pallas_call | solution.py:117
  (73 shorter events, 21.6 us)
Async XLA Ops:
  0.6 46.0 %copy-start = (bf16[3,4,8,128,128]{4,3,2,1,0:T(8,128)(2,1)S(1)}, bf16[3,4,8,128,128]{4,3,2,1,0:T(8,128)(2,1)}, u32[]{:S(2)}) copy-start(bf16[3,4,8,128,128]{4,3,2,1,0:T(8,128)(2,1)} %param.14) | copy-start | bytes 9437188
  1.6 29.9 %collective-permute-start.12 = (bf16[16,512]{1,0:T(8,128)(2,1)S(1)}, bf16[16,512]{1,0:T(8,128)(2,1)S(1)}, u32[]{:S(2)}, u32[]{:S(2)}) collective-permute-start(bf16[16,512]{1,0:T(8,128)(2,1)S(1)} %convert_element_type.20), channel_id=1, source_target_pairs={{0,1},{1,2},{2,3},{3,4},{4,5},{5,6},{6,7},{7,8},{8,9},{9,10},{10,1... | collective-permute-start | bytes 49160 | tf_op jit(solution)/shard_map/ppermute | solution.py:20
  4.1 27.4 %collective-permute-start.13 = (bf16[16,512]{1,0:T(8,128)(2,1)S(1)}, bf16[16,512]{1,0:T(8,128)(2,1)}, u32[]{:S(2)}, u32[]{:S(2)}) collective-permute-start(bf16[16,512]{1,0:T(8,128)(2,1)S(1)} %convert_element_type.20), channel_id=1, source_target_pairs={{1,0},{2,1},{3,2},{4,3},{5,4},{6,5},{7,6},{8,7},{9,8},{10,9},{11,1... | collective-permute-start | bytes 49160 | tf_op jit(solution)/shard_map/ppermute | solution.py:23
  6.5 10.0 %collective-permute-start.5 = (bf16[1,4,1024]{2,1,0:T(4,128)(2,1)S(1)}, bf16[1,4,1024]{2,1,0:T(4,128)(2,1)S(1)}, u32[]{:S(2)}, u32[]{:S(2)}) collective-permute-start(bf16[1,4,1024]{2,1,0:T(4,128)(2,1)S(1)} %reshape.167), channel_id=1, source_target_pairs={{0,4},{4,0},{8,12},{12,8},{16,20},{20,16},{24,28},{28,24},{1,5},{5... | collective-permute-start | bytes 24584 | tf_op jit(solution)/shard_map/ppermute | solution.py:53
  16.5 3.8 %collective-permute-start.6 = (bf16[2,4,1024]{2,1,0:T(4,128)(2,1)S(1)}, bf16[2,4,1024]{2,1,0:T(4,128)(2,1)S(1)}, u32[]{:S(2)}, u32[]{:S(2)}) collective-permute-start(bf16[2,4,1024]{2,1,0:T(4,128)(2,1)S(1)} %pad_maximum_fusion.3), channel_id=1, source_target_pairs={{0,8},{4,12},{8,0},{12,4},{16,24},{20,28},{24,16},{28,20},{1,9},{5... | collective-permute-start | bytes 49160 | tf_op jit(solution)/shard_map/ppermute | solution.py:53
  20.3 4.9 %collective-permute-start.7 = (bf16[4,4,1024]{2,1,0:T(4,128)(2,1)S(1)}, bf16[4,4,1024]{2,1,0:T(4,128)(2,1)S(1)}, u32[]{:S(2)}, u32[]{:S(2)}) collective-permute-start(bf16[4,4,1024]{2,1,0:T(4,128)(2,1)S(1)} %pad_maximum_fusion.2), channel_id=1, source_target_pairs={{0,16},{4,20},{8,24},{12,28},{16,0},{20,4},{24,8},{28,12},{1,17},{... | collective-permute-start | bytes 98312 | tf_op jit(solution)/shard_map/ppermute | solution.py:53
  25.2 1.3 %collective-permute-start.8 = (bf16[8,4,1024]{2,1,0:T(4,128)(2,1)S(1)}, bf16[8,4,1024]{2,1,0:T(4,128)(2,1)S(1)}, u32[]{:S(2)}, u32[]{:S(2)}) collective-permute-start(bf16[8,4,1024]{2,1,0:T(4,128)(2,1)S(1)} %constant_dynamic-update-slice_fusion), channel_id=1, source_target_pairs={{0,1},{1,0},{2,3},{3,2},{4,5},{5,4},{6,7},{7,6},{8,9},{9,8},{10,11... | collective-permute-start | bytes 196616 | tf_op jit(solution)/shard_map/ppermute | solution.py:53
  26.6 6.8 %collective-permute-start.9 = (bf16[8,8,1024]{2,1,0:T(8,128)(2,1)S(1)}, bf16[8,8,1024]{2,1,0:T(8,128)(2,1)}, u32[]{:S(2)}, u32[]{:S(2)}) collective-permute-start(bf16[8,8,1024]{2,1,0:T(8,128)(2,1)S(1)} %pad_maximum_fusion.1), channel_id=1, source_target_pairs={{0,2},{1,3},{2,0},{3,1},{4,6},{5,7},{6,4},{7,5},{8,10},{9,11},{10,... | collective-permute-start | bytes 393224 | tf_op jit(solution)/shard_map/ppermute | solution.py:53
  36.7 9.9 %copy-start.1 = (bf16[32,16,128]{2,1,0:T(8,128)(2,1)S(1)}, bf16[32,16,128]{2,1,0:T(8,128)(2,1)}, u32[]{:S(2)}) copy-start(bf16[32,16,128]{2,1,0:T(8,128)(2,1)} %gather_fusion.1) | copy-start | bytes 393220
  45.2 4.6 %collective-permute-start.10 = (f32[8,16,64]{2,1,0:T(8,128)}, f32[8,16,64]{2,1,0:T(8,128)}, u32[]{:S(2)}, u32[]{:S(2)}) collective-permute-start(f32[8,16,64]{2,1,0:T(8,128)} %bitcast.114), channel_id=1, source_target_pairs={{0,2},{1,3},{2,0},{3,1},{4,6},{5,7},{6,4},{7,5},{8,10},{9,11},{10,... | collective-permute-start | bytes 98312 | tf_op jit(solution)/shard_map/ppermute | solution.py:71
  50.6 1.3 %collective-permute-start.11 = (f32[4,16,64]{2,1,0:T(8,128)S(1)}, f32[4,16,64]{2,1,0:T(8,128)S(1)}, u32[]{:S(2)}, u32[]{:S(2)}) collective-permute-start(f32[4,16,64]{2,1,0:T(8,128)S(1)} %dynamic-slice_bitcast_fusion), channel_id=1, source_target_pairs={{0,1},{1,0},{2,3},{3,2},{4,5},{5,4},{6,7},{7,6},{8,9},{9,8},{10,11... | collective-permute-start | bytes 49160 | tf_op jit(solution)/shard_map/ppermute | solution.py:71
  54.2 1.2 %collective-permute-start.14 = (f32[80,16]{0,1:T(8,128)S(1)}, f32[80,16]{0,1:T(8,128)S(1)}, u32[]{:S(2)}, u32[]{:S(2)}) collective-permute-start(f32[80,16]{0,1:T(8,128)S(1)} %pad_maximum_fusion.4), channel_id=1, source_target_pairs={{0,1},{1,0},{2,3},{3,2},{4,5},{5,4},{6,7},{7,6},{8,9},{9,8},{10,11... | collective-permute-start | bytes 15368 | tf_op jit(solution)/shard_map/ppermute | solution.py:41
  55.5 3.7 %collective-permute-start.15 = (f32[80,16]{0,1:T(8,128)S(1)}, f32[80,16]{0,1:T(8,128)S(1)}, u32[]{:S(2)}, u32[]{:S(2)}) collective-permute-start(f32[80,16]{0,1:T(8,128)S(1)} %fusion.49), channel_id=1, source_target_pairs={{0,2},{1,3},{2,0},{3,1},{4,6},{5,7},{6,4},{7,5},{8,10},{9,11},{10,... | collective-permute-start | bytes 15368 | tf_op jit(solution)/shard_map/ppermute | solution.py:41
  59.2 3.7 %collective-permute-start.16 = (f32[80,16]{0,1:T(8,128)S(1)}, f32[80,16]{0,1:T(8,128)S(1)}, u32[]{:S(2)}, u32[]{:S(2)}) collective-permute-start(f32[80,16]{0,1:T(8,128)S(1)} %add.137), channel_id=1, source_target_pairs={{0,4},{1,5},{2,6},{3,7},{4,0},{5,1},{6,2},{7,3},{8,12},{9,13},{10,... | collective-permute-start | bytes 15368 | tf_op jit(solution)/shard_map/ppermute | solution.py:41
  62.8 3.7 %collective-permute-start.17 = (f32[80,16]{0,1:T(8,128)S(1)}, f32[80,16]{0,1:T(8,128)S(1)}, u32[]{:S(2)}, u32[]{:S(2)}) collective-permute-start(f32[80,16]{0,1:T(8,128)S(1)} %add.138), channel_id=1, source_target_pairs={{0,8},{1,9},{2,10},{3,11},{4,12},{5,13},{6,14},{7,15},{8,0},{9,1},... | collective-permute-start | bytes 15368 | tf_op jit(solution)/shard_map/ppermute | solution.py:41
  66.5 4.5 %collective-permute-start.18 = (f32[80,16]{0,1:T(8,128)S(1)}, f32[80,16]{0,1:T(8,128)S(1)}, u32[]{:S(2)}, u32[]{:S(2)}) collective-permute-start(f32[80,16]{0,1:T(8,128)S(1)} %add.139), channel_id=1, source_target_pairs={{0,16},{1,17},{2,18},{3,19},{4,20},{5,21},{6,22},{7,23},{8,24},{9,... | collective-permute-start | bytes 15368 | tf_op jit(solution)/shard_map/ppermute | solution.py:41
  71.0 5.4 %copy-start.2 = (f32[80,16]{0,1:T(8,128)}, f32[80,16]{0,1:T(8,128)S(1)}, u32[]{:S(2)}) copy-start(f32[80,16]{0,1:T(8,128)S(1)} %add.140) | copy-start | bytes 15364

commit v19 on v13

--- a/solution.py
+++ b/solution.py
@@ -196,9 +196,8 @@
     residue = applied - jnp.dot(coeffs.T, krylov, precision=highest)
     short_gram = (outer - jnp.dot(coeffs.T, coeffs, precision=highest)) / total_points
     eye = jnp.eye(vec_count, dtype=jnp.bool_)
-    short_diag = jnp.sum(jnp.where(eye, short_gram, 0.0), axis=0)
     outer_diag = jnp.sum(jnp.where(eye, outer, 0.0), axis=0)
-    kept = short_diag * (64 * total_points) >= outer_diag
+    kept = (outer_diag - jnp.sum(coeffs * coeffs, axis=0)) * 64 >= outer_diag
     def exact_gram():
         part = jnp.dot(residue, residue.T, precision=highest)
         return butterfly_sum(part, both_axes) / total_points

time: 69.5 us -> 70.9 us (1.020)
  other arithmetic: 6.59 us -> 7.3 us
where the time goes in v19:
time: 70.9 us; the launch traced here: 70.5 us
  starting transfers between devices  22.5 us (32%)
  waiting for transfers between devices  18.2 us (26%)
  local copies, waits for them, and re-layouts  9.91 us (14%)
  other arithmetic  7.3 us (10%)
  matrix products  7.24 us (10%)
  Pallas kernels  3.12 us (4%)
  between operations  2.11 us (3%)
    ppermute x5, starting transfers between devices, xor_gather(): block = jnp.concatenate([block, lax.ppermute(block, axis, route)], axis=dim)  10.8 us
    ppermute x5, waiting for transfers between devices, butterfly_sum(): block = block + lax.ppermute(block, axes, route)  10.3 us
    ppermute x5, starting transfers between devices, butterfly_sum(): block = block + lax.ppermute(block, axes, route)  6.35 us
    reshape x1, local copies, waits for them, and re-layouts, on_device(): couple = coupling.reshape(3, group_size, slot_count, rank_width, rank_width)  5.63 us
    ppermute x5, waiting for transfers between devices, xor_gather(): block = jnp.concatenate([block, lax.ppermute(block, axis, route)], axis=dim)  5.01 us
    dot_general x1, matrix products, on_device(): jnp.einsum('cfvl,jcfkl->cfvjk', sources, couple, preferred_element_type=j...  4.31 us
    pallas_call x1, Pallas kernels, chol_solve(): pl.pallas_call(chol_solve_kernel, out_shape=(jax.ShapeDtypeStruct((size,...  3.12 us
    ppermute x2, waiting for transfers between devices, butterfly_scatter(): parts = keep + lax.ppermute(give, axis, route)  2.87 us
  transfers between devices with their start and end apart: 14, of which 10 were waited for; matrix products, arithmetic and copies ran while one was open for 20% of the time, Pallas kernels for 0%

profile of v19, /device:TPU:0, one launch (start us, length us, event | category | flops | bytes accessed | tf_op | source)
XLA Modules:
  0.0 70.5 jit_solution(5872150381616904990)
XLA Ops:
  1.6 2.5 %collective-permute-start.12 = (bf16[16,512]{1,0:T(8,128)(2,1)S(1)}, bf16[16,512]{1,0:T(8,128)(2,1)S(1)}, u32[]{:S(2)}, u32[]{:S(2)}) collective-permute-start(bf16[16,512]{1,0:T(8,128)(2,1)S(1)} %convert_element_type.20), channel_id=1, source_target_pairs={{0,1},{1,2},{2,3},{3,4},{4,5},{5,6},{6,7},{7,8},{8,9},{9,10},{10,1... | collective-permute-start | bytes 49160 | tf_op jit(solution)/shard_map/ppermute | solution.py:20
  4.1 1.3 %collective-permute-start.13 = (bf16[16,512]{1,0:T(8,128)(2,1)S(1)}, bf16[16,512]{1,0:T(8,128)(2,1)S(1)}, u32[]{:S(2)}, u32[]{:S(2)}) collective-permute-start(bf16[16,512]{1,0:T(8,128)(2,1)S(1)} %convert_element_type.20), channel_id=1, source_target_pairs={{1,0},{2,1},{3,2},{4,3},{5,4},{6,5},{7,6},{8,7},{9,8},{10,9},{11,1... | collective-permute-start | bytes 49160 | tf_op jit(solution)/shard_map/ppermute | solution.py:23
  5.4 1.0 %convolution_convert_fusion = bf16[4,16,64]{2,1,0:T(8,128)(2,1)S(1)} fusion(bf16[4,64,128]{2,1,0:T(8,128)(2,1)} %param.13, f32[16,512]{1,0:T(8,128)} %param.11), kind=kOutput, calls=%fused_computation.10 | convolution fusion | flops 1060864 | bytes 106496 | tf_op jit(solution)/shard_map/cki,vci->cvk/dot_general | solution.py:148
  6.5 5.8 %collective-permute-start.5 = (bf16[1,4,1024]{2,1,0:T(4,128)(2,1)S(1)}, bf16[1,4,1024]{2,1,0:T(4,128)(2,1)S(1)}, u32[]{:S(2)}, u32[]{:S(2)}) collective-permute-start(bf16[1,4,1024]{2,1,0:T(4,128)(2,1)S(1)} %reshape.117), channel_id=1, source_target_pairs={{0,4},{4,0},{8,12},{12,8},{16,20},{20,16},{24,28},{28,24},{1,5},{5... | collective-permute-start | bytes 24584 | tf_op jit(solution)/shard_map/ppermute | solution.py:53
  16.9 1.6 %collective-permute-start.6 = (bf16[2,4,1024]{2,1,0:T(4,128)(2,1)S(1)}, bf16[2,4,1024]{2,1,0:T(4,128)(2,1)S(1)}, u32[]{:S(2)}, u32[]{:S(2)}) collective-permute-start(bf16[2,4,1024]{2,1,0:T(4,128)(2,1)S(1)} %pad_maximum_fusion.3), channel_id=1, source_target_pairs={{0,8},{4,12},{8,0},{12,4},{16,24},{20,28},{24,16},{28,20},{1,9},{5... | collective-permute-start | bytes 49160 | tf_op jit(solution)/shard_map/ppermute | solution.py:53
  18.5 2.1 %collective-permute-done.6 = bf16[2,4,1024]{2,1,0:T(4,128)(2,1)S(1)} collective-permute-done((bf16[2,4,1024]{2,1,0:T(4,128)(2,1)S(1)}, bf16[2,4,1024]{2,1,0:T(4,128)(2,1)S(1)}, u32[]{:S(2)}, u32[]{:S(2)}) %collective-permute-start.6) | collective-permute-done | bytes 16416 | tf_op jit(solution)/shard_map/ppermute | solution.py:53
  20.7 2.7 %collective-permute-start.7 = (bf16[4,4,1024]{2,1,0:T(4,128)(2,1)S(1)}, bf16[4,4,1024]{2,1,0:T(4,128)(2,1)S(1)}, u32[]{:S(2)}, u32[]{:S(2)}) collective-permute-start(bf16[4,4,1024]{2,1,0:T(4,128)(2,1)S(1)} %pad_maximum_fusion.2), channel_id=1, source_target_pairs={{0,16},{4,20},{8,24},{12,28},{16,0},{20,4},{24,8},{28,12},{1,17},{... | collective-permute-start | bytes 98312 | tf_op jit(solution)/shard_map/ppermute | solution.py:53
  23.4 2.2 %collective-permute-done.7 = bf16[4,4,1024]{2,1,0:T(4,128)(2,1)S(1)} collective-permute-done((bf16[4,4,1024]{2,1,0:T(4,128)(2,1)S(1)}, bf16[4,4,1024]{2,1,0:T(4,128)(2,1)S(1)}, u32[]{:S(2)}, u32[]{:S(2)}) %collective-permute-start.7) | collective-permute-done | bytes 32800 | tf_op jit(solution)/shard_map/ppermute | solution.py:53
  27.7 5.6 %reshape.121 = bf16[3,16,4,64,64]{4,3,2,1,0:T(8,128)(2,1)} reshape(bf16[3,16,4,4096]{3,2,1,0:T(4,128)(2,1)} %param.16) | data formatting | bytes 3145728 | tf_op jit(solution)/shard_map/reshape | solution.py:170
  33.3 1.2 %gather_fusion.1 = bf16[32,16,128]{2,1,0:T(8,128)(2,1)} fusion(bf16[16,12,128]{2,0,1:T(8,128)(2,1)S(1)} %copy_bitcast_fusion, s32[1024]{0:T(1024)S(1)} %pad_clamp_fusion), kind=kCustom, calls=%fused_computation.1 | custom fusion | bytes 262272 | tf_op jit(solution)/shard_map/gather | solution.py:181
  34.6 1.0 %pad_maximum_fusion = bf16[8,16,1024]{2,1,0:T(8,128)(2,1)S(1)} fusion(bf16[8,8,1024]{2,1,0:T(8,128)(2,1)} %collective-permute-done.9, bf16[8,4,1024]{2,1,0:T(4,128)(2,1)S(1)} %collective-permute-done.8, bf16[8,4,1024]{2,1,0:T(4,128)(2,1)S(1)} %constant_dynamic-update-slice_fusion), kind=kLoop, calls=%fused_computation.13 | loop fusion | flops 786432 | bytes 524288 | tf_op jit(solution)/shard_map/concatenate | solution.py:53
  37.3 4.3 %multiply_reduce_fusion = f32[16,16,64]{2,1,0:T(8,128)S(1)} fusion(bf16[3,16,4,64,64]{4,3,2,1,0:T(8,128)(2,1)} %reshape.121, f32[16,4,3,64]{3,2,1,0:T(4,128)} %broadcast_multiply_fusion, bf16[16,4,16,64]{3,2,1,0:T(8,128)(2,1)} %reshape.120, pred[16,4,64]{2,1,0:T(4,128)(4,1)} %get-tuple-element.31), kind=kOutput, calls=%fused_computation.6 | convolution fusion | flops 25608192 | bytes 1822720 | tf_op jit(solution)/shard_map/cfvl,jcfkl->cfvjk/dot_general | solution.py:171
  41.7 1.5 %collective-permute-start.10 = (f32[8,16,64]{2,1,0:T(8,128)S(1)}, f32[8,16,64]{2,1,0:T(8,128)S(1)}, u32[]{:S(2)}, u32[]{:S(2)}) collective-permute-start(f32[8,16,64]{2,1,0:T(8,128)S(1)} %dynamic-slice_bitcast_fusion), channel_id=1, source_target_pairs={{0,2},{1,3},{2,0},{3,1},{4,6},{5,7},{6,4},{7,5},{8,10},{9,11},{10,... | collective-permute-start | bytes 98312 | tf_op jit(solution)/shard_map/ppermute | solution.py:71
  44.1 1.9 %collective-permute-done.10 = f32[8,16,64]{2,1,0:T(8,128)S(1)} collective-permute-done((f32[8,16,64]{2,1,0:T(8,128)S(1)}, f32[8,16,64]{2,1,0:T(8,128)S(1)}, u32[]{:S(2)}, u32[]{:S(2)}) %collective-permute-start.10) | collective-permute-done | bytes 32800 | tf_op jit(solution)/shard_map/ppermute | solution.py:71
  46.4 1.0 %collective-permute-done.11 = f32[4,16,64]{2,1,0:T(8,128)S(1)} collective-permute-done((f32[4,16,64]{2,1,0:T(8,128)S(1)}, f32[4,16,64]{2,1,0:T(8,128)S(1)}, u32[]{:S(2)}, u32[]{:S(2)}) %collective-permute-start.11) | collective-permute-done | bytes 16416 | tf_op jit(solution)/shard_map/ppermute | solution.py:71
  48.1 1.0 %collective-permute-done.14 = f32[80,16]{0,1:T(8,128)S(1)} collective-permute-done((f32[80,16]{0,1:T(8,128)S(1)}, f32[80,16]{0,1:T(8,128)S(1)}, u32[]{:S(2)}, u32[]{:S(2)}) %collective-permute-start.14) | collective-permute-done | bytes 5152 | tf_op jit(solution)/shard_map/ppermute | solution.py:41
  49.2 1.4 %collective-permute-start.15 = (f32[80,16]{0,1:T(8,128)S(1)}, f32[80,16]{0,1:T(8,128)S(1)}, u32[]{:S(2)}, u32[]{:S(2)}) collective-permute-start(f32[80,16]{0,1:T(8,128)S(1)} %fusion.55), channel_id=1, source_target_pairs={{0,2},{1,3},{2,0},{3,1},{4,6},{5,7},{6,4},{7,5},{8,10},{9,11},{10,... | collective-permute-start | bytes 15368 | tf_op jit(solution)/shard_map/ppermute | solution.py:41
  50.6 2.2 %collective-permute-done.15 = f32[80,16]{0,1:T(8,128)S(1)} collective-permute-done((f32[80,16]{0,1:T(8,128)S(1)}, f32[80,16]{0,1:T(8,128)S(1)}, u32[]{:S(2)}, u32[]{:S(2)}) %collective-permute-start.15) | collective-permute-done | bytes 5152 | tf_op jit(solution)/shard_map/ppermute | solution.py:41
  53.4 3.1 %collective-permute-done.16 = f32[80,16]{0,1:T(8,128)S(1)} collective-permute-done((f32[80,16]{0,1:T(8,128)S(1)}, f32[80,16]{0,1:T(8,128)S(1)}, u32[]{:S(2)}, u32[]{:S(2)}) %collective-permute-start.16) | collective-permute-done | bytes 5152 | tf_op jit(solution)/shard_map/ppermute | solution.py:41
  56.5 1.6 %collective-permute-start.17 = (f32[80,16]{0,1:T(8,128)S(1)}, f32[80,16]{0,1:T(8,128)S(1)}, u32[]{:S(2)}, u32[]{:S(2)}) collective-permute-start(f32[80,16]{0,1:T(8,128)S(1)} %add.132), channel_id=1, source_target_pairs={{0,8},{1,9},{2,10},{3,11},{4,12},{5,13},{6,14},{7,15},{8,0},{9,1},... | collective-permute-start | bytes 15368 | tf_op jit(solution)/shard_map/ppermute | solution.py:41
  58.1 2.1 %collective-permute-done.17 = f32[80,16]{0,1:T(8,128)S(1)} collective-permute-done((f32[80,16]{0,1:T(8,128)S(1)}, f32[80,16]{0,1:T(8,128)S(1)}, u32[]{:S(2)}, u32[]{:S(2)}) %collective-permute-start.17) | collective-permute-done | bytes 5152 | tf_op jit(solution)/shard_map/ppermute | solution.py:41
  60.2 2.6 %collective-permute-start.18 = (f32[80,16]{0,1:T(8,128)S(1)}, f32[80,16]{0,1:T(8,128)S(1)}, u32[]{:S(2)}, u32[]{:S(2)}) collective-permute-start(f32[80,16]{0,1:T(8,128)S(1)} %add.133), channel_id=1, source_target_pairs={{0,16},{1,17},{2,18},{3,19},{4,20},{5,21},{6,22},{7,23},{8,24},{9,... | collective-permute-start | bytes 15368 | tf_op jit(solution)/shard_map/ppermute | solution.py:41
  62.8 1.9 %collective-permute-done.18 = f32[80,16]{0,1:T(8,128)S(1)} collective-permute-done((f32[80,16]{0,1:T(8,128)S(1)}, f32[80,16]{0,1:T(8,128)S(1)}, u32[]{:S(2)}, u32[]{:S(2)}) %collective-permute-start.18) | collective-permute-done | bytes 5152 | tf_op jit(solution)/shard_map/ppermute | solution.py:41
  67.3 3.1 %shard_map.112 = (f32[16,16]{1,0:T(8,128)}, f32[16,512]{1,0:T(8,128)}) custom-call(f32[16,16]{1,0:T(8,128)} %broadcast_multiply_fusion.1.gram_ref, f32[16,512]{1,0:T(8,128)S(1)} %convolution_subtract_fusion.residue_ref), custom_call_target="tpu_custom_call" | custom-call | flops 540672 | bytes 67584 | tf_op jit(solution)/shard_map/pallas_call | solution.py:117
  (68 shorter events, 13.6 us)
Async XLA Ops:
  0.6 42.5 %copy-start = (bf16[3,4,8,128,128]{4,3,2,1,0:T(8,128)(2,1)S(1)}, bf16[3,4,8,128,128]{4,3,2,1,0:T(8,128)(2,1)}, u32[]{:S(2)}) copy-start(bf16[3,4,8,128,128]{4,3,2,1,0:T(8,128)(2,1)} %param.14) | copy-start | bytes 9437188
  1.6 31.7 %collective-permute-start.12 = (bf16[16,512]{1,0:T(8,128)(2,1)S(1)}, bf16[16,512]{1,0:T(8,128)(2,1)S(1)}, u32[]{:S(2)}, u32[]{:S(2)}) collective-permute-start(bf16[16,512]{1,0:T(8,128)(2,1)S(1)} %convert_element_type.20), channel_id=1, source_target_pairs={{0,1},{1,2},{2,3},{3,4},{4,5},{5,6},{6,7},{7,8},{8,9},{9,10},{10,1... | collective-permute-start | bytes 49160 | tf_op jit(solution)/shard_map/ppermute | solution.py:20
  4.1 29.2 %collective-permute-start.13 = (bf16[16,512]{1,0:T(8,128)(2,1)S(1)}, bf16[16,512]{1,0:T(8,128)(2,1)S(1)}, u32[]{:S(2)}, u32[]{:S(2)}) collective-permute-start(bf16[16,512]{1,0:T(8,128)(2,1)S(1)} %convert_element_type.20), channel_id=1, source_target_pairs={{1,0},{2,1},{3,2},{4,3},{5,4},{6,5},{7,6},{8,7},{9,8},{10,9},{11,1... | collective-permute-start | bytes 49160 | tf_op jit(solution)/shard_map/ppermute | solution.py:23
  6.5 10.4 %collective-permute-start.5 = (bf16[1,4,1024]{2,1,0:T(4,128)(2,1)S(1)}, bf16[1,4,1024]{2,1,0:T(4,128)(2,1)S(1)}, u32[]{:S(2)}, u32[]{:S(2)}) collective-permute-start(bf16[1,4,1024]{2,1,0:T(4,128)(2,1)S(1)} %reshape.117), channel_id=1, source_target_pairs={{0,4},{4,0},{8,12},{12,8},{16,20},{20,16},{24,28},{28,24},{1,5},{5... | collective-permute-start | bytes 24584 | tf_op jit(solution)/shard_map/ppermute | solution.py:53
  16.9 3.8 %collective-permute-start.6 = (bf16[2,4,1024]{2,1,0:T(4,128)(2,1)S(1)}, bf16[2,4,1024]{2,1,0:T(4,128)(2,1)S(1)}, u32[]{:S(2)}, u32[]{:S(2)}) collective-permute-start(bf16[2,4,1024]{2,1,0:T(4,128)(2,1)S(1)} %pad_maximum_fusion.3), channel_id=1, source_target_pairs={{0,8},{4,12},{8,0},{12,4},{16,24},{20,28},{24,16},{28,20},{1,9},{5... | collective-permute-start | bytes 49160 | tf_op jit(solution)/shard_map/ppermute | solution.py:53
  20.7 4.9 %collective-permute-start.7 = (bf16[4,4,1024]{2,1,0:T(4,128)(2,1)S(1)}, bf16[4,4,1024]{2,1,0:T(4,128)(2,1)S(1)}, u32[]{:S(2)}, u32[]{:S(2)}) collective-permute-start(bf16[4,4,1024]{2,1,0:T(4,128)(2,1)S(1)} %pad_maximum_fusion.2), channel_id=1, source_target_pairs={{0,16},{4,20},{8,24},{12,28},{16,0},{20,4},{24,8},{28,12},{1,17},{... | collective-permute-start | bytes 98312 | tf_op jit(solution)/shard_map/ppermute | solution.py:53
  25.6 1.3 %collective-permute-start.8 = (bf16[8,4,1024]{2,1,0:T(4,128)(2,1)S(1)}, bf16[8,4,1024]{2,1,0:T(4,128)(2,1)S(1)}, u32[]{:S(2)}, u32[]{:S(2)}) collective-permute-start(bf16[8,4,1024]{2,1,0:T(4,128)(2,1)S(1)} %constant_dynamic-update-slice_fusion), channel_id=1, source_target_pairs={{0,1},{1,0},{2,3},{3,2},{4,5},{5,4},{6,7},{7,6},{8,9},{9,8},{10,11... | collective-permute-start | bytes 196616 | tf_op jit(solution)/shard_map/ppermute | solution.py:53
  27.0 7.6 %collective-permute-start.9 = (bf16[8,8,1024]{2,1,0:T(8,128)(2,1)S(1)}, bf16[8,8,1024]{2,1,0:T(8,128)(2,1)}, u32[]{:S(2)}, u32[]{:S(2)}) collective-permute-start(bf16[8,8,1024]{2,1,0:T(8,128)(2,1)S(1)} %pad_maximum_fusion.1), channel_id=1, source_target_pairs={{0,2},{1,3},{2,0},{3,1},{4,6},{5,7},{6,4},{7,5},{8,10},{9,11},{10,... | collective-permute-start | bytes 393224 | tf_op jit(solution)/shard_map/ppermute | solution.py:53
  36.4 6.8 %copy-start.1 = (bf16[32,16,128]{2,1,0:T(8,128)(2,1)S(1)}, bf16[32,16,128]{2,1,0:T(8,128)(2,1)}, u32[]{:S(2)}) copy-start(bf16[32,16,128]{2,1,0:T(8,128)(2,1)} %gather_fusion.1) | copy-start | bytes 393220
  37.3 10.0 %copy-start.3 = (bf16[4,64,128]{2,1,0:T(8,128)(2,1)S(1)}, bf16[4,64,128]{2,1,0:T(8,128)(2,1)}, u32[]{:S(2)}) copy-start(bf16[4,64,128]{2,1,0:T(8,128)(2,1)} %param.13) | copy-start | bytes 196612
  37.3 10.3 %copy-start.2 = (f32[64,512]{1,0:T(8,128)S(1)}, f32[64,512]{1,0:T(8,128)}, u32[]{:S(2)}) copy-start(f32[64,512]{1,0:T(8,128)} %param.19) | copy-start | bytes 393220
  41.7 4.3 %collective-permute-start.10 = (f32[8,16,64]{2,1,0:T(8,128)S(1)}, f32[8,16,64]{2,1,0:T(8,128)S(1)}, u32[]{:S(2)}, u32[]{:S(2)}) collective-permute-start(f32[8,16,64]{2,1,0:T(8,128)S(1)} %dynamic-slice_bitcast_fusion), channel_id=1, source_target_pairs={{0,2},{1,3},{2,0},{3,1},{4,6},{5,7},{6,4},{7,5},{8,10},{9,11},{10,... | collective-permute-start | bytes 98312 | tf_op jit(solution)/shard_map/ppermute | solution.py:71
  46.0 1.3 %collective-permute-start.11 = (f32[4,16,64]{2,1,0:T(8,128)S(1)}, f32[4,16,64]{2,1,0:T(8,128)S(1)}, u32[]{:S(2)}, u32[]{:S(2)}) collective-permute-start(f32[4,16,64]{2,1,0:T(8,128)S(1)} %dynamic-slice_bitcast_fusion.1), channel_id=1, source_target_pairs={{0,1},{1,0},{2,3},{3,2},{4,5},{5,4},{6,7},{7,6},{8,9},{9,8},{10,11... | collective-permute-start | bytes 49160 | tf_op jit(solution)/shard_map/ppermute | solution.py:71
  47.9 1.2 %collective-permute-start.14 = (f32[80,16]{0,1:T(8,128)S(1)}, f32[80,16]{0,1:T(8,128)S(1)}, u32[]{:S(2)}, u32[]{:S(2)}) collective-permute-start(f32[80,16]{0,1:T(8,128)S(1)} %pad_maximum_fusion.4), channel_id=1, source_target_pairs={{0,1},{1,0},{2,3},{3,2},{4,5},{5,4},{6,7},{7,6},{8,9},{9,8},{10,11... | collective-permute-start | bytes 15368 | tf_op jit(solution)/shard_map/ppermute | solution.py:41
  49.2 3.7 %collective-permute-start.15 = (f32[80,16]{0,1:T(8,128)S(1)}, f32[80,16]{0,1:T(8,128)S(1)}, u32[]{:S(2)}, u32[]{:S(2)}) collective-permute-start(f32[80,16]{0,1:T(8,128)S(1)} %fusion.55), channel_id=1, source_target_pairs={{0,2},{1,3},{2,0},{3,1},{4,6},{5,7},{6,4},{7,5},{8,10},{9,11},{10,... | collective-permute-start | bytes 15368 | tf_op jit(solution)/shard_map/ppermute | solution.py:41
  52.8 3.7 %collective-permute-start.16 = (f32[80,16]{0,1:T(8,128)S(1)}, f32[80,16]{0,1:T(8,128)S(1)}, u32[]{:S(2)}, u32[]{:S(2)}) collective-permute-start(f32[80,16]{0,1:T(8,128)S(1)} %add.131), channel_id=1, source_target_pairs={{0,4},{1,5},{2,6},{3,7},{4,0},{5,1},{6,2},{7,3},{8,12},{9,13},{10,... | collective-permute-start | bytes 15368 | tf_op jit(solution)/shard_map/ppermute | solution.py:41
  56.5 3.7 %collective-permute-start.17 = (f32[80,16]{0,1:T(8,128)S(1)}, f32[80,16]{0,1:T(8,128)S(1)}, u32[]{:S(2)}, u32[]{:S(2)}) collective-permute-start(f32[80,16]{0,1:T(8,128)S(1)} %add.132), channel_id=1, source_target_pairs={{0,8},{1,9},{2,10},{3,11},{4,12},{5,13},{6,14},{7,15},{8,0},{9,1},... | collective-permute-start | bytes 15368 | tf_op jit(solution)/shard_map/ppermute | solution.py:41
  60.2 4.5 %collective-permute-start.18 = (f32[80,16]{0,1:T(8,128)S(1)}, f32[80,16]{0,1:T(8,128)S(1)}, u32[]{:S(2)}, u32[]{:S(2)}) collective-permute-start(f32[80,16]{0,1:T(8,128)S(1)} %add.133), channel_id=1, source_target_pairs={{0,16},{1,17},{2,18},{3,19},{4,20},{5,21},{6,22},{7,23},{8,24},{9,... | collective-permute-start | bytes 15368 | tf_op jit(solution)/shard_map/ppermute | solution.py:41
  64.8 5.6 %copy-start.4 = (f32[64,16]{0,1:T(8,128)}, f32[64,16]{0,1:T(8,128)S(1)}, u32[]{:S(2)}) copy-start(f32[64,16]{0,1:T(8,128)S(1)} %get-tuple-element.28) | copy-start | bytes 12292

commit v20 on v13

--- a/solution.py
+++ b/solution.py
@@ -101,7 +101,7 @@
         low = jnp.where(cols == step, low_column, low)
         left = left - low_column * low_row
     chol_ref[...] = low
-    block = residue_ref[...]
+    block = jnp.where(rows == cols, 1.0, 0.0)
     for step in range(size):
         low_column = jnp.sum(jnp.where(cols == step, low, 0.0), axis=1, keepdims=True)
         diagonal = jnp.sum(jnp.where(row_ids == step, low_column, 0.0), axis=0, keepdims=True)
@@ -109,7 +109,7 @@
         block = jnp.where(
             row_ids == step, solved, jnp.where(row_ids > step, block - low_column * solved, block)
         )
-    block_ref[...] = block
+    block_ref[...] = jnp.dot(block, residue_ref[...], precision=lax.Precision.HIGHEST)
 
 
 def chol_solve(gram_matrix, residue):

time: 69.5 us -> 69.7 us (level)
  no operation moved by 1% of the time
where the time goes in v20:
time: 69.7 us; the launch traced here: 69.3 us
  starting transfers between devices  22.5 us (32%)
  waiting for transfers between devices  18.2 us (26%)
  local copies, waits for them, and re-layouts  9.88 us (14%)
  matrix products  7.35 us (11%)
  other arithmetic  6.59 us (9%)
  Pallas kernels  2.59 us (4%)
  between operations  2.1 us (3%)
    ppermute x5, starting transfers between devices, xor_gather(): block = jnp.concatenate([block, lax.ppermute(block, axis, route)], axis=dim)  10.8 us
    ppermute x5, waiting for transfers between devices, butterfly_sum(): block = block + lax.ppermute(block, axes, route)  10.3 us
    ppermute x5, starting transfers between devices, butterfly_sum(): block = block + lax.ppermute(block, axes, route)  6.35 us
    reshape x1, local copies, waits for them, and re-layouts, on_device(): couple = coupling.reshape(3, group_size, slot_count, rank_width, rank_width)  5.63 us
    ppermute x5, waiting for transfers between devices, xor_gather(): block = jnp.concatenate([block, lax.ppermute(block, axis, route)], axis=dim)  5.01 us
    dot_general x1, matrix products, on_device(): jnp.einsum('cfvl,jcfkl->cfvjk', sources, couple, preferred_element_type=j...  4.31 us
    ppermute x2, waiting for transfers between devices, butterfly_scatter(): parts = keep + lax.ppermute(give, axis, route)  2.87 us
    pallas_call x1, Pallas kernels, chol_solve(): pl.pallas_call(chol_solve_kernel, out_shape=(jax.ShapeDtypeStruct((size,...  2.59 us
  transfers between devices with their start and end apart: 14, of which 10 were waited for; matrix products, arithmetic and copies ran while one was open for 20% of the time, Pallas kernels for 0%

profile of v20, /device:TPU:0, one launch (start us, length us, event | category | flops | bytes accessed | tf_op | source)
XLA Modules:
  0.0 69.3 jit_solution(15884732217929231964)
XLA Ops:
  1.6 2.5 %collective-permute-start.12 = (bf16[16,512]{1,0:T(8,128)(2,1)S(1)}, bf16[16,512]{1,0:T(8,128)(2,1)S(1)}, u32[]{:S(2)}, u32[]{:S(2)}) collective-permute-start(bf16[16,512]{1,0:T(8,128)(2,1)S(1)} %convert_element_type.20), channel_id=1, source_target_pairs={{0,1},{1,2},{2,3},{3,4},{4,5},{5,6},{6,7},{7,8},{8,9},{9,10},{10,1... | collective-permute-start | bytes 49160 | tf_op jit(solution)/shard_map/ppermute | solution.py:20
  4.1 1.3 %collective-permute-start.13 = (bf16[16,512]{1,0:T(8,128)(2,1)S(1)}, bf16[16,512]{1,0:T(8,128)(2,1)S(1)}, u32[]{:S(2)}, u32[]{:S(2)}) collective-permute-start(bf16[16,512]{1,0:T(8,128)(2,1)S(1)} %convert_element_type.20), channel_id=1, source_target_pairs={{1,0},{2,1},{3,2},{4,3},{5,4},{6,5},{7,6},{8,7},{9,8},{10,9},{11,1... | collective-permute-start | bytes 49160 | tf_op jit(solution)/shard_map/ppermute | solution.py:23
  5.4 1.0 %convolution_convert_fusion = bf16[4,16,64]{2,1,0:T(8,128)(2,1)S(1)} fusion(bf16[4,64,128]{2,1,0:T(8,128)(2,1)} %param.13, f32[16,512]{1,0:T(8,128)} %param.11), kind=kOutput, calls=%fused_computation.11 | convolution fusion | flops 1060864 | bytes 106496 | tf_op jit(solution)/shard_map/cki,vci->cvk/dot_general | solution.py:148
  6.5 5.8 %collective-permute-start.5 = (bf16[1,4,1024]{2,1,0:T(4,128)(2,1)S(1)}, bf16[1,4,1024]{2,1,0:T(4,128)(2,1)S(1)}, u32[]{:S(2)}, u32[]{:S(2)}) collective-permute-start(bf16[1,4,1024]{2,1,0:T(4,128)(2,1)S(1)} %reshape.117), channel_id=1, source_target_pairs={{0,4},{4,0},{8,12},{12,8},{16,20},{20,16},{24,28},{28,24},{1,5},{5... | collective-permute-start | bytes 24584 | tf_op jit(solution)/shard_map/ppermute | solution.py:53
  16.9 1.6 %collective-permute-start.6 = (bf16[2,4,1024]{2,1,0:T(4,128)(2,1)S(1)}, bf16[2,4,1024]{2,1,0:T(4,128)(2,1)S(1)}, u32[]{:S(2)}, u32[]{:S(2)}) collective-permute-start(bf16[2,4,1024]{2,1,0:T(4,128)(2,1)S(1)} %pad_maximum_fusion.3), channel_id=1, source_target_pairs={{0,8},{4,12},{8,0},{12,4},{16,24},{20,28},{24,16},{28,20},{1,9},{5... | collective-permute-start | bytes 49160 | tf_op jit(solution)/shard_map/ppermute | solution.py:53
  18.5 2.1 %collective-permute-done.6 = bf16[2,4,1024]{2,1,0:T(4,128)(2,1)S(1)} collective-permute-done((bf16[2,4,1024]{2,1,0:T(4,128)(2,1)S(1)}, bf16[2,4,1024]{2,1,0:T(4,128)(2,1)S(1)}, u32[]{:S(2)}, u32[]{:S(2)}) %collective-permute-start.6) | collective-permute-done | bytes 16416 | tf_op jit(solution)/shard_map/ppermute | solution.py:53
  20.7 2.7 %collective-permute-start.7 = (bf16[4,4,1024]{2,1,0:T(4,128)(2,1)S(1)}, bf16[4,4,1024]{2,1,0:T(4,128)(2,1)S(1)}, u32[]{:S(2)}, u32[]{:S(2)}) collective-permute-start(bf16[4,4,1024]{2,1,0:T(4,128)(2,1)S(1)} %pad_maximum_fusion.2), channel_id=1, source_target_pairs={{0,16},{4,20},{8,24},{12,28},{16,0},{20,4},{24,8},{28,12},{1,17},{... | collective-permute-start | bytes 98312 | tf_op jit(solution)/shard_map/ppermute | solution.py:53
  23.4 2.2 %collective-permute-done.7 = bf16[4,4,1024]{2,1,0:T(4,128)(2,1)S(1)} collective-permute-done((bf16[4,4,1024]{2,1,0:T(4,128)(2,1)S(1)}, bf16[4,4,1024]{2,1,0:T(4,128)(2,1)S(1)}, u32[]{:S(2)}, u32[]{:S(2)}) %collective-permute-start.7) | collective-permute-done | bytes 32800 | tf_op jit(solution)/shard_map/ppermute | solution.py:53
  27.7 5.6 %reshape.121 = bf16[3,16,4,64,64]{4,3,2,1,0:T(8,128)(2,1)} reshape(bf16[3,16,4,4096]{3,2,1,0:T(4,128)(2,1)} %param.16) | data formatting | bytes 3145728 | tf_op jit(solution)/shard_map/reshape | solution.py:170
  33.3 1.2 %gather_fusion.1 = bf16[32,16,128]{2,1,0:T(8,128)(2,1)} fusion(bf16[16,12,128]{2,0,1:T(8,128)(2,1)S(1)} %copy_bitcast_fusion, s32[1024]{0:T(1024)S(1)} %pad_clamp_fusion), kind=kCustom, calls=%fused_computation.1 | custom fusion | bytes 262272 | tf_op jit(solution)/shard_map/gather | solution.py:181
  34.5 1.0 %pad_maximum_fusion = bf16[8,16,1024]{2,1,0:T(8,128)(2,1)S(1)} fusion(bf16[8,8,1024]{2,1,0:T(8,128)(2,1)} %collective-permute-done.9, bf16[8,4,1024]{2,1,0:T(4,128)(2,1)S(1)} %collective-permute-done.8, bf16[8,4,1024]{2,1,0:T(4,128)(2,1)S(1)} %constant_dynamic-update-slice_fusion), kind=kLoop, calls=%fused_computation.16 | loop fusion | flops 786432 | bytes 524288 | tf_op jit(solution)/shard_map/concatenate | solution.py:53
  37.3 4.3 %multiply_reduce_fusion = f32[16,16,64]{2,1,0:T(8,128)S(1)} fusion(bf16[3,16,4,64,64]{4,3,2,1,0:T(8,128)(2,1)} %reshape.121, f32[16,4,3,64]{3,2,1,0:T(4,128)} %broadcast_multiply_fusion, bf16[16,4,16,64]{3,2,1,0:T(8,128)(2,1)} %reshape.120, pred[16,4,64]{2,1,0:T(4,128)(4,1)} %get-tuple-element.14), kind=kOutput, calls=%fused_computation.7 | convolution fusion | flops 25608192 | bytes 1822720 | tf_op jit(solution)/shard_map/cfvl,jcfkl->cfvjk/dot_general | solution.py:171
  41.6 1.5 %collective-permute-start.10 = (f32[8,16,64]{2,1,0:T(8,128)S(1)}, f32[8,16,64]{2,1,0:T(8,128)S(1)}, u32[]{:S(2)}, u32[]{:S(2)}) collective-permute-start(f32[8,16,64]{2,1,0:T(8,128)S(1)} %dynamic-slice_bitcast_fusion), channel_id=1, source_target_pairs={{0,2},{1,3},{2,0},{3,1},{4,6},{5,7},{6,4},{7,5},{8,10},{9,11},{10,... | collective-permute-start | bytes 98312 | tf_op jit(solution)/shard_map/ppermute | solution.py:71
  44.1 1.9 %collective-permute-done.10 = f32[8,16,64]{2,1,0:T(8,128)S(1)} collective-permute-done((f32[8,16,64]{2,1,0:T(8,128)S(1)}, f32[8,16,64]{2,1,0:T(8,128)S(1)}, u32[]{:S(2)}, u32[]{:S(2)}) %collective-permute-start.10) | collective-permute-done | bytes 32800 | tf_op jit(solution)/shard_map/ppermute | solution.py:71
  46.3 1.0 %collective-permute-done.11 = f32[4,16,64]{2,1,0:T(8,128)S(1)} collective-permute-done((f32[4,16,64]{2,1,0:T(8,128)S(1)}, f32[4,16,64]{2,1,0:T(8,128)S(1)}, u32[]{:S(2)}, u32[]{:S(2)}) %collective-permute-start.11) | collective-permute-done | bytes 16416 | tf_op jit(solution)/shard_map/ppermute | solution.py:71
  48.1 1.0 %collective-permute-done.14 = f32[80,16]{0,1:T(8,128)S(1)} collective-permute-done((f32[80,16]{0,1:T(8,128)S(1)}, f32[80,16]{0,1:T(8,128)S(1)}, u32[]{:S(2)}, u32[]{:S(2)}) %collective-permute-start.14) | collective-permute-done | bytes 5152 | tf_op jit(solution)/shard_map/ppermute | solution.py:41
  49.1 1.4 %collective-permute-start.15 = (f32[80,16]{0,1:T(8,128)S(1)}, f32[80,16]{0,1:T(8,128)S(1)}, u32[]{:S(2)}, u32[]{:S(2)}) collective-permute-start(f32[80,16]{0,1:T(8,128)S(1)} %fusion.54), channel_id=1, source_target_pairs={{0,2},{1,3},{2,0},{3,1},{4,6},{5,7},{6,4},{7,5},{8,10},{9,11},{10,... | collective-permute-start | bytes 15368 | tf_op jit(solution)/shard_map/ppermute | solution.py:41
  50.6 2.2 %collective-permute-done.15 = f32[80,16]{0,1:T(8,128)S(1)} collective-permute-done((f32[80,16]{0,1:T(8,128)S(1)}, f32[80,16]{0,1:T(8,128)S(1)}, u32[]{:S(2)}, u32[]{:S(2)}) %collective-permute-start.15) | collective-permute-done | bytes 5152 | tf_op jit(solution)/shard_map/ppermute | solution.py:41
  53.4 3.1 %collective-permute-done.16 = f32[80,16]{0,1:T(8,128)S(1)} collective-permute-done((f32[80,16]{0,1:T(8,128)S(1)}, f32[80,16]{0,1:T(8,128)S(1)}, u32[]{:S(2)}, u32[]{:S(2)}) %collective-permute-start.16) | collective-permute-done | bytes 5152 | tf_op jit(solution)/shard_map/ppermute | solution.py:41
  56.5 1.6 %collective-permute-start.17 = (f32[80,16]{0,1:T(8,128)S(1)}, f32[80,16]{0,1:T(8,128)S(1)}, u32[]{:S(2)}, u32[]{:S(2)}) collective-permute-start(f32[80,16]{0,1:T(8,128)S(1)} %add.132), channel_id=1, source_target_pairs={{0,8},{1,9},{2,10},{3,11},{4,12},{5,13},{6,14},{7,15},{8,0},{9,1},... | collective-permute-start | bytes 15368 | tf_op jit(solution)/shard_map/ppermute | solution.py:41
  58.0 2.1 %collective-permute-done.17 = f32[80,16]{0,1:T(8,128)S(1)} collective-permute-done((f32[80,16]{0,1:T(8,128)S(1)}, f32[80,16]{0,1:T(8,128)S(1)}, u32[]{:S(2)}, u32[]{:S(2)}) %collective-permute-start.17) | collective-permute-done | bytes 5152 | tf_op jit(solution)/shard_map/ppermute | solution.py:41
  60.1 2.6 %collective-permute-start.18 = (f32[80,16]{0,1:T(8,128)S(1)}, f32[80,16]{0,1:T(8,128)S(1)}, u32[]{:S(2)}, u32[]{:S(2)}) collective-permute-start(f32[80,16]{0,1:T(8,128)S(1)} %add.133), channel_id=1, source_target_pairs={{0,16},{1,17},{2,18},{3,19},{4,20},{5,21},{6,22},{7,23},{8,24},{9,... | collective-permute-start | bytes 15368 | tf_op jit(solution)/shard_map/ppermute | solution.py:41
  62.7 1.9 %collective-permute-done.18 = f32[80,16]{0,1:T(8,128)S(1)} collective-permute-done((f32[80,16]{0,1:T(8,128)S(1)}, f32[80,16]{0,1:T(8,128)S(1)}, u32[]{:S(2)}, u32[]{:S(2)}) %collective-permute-start.18) | collective-permute-done | bytes 5152 | tf_op jit(solution)/shard_map/ppermute | solution.py:41
  66.7 2.6 %shard_map.112 = (f32[16,16]{1,0:T(8,128)}, f32[16,512]{1,0:T(8,128)}) custom-call(f32[16,16]{1,0:T(8,128)S(1)} %get-tuple-element.18.gram_ref, f32[16,512]{1,0:T(8,128)S(1)} %convolution_subtract_fusion.residue_ref), custom_call_target="tpu_custom_call" | custom-call | flops 540672 | bytes 67584 | tf_op jit(solution)/shard_map/pallas_call | solution.py:117
  (65 shorter events, 12.9 us)
Async XLA Ops:
  0.6 42.5 %copy-start = (bf16[3,4,8,128,128]{4,3,2,1,0:T(8,128)(2,1)S(1)}, bf16[3,4,8,128,128]{4,3,2,1,0:T(8,128)(2,1)}, u32[]{:S(2)}) copy-start(bf16[3,4,8,128,128]{4,3,2,1,0:T(8,128)(2,1)} %param.14) | copy-start | bytes 9437188
  1.6 31.7 %collective-permute-start.12 = (bf16[16,512]{1,0:T(8,128)(2,1)S(1)}, bf16[16,512]{1,0:T(8,128)(2,1)S(1)}, u32[]{:S(2)}, u32[]{:S(2)}) collective-permute-start(bf16[16,512]{1,0:T(8,128)(2,1)S(1)} %convert_element_type.20), channel_id=1, source_target_pairs={{0,1},{1,2},{2,3},{3,4},{4,5},{5,6},{6,7},{7,8},{8,9},{9,10},{10,1... | collective-permute-start | bytes 49160 | tf_op jit(solution)/shard_map/ppermute | solution.py:20
  4.1 29.2 %collective-permute-start.13 = (bf16[16,512]{1,0:T(8,128)(2,1)S(1)}, bf16[16,512]{1,0:T(8,128)(2,1)S(1)}, u32[]{:S(2)}, u32[]{:S(2)}) collective-permute-start(bf16[16,512]{1,0:T(8,128)(2,1)S(1)} %convert_element_type.20), channel_id=1, source_target_pairs={{1,0},{2,1},{3,2},{4,3},{5,4},{6,5},{7,6},{8,7},{9,8},{10,9},{11,1... | collective-permute-start | bytes 49160 | tf_op jit(solution)/shard_map/ppermute | solution.py:23
  6.5 10.4 %collective-permute-start.5 = (bf16[1,4,1024]{2,1,0:T(4,128)(2,1)S(1)}, bf16[1,4,1024]{2,1,0:T(4,128)(2,1)S(1)}, u32[]{:S(2)}, u32[]{:S(2)}) collective-permute-start(bf16[1,4,1024]{2,1,0:T(4,128)(2,1)S(1)} %reshape.117), channel_id=1, source_target_pairs={{0,4},{4,0},{8,12},{12,8},{16,20},{20,16},{24,28},{28,24},{1,5},{5... | collective-permute-start | bytes 24584 | tf_op jit(solution)/shard_map/ppermute | solution.py:53
  16.9 3.8 %collective-permute-start.6 = (bf16[2,4,1024]{2,1,0:T(4,128)(2,1)S(1)}, bf16[2,4,1024]{2,1,0:T(4,128)(2,1)S(1)}, u32[]{:S(2)}, u32[]{:S(2)}) collective-permute-start(bf16[2,4,1024]{2,1,0:T(4,128)(2,1)S(1)} %pad_maximum_fusion.3), channel_id=1, source_target_pairs={{0,8},{4,12},{8,0},{12,4},{16,24},{20,28},{24,16},{28,20},{1,9},{5... | collective-permute-start | bytes 49160 | tf_op jit(solution)/shard_map/ppermute | solution.py:53
  20.7 4.9 %collective-permute-start.7 = (bf16[4,4,1024]{2,1,0:T(4,128)(2,1)S(1)}, bf16[4,4,1024]{2,1,0:T(4,128)(2,1)S(1)}, u32[]{:S(2)}, u32[]{:S(2)}) collective-permute-start(bf16[4,4,1024]{2,1,0:T(4,128)(2,1)S(1)} %pad_maximum_fusion.2), channel_id=1, source_target_pairs={{0,16},{4,20},{8,24},{12,28},{16,0},{20,4},{24,8},{28,12},{1,17},{... | collective-permute-start | bytes 98312 | tf_op jit(solution)/shard_map/ppermute | solution.py:53
  25.6 1.3 %collective-permute-start.8 = (bf16[8,4,1024]{2,1,0:T(4,128)(2,1)S(1)}, bf16[8,4,1024]{2,1,0:T(4,128)(2,1)S(1)}, u32[]{:S(2)}, u32[]{:S(2)}) collective-permute-start(bf16[8,4,1024]{2,1,0:T(4,128)(2,1)S(1)} %constant_dynamic-update-slice_fusion), channel_id=1, source_target_pairs={{0,1},{1,0},{2,3},{3,2},{4,5},{5,4},{6,7},{7,6},{8,9},{9,8},{10,11... | collective-permute-start | bytes 196616 | tf_op jit(solution)/shard_map/ppermute | solution.py:53
  27.0 7.5 %collective-permute-start.9 = (bf16[8,8,1024]{2,1,0:T(8,128)(2,1)S(1)}, bf16[8,8,1024]{2,1,0:T(8,128)(2,1)}, u32[]{:S(2)}, u32[]{:S(2)}) collective-permute-start(bf16[8,8,1024]{2,1,0:T(8,128)(2,1)S(1)} %pad_maximum_fusion.1), channel_id=1, source_target_pairs={{0,2},{1,3},{2,0},{3,1},{4,6},{5,7},{6,4},{7,5},{8,10},{9,11},{10,... | collective-permute-start | bytes 393224 | tf_op jit(solution)/shard_map/ppermute | solution.py:53
  36.4 6.8 %copy-start.1 = (bf16[32,16,128]{2,1,0:T(8,128)(2,1)S(1)}, bf16[32,16,128]{2,1,0:T(8,128)(2,1)}, u32[]{:S(2)}) copy-start(bf16[32,16,128]{2,1,0:T(8,128)(2,1)} %gather_fusion.1) | copy-start | bytes 393220
  37.3 10.0 %copy-start.4 = (bf16[4,64,128]{2,1,0:T(8,128)(2,1)S(1)}, bf16[4,64,128]{2,1,0:T(8,128)(2,1)}, u32[]{:S(2)}) copy-start(bf16[4,64,128]{2,1,0:T(8,128)(2,1)} %param.13) | copy-start | bytes 196612
  37.3 10.3 %copy-start.2 = (f32[64,512]{1,0:T(8,128)S(1)}, f32[64,512]{1,0:T(8,128)}, u32[]{:S(2)}) copy-start(f32[64,512]{1,0:T(8,128)} %param.19) | copy-start | bytes 393220
  41.6 4.3 %collective-permute-start.10 = (f32[8,16,64]{2,1,0:T(8,128)S(1)}, f32[8,16,64]{2,1,0:T(8,128)S(1)}, u32[]{:S(2)}, u32[]{:S(2)}) collective-permute-start(f32[8,16,64]{2,1,0:T(8,128)S(1)} %dynamic-slice_bitcast_fusion), channel_id=1, source_target_pairs={{0,2},{1,3},{2,0},{3,1},{4,6},{5,7},{6,4},{7,5},{8,10},{9,11},{10,... | collective-permute-start | bytes 98312 | tf_op jit(solution)/shard_map/ppermute | solution.py:71
  46.0 1.3 %collective-permute-start.11 = (f32[4,16,64]{2,1,0:T(8,128)S(1)}, f32[4,16,64]{2,1,0:T(8,128)S(1)}, u32[]{:S(2)}, u32[]{:S(2)}) collective-permute-start(f32[4,16,64]{2,1,0:T(8,128)S(1)} %dynamic-slice_bitcast_fusion.1), channel_id=1, source_target_pairs={{0,1},{1,0},{2,3},{3,2},{4,5},{5,4},{6,7},{7,6},{8,9},{9,8},{10,11... | collective-permute-start | bytes 49160 | tf_op jit(solution)/shard_map/ppermute | solution.py:71
  47.9 1.2 %collective-permute-start.14 = (f32[80,16]{0,1:T(8,128)S(1)}, f32[80,16]{0,1:T(8,128)S(1)}, u32[]{:S(2)}, u32[]{:S(2)}) collective-permute-start(f32[80,16]{0,1:T(8,128)S(1)} %pad_maximum_fusion.4), channel_id=1, source_target_pairs={{0,1},{1,0},{2,3},{3,2},{4,5},{5,4},{6,7},{7,6},{8,9},{9,8},{10,11... | collective-permute-start | bytes 15368 | tf_op jit(solution)/shard_map/ppermute | solution.py:41
  49.1 3.7 %collective-permute-start.15 = (f32[80,16]{0,1:T(8,128)S(1)}, f32[80,16]{0,1:T(8,128)S(1)}, u32[]{:S(2)}, u32[]{:S(2)}) collective-permute-start(f32[80,16]{0,1:T(8,128)S(1)} %fusion.54), channel_id=1, source_target_pairs={{0,2},{1,3},{2,0},{3,1},{4,6},{5,7},{6,4},{7,5},{8,10},{9,11},{10,... | collective-permute-start | bytes 15368 | tf_op jit(solution)/shard_map/ppermute | solution.py:41
  52.8 3.7 %collective-permute-start.16 = (f32[80,16]{0,1:T(8,128)S(1)}, f32[80,16]{0,1:T(8,128)S(1)}, u32[]{:S(2)}, u32[]{:S(2)}) collective-permute-start(f32[80,16]{0,1:T(8,128)S(1)} %add.131), channel_id=1, source_target_pairs={{0,4},{1,5},{2,6},{3,7},{4,0},{5,1},{6,2},{7,3},{8,12},{9,13},{10,... | collective-permute-start | bytes 15368 | tf_op jit(solution)/shard_map/ppermute | solution.py:41
  56.5 3.7 %collective-permute-start.17 = (f32[80,16]{0,1:T(8,128)S(1)}, f32[80,16]{0,1:T(8,128)S(1)}, u32[]{:S(2)}, u32[]{:S(2)}) collective-permute-start(f32[80,16]{0,1:T(8,128)S(1)} %add.132), channel_id=1, source_target_pairs={{0,8},{1,9},{2,10},{3,11},{4,12},{5,13},{6,14},{7,15},{8,0},{9,1},... | collective-permute-start | bytes 15368 | tf_op jit(solution)/shard_map/ppermute | solution.py:41
  60.1 4.5 %collective-permute-start.18 = (f32[80,16]{0,1:T(8,128)S(1)}, f32[80,16]{0,1:T(8,128)S(1)}, u32[]{:S(2)}, u32[]{:S(2)}) collective-permute-start(f32[80,16]{0,1:T(8,128)S(1)} %add.133), channel_id=1, source_target_pairs={{0,16},{1,17},{2,18},{3,19},{4,20},{5,21},{6,22},{7,23},{8,24},{9,... | collective-permute-start | bytes 15368 | tf_op jit(solution)/shard_map/ppermute | solution.py:41
  64.7 4.6 %copy-start.3 = (f32[80,16]{0,1:T(8,128)}, f32[80,16]{0,1:T(8,128)S(1)}, u32[]{:S(2)}) copy-start(f32[80,16]{0,1:T(8,128)S(1)} %add.134) | copy-start | bytes 15364
